TPU v7x, 128 devices: a whole 4x4x4 slice. The times are simulated.
128 devices in a mesh: task: 4 (over x), ex: 32 (over z, y, core).
Axes of the slice: x: 4, y: 4, z: 4, core: 2. Of those that a mesh axis runs over, the one named last changes fastest.
Arguments:
- feats: bfloat16 [1536, 8, 8, 512], P(('task', 'ex')), may hold values from -25 to 25
- targets: int32 [1536, 64], P(('task', 'ex')), may hold values from 0 to 9
- task_of: int32 [1536], P(('task', 'ex')), may hold values from 0 to 3, as said below
- counts: int32 [4], P('task'), may hold values from 192 to 576, as said below
- down_w: float32 [4, 3, 3, 512, 256], P('task'), may hold values from -0.09375 to 0.09375
- up_w: float32 [4, 256, 512], P('task'), may hold values from -0.375 to 0.375
- head: bfloat16 [512, 10], replicated, may hold values from -0.14941406 to 0.14941406
Outputs:
- down_new: float32 [4, 3, 3, 512, 256], P('task', None, None, 'ex')
- up_new: float32 [4, 256, 512], P('task', 'ex')
- losses: float32 [4, 2], P('task')
Inputs may be any that keep to these rules, and one draw needn't show every extreme that they name: The 12 rows of each device's block of task_of are the examples augmented on that device; each example is trained in the group of its task on the device with the same ex index as the device that holds it. The rows of one device name one task at most 6 times, and some device does so; the devices of one ex index hold together at most 24 examples of one task, and some task reaches that. counts[g] is the number of rows of task_of equal to g; both bounds are reached.
All inputs are finite; a program needn't handle non-finite values.
Results may differ from a plain program's by a relative error of at most 0.002.
Values may be sent and summed in bfloat16 or wider, within the bound.
No kernel may reach another device: no remote copies, remote signals or barrier semaphores. Data moves between devices by JAX's collectives and lax.ppermute only.
A program may use at most 128 MiB of HBM per device.

v0:
```python
import jax
import jax.numpy as jnp
from jax import lax
from jax.sharding import PartitionSpec as P

CHANNELS = 512
INNER = 256
TRAIN_STEPS = 2


def shifted_windows(grids):
    count_rows = grids.shape[0]
    side = grids.shape[1]
    padded = jnp.pad(grids, ((0, 0), (1, 1), (1, 1), (0, 0)))
    windows = []
    for offset_index in range(9):
        row_shift = offset_index // 3
        col_shift = offset_index % 3
        window = padded[:, row_shift : row_shift + side, col_shift : col_shift + side, :]
        windows.append(window.reshape(count_rows * side * side, grids.shape[3]))
    return windows


def contract_rows(left, right):
    return lax.dot_general(
        left, right, (((0,), (0,)), ((), ())), preferred_element_type=jnp.float32
    )


def train_pass(grids, labels, down_low, up_low, head, count):
    windows = shifted_windows(grids)
    flat_rows = windows[0].shape[0]
    middle = jnp.zeros((flat_rows, down_low.shape[3]), jnp.float32)
    for offset_index in range(9):
        middle = middle + jnp.dot(
            windows[offset_index],
            down_low[offset_index // 3, offset_index % 3],
            preferred_element_type=jnp.float32,
        )
    active = jax.nn.silu(middle).astype(jnp.bfloat16)
    hidden = grids.reshape(flat_rows, grids.shape[3]).astype(jnp.float32) + jnp.dot(
        active, up_low, preferred_element_type=jnp.float32
    )
    inverse = lax.rsqrt(jnp.mean(hidden * hidden, axis=-1, keepdims=True) + 1e-06)
    normed = hidden * inverse
    head_wide = head.astype(jnp.float32)
    logits = jnp.dot(
        normed, head_wide, precision=lax.Precision.HIGHEST, preferred_element_type=jnp.float32
    )
    flat_labels = labels.reshape(flat_rows)
    living = (flat_labels >= 0).astype(jnp.float32)
    onehot = (flat_labels[:, None] == jnp.arange(head.shape[1], dtype=jnp.int32)[None, :]).astype(
        jnp.float32
    )
    powers = jnp.exp(logits)
    totals = jnp.sum(powers, axis=-1)
    loss_sum = jnp.sum((jnp.log(totals) - jnp.sum(logits * onehot, axis=-1)) * living)
    dlogits = (powers / totals[:, None] - onehot) * living[:, None] / count
    dnormed = lax.dot_general(
        dlogits,
        head_wide,
        (((1,), (1,)), ((), ())),
        precision=lax.Precision.HIGHEST,
        preferred_element_type=jnp.float32,
    )
    dhidden = (
        inverse * (dnormed - normed * jnp.mean(dnormed * normed, axis=-1, keepdims=True))
    ).astype(jnp.bfloat16)
    grad_up = contract_rows(active, dhidden)
    dactive = lax.dot_general(
        dhidden, up_low, (((1,), (1,)), ((), ())), preferred_element_type=jnp.float32
    )
    sigmoid = jax.nn.sigmoid(middle)
    dmiddle = (dactive * sigmoid * (1.0 + middle * (1.0 - sigmoid))).astype(jnp.bfloat16)
    grad_down = jnp.stack([contract_rows(window, dmiddle) for window in windows])
    grad_down = grad_down.reshape(3, 3, grids.shape[3], down_low.shape[3])
    return (loss_sum, grad_down, grad_up)


def step_scale(squares, entries):
    return 0.004 * lax.rsqrt(squares / entries + 1e-06)


def shards(feats, targets, task_of, counts, down_w, up_w, head):
    groups = lax.axis_size("task")
    peers = lax.axis_size("ex")
    sources = feats.shape[0]
    side = feats.shape[1]
    chans = feats.shape[3]
    cells = side * side
    bucket = (2 * sources + groups - 1) // groups
    holding = 2 * sources
    order = jnp.arange(sources, dtype=jnp.int32)
    earlier = (task_of[:, None] == task_of[None, :]) & (order[None, :] < order[:, None])
    position = jnp.sum(earlier.astype(jnp.int32), axis=1)
    send_feats = (
        jnp.zeros((groups, bucket, side, side, chans), jnp.bfloat16)
        .at[task_of, position]
        .set(feats)
    )
    send_labels = (
        jnp.full((groups, bucket, cells), -1.0, jnp.bfloat16)
        .at[task_of, position]
        .set(targets.astype(jnp.bfloat16))
    )
    come_feats, come_labels = (
        lax.all_to_all(send_feats, "task", split_axis=0, concat_axis=0, tiled=True),
        lax.all_to_all(send_labels, "task", split_axis=0, concat_axis=0, tiled=True),
    )
    come_feats = come_feats.reshape(groups * bucket, side, side, chans)
    come_labels = come_labels.reshape(groups * bucket, cells).astype(jnp.int32)
    present = come_labels[:, 0] >= 0
    slots = jnp.where(present, jnp.cumsum(present.astype(jnp.int32)) - 1, holding)
    held_feats = (
        jnp.zeros((holding, side, side, chans), jnp.bfloat16).at[slots].set(come_feats, mode="drop")
    )
    held_labels = jnp.full((holding, cells), -1, jnp.int32).at[slots].set(come_labels, mode="drop")
    count = counts[0].astype(jnp.float32)
    entries = 10.0 * CHANNELS * INNER
    ex_place = lax.axis_index("ex")
    part_chans = down_w.shape[3] // peers
    part_inner = up_w.shape[1] // peers
    collected = []
    down = down_w[0]
    upper = up_w[0]
    for update_round in range(TRAIN_STEPS):
        loss_sum, grad_down, grad_up = train_pass(
            held_feats,
            held_labels,
            down.astype(jnp.bfloat16),
            upper.astype(jnp.bfloat16),
            head,
            count,
        )
        grad_down, grad_up, loss_total = lax.psum((grad_down, grad_up, loss_sum), "ex")
        scale = step_scale(jnp.sum(grad_down * grad_down) + jnp.sum(grad_up * grad_up), entries)
        down = down - scale * grad_down
        upper = upper - scale * grad_up
        collected.append(loss_total / (count * cells))
    down_own = lax.dynamic_slice_in_dim(down, ex_place * part_chans, part_chans, 2)
    up_own = lax.dynamic_slice_in_dim(upper, ex_place * part_inner, part_inner, 0)
    return (down_own[None], up_own[None], jnp.stack(collected)[None])


def solution(mesh):
    placed = (
        P(("task", "ex"), None, None, None),
        P(("task", "ex"), None),
        P(("task", "ex")),
        P("task"),
        P("task", None, None, None, None),
        P("task", None, None),
        P(),
    )
    return jax.shard_map(
        shards,
        mesh=mesh,
        in_specs=placed,
        out_specs=(P("task", None, None, "ex", None), P("task", "ex", None), P("task", None)),
        check_vma=False,
    )
```

profile of v0, /device:TPU:0, one launch (start us, length us, event | category | flops | bytes accessed | tf_op | source)
XLA Modules:
  0.0 384.4 jit_solution(5709887441990553691)
XLA Ops:
  11.3 4.4 %all-to-all-start = ((bf16[4,2,192]{2,1,0:T(2,128)(2,1)}), bf16[4,2,192]{2,1,0:T(2,128)(2,1)S(1)}, u32[]{:S(2)}, u32[]{:S(2)}) async-start(bf16[4,2,192]{2,1,0:T(2,128)(2,1)} %reshape.167), calls=%async_computation | async-start | bytes 8192 | tf_op jit(solution)/shard_map/all_to_all | solution.py:108
  17.1 2.9 scatter_fusion.1
  21.0 3.7 all-to-all-start.1
  25.4 4.0 %bitcast_convert_fusion = bf16[3,3,512,256]{3,2,1,0:T(8,128)(2,1)} fusion(f32[1,3,3,512,256]{4,3,2,1,0:T(8,128)} %param.11), kind=kLoop, calls=%fused_computation.13 | loop fusion | flops 1179648 | bytes 7077888 | tf_op jit(solution)/shard_map/convert_element_type | solution.py:130
  30.5 14.5 %all-to-all-done.1 = bf16[4,6,8,8,512]{4,3,2,1,0:T(8,128)(2,1)S(1)} async-done(((bf16[4,6,8,8,512]{4,3,2,1,0:T(8,128)(2,1)}), bf16[4,6,8,8,512]{4,3,2,1,0:T(8,128)(2,1)S(1)}, u32[]{:S(2)}, u32[]{:S(2)}) %all-to-all-start.1) | async-done | bytes 1572896 | tf_op jit(solution)/shard_map/all_to_all | solution.py:107
  45.1 1.7 scatter_fusion.2
  46.8 4.6 %pad_slice_fusion = (bf16[24,8,8,512]{3,2,1,0:T(8,128)(2,1)S(1)}, bf16[24,8,8,512]{3,2,1,0:T(8,128)(2,1)}, bf16[24,8,8,512]{3,2,1,0:T(8,128)(2,1)}, bf16[24,8,8,...) fusion(bf16[24,8,8,512]{3,2,1,0:T(8,128)(2,1)S(1)} %scatter_fus, ...), kind=kLoop, calls=%fused_computation.4 | loop fusion | bytes 14155776 | tf_op jit(solution)/shard_map/slice | solution.py:19
  51.4 1.9 copy.16
  53.3 2.1 fusion.29
  55.5 1.7 convolution_add_fusion.15
  68.1 1.6 multiply_reduce_fusion.4
  70.5 1.4 fusion.61
  73.4 1.4 fusion.27
  74.8 1.4 fusion.26
  76.2 12.6 %fusion.25 = f32[9,512,256]{2,1,0:T(8,128)} fusion(f32[9,512,256]{2,1,0:T(8,128)} %fusion.26, bf16[1536,512]{1,0:T(8,128)(2,1)S(1)} %bitcast.278, bf16[1536,256]{1,0:T(8,128)(2,1)S(1)} %fusion.6), kind=kOutput, calls=%fused_computation.87 | convolution fusion | flops 402653184 | bytes 2883584 | tf_op jit(solution)/shard_map/dot_general | solution.py:25
  88.9 1.4 fusion.24
  90.3 1.4 fusion.23
  91.7 1.4 fusion.22
  94.5 1.4 fusion.20
  95.9 1.4 fusion.19
  97.4 114.4 %all-reduce.9.cloned.1.call-done = (f32[3,3,512,256]{3,2,1,0:T(8,128)}, f32[256,512]{1,0:T(8,128)}) async-done(((f32[3,3,512,256]{3,2,1,0:T(8,128)}, f32[256,512]{1,0:T(8,128)}), (f32[3,3,512,256]{3,2,1,0:T(8,128)}, f32[256,512]{1,0:T(8,128)})) %all-reduce.9.cloned.1.call-update) | async-done | bytes 5242896 | tf_op jit(solution)/shard_map/psum | solution.py:135
  211.8 1.8 multiply_reduce_fusion.7
  213.6 4.2 %multiply_reduce_fusion.1 = f32[]{:T(128)} fusion(f32[3,3,512,256]{3,2,1,0:T(8,128)} %get-tuple-element.13), kind=kLoop, calls=%fused_computation.15 | loop fusion | flops 2359295 | bytes 4718596 | tf_op jit(solution)/shard_map/reduce_sum | solution.py:136
  220.4 6.9 %fusion.65 = (bf16[3,3,512,256]{3,2,1,0:T(8,128)(2,1)S(1)}, f32[3,3,512,256]{3,2,1,0:T(8,128)}) fusion(f32[3,3,512,256]{3,2,1,0:T(8,128)} %get-tuple-element.13, f32[]{:T(128)S(6)} %mul.174, f32[1,3,3,512,256]{4,3,2,1,0:T(8,128)} %param.11), kind=kLoop, calls=%fused_computation.178 | loop fusion | flops 3538944 | bytes 16515076 | tf_op jit(solution)/shard_map/convert_element_type | solution.py:130
  240.4 1.7 multiply_reduce_fusion.2
  242.9 1.5 fusion.62
  251.0 2.2 copy-done.16
  254.1 67.0 %all-reduce.1 = (f32[]{:T(128)}, f32[]{:T(128)}) all-reduce(f32[]{:T(128)} %get-tuple-element.8, f32[]{:T(128)} %get-tuple-element.7), channel_id=1, replica_groups=mesh['task'=4,'ex'=32] {'ex'}, use_global_device_ids=true, to_apply=%region_25.26 | all-reduce | flops 2 | bytes 16 | tf_op jit(solution)/shard_map/psum | solution.py:135
  323.0 44.1 %all-reduce.7.cloned.1.call-done = (f32[3,3,512,256]{3,2,1,0:T(8,128)}, f32[256,512]{1,0:T(8,128)}) async-done(((f32[3,3,512,256]{3,2,1,0:T(8,128)}, f32[256,512]{1,0:T(8,128)}), (f32[3,3,512,256]{3,2,1,0:T(8,128)}, f32[256,512]{1,0:T(8,128)})) %all-reduce.7.cloned.1.call-update) | async-done | bytes 5242896 | tf_op jit(solution)/shard_map/psum | solution.py:135
  367.1 1.8 multiply_reduce_fusion.6
  368.8 4.2 %multiply_reduce_fusion = f32[]{:T(128)} fusion(f32[3,3,512,256]{3,2,1,0:T(8,128)} %get-tuple-element.11), kind=kLoop, calls=%fused_computation.14 | loop fusion | flops 2359295 | bytes 4718596 | tf_op jit(solution)/shard_map/reduce_sum | solution.py:136
  375.7 1.7 fusion.30
  (112 shorter events, 46.6 us)
Async XLA Ops:
  7.2 59.7 %copy-start = (bf16[512,10]{0,1:T(8,128)(2,1)S(1)}, bf16[512,10]{0,1:T(8,128)(2,1)}, u32[]{:S(2)}) copy-start(bf16[512,10]{0,1:T(8,128)(2,1)} %param.13) | copy-start | bytes 30724
  7.2 9.9 %copy-start.19 = (bf16[12,8,8,512]{3,2,1,0:T(8,128)(2,1)S(1)}, bf16[12,8,8,512]{3,2,1,0:T(8,128)(2,1)}, u32[]{:S(2)}) copy-start(bf16[12,8,8,512]{3,2,1,0:T(8,128)(2,1)} %param.7) | copy-start | bytes 2359300
  11.3 9.7 %all-to-all-start = ((bf16[4,2,192]{2,1,0:T(2,128)(2,1)}), bf16[4,2,192]{2,1,0:T(2,128)(2,1)S(1)}, u32[]{:S(2)}, u32[]{:S(2)}) async-start(bf16[4,2,192]{2,1,0:T(2,128)(2,1)} %reshape.167), calls=%async_computation | async-start | bytes 8192 | tf_op jit(solution)/shard_map/all_to_all | solution.py:108
  21.0 23.9 %all-to-all-start.1 = ((bf16[4,6,8,8,512]{4,3,2,1,0:T(8,128)(2,1)}), bf16[4,6,8,8,512]{4,3,2,1,0:T(8,128)(2,1)S(1)}, u32[]{:S(2)}, u32[]{:S(2)}) async-start(bf16[4,6,8,8,512]{4,3,2,1,0:T(8,128)(2,1)} %scatter_fusion.1), calls=%async_computation.1 | async-start | bytes 3145728 | tf_op jit(solution)/shard_map/all_to_all | solution.py:107
  24.8 187.0 %all-reduce.9.cloned.1.call-start = ((), (), s32[]{:S(2)}) async-start(), calls=%async_computation.3 | async-start | bytes 10485760 | tf_op jit(solution)/shard_map/psum | solution.py:135
  53.3 2.1 copy-start.11
  55.4 1.7 copy-start.9
  55.5 2.2 copy-start.15
  57.7 1.4 copy-start.7
  59.6 1.4 copy-start.5
  61.1 1.4 copy-start.3
  62.5 1.4 copy-start.1
  64.4 1.4 copy-start.17
  64.5 1.5 copy-start.21
  72.0 1.4 copy-start.13
  97.4 269.7 %all-reduce.7.cloned.1.call-start = ((), (), s32[]{:S(2)}) async-start(), calls=%async_computation.2 | async-start | bytes 10485760 | tf_op jit(solution)/shard_map/psum | solution.py:135
  220.4 24.0 %copy-start.20 = (f32[256,512]{1,0:T(8,128)}, f32[256,512]{1,0:T(8,128)S(1)}, u32[]{:S(2)}) copy-start(f32[256,512]{1,0:T(8,128)S(1)} %bitcast_subtract_fusion.1) | copy-start | bytes 1572868
  220.4 6.9 %copy-start.14 = (bf16[24,8,8,512]{3,2,1,0:T(8,128)(2,1)S(1)}, bf16[24,8,8,512]{3,2,1,0:T(8,128)(2,1)}, u32[]{:S(2)}) copy-start(bf16[24,8,8,512]{3,2,1,0:T(8,128)(2,1)} %get-tuple-element.26) | copy-start | bytes 4718596
  227.2 1.4 copy-start.12
  228.6 1.4 copy-start.10
  230.1 1.4 copy-start.8
  232.0 1.4 copy-start.6
  233.4 1.4 copy-start.4
  234.9 1.4 copy-start.2
  236.8 1.4 copy-start.18
  251.0 2.2 copy-start.16
Sparse Core Ops, SparseCore 0:
  97.5 114.2 all-reduce.8
  253.4 113.6 all-reduce.6
where the time goes:
time: 390 us; the launch traced here: 384 us
  waiting for transfers between devices  174 us (45%)
  blocking collectives  67 us (17%)
  matrix products  54.7 us (14%)
  other arithmetic  32.3 us (8%)
  local copies, waits for them, and re-layouts  28.8 us (7%)
  between operations  19.4 us (5%)
  starting transfers between devices  8.19 us (2%)
    psum x2, waiting for transfers between devices, shards(): lax.psum((grad_down, grad_up, loss_sum), 'ex')  158 us
    psum x1, blocking collectives, shards(): lax.psum((grad_down, grad_up, loss_sum), 'ex')  67 us
    dot_general x20, matrix products, contract_rows(): lax.dot_general(left, right, (((0,), (0,)), ((), ())), preferred_element_...  32.6 us
    all_to_all x1, waiting for transfers between devices, shards(): lax.all_to_all(send_feats, 'task', split_axis=0, concat_axis=0, tiled=True)  14.5 us
    unnamed x46, local copies, waits for them, and re-layouts  14.2 us
    dot_general x18, matrix products, train_pass(): jnp.dot(windows[offset_index], down_low[offset_index // 3, offset_index %...  12.9 us
    convert_element_type x2, other arithmetic, shards(): down.astype(jnp.bfloat16)  10.9 us
    reduce_sum x2, other arithmetic, shards(): jnp.sum(grad_down * grad_down) + jnp.sum(grad_up * grad_up)  8.31 us
  transfers between devices with their start and end apart: 4, of which 4 were waited for; matrix products, arithmetic and copies ran while one was open for 3% of the time, Pallas kernels for 0%

commit v1 on v0

--- a/solution.py
+++ b/solution.py
@@ -107,38 +107,33 @@
         lax.all_to_all(send_feats, "task", split_axis=0, concat_axis=0, tiled=True),
         lax.all_to_all(send_labels, "task", split_axis=0, concat_axis=0, tiled=True),
     )
-    come_feats = come_feats.reshape(groups * bucket, side, side, chans)
-    come_labels = come_labels.reshape(groups * bucket, cells).astype(jnp.int32)
-    present = come_labels[:, 0] >= 0
-    slots = jnp.where(present, jnp.cumsum(present.astype(jnp.int32)) - 1, holding)
-    held_feats = (
-        jnp.zeros((holding, side, side, chans), jnp.bfloat16).at[slots].set(come_feats, mode="drop")
-    )
-    held_labels = jnp.full((holding, cells), -1, jnp.int32).at[slots].set(come_labels, mode="drop")
+    held_feats = come_feats.reshape(groups * bucket, side, side, chans)
+    held_labels = come_labels.reshape(groups * bucket, cells).astype(jnp.int32)
     count = counts[0].astype(jnp.float32)
     entries = 10.0 * CHANNELS * INNER
     ex_place = lax.axis_index("ex")
     part_chans = down_w.shape[3] // peers
     part_inner = up_w.shape[1] // peers
     collected = []
-    down = down_w[0]
-    upper = up_w[0]
+    down_low = down_w[0].astype(jnp.bfloat16)
+    upper_low = up_w[0].astype(jnp.bfloat16)
+    down_own = lax.dynamic_slice_in_dim(down_w[0], ex_place * part_chans, part_chans, 2)
+    up_own = lax.dynamic_slice_in_dim(up_w[0], ex_place * part_inner, part_inner, 0)
     for update_round in range(TRAIN_STEPS):
         loss_sum, grad_down, grad_up = train_pass(
-            held_feats,
-            held_labels,
-            down.astype(jnp.bfloat16),
-            upper.astype(jnp.bfloat16),
-            head,
-            count,
+            held_feats, held_labels, down_low, upper_low, head, count
         )
-        grad_down, grad_up, loss_total = lax.psum((grad_down, grad_up, loss_sum), "ex")
-        scale = step_scale(jnp.sum(grad_down * grad_down) + jnp.sum(grad_up * grad_up), entries)
-        down = down - scale * grad_down
-        upper = upper - scale * grad_up
-        collected.append(loss_total / (count * cells))
-    down_own = lax.dynamic_slice_in_dim(down, ex_place * part_chans, part_chans, 2)
-    up_own = lax.dynamic_slice_in_dim(upper, ex_place * part_inner, part_inner, 0)
+        grad_down = lax.psum_scatter(grad_down, "ex", scatter_dimension=2, tiled=True)
+        grad_up = lax.psum_scatter(grad_up, "ex", scatter_dimension=0, tiled=True)
+        squares = jnp.sum(grad_down * grad_down) + jnp.sum(grad_up * grad_up)
+        totals = lax.psum(jnp.stack([squares, loss_sum]), "ex")
+        scale = step_scale(totals[0], entries)
+        down_own = down_own - scale * grad_down
+        up_own = up_own - scale * grad_up
+        collected.append(totals[1] / (count * cells))
+        if update_round + 1 < TRAIN_STEPS:
+            down_low = lax.all_gather(down_own.astype(jnp.bfloat16), "ex", axis=2, tiled=True)
+            upper_low = lax.all_gather(up_own.astype(jnp.bfloat16), "ex", axis=0, tiled=True)
     return (down_own[None], up_own[None], jnp.stack(collected)[None])
 
 

time: 390 us -> 619 us (1.59)
  waiting for transfers between devices: 174 us -> 332 us
  blocking collectives: 67 us -> 148 us
  other arithmetic: 32.3 us -> 22.3 us
    reduce_scatter x0 -> x4, waiting for transfers between devices: none -> 297 us  [the longest x2 172 us: shards(): lax.psum_scatter(grad_down, 'ex', scatter_dimension=2, tiled=True)]
    psum x2 -> x0, waiting for transfers between devices: 158 us -> none  [shards(): lax.psum((grad_down, grad_up, loss_sum), 'ex')]
    psum x1 -> x2, blocking collectives: 67 us -> 126 us  [shards(): totals = lax.psum(jnp.stack([squares, loss_sum]), 'ex')]
    all_gather x0 -> x1, blocking collectives: none -> 21.9 us  [shards(): lax.all_gather(up_own.astype(jnp.bfloat16), 'ex', axis=0, tiled=True)]
    all_gather x0 -> x1, waiting for transfers between devices: none -> 18.9 us  [shards(): lax.all_gather(down_own.astype(jnp.bfloat16), 'ex', axis=2, tiled=True)]
    dot_general x20, matrix products: 32.6 us -> 24.7 us  [contract_rows(): lax.dot_general(left, right, (((0,), (0,)), ((), ())), preferred_element_...]
    unnamed x46 -> x80, local copies, waits for them, and re-layouts: 14.2 us -> 14.5 us
  transfers between devices with their start and end apart: 4 -> 7, of which waited for: 4 -> 7; matrix products, arithmetic and copies ran while one was open for 3% -> 6% of each run, Pallas kernels for 0% -> 0%
where the time goes in v1:
time: 619 us; the launch traced here: 607 us
  waiting for transfers between devices  332 us (54%)
  blocking collectives  148 us (24%)
  matrix products  50.6 us (8%)
  local copies, waits for them, and re-layouts  25.1 us (4%)
  other arithmetic  22.3 us (4%)
  between operations  20.5 us (3%)
  starting transfers between devices  8.84 us (1%)
    reduce_scatter x2, waiting for transfers between devices, shards(): lax.psum_scatter(grad_down, 'ex', scatter_dimension=2, tiled=True)  172 us
    psum x2, blocking collectives, shards(): totals = lax.psum(jnp.stack([squares, loss_sum]), 'ex')  126 us
    reduce_scatter x2, waiting for transfers between devices, shards(): grad_up = lax.psum_scatter(grad_up, 'ex', scatter_dimension=0, tiled=True)  125 us
    dot_general x20, matrix products, contract_rows(): lax.dot_general(left, right, (((0,), (0,)), ((), ())), preferred_element_...  24.7 us
    all_gather x1, blocking collectives, shards(): lax.all_gather(up_own.astype(jnp.bfloat16), 'ex', axis=0, tiled=True)  21.9 us
    all_gather x1, waiting for transfers between devices, shards(): lax.all_gather(down_own.astype(jnp.bfloat16), 'ex', axis=2, tiled=True)  18.9 us
    all_to_all x1, waiting for transfers between devices, shards(): lax.all_to_all(send_feats, 'task', split_axis=0, concat_axis=0, tiled=True)  15.3 us
    unnamed x80, local copies, waits for them, and re-layouts  14.5 us
  transfers between devices with their start and end apart: 7, of which 7 were waited for; matrix products, arithmetic and copies ran while one was open for 6% of the time, Pallas kernels for 0%

profile of v1, /device:TPU:0, one launch (start us, length us, event | category | flops | bytes accessed | tf_op | source)
XLA Modules:
  0.0 607.4 jit_solution(9756148746571973095)
XLA Ops:
  11.3 4.4 all-to-all-start.1
  17.1 2.9 scatter_fusion
  21.0 3.8 all-to-all-start
  25.5 4.0 convert_bitcast_fusion
  29.6 15.3 %all-to-all-done = bf16[4,6,8,8,512]{4,3,2,1,0:T(8,128)(2,1)S(1)} async-done(((bf16[4,6,8,8,512]{4,3,2,1,0:T(8,128)(2,1)}), bf16[4,6,8,8,512]{4,3,2,1,0:T(8,128)(2,1)S(1)}, u32[]{:S(2)}, u32[]{:S(2)}) %all-to-all-start) | async-done | bytes 1572896 | tf_op jit(solution)/shard_map/all_to_all | solution.py:107
  45.0 1.6 copy.16
  46.5 2.3 pad_slice_fusion
  58.1 1.7 multiply_reduce_fusion.2
  61.8 1.5 fusion.60
  63.2 3.7 fusion.6
  67.4 3.2 fusion.27
  72.0 1.4 fusion.25
  73.4 1.4 fusion.24
  82.7 62.5 %reduce-scatter.7.cloned.1.call-done = f32[8,512]{1,0:T(8,128)} async-done(((f32[256,512]{1,0:T(8,128)}), f32[8,512]{1,0:T(8,128)}) %reduce-scatter.7.cloned.1.call-update) | async-done | bytes 16400 | tf_op jit(solution)/shard_map/reduce_scatter | solution.py:127
  146.5 85.8 %reduce-scatter.5.cloned.1.call-done = f32[3,3,16,256]{3,2,1,0:T(8,128)} async-done(((f32[3,3,512,256]{3,2,1,0:T(8,128)}), f32[3,3,16,256]{3,2,1,0:T(8,128)}) %reduce-scatter.5.cloned.1.call-update) | async-done | bytes 147472 | tf_op jit(solution)/shard_map/reduce_scatter | solution.py:126
  232.4 1.6 multiply_reduce_fusion.5
  235.9 63.1 %psum.14 = f32[2]{0:T(128)S(1)} all-reduce(f32[2]{0:T(128)S(1)} %pad_maximum_fusion), channel_id=1, replica_groups=mesh['task'=4,'ex'=32] {'ex'}, use_global_device_ids=true, to_apply=%region_12.13 | all-reduce | flops 2 | bytes 16 | tf_op jit(solution)/shard_map/psum | solution.py:129
  300.2 1.6 fusion.54
  302.7 21.9 %all_gather.7 = bf16[256,512]{1,0:T(8,128)(2,1)S(1)} all-gather(bf16[8,512]{1,0:T(8,128)(2,1)S(1)} %fusion.56), channel_id=1, replica_groups=mesh['task'=4,'ex'=32] {'ex'}, dimensions={0}, use_global_device_ids=true | all-gather | bytes 270336 | tf_op jit(solution)/shard_map/all_gather | solution.py:136
  324.6 18.9 %all-gather.2.cloned.1.call-done = bf16[3,3,512,256]{3,2,1,0:T(8,128)(2,1)} async-done(((bf16[3,3,16,256]{3,2,1,0:T(8,128)(2,1)}), bf16[3,3,512,256]{3,2,1,0:T(8,128)(2,1)}) %all-gather.2.cloned.1.call-update) | async-done | bytes 2359312 | tf_op jit(solution)/shard_map/all_gather | solution.py:135
  343.5 2.1 fusion.28
  345.6 1.7 convolution_add_fusion.7
  358.1 1.6 multiply_reduce_fusion
  360.6 1.7 fusion.7
  362.3 1.4 fusion.61
  364.0 2.4 fusion.18
  375.3 2.1 copy-done.27
  378.2 62.6 %reduce-scatter.11.cloned.1.call-done = f32[8,512]{1,0:T(8,128)} async-done(((f32[256,512]{1,0:T(8,128)}), f32[8,512]{1,0:T(8,128)}) %reduce-scatter.11.cloned.1.call-update) | async-done | bytes 16400 | tf_op jit(solution)/shard_map/reduce_scatter | solution.py:127
  442.1 85.7 %reduce-scatter.9.cloned.1.call-done = f32[3,3,16,256]{3,2,1,0:T(8,128)} async-done(((f32[3,3,512,256]{3,2,1,0:T(8,128)}), f32[3,3,16,256]{3,2,1,0:T(8,128)}) %reduce-scatter.9.cloned.1.call-update) | async-done | bytes 147472 | tf_op jit(solution)/shard_map/reduce_scatter | solution.py:126
  527.8 1.6 multiply_reduce_fusion.4
  532.0 63.1 %psum.15 = f32[2]{0:T(128)S(1)} all-reduce(f32[2]{0:T(128)S(1)} %pad_maximum_fusion.1), channel_id=1, replica_groups=mesh['task'=4,'ex'=32] {'ex'}, use_global_device_ids=true, to_apply=%region_22.23 | all-reduce | flops 2 | bytes 16 | tf_op jit(solution)/shard_map/psum | solution.py:129
  597.7 1.7 subtract_bitcast_fusion
  (155 shorter events, 56.7 us)
Async XLA Ops:
  7.2 49.7 %copy-start = (bf16[512,10]{0,1:T(8,128)(2,1)S(1)}, bf16[512,10]{0,1:T(8,128)(2,1)}, u32[]{:S(2)}) copy-start(bf16[512,10]{0,1:T(8,128)(2,1)} %param.13) | copy-start | bytes 30724
  7.2 9.9 %copy-start.34 = (bf16[12,8,8,512]{3,2,1,0:T(8,128)(2,1)S(1)}, bf16[12,8,8,512]{3,2,1,0:T(8,128)(2,1)}, u32[]{:S(2)}) copy-start(bf16[12,8,8,512]{3,2,1,0:T(8,128)(2,1)} %param.7) | copy-start | bytes 2359300
  11.3 9.7 %all-to-all-start.1 = ((bf16[4,2,192]{2,1,0:T(2,128)(2,1)}), bf16[4,2,192]{2,1,0:T(2,128)(2,1)S(1)}, u32[]{:S(2)}, u32[]{:S(2)}) async-start(bf16[4,2,192]{2,1,0:T(2,128)(2,1)} %reshape.158), calls=%async_computation.1 | async-start | bytes 8192 | tf_op jit(solution)/shard_map/all_to_all | solution.py:108
  21.0 23.9 %all-to-all-start = ((bf16[4,6,8,8,512]{4,3,2,1,0:T(8,128)(2,1)}), bf16[4,6,8,8,512]{4,3,2,1,0:T(8,128)(2,1)S(1)}, u32[]{:S(2)}, u32[]{:S(2)}) async-start(bf16[4,6,8,8,512]{4,3,2,1,0:T(8,128)(2,1)} %scatter_fusion), calls=%async_computation | async-start | bytes 3145728 | tf_op jit(solution)/shard_map/all_to_all | solution.py:107
  24.8 120.4 %reduce-scatter.7.cloned.1.call-start = ((), (), s32[]{:S(2)}) async-start(), calls=%async_computation.7 | async-start | bytes 540672 | tf_op jit(solution)/shard_map/reduce_scatter | solution.py:127
  46.5 2.4 copy-start.26
  48.9 1.8 copy-start.21
  48.9 2.1 copy-start.25
  48.9 2.6 copy-start.13
  48.9 3.8 copy-start.9
  48.9 4.4 copy-start.5
  48.9 5.0 copy-start.1
  54.5 1.5 copy-start.36
  56.0 4.6 copy-start.29
  67.0 165.4 %reduce-scatter.5.cloned.1.call-start = ((), (), s32[]{:S(2)}) async-start(), calls=%async_computation.6 | async-start | bytes 4866048 | tf_op jit(solution)/shard_map/reduce_scatter | solution.py:126
  67.4 3.2 copy-start.22
  67.4 3.2 copy-start.38
  70.6 1.4 copy-start.18
  72.0 1.4 copy-start.14
  76.3 1.4 copy-start.6
  77.7 1.4 copy-start.2
  81.9 261.5 %all-gather.2.cloned.1.call-start = ((), (), s32[]{:S(2)}) async-start(), calls=%async_computation.8 | async-start | bytes 2433024 | tf_op jit(solution)/shard_map/all_gather | solution.py:135
  301.9 138.9 %reduce-scatter.11.cloned.1.call-start = ((), (), s32[]{:S(2)}) async-start(), calls=%async_computation.10 | async-start | bytes 540672 | tf_op jit(solution)/shard_map/reduce_scatter | solution.py:127
  343.5 2.1 copy-start.23
  345.6 1.7 copy-start.19
  345.6 2.2 copy-start.28
  363.7 164.1 %reduce-scatter.9.cloned.1.call-start = ((), (), s32[]{:S(2)}) async-start(), calls=%async_computation.9 | async-start | bytes 4866048 | tf_op jit(solution)/shard_map/reduce_scatter | solution.py:126
  364.0 2.4 copy-start.24
  364.0 2.4 copy-start.37
  375.3 2.1 copy-start.27
  377.4 220.2 %copy-start.33 = (f32[3,3,16,256]{3,2,1,0:T(8,128)S(1)}, f32[3,3,16,256]{3,2,1,0:T(8,128)}, u32[]{:S(2)}) copy-start(f32[3,3,16,256]{3,2,1,0:T(8,128)} %reduce-scatter.5.cloned.1.call-done) | copy-start | bytes 442372
  377.4 221.9 %copy-start.35 = (f32[8,512]{1,0:T(8,128)S(1)}, f32[8,512]{1,0:T(8,128)}, u32[]{:S(2)}) copy-start(f32[8,512]{1,0:T(8,128)} %reduce-scatter.7.cloned.1.call-done) | copy-start | bytes 49156
  (14 other events, 19.3 us)
Sparse Core Ops, SparseCore 0:
  67.1 78.0 reduce-scatter.6
  148.9 83.4 reduce-scatter.4
  302.0 41.3 all-gather.1
  363.9 76.8 reduce-scatter.10
  444.4 83.3 reduce-scatter.8

commit v2 on v1

--- a/solution.py
+++ b/solution.py
@@ -81,15 +81,34 @@
     return 0.004 * lax.rsqrt(squares / entries + 1e-06)
 
 
+def partner_swap(value, bit, peers):
+    return lax.ppermute(value, "ex", perm=[(i, i ^ (1 << bit)) for i in range(peers)])
+
+
+def halve_sum(value, axis, bit, place, peers):
+    mine = (place >> bit) & 1
+    keep = lax.dynamic_index_in_dim(value, mine, axis, keepdims=False)
+    give = lax.dynamic_index_in_dim(value, 1 - mine, axis, keepdims=False)
+    return keep + partner_swap(give, bit, peers)
+
+
+def double_join(value, axis, bit, place, peers):
+    mine = (place >> bit) & 1
+    other = partner_swap(value, bit, peers)
+    first = jnp.where(mine == 0, value, other)
+    second = jnp.where(mine == 0, other, value)
+    return jnp.stack([first, second], axis=axis)
+
+
 def shards(feats, targets, task_of, counts, down_w, up_w, head):
     groups = lax.axis_size("task")
     peers = lax.axis_size("ex")
+    levels = peers.bit_length() - 1
     sources = feats.shape[0]
     side = feats.shape[1]
     chans = feats.shape[3]
     cells = side * side
     bucket = (2 * sources + groups - 1) // groups
-    holding = 2 * sources
     order = jnp.arange(sources, dtype=jnp.int32)
     earlier = (task_of[:, None] == task_of[None, :]) & (order[None, :] < order[:, None])
     position = jnp.sum(earlier.astype(jnp.int32), axis=1)
@@ -111,29 +130,41 @@
     held_labels = come_labels.reshape(groups * bucket, cells).astype(jnp.int32)
     count = counts[0].astype(jnp.float32)
     entries = 10.0 * CHANNELS * INNER
-    ex_place = lax.axis_index("ex")
+    place = lax.axis_index("ex")
     part_chans = down_w.shape[3] // peers
     part_inner = up_w.shape[1] // peers
+    inner = down_w.shape[4]
     collected = []
     down_low = down_w[0].astype(jnp.bfloat16)
     upper_low = up_w[0].astype(jnp.bfloat16)
-    down_own = lax.dynamic_slice_in_dim(down_w[0], ex_place * part_chans, part_chans, 2)
-    up_own = lax.dynamic_slice_in_dim(up_w[0], ex_place * part_inner, part_inner, 0)
+    down_own = lax.dynamic_slice_in_dim(down_w[0], place * part_chans, part_chans, 2)
+    up_own = lax.dynamic_slice_in_dim(up_w[0], place * part_inner, part_inner, 0)
+    bits_shape = (2,) * levels
     for update_round in range(TRAIN_STEPS):
         loss_sum, grad_down, grad_up = train_pass(
             held_feats, held_labels, down_low, upper_low, head, count
         )
-        grad_down = lax.psum_scatter(grad_down, "ex", scatter_dimension=2, tiled=True)
-        grad_up = lax.psum_scatter(grad_up, "ex", scatter_dimension=0, tiled=True)
+        grad_down = grad_down.reshape((3, 3) + bits_shape + (part_chans, inner))
+        grad_up = grad_up.reshape(bits_shape + (part_inner, up_w.shape[2]))
+        for bit in range(levels):
+            grad_down = halve_sum(grad_down, 2 + levels - 1 - bit, bit, place, peers)
+            grad_up = halve_sum(grad_up, levels - 1 - bit, bit, place, peers)
         squares = jnp.sum(grad_down * grad_down) + jnp.sum(grad_up * grad_up)
-        totals = lax.psum(jnp.stack([squares, loss_sum]), "ex")
+        totals = jnp.stack([squares, loss_sum])
+        for bit in range(levels):
+            totals = totals + partner_swap(totals, bit, peers)
         scale = step_scale(totals[0], entries)
         down_own = down_own - scale * grad_down
         up_own = up_own - scale * grad_up
         collected.append(totals[1] / (count * cells))
         if update_round + 1 < TRAIN_STEPS:
-            down_low = lax.all_gather(down_own.astype(jnp.bfloat16), "ex", axis=2, tiled=True)
-            upper_low = lax.all_gather(up_own.astype(jnp.bfloat16), "ex", axis=0, tiled=True)
+            down_low = down_own.astype(jnp.bfloat16)
+            upper_low = up_own.astype(jnp.bfloat16)
+            for step_index, bit in enumerate(reversed(range(levels))):
+                down_low = double_join(down_low, 2 + step_index, bit, place, peers)
+                upper_low = double_join(upper_low, step_index, bit, place, peers)
+            down_low = down_low.reshape(down_w.shape[1:])
+            upper_low = upper_low.reshape(up_w.shape[1:])
     return (down_own[None], up_own[None], jnp.stack(collected)[None])
 
 

time: 619 us -> 350 us (0.57); the launches traced: 607 us -> 346 us
  waiting for transfers between devices: 332 us -> 159 us
  blocking collectives: 148 us -> 0 us
  starting transfers between devices: 8.84 us -> 72.7 us
  matrix products: 50.6 us -> 33.1 us
  other arithmetic: 22.3 us -> 39.3 us
  between operations: 20.5 us -> 8.13 us
  local copies, waits for them, and re-layouts: 25.1 us -> 33.3 us
    reduce_scatter x4 -> x0, waiting for transfers between devices: 297 us -> none  [the longest x2 172 us: shards(): lax.psum_scatter(grad_down, 'ex', scatter_dimension=2, tiled=True)]
    ppermute x0 -> x40, waiting for transfers between devices: none -> 143 us  [partner_swap(): lax.ppermute(value, 'ex', perm=[(i, i ^ 1 << bit) for i in range(peers)])]
    psum x2 -> x0, blocking collectives: 126 us -> none  [shards(): totals = lax.psum(jnp.stack([squares, loss_sum]), 'ex')]
    ppermute x0 -> x40, starting transfers between devices: none -> 64.5 us  [partner_swap(): lax.ppermute(value, 'ex', perm=[(i, i ^ 1 << bit) for i in range(peers)])]
    all_gather x1 -> x0, blocking collectives: 21.9 us -> none  [shards(): lax.all_gather(up_own.astype(jnp.bfloat16), 'ex', axis=0, tiled=True)]
    all_gather x1 -> x0, waiting for transfers between devices: 18.9 us -> none  [shards(): lax.all_gather(down_own.astype(jnp.bfloat16), 'ex', axis=2, tiled=True)]
    add x0 -> x26, other arithmetic: none -> 13.5 us  [the longest x16 10.6 us: halve_sum(): return keep + partner_swap(give, bit, peers)]
    dot_general x20, matrix products: 24.7 us -> 13 us  [contract_rows(): lax.dot_general(left, right, (((0,), (0,)), ((), ())), preferred_element_...]
  transfers between devices with their start and end apart: 7 -> 42, of which waited for: 7 -> 34; matrix products, arithmetic and copies ran while one was open for 6% -> 7% of each run, Pallas kernels for 0% -> 0%
where the time goes in v2:
time: 350 us; the launch traced here: 346 us
  waiting for transfers between devices  159 us (45%)
  starting transfers between devices  72.7 us (21%)
  other arithmetic  39.3 us (11%)
  local copies, waits for them, and re-layouts  33.3 us (10%)
  matrix products  33.1 us (9%)
  between operations  8.13 us (2%)
    ppermute x40, waiting for transfers between devices, partner_swap(): lax.ppermute(value, 'ex', perm=[(i, i ^ 1 << bit) for i in range(peers)])  143 us
    ppermute x40, starting transfers between devices, partner_swap(): lax.ppermute(value, 'ex', perm=[(i, i ^ 1 << bit) for i in range(peers)])  64.5 us
    all_to_all x1, waiting for transfers between devices, shards(): lax.all_to_all(send_feats, 'task', split_axis=0, concat_axis=0, tiled=True)  15.4 us
    unnamed x96, local copies, waits for them, and re-layouts  13.2 us
    dot_general x20, matrix products, contract_rows(): lax.dot_general(left, right, (((0,), (0,)), ((), ())), preferred_element_...  13 us
    add x16, other arithmetic, halve_sum(): return keep + partner_swap(give, bit, peers)  10.6 us
    dot_general x18, matrix products, train_pass(): jnp.dot(windows[offset_index], down_low[offset_index // 3, offset_index %...  10.4 us
    another operation x20, other arithmetic, double_join(): return jnp.stack([first, second], axis=axis)  8.18 us
  transfers between devices with their start and end apart: 42, of which 34 were waited for; matrix products, arithmetic and copies ran while one was open for 7% of the time, Pallas kernels for 0%

profile of v2, /device:TPU:0, one launch (start us, length us, event | category | flops | bytes accessed | tf_op | source)
XLA Modules:
  0.0 346.0 jit_solution(6309278071356631099)
XLA Ops:
  4.8 4.4 %all-to-all-start.1 = ((bf16[4,2,192]{2,1,0:T(2,128)(2,1)}), bf16[4,2,192]{2,1,0:T(2,128)(2,1)S(1)}, u32[]{:S(2)}, u32[]{:S(2)}) async-start(bf16[4,2,192]{2,1,0:T(2,128)(2,1)} %reshape.166), calls=%async_computation.1 | async-start | bytes 8192 | tf_op jit(solution)/shard_map/all_to_all | solution.py:127
  10.5 3.0 scatter_fusion
  14.5 3.8 %all-to-all-start = ((bf16[4,6,8,8,512]{4,3,2,1,0:T(8,128)(2,1)}), bf16[4,6,8,8,512]{4,3,2,1,0:T(8,128)(2,1)S(1)}, u32[]{:S(2)}, u32[]{:S(2)}) async-start(bf16[4,6,8,8,512]{4,3,2,1,0:T(8,128)(2,1)} %scatter_fusion), calls=%async_computation | async-start | bytes 3145728 | tf_op jit(solution)/shard_map/all_to_all | solution.py:126
  19.0 4.0 %convert_bitcast_fusion = bf16[3,3,512,256]{3,2,1,0:T(8,128)(2,1)} fusion(f32[1,3,3,512,256]{4,3,2,1,0:T(8,128)} %param.11), kind=kLoop, calls=%fused_computation.49 | loop fusion | flops 1179648 | bytes 7077888 | tf_op jit(solution)/shard_map/convert_element_type | solution.py:138
  23.2 15.4 %all-to-all-done = bf16[4,6,8,8,512]{4,3,2,1,0:T(8,128)(2,1)S(1)} async-done(((bf16[4,6,8,8,512]{4,3,2,1,0:T(8,128)(2,1)}), bf16[4,6,8,8,512]{4,3,2,1,0:T(8,128)(2,1)S(1)}, u32[]{:S(2)}, u32[]{:S(2)}) %all-to-all-start) | async-done | bytes 1572896 | tf_op jit(solution)/shard_map/all_to_all | solution.py:126
  65.3 4.9 %collective-permute-done = f32[3,3,2,2,2,2,16,256]{7,6,4,3,2,1,0,5:T(8,128)} collective-permute-done((f32[3,3,2,2,2,2,16,256]{7,6,4,3,2,1,0,5:T(8,128)}, f32[3,3,2,2,2,2,16,256]{7,6,4,3,2,1,0,5:T(8,128)}, u32[]{:S(2)}, u32[]{:S(2)}) %collective-permute-start) | collective-permute-done | bytes 2359328 | tf_op jit(solution)/shard_map/ppermute | solution.py:85
  70.2 3.0 bitcast_add_fusion.1
  79.8 25.7 %collective-permute-done.6 = f32[2,2,2,8,512]{4,3,2,1,0:T(8,128)} collective-permute-done((f32[2,2,2,8,512]{4,3,2,1,0:T(8,128)S(1)}, f32[2,2,2,8,512]{4,3,2,1,0:T(8,128)}, u32[]{:S(2)}, u32[]{:S(2)}) %collective-permute-start.6) | collective-permute-done | bytes 131104 | tf_op jit(solution)/shard_map/ppermute | solution.py:85
  110.3 3.1 collective-permute-start.2
  114.5 13.4 %collective-permute-done.7 = f32[2,2,8,512]{3,2,1,0:T(8,128)S(1)} collective-permute-done((f32[2,2,8,512]{3,2,1,0:T(8,128)S(1)}, f32[2,2,8,512]{3,2,1,0:T(8,128)S(1)}, u32[]{:S(2)}, u32[]{:S(2)}) %collective-permute-start.7) | collective-permute-done | bytes 65568 | tf_op jit(solution)/shard_map/ppermute | solution.py:85
  132.0 3.9 %collective-permute-start.9 = (f32[8,512]{1,0:T(8,128)S(1)}, f32[8,512]{1,0:T(8,128)S(1)}, u32[]{:S(2)}, u32[]{:S(2)}) collective-permute-start(f32[8,512]{1,0:T(8,128)S(1)} %dynamic-slice_bitcast_fusion.14), channel_id=1, source_target_pairs={{0,16},{1,17},{2,18},{3,19},{4,20},{5,21},{6,22},{7,23},{8,24},{9,... | collective-permute-start | bytes 49160 | tf_op jit(solution)/shard_map/ppermute | solution.py:85
  135.9 2.8 collective-permute-done.3
  138.8 4.1 %collective-permute-start.4 = (f32[3,3,16,256]{3,2,1,0:T(8,128)S(1)}, f32[3,3,16,256]{3,2,1,0:T(8,128)S(1)}, u32[]{:S(2)}, u32[]{:S(2)}) collective-permute-start(f32[3,3,16,256]{3,2,1,0:T(8,128)S(1)} %dynamic-slice_bitcast_fusion.6), channel_id=1, source_target_pairs={{0,16},{1,17},{2,18},{3,19},{4,20},{5,21},{6,22},{7,23},{8,24},{9,... | collective-permute-start | bytes 442376 | tf_op jit(solution)/shard_map/ppermute | solution.py:85
  155.6 3.0 collective-permute-start.12
  160.9 3.4 collective-permute-done.13
  164.3 3.5 %collective-permute-start.14 = (f32[2]{0:T(128)S(1)}, f32[2]{0:T(128)S(1)}, u32[]{:S(2)}, u32[]{:S(2)}) collective-permute-start(f32[2]{0:T(128)S(1)} %add.326), channel_id=1, source_target_pairs={{0,16},{1,17},{2,18},{3,19},{4,20},{5,21},{6,22},{7,23},{8,24},{9,... | collective-permute-start | bytes 32 | tf_op jit(solution)/shard_map/ppermute | solution.py:85
  172.4 3.5 %collective-permute-start.15 = (bf16[3,3,16,256]{3,2,1,0:T(8,128)(2,1)S(1)}, bf16[3,3,16,256]{3,2,1,0:T(8,128)(2,1)S(1)}, u32[]{:S(2)}, u32[]{:S(2)}) collective-permute-start(bf16[3,3,16,256]{3,2,1,0:T(8,128)(2,1)S(1)} %get-tuple-element.7), channel_id=1, source_target_pairs={{0,16},{1,17},{2,18},{3,19},{4,20},{5,21},{6,22},{7,23},{8,24},{9,... | collective-permute-start | bytes 221192 | tf_op jit(solution)/shard_map/ppermute | solution.py:85
  175.9 2.9 collective-permute-done.15
  178.9 5.2 %collective-permute-done.16 = bf16[3,3,2,16,256]{4,3,2,1,0:T(8,128)(2,1)} collective-permute-done((bf16[3,3,2,16,256]{4,3,2,1,0:T(8,128)(2,1)S(1)}, bf16[3,3,2,16,256]{4,3,2,1,0:T(8,128)(2,1)}, u32[]{:S(2)}, u32[]{:S(2)}) %collective-permute-start.16) | collective-permute-done | bytes 147488 | tf_op jit(solution)/shard_map/ppermute | solution.py:85
  189.3 3.4 collective-permute-start.20
  197.5 2.8 collective-permute-start.18
  200.4 3.7 %collective-permute-done.21 = bf16[2,8,512]{2,1,0:T(8,128)(2,1)S(1)} collective-permute-done((bf16[2,8,512]{2,1,0:T(8,128)(2,1)S(1)}, bf16[2,8,512]{2,1,0:T(8,128)(2,1)S(1)}, u32[]{:S(2)}, u32[]{:S(2)}) %collective-permute-start.21) | collective-permute-done | bytes 16416 | tf_op jit(solution)/shard_map/ppermute | solution.py:85
  204.2 3.8 %collective-permute-start.22 = (bf16[2,2,8,512]{3,2,1,0:T(8,128)(2,1)S(1)}, bf16[2,2,8,512]{3,2,1,0:T(8,128)(2,1)S(1)}, u32[]{:S(2)}, u32[]{:S(2)}) collective-permute-start(bf16[2,2,8,512]{3,2,1,0:T(8,128)(2,1)S(1)} %pad_maximum_fusion.8), channel_id=1, source_target_pairs={{0,4},{1,5},{2,6},{3,7},{4,0},{5,1},{6,2},{7,3},{8,12},{9,13},{10,... | collective-permute-start | bytes 98312 | tf_op jit(solution)/shard_map/ppermute | solution.py:85
  213.1 3.7 %collective-permute-done.23 = bf16[2,2,2,8,512]{4,3,2,1,0:T(8,128)(2,1)S(1)} collective-permute-done((bf16[2,2,2,8,512]{4,3,2,1,0:T(8,128)(2,1)S(1)}, bf16[2,2,2,8,512]{4,3,2,1,0:T(8,128)(2,1)S(1)}, u32[]{:S(2)}, u32[]{:S(2)}) %collective-permute-start.23) | collective-permute-done | bytes 65568 | tf_op jit(solution)/shard_map/ppermute | solution.py:85
  245.7 4.4 %collective-permute-done.25 = f32[3,3,2,2,2,2,16,256]{7,6,4,3,2,1,0,5:T(8,128)S(1)} collective-permute-done((f32[3,3,2,2,2,2,16,256]{7,6,4,3,2,1,0,5:T(8,128)S(1)}, f32[3,3,2,2,2,2,16,256]{7,6,4,3,2,1,0,5:T(8,128)S(1)}, u32[]{:S(2)}, u32[]{:S(2)}) %collective-permute-start.25) | collective-permute-done | bytes 2359328 | tf_op jit(solution)/shard_map/ppermute | solution.py:85
  257.1 25.9 %collective-permute-done.31 = f32[2,2,2,8,512]{4,3,2,1,0:T(8,128)S(1)} collective-permute-done((f32[2,2,2,8,512]{4,3,2,1,0:T(8,128)S(1)}, f32[2,2,2,8,512]{4,3,2,1,0:T(8,128)S(1)}, u32[]{:S(2)}, u32[]{:S(2)}) %collective-permute-start.31) | collective-permute-done | bytes 131104 | tf_op jit(solution)/shard_map/ppermute | solution.py:85
  285.6 2.8 collective-permute-start.27
  289.3 13.8 %collective-permute-done.32 = f32[2,2,8,512]{3,2,1,0:T(8,128)S(1)} collective-permute-done((f32[2,2,8,512]{3,2,1,0:T(8,128)S(1)}, f32[2,2,8,512]{3,2,1,0:T(8,128)S(1)}, u32[]{:S(2)}, u32[]{:S(2)}) %collective-permute-start.32) | collective-permute-done | bytes 65568 | tf_op jit(solution)/shard_map/ppermute | solution.py:85
  307.5 3.0 collective-permute-start.34
  312.6 3.0 collective-permute-start.29
  328.2 2.9 collective-permute-start.37
  336.9 3.0 collective-permute-start.39
  (304 shorter events, 148.7 us)
Async XLA Ops:
  4.8 9.7 %all-to-all-start.1 = ((bf16[4,2,192]{2,1,0:T(2,128)(2,1)}), bf16[4,2,192]{2,1,0:T(2,128)(2,1)S(1)}, u32[]{:S(2)}, u32[]{:S(2)}) async-start(bf16[4,2,192]{2,1,0:T(2,128)(2,1)} %reshape.166), calls=%async_computation.1 | async-start | bytes 8192 | tf_op jit(solution)/shard_map/all_to_all | solution.py:127
  14.5 24.0 %all-to-all-start = ((bf16[4,6,8,8,512]{4,3,2,1,0:T(8,128)(2,1)}), bf16[4,6,8,8,512]{4,3,2,1,0:T(8,128)(2,1)S(1)}, u32[]{:S(2)}, u32[]{:S(2)}) async-start(bf16[4,6,8,8,512]{4,3,2,1,0:T(8,128)(2,1)} %scatter_fusion), calls=%async_computation | async-start | bytes 3145728 | tf_op jit(solution)/shard_map/all_to_all | solution.py:126
  65.3 4.9 %collective-permute-start = (f32[3,3,2,2,2,2,16,256]{7,6,4,3,2,1,0,5:T(8,128)}, f32[3,3,2,2,2,2,16,256]{7,6,4,3,2,1,0,5:T(8,128)}, u32[]{:S(2)}, u32[]{:S(2)}) collective-permute-start(f32[3,3,2,2,2,2,16,256]{7,6,4,3,2,1,0,5:T(8,128)} %bitcast.407), channel_id=1, source_target_pairs={{0,1},{1,0},{2,3},{3,2},{4,5},{5,4},{6,7},{7,6},{8,9},{9,8},{10,11... | collective-permute-start | bytes 7077896 | tf_op jit(solution)/shard_map/ppermute | solution.py:85
  74.4 32.1 %collective-permute-start.1 = (f32[3,3,2,2,2,16,256]{6,5,4,3,2,1,0:T(8,128)}, f32[3,3,2,2,2,16,256]{6,5,4,3,2,1,0:T(8,128)}, u32[]{:S(2)}, u32[]{:S(2)}) collective-permute-start(f32[3,3,2,2,2,16,256]{6,5,4,3,2,1,0:T(8,128)} %dynamic-slice_bitcast_fusion.1), channel_id=1, source_target_pairs={{0,2},{1,3},{2,0},{3,1},{4,6},{5,7},{6,4},{7,5},{8,10},{9,11},{10,... | collective-permute-start | bytes 3538952 | tf_op jit(solution)/shard_map/ppermute | solution.py:85
  78.4 27.2 %collective-permute-start.6 = (f32[2,2,2,8,512]{4,3,2,1,0:T(8,128)S(1)}, f32[2,2,2,8,512]{4,3,2,1,0:T(8,128)}, u32[]{:S(2)}, u32[]{:S(2)}) collective-permute-start(f32[2,2,2,8,512]{4,3,2,1,0:T(8,128)S(1)} %dynamic-slice_bitcast_fusion.8), channel_id=1, source_target_pairs={{0,2},{1,3},{2,0},{3,1},{4,6},{5,7},{6,4},{7,5},{8,10},{9,11},{10,... | collective-permute-start | bytes 393224 | tf_op jit(solution)/shard_map/ppermute | solution.py:85
  110.3 19.6 %collective-permute-start.2 = (f32[3,3,2,2,16,256]{5,4,3,2,1,0:T(8,128)}, f32[3,3,2,2,16,256]{5,4,3,2,1,0:T(8,128)}, u32[]{:S(2)}, u32[]{:S(2)}) collective-permute-start(f32[3,3,2,2,16,256]{5,4,3,2,1,0:T(8,128)} %dynamic-slice_bitcast_fusion.3), channel_id=1, source_target_pairs={{0,4},{1,5},{2,6},{3,7},{4,0},{5,1},{6,2},{7,3},{8,12},{9,13},{10,... | collective-permute-start | bytes 1769480 | tf_op jit(solution)/shard_map/ppermute | solution.py:85
  113.4 14.5 %collective-permute-start.7 = (f32[2,2,8,512]{3,2,1,0:T(8,128)S(1)}, f32[2,2,8,512]{3,2,1,0:T(8,128)S(1)}, u32[]{:S(2)}, u32[]{:S(2)}) collective-permute-start(f32[2,2,8,512]{3,2,1,0:T(8,128)S(1)} %dynamic-slice_bitcast_fusion.10), channel_id=1, source_target_pairs={{0,4},{1,5},{2,6},{3,7},{4,0},{5,1},{6,2},{7,3},{8,12},{9,13},{10,... | collective-permute-start | bytes 196616 | tf_op jit(solution)/shard_map/ppermute | solution.py:85
  128.0 4.0 %collective-permute-start.8 = (f32[2,8,512]{2,1,0:T(8,128)S(1)}, f32[2,8,512]{2,1,0:T(8,128)S(1)}, u32[]{:S(2)}, u32[]{:S(2)}) collective-permute-start(f32[2,8,512]{2,1,0:T(8,128)S(1)} %dynamic-slice_bitcast_fusion.12), channel_id=1, source_target_pairs={{0,8},{1,9},{2,10},{3,11},{4,12},{5,13},{6,14},{7,15},{8,0},{9,1},... | collective-permute-start | bytes 98312 | tf_op jit(solution)/shard_map/ppermute | solution.py:85
  131.3 7.4 %collective-permute-start.3 = (f32[3,3,2,16,256]{4,3,2,1,0:T(8,128)S(1)}, f32[3,3,2,16,256]{4,3,2,1,0:T(8,128)S(1)}, u32[]{:S(2)}, u32[]{:S(2)}) collective-permute-start(f32[3,3,2,16,256]{4,3,2,1,0:T(8,128)S(1)} %dynamic-slice_bitcast_fusion.4), channel_id=1, source_target_pairs={{0,8},{1,9},{2,10},{3,11},{4,12},{5,13},{6,14},{7,15},{8,0},{9,1},... | collective-permute-start | bytes 884744 | tf_op jit(solution)/shard_map/ppermute | solution.py:85
  132.0 11.5 %collective-permute-start.9 = (f32[8,512]{1,0:T(8,128)S(1)}, f32[8,512]{1,0:T(8,128)S(1)}, u32[]{:S(2)}, u32[]{:S(2)}) collective-permute-start(f32[8,512]{1,0:T(8,128)S(1)} %dynamic-slice_bitcast_fusion.14), channel_id=1, source_target_pairs={{0,16},{1,17},{2,18},{3,19},{4,20},{5,21},{6,22},{7,23},{8,24},{9,... | collective-permute-start | bytes 49160 | tf_op jit(solution)/shard_map/ppermute | solution.py:85
  138.8 7.2 %collective-permute-start.4 = (f32[3,3,16,256]{3,2,1,0:T(8,128)S(1)}, f32[3,3,16,256]{3,2,1,0:T(8,128)S(1)}, u32[]{:S(2)}, u32[]{:S(2)}) collective-permute-start(f32[3,3,16,256]{3,2,1,0:T(8,128)S(1)} %dynamic-slice_bitcast_fusion.6), channel_id=1, source_target_pairs={{0,16},{1,17},{2,18},{3,19},{4,20},{5,21},{6,22},{7,23},{8,24},{9,... | collective-permute-start | bytes 442376 | tf_op jit(solution)/shard_map/ppermute | solution.py:85
  155.6 5.1 %collective-permute-start.12 = (f32[2]{0:T(128)S(1)}, f32[2]{0:T(128)S(1)}, u32[]{:S(2)}, u32[]{:S(2)}) collective-permute-start(f32[2]{0:T(128)S(1)} %fusion.131), channel_id=1, source_target_pairs={{0,4},{1,5},{2,6},{3,7},{4,0},{5,1},{6,2},{7,3},{8,12},{9,13},{10,... | collective-permute-start | bytes 32 | tf_op jit(solution)/shard_map/ppermute | solution.py:85
  164.3 5.1 %collective-permute-start.14 = (f32[2]{0:T(128)S(1)}, f32[2]{0:T(128)S(1)}, u32[]{:S(2)}, u32[]{:S(2)}) collective-permute-start(f32[2]{0:T(128)S(1)} %add.326), channel_id=1, source_target_pairs={{0,16},{1,17},{2,18},{3,19},{4,20},{5,21},{6,22},{7,23},{8,24},{9,... | collective-permute-start | bytes 32 | tf_op jit(solution)/shard_map/ppermute | solution.py:85
  172.4 6.4 %collective-permute-start.15 = (bf16[3,3,16,256]{3,2,1,0:T(8,128)(2,1)S(1)}, bf16[3,3,16,256]{3,2,1,0:T(8,128)(2,1)S(1)}, u32[]{:S(2)}, u32[]{:S(2)}) collective-permute-start(bf16[3,3,16,256]{3,2,1,0:T(8,128)(2,1)S(1)} %get-tuple-element.7), channel_id=1, source_target_pairs={{0,16},{1,17},{2,18},{3,19},{4,20},{5,21},{6,22},{7,23},{8,24},{9,... | collective-permute-start | bytes 221192 | tf_op jit(solution)/shard_map/ppermute | solution.py:85
  178.8 5.3 %collective-permute-start.16 = (bf16[3,3,2,16,256]{4,3,2,1,0:T(8,128)(2,1)S(1)}, bf16[3,3,2,16,256]{4,3,2,1,0:T(8,128)(2,1)}, u32[]{:S(2)}, u32[]{:S(2)}) collective-permute-start(bf16[3,3,2,16,256]{4,3,2,1,0:T(8,128)(2,1)S(1)} %pad_maximum_fusion.5), channel_id=1, source_target_pairs={{0,8},{1,9},{2,10},{3,11},{4,12},{5,13},{6,14},{7,15},{8,0},{9,1},... | collective-permute-start | bytes 442376 | tf_op jit(solution)/shard_map/ppermute | solution.py:85
  185.8 8.9 %collective-permute-start.17 = (bf16[3,3,2,2,16,256]{5,4,3,2,1,0:T(8,128)(2,1)S(1)}, bf16[3,3,2,2,16,256]{5,4,3,2,1,0:T(8,128)(2,1)}, u32[]{:S(2)}, u32[]{:S(2)}) collective-permute-start(bf16[3,3,2,2,16,256]{5,4,3,2,1,0:T(8,128)(2,1)S(1)} %pad_maximum_fusion.3), channel_id=1, source_target_pairs={{0,4},{1,5},{2,6},{3,7},{4,0},{5,1},{6,2},{7,3},{8,12},{9,13},{10,... | collective-permute-start | bytes 884744 | tf_op jit(solution)/shard_map/ppermute | solution.py:85
  189.3 11.0 %collective-permute-start.20 = (bf16[8,512]{1,0:T(8,128)(2,1)S(1)}, bf16[8,512]{1,0:T(8,128)(2,1)S(1)}, u32[]{:S(2)}, u32[]{:S(2)}) collective-permute-start(bf16[8,512]{1,0:T(8,128)(2,1)S(1)} %get-tuple-element.9), channel_id=1, source_target_pairs={{0,16},{1,17},{2,18},{3,19},{4,20},{5,21},{6,22},{7,23},{8,24},{9,... | collective-permute-start | bytes 24584 | tf_op jit(solution)/shard_map/ppermute | solution.py:85
  197.5 11.0 %collective-permute-start.18 = (bf16[3,3,2,2,2,16,256]{6,5,4,3,2,1,0:T(8,128)(2,1)}, bf16[3,3,2,2,2,16,256]{6,5,4,3,2,1,0:T(8,128)(2,1)}, u32[]{:S(2)}, u32[]{:S(2)}) collective-permute-start(bf16[3,3,2,2,2,16,256]{6,5,4,3,2,1,0:T(8,128)(2,1)} %pad_maximum_fusion.2), channel_id=1, source_target_pairs={{0,2},{1,3},{2,0},{3,1},{4,6},{5,7},{6,4},{7,5},{8,10},{9,11},{10,... | collective-permute-start | bytes 1769480 | tf_op jit(solution)/shard_map/ppermute | solution.py:85
  204.2 8.2 %collective-permute-start.22 = (bf16[2,2,8,512]{3,2,1,0:T(8,128)(2,1)S(1)}, bf16[2,2,8,512]{3,2,1,0:T(8,128)(2,1)S(1)}, u32[]{:S(2)}, u32[]{:S(2)}) collective-permute-start(bf16[2,2,8,512]{3,2,1,0:T(8,128)(2,1)S(1)} %pad_maximum_fusion.8), channel_id=1, source_target_pairs={{0,4},{1,5},{2,6},{3,7},{4,0},{5,1},{6,2},{7,3},{8,12},{9,13},{10,... | collective-permute-start | bytes 98312 | tf_op jit(solution)/shard_map/ppermute | solution.py:85
  211.0 8.1 %collective-permute-start.19 = (bf16[3,3,2,2,2,2,16,256]{7,6,5,4,3,2,1,0:T(8,128)(2,1)}, bf16[3,3,2,2,2,2,16,256]{7,6,5,4,3,2,1,0:T(8,128)(2,1)}, u32[]{:S(2)}, u32[]{:S(2)}) collective-permute-start(bf16[3,3,2,2,2,2,16,256]{7,6,5,4,3,2,1,0:T(8,128)(2,1)} %pad_maximum_fusion.1), channel_id=1, source_target_pairs={{0,1},{1,0},{2,3},{3,2},{4,5},{5,4},{6,7},{7,6},{8,9},{9,8},{10,11... | collective-permute-start | bytes 3538952 | tf_op jit(solution)/shard_map/ppermute | solution.py:85
  212.4 4.3 %collective-permute-start.23 = (bf16[2,2,2,8,512]{4,3,2,1,0:T(8,128)(2,1)S(1)}, bf16[2,2,2,8,512]{4,3,2,1,0:T(8,128)(2,1)S(1)}, u32[]{:S(2)}, u32[]{:S(2)}) collective-permute-start(bf16[2,2,2,8,512]{4,3,2,1,0:T(8,128)(2,1)S(1)} %pad_maximum_fusion.7), channel_id=1, source_target_pairs={{0,2},{1,3},{2,0},{3,1},{4,6},{5,7},{6,4},{7,5},{8,10},{9,11},{10,... | collective-permute-start | bytes 196616 | tf_op jit(solution)/shard_map/ppermute | solution.py:85
  245.5 4.6 %collective-permute-start.25 = (f32[3,3,2,2,2,2,16,256]{7,6,4,3,2,1,0,5:T(8,128)S(1)}, f32[3,3,2,2,2,2,16,256]{7,6,4,3,2,1,0,5:T(8,128)S(1)}, u32[]{:S(2)}, u32[]{:S(2)}) collective-permute-start(f32[3,3,2,2,2,2,16,256]{7,6,4,3,2,1,0,5:T(8,128)S(1)} %bitcast.462), channel_id=1, source_target_pairs={{0,1},{1,0},{2,3},{3,2},{4,5},{5,4},{6,7},{7,6},{8,9},{9,8},{10,11... | collective-permute-start | bytes 7077896 | tf_op jit(solution)/shard_map/ppermute | solution.py:85
  251.9 31.1 %collective-permute-start.26 = (f32[3,3,2,2,2,16,256]{6,5,4,3,2,1,0:T(8,128)}, f32[3,3,2,2,2,16,256]{6,5,4,3,2,1,0:T(8,128)}, u32[]{:S(2)}, u32[]{:S(2)}) collective-permute-start(f32[3,3,2,2,2,16,256]{6,5,4,3,2,1,0:T(8,128)} %dynamic-slice_bitcast_fusion), channel_id=1, source_target_pairs={{0,2},{1,3},{2,0},{3,1},{4,6},{5,7},{6,4},{7,5},{8,10},{9,11},{10,... | collective-permute-start | bytes 3538952 | tf_op jit(solution)/shard_map/ppermute | solution.py:85
  255.1 27.8 %collective-permute-start.31 = (f32[2,2,2,8,512]{4,3,2,1,0:T(8,128)S(1)}, f32[2,2,2,8,512]{4,3,2,1,0:T(8,128)S(1)}, u32[]{:S(2)}, u32[]{:S(2)}) collective-permute-start(f32[2,2,2,8,512]{4,3,2,1,0:T(8,128)S(1)} %dynamic-slice_bitcast_fusion.7), channel_id=1, source_target_pairs={{0,2},{1,3},{2,0},{3,1},{4,6},{5,7},{6,4},{7,5},{8,10},{9,11},{10,... | collective-permute-start | bytes 393224 | tf_op jit(solution)/shard_map/ppermute | solution.py:85
  285.6 17.6 %collective-permute-start.27 = (f32[3,3,2,2,16,256]{5,4,3,2,1,0:T(8,128)S(1)}, f32[3,3,2,2,16,256]{5,4,3,2,1,0:T(8,128)S(1)}, u32[]{:S(2)}, u32[]{:S(2)}) collective-permute-start(f32[3,3,2,2,16,256]{5,4,3,2,1,0:T(8,128)S(1)} %dynamic-slice_bitcast_fusion.2), channel_id=1, source_target_pairs={{0,4},{1,5},{2,6},{3,7},{4,0},{5,1},{6,2},{7,3},{8,12},{9,13},{10,... | collective-permute-start | bytes 1769480 | tf_op jit(solution)/shard_map/ppermute | solution.py:85
  288.5 14.7 %collective-permute-start.32 = (f32[2,2,8,512]{3,2,1,0:T(8,128)S(1)}, f32[2,2,8,512]{3,2,1,0:T(8,128)S(1)}, u32[]{:S(2)}, u32[]{:S(2)}) collective-permute-start(f32[2,2,8,512]{3,2,1,0:T(8,128)S(1)} %dynamic-slice_bitcast_fusion.9), channel_id=1, source_target_pairs={{0,4},{1,5},{2,6},{3,7},{4,0},{5,1},{6,2},{7,3},{8,12},{9,13},{10,... | collective-permute-start | bytes 196616 | tf_op jit(solution)/shard_map/ppermute | solution.py:85
  303.2 4.3 %collective-permute-start.33 = (f32[2,8,512]{2,1,0:T(8,128)S(1)}, f32[2,8,512]{2,1,0:T(8,128)S(1)}, u32[]{:S(2)}, u32[]{:S(2)}) collective-permute-start(f32[2,8,512]{2,1,0:T(8,128)S(1)} %dynamic-slice_bitcast_fusion.11), channel_id=1, source_target_pairs={{0,8},{1,9},{2,10},{3,11},{4,12},{5,13},{6,14},{7,15},{8,0},{9,1},... | collective-permute-start | bytes 98312 | tf_op jit(solution)/shard_map/ppermute | solution.py:85
  304.6 8.0 %collective-permute-start.28 = (f32[3,3,2,16,256]{4,3,1,0,2:T(8,128)S(1)}, f32[3,3,2,16,256]{4,3,1,0,2:T(8,128)S(1)}, u32[]{:S(2)}, u32[]{:S(2)}) collective-permute-start(f32[3,3,2,16,256]{4,3,1,0,2:T(8,128)S(1)} %bitcast.465), channel_id=1, source_target_pairs={{0,8},{1,9},{2,10},{3,11},{4,12},{5,13},{6,14},{7,15},{8,0},{9,1},... | collective-permute-start | bytes 884744 | tf_op jit(solution)/shard_map/ppermute | solution.py:85
  307.5 8.7 %collective-permute-start.34 = (f32[8,512]{1,0:T(8,128)S(1)}, f32[8,512]{1,0:T(8,128)S(1)}, u32[]{:S(2)}, u32[]{:S(2)}) collective-permute-start(f32[8,512]{1,0:T(8,128)S(1)} %dynamic-slice_bitcast_fusion.13), channel_id=1, source_target_pairs={{0,16},{1,17},{2,18},{3,19},{4,20},{5,21},{6,22},{7,23},{8,24},{9,... | collective-permute-start | bytes 49160 | tf_op jit(solution)/shard_map/ppermute | solution.py:85
  312.6 6.7 %collective-permute-start.29 = (f32[3,3,16,256]{3,2,1,0:T(8,128)S(1)}, f32[3,3,16,256]{3,2,1,0:T(8,128)S(1)}, u32[]{:S(2)}, u32[]{:S(2)}) collective-permute-start(f32[3,3,16,256]{3,2,1,0:T(8,128)S(1)} %dynamic-slice_bitcast_fusion.5), channel_id=1, source_target_pairs={{0,16},{1,17},{2,18},{3,19},{4,20},{5,21},{6,22},{7,23},{8,24},{9,... | collective-permute-start | bytes 442376 | tf_op jit(solution)/shard_map/ppermute | solution.py:85
  328.2 5.1 %collective-permute-start.37 = (f32[2]{0:T(128)S(1)}, f32[2]{0:T(128)S(1)}, u32[]{:S(2)}, u32[]{:S(2)}) collective-permute-start(f32[2]{0:T(128)S(1)} %fusion.130), channel_id=1, source_target_pairs={{0,4},{1,5},{2,6},{3,7},{4,0},{5,1},{6,2},{7,3},{8,12},{9,13},{10,... | collective-permute-start | bytes 32 | tf_op jit(solution)/shard_map/ppermute | solution.py:85
  336.9 5.1 %collective-permute-start.39 = (f32[2]{0:T(128)S(1)}, f32[2]{0:T(128)S(1)}, u32[]{:S(2)}, u32[]{:S(2)}) collective-permute-start(f32[2]{0:T(128)S(1)} %add.356), channel_id=1, source_target_pairs={{0,16},{1,17},{2,18},{3,19},{4,20},{5,21},{6,22},{7,23},{8,24},{9,... | collective-permute-start | bytes 32 | tf_op jit(solution)/shard_map/ppermute | solution.py:85
  (57 other events, 453.3 us)

commit v3 on v2

--- a/solution.py
+++ b/solution.py
@@ -81,23 +81,33 @@
     return 0.004 * lax.rsqrt(squares / entries + 1e-06)
 
 
-def partner_swap(value, bit, peers):
-    return lax.ppermute(value, "ex", perm=[(i, i ^ (1 << bit)) for i in range(peers)])
-
-
-def halve_sum(value, axis, bit, place, peers):
+def partner_swap(value, pairs):
+    return lax.ppermute(value, "ex", perm=pairs)
+
+
+def stage_pairs(bits_of, peers):
+    return [(i, i ^ (1 << bits_of[i % 2])) for i in range(peers)]
+
+
+def halve_sum(value, axis, bit, pairs, place):
     mine = (place >> bit) & 1
     keep = lax.dynamic_index_in_dim(value, mine, axis, keepdims=False)
     give = lax.dynamic_index_in_dim(value, 1 - mine, axis, keepdims=False)
-    return keep + partner_swap(give, bit, peers)
-
-
-def double_join(value, axis, bit, place, peers):
+    return keep + partner_swap(give, pairs)
+
+
+def double_join(value, axis, bit, pairs, place):
     mine = (place >> bit) & 1
-    other = partner_swap(value, bit, peers)
+    other = partner_swap(value, pairs)
     first = jnp.where(mine == 0, value, other)
     second = jnp.where(mine == 0, other, value)
     return jnp.stack([first, second], axis=axis)
+
+
+def swap_bit_axes(value, lead, levels):
+    order = list(range(value.ndim))
+    order[lead : lead + 4] = [lead + 2, lead + 3, lead, lead + 1]
+    return jnp.transpose(value, order)
 
 
 def shards(feats, targets, task_of, counts, down_w, up_w, head):
@@ -140,19 +150,28 @@
     down_own = lax.dynamic_slice_in_dim(down_w[0], place * part_chans, part_chans, 2)
     up_own = lax.dynamic_slice_in_dim(up_w[0], place * part_inner, part_inner, 0)
     bits_shape = (2,) * levels
+    core = place % 2
+    second_core = core == 1
+    orders = ([0, 1, 2, 3, 4], [0, 3, 4, 1, 2])
     for update_round in range(TRAIN_STEPS):
         loss_sum, grad_down, grad_up = train_pass(
             held_feats, held_labels, down_low, upper_low, head, count
         )
         grad_down = grad_down.reshape((3, 3) + bits_shape + (part_chans, inner))
         grad_up = grad_up.reshape(bits_shape + (part_inner, up_w.shape[2]))
-        for bit in range(levels):
-            grad_down = halve_sum(grad_down, 2 + levels - 1 - bit, bit, place, peers)
-            grad_up = halve_sum(grad_up, levels - 1 - bit, bit, place, peers)
+        for stage in range(levels):
+            if stage == 1:
+                grad_down = jnp.where(second_core, swap_bit_axes(grad_down, 2, levels), grad_down)
+                grad_up = jnp.where(second_core, swap_bit_axes(grad_up, 0, levels), grad_up)
+            bits_of = (orders[0][stage], orders[1][stage])
+            pairs = stage_pairs(bits_of, peers)
+            bit = jnp.where(second_core, bits_of[1], bits_of[0])
+            grad_down = halve_sum(grad_down, 2 + levels - 1 - stage, bit, pairs, place)
+            grad_up = halve_sum(grad_up, levels - 1 - stage, bit, pairs, place)
         squares = jnp.sum(grad_down * grad_down) + jnp.sum(grad_up * grad_up)
         totals = jnp.stack([squares, loss_sum])
         for bit in range(levels):
-            totals = totals + partner_swap(totals, bit, peers)
+            totals = totals + partner_swap(totals, stage_pairs((bit, bit), peers))
         scale = step_scale(totals[0], entries)
         down_own = down_own - scale * grad_down
         up_own = up_own - scale * grad_up
@@ -160,9 +179,16 @@
         if update_round + 1 < TRAIN_STEPS:
             down_low = down_own.astype(jnp.bfloat16)
             upper_low = up_own.astype(jnp.bfloat16)
-            for step_index, bit in enumerate(reversed(range(levels))):
-                down_low = double_join(down_low, 2 + step_index, bit, place, peers)
-                upper_low = double_join(upper_low, step_index, bit, place, peers)
+            for step_index in range(levels):
+                stage = levels - 1 - step_index
+                if stage == 0:
+                    down_low = jnp.where(second_core, swap_bit_axes(down_low, 2, levels), down_low)
+                    upper_low = jnp.where(second_core, swap_bit_axes(upper_low, 0, levels), upper_low)
+                bits_of = (orders[0][stage], orders[1][stage])
+                pairs = stage_pairs(bits_of, peers)
+                bit = jnp.where(second_core, bits_of[1], bits_of[0])
+                down_low = double_join(down_low, 2 + step_index, bit, pairs, place)
+                upper_low = double_join(upper_low, step_index, bit, pairs, place)
             down_low = down_low.reshape(down_w.shape[1:])
             upper_low = upper_low.reshape(up_w.shape[1:])
     return (down_own[None], up_own[None], jnp.stack(collected)[None])

time: 350 us -> 297 us (0.85)
  waiting for transfers between devices: 159 us -> 120 us
  local copies, waits for them, and re-layouts: 33.3 us -> 25.5 us
  other arithmetic: 39.3 us -> 35 us
    ppermute x40, waiting for transfers between devices: 143 us -> 104 us  [partner_swap(): return lax.ppermute(value, 'ex', perm=pairs)]
    select_n x0 -> x6, other arithmetic: none -> 7.21 us  [the longest x2 5.59 us: shards(): jnp.where(second_core, swap_bit_axes(grad_down, 2, levels), grad_down)]
    add x26 -> x22, other arithmetic: 13.5 us -> 7.37 us  [the longest x12 4.47 us: halve_sum(): return keep + partner_swap(give, pairs)]
    another operation x20 -> x18, other arithmetic: 8.18 us -> 3.79 us  [double_join(): return jnp.stack([first, second], axis=axis)]
    unnamed x96 -> x60, local copies, waits for them, and re-layouts: 13.2 us -> 11.5 us
  transfers between devices with their start and end apart: 42 -> 42, of which waited for: 34 -> 33; matrix products, arithmetic and copies ran while one was open for 7% -> 6% of each run, Pallas kernels for 0% -> 0%
where the time goes in v3:
time: 297 us; the launch traced here: 293 us
  waiting for transfers between devices  120 us (40%)
  starting transfers between devices  71.5 us (24%)
  other arithmetic  35 us (12%)
  matrix products  32.5 us (11%)
  local copies, waits for them, and re-layouts  25.5 us (9%)
  between operations  7.93 us (3%)
    ppermute x40, waiting for transfers between devices, partner_swap(): return lax.ppermute(value, 'ex', perm=pairs)  104 us
    ppermute x40, starting transfers between devices, partner_swap(): return lax.ppermute(value, 'ex', perm=pairs)  63.4 us
    all_to_all x1, waiting for transfers between devices, shards(): lax.all_to_all(send_feats, 'task', split_axis=0, concat_axis=0, tiled=True)  15.3 us
    dot_general x20, matrix products, contract_rows(): lax.dot_general(left, right, (((0,), (0,)), ((), ())), preferred_element_...  13 us
    unnamed x60, local copies, waits for them, and re-layouts  11.5 us
    dot_general x18, matrix products, train_pass(): jnp.dot(windows[offset_index], down_low[offset_index // 3, offset_index %...  10.4 us
  transfers between devices with their start and end apart: 42, of which 33 were waited for; matrix products, arithmetic and copies ran while one was open for 6% of the time, Pallas kernels for 0%

profile of v3, /device:TPU:0, one launch (start us, length us, event | category | flops | bytes accessed | tf_op | source)
XLA Modules:
  0.0 292.8 jit_solution(13248215748388075830)
XLA Ops:
  4.8 4.4 %all-to-all-start.1 = ((bf16[4,2,192]{2,1,0:T(2,128)(2,1)}), bf16[4,2,192]{2,1,0:T(2,128)(2,1)S(1)}, u32[]{:S(2)}, u32[]{:S(2)}) async-start(bf16[4,2,192]{2,1,0:T(2,128)(2,1)} %reshape.166), calls=%async_computation.1 | async-start | bytes 8192 | tf_op jit(solution)/shard_map/all_to_all | solution.py:137
  10.5 2.9 scatter_fusion
  14.5 3.7 %all-to-all-start = ((bf16[4,6,8,8,512]{4,3,2,1,0:T(8,128)(2,1)}), bf16[4,6,8,8,512]{4,3,2,1,0:T(8,128)(2,1)S(1)}, u32[]{:S(2)}, u32[]{:S(2)}) async-start(bf16[4,6,8,8,512]{4,3,2,1,0:T(8,128)(2,1)} %scatter_fusion), calls=%async_computation | async-start | bytes 3145728 | tf_op jit(solution)/shard_map/all_to_all | solution.py:136
  18.9 4.0 %convert_bitcast_fusion = bf16[3,3,512,256]{3,2,1,0:T(8,128)(2,1)} fusion(f32[1,3,3,512,256]{4,3,2,1,0:T(8,128)} %param.11), kind=kLoop, calls=%fused_computation.51 | loop fusion | flops 1179648 | bytes 7077888 | tf_op jit(solution)/shard_map/convert_element_type | solution.py:148
  23.1 15.3 %all-to-all-done = bf16[4,6,8,8,512]{4,3,2,1,0:T(8,128)(2,1)S(1)} async-done(((bf16[4,6,8,8,512]{4,3,2,1,0:T(8,128)(2,1)}), bf16[4,6,8,8,512]{4,3,2,1,0:T(8,128)(2,1)S(1)}, u32[]{:S(2)}, u32[]{:S(2)}) %all-to-all-start) | async-done | bytes 1572896 | tf_op jit(solution)/shard_map/all_to_all | solution.py:136
  39.1 2.6 pad_slice_fusion
  62.5 4.9 %collective-permute-done = f32[3,3,2,2,2,2,16,256]{7,6,5,4,3,2,1,0:T(8,128)} collective-permute-done((f32[3,3,2,2,2,2,16,256]{7,6,5,4,3,2,1,0:T(8,128)}, f32[3,3,2,2,2,2,16,256]{7,6,5,4,3,2,1,0:T(8,128)}, u32[]{:S(2)}, u32[]{:S(2)}) %collective-permute-start) | collective-permute-done | bytes 2359328 | tf_op jit(solution)/shard_map/ppermute | solution.py:85
  67.3 5.0 %copy_select_fusion.1 = f32[3,3,2,2,2,2,16,256]{7,6,5,4,3,2,1,0:T(8,128)S(1)} fusion(pred[]{:T(512)S(6)} %eq.26, f32[3,3,2,2,2,2,16,256]{7,6,5,4,3,2,1,0:T(8,128)} %collective-permute-done, f32[3,3,2,2,2,2,2,16,256]{8,7,6,5,4,3,2,1,0:T(8,128)} %bitcast.491, s32[]{:T(128)S(6)} %select_n.279), kind=kLoop, calls=%fused_computation.48 | loop fusion | flops 1769472 | bytes 11798016 | tf_op jit(solution)/shard_map/jit(_where)/select_n | solution.py:164
  79.1 12.4 %collective-permute-done.6 = f32[2,2,2,8,512]{4,3,1,0,2:T(8,128)S(1)} collective-permute-done((f32[2,2,2,8,512]{4,3,1,0,2:T(8,128)S(1)}, f32[2,2,2,8,512]{4,3,1,0,2:T(8,128)S(1)}, u32[]{:S(2)}, u32[]{:S(2)}) %collective-permute-start.6) | collective-permute-done | bytes 131104 | tf_op jit(solution)/shard_map/ppermute | solution.py:85
  94.1 3.3 %collective-permute-start.2 = (f32[3,3,2,2,16,256]{5,4,3,2,1,0:T(8,128)S(1)}, f32[3,3,2,2,16,256]{5,4,3,2,1,0:T(8,128)S(1)}, u32[]{:S(2)}, u32[]{:S(2)}) collective-permute-start(f32[3,3,2,2,16,256]{5,4,3,2,1,0:T(8,128)S(1)} %dynamic-slice_bitcast_fusion.4), channel_id=1, source_target_pairs={{0,4},{1,17},{2,6},{3,19},{4,0},{5,21},{6,2},{7,23},{8,12},{9,25},... | collective-permute-start | bytes 1769480 | tf_op jit(solution)/shard_map/ppermute | solution.py:85
  97.8 8.5 %collective-permute-done.7 = f32[2,2,8,512]{3,2,1,0:T(8,128)S(1)} collective-permute-done((f32[2,2,8,512]{3,2,1,0:T(8,128)S(1)}, f32[2,2,8,512]{3,2,1,0:T(8,128)S(1)}, u32[]{:S(2)}, u32[]{:S(2)}) %collective-permute-start.7) | collective-permute-done | bytes 65568 | tf_op jit(solution)/shard_map/ppermute | solution.py:85
  110.3 4.0 %collective-permute-start.9 = (f32[8,512]{1,0:T(8,128)S(1)}, f32[8,512]{1,0:T(8,128)S(1)}, u32[]{:S(2)}, u32[]{:S(2)}) collective-permute-start(f32[8,512]{1,0:T(8,128)S(1)} %dynamic-slice_bitcast_fusion.17), channel_id=1, source_target_pairs={{0,16},{1,5},{2,18},{3,7},{4,20},{5,1},{6,22},{7,3},{8,24},{9,13},... | collective-permute-start | bytes 49160 | tf_op jit(solution)/shard_map/ppermute | solution.py:85
  116.4 3.7 %collective-permute-start.4 = (f32[3,3,16,256]{3,2,1,0:T(8,128)S(1)}, f32[3,3,16,256]{3,2,1,0:T(8,128)S(1)}, u32[]{:S(2)}, u32[]{:S(2)}) collective-permute-start(f32[3,3,16,256]{3,2,1,0:T(8,128)S(1)} %dynamic-slice_bitcast_fusion.10), channel_id=1, source_target_pairs={{0,16},{1,5},{2,18},{3,7},{4,20},{5,1},{6,22},{7,3},{8,24},{9,13},... | collective-permute-start | bytes 442376 | tf_op jit(solution)/shard_map/ppermute | solution.py:85
  132.0 3.2 %collective-permute-start.12 = (f32[2]{0:T(128)S(1)}, f32[2]{0:T(128)S(1)}, u32[]{:S(2)}, u32[]{:S(2)}) collective-permute-start(f32[2]{0:T(128)S(1)} %fusion.143), channel_id=1, source_target_pairs={{0,4},{1,5},{2,6},{3,7},{4,0},{5,1},{6,2},{7,3},{8,12},{9,13},{10,... | collective-permute-start | bytes 32 | tf_op jit(solution)/shard_map/ppermute | solution.py:85
  137.2 3.5 %collective-permute-done.13 = f32[2]{0:T(128)S(1)} collective-permute-done((f32[2]{0:T(128)S(1)}, f32[2]{0:T(128)S(1)}, u32[]{:S(2)}, u32[]{:S(2)}) %collective-permute-start.13) | collective-permute-done | bytes 40 | tf_op jit(solution)/shard_map/ppermute | solution.py:85
  140.7 3.5 %collective-permute-start.14 = (f32[2]{0:T(128)S(1)}, f32[2]{0:T(128)S(1)}, u32[]{:S(2)}, u32[]{:S(2)}) collective-permute-start(f32[2]{0:T(128)S(1)} %add.331), channel_id=1, source_target_pairs={{0,16},{1,17},{2,18},{3,19},{4,20},{5,21},{6,22},{7,23},{8,24},{9,... | collective-permute-start | bytes 32 | tf_op jit(solution)/shard_map/ppermute | solution.py:85
  148.0 3.6 %collective-permute-start.15 = (bf16[3,3,16,256]{3,2,1,0:T(8,128)(2,1)S(1)}, bf16[3,3,16,256]{3,2,1,0:T(8,128)(2,1)S(1)}, u32[]{:S(2)}, u32[]{:S(2)}) collective-permute-start(bf16[3,3,16,256]{3,2,1,0:T(8,128)(2,1)S(1)} %get-tuple-element.7), channel_id=1, source_target_pairs={{0,16},{1,5},{2,18},{3,7},{4,20},{5,1},{6,22},{7,3},{8,24},{9,13},... | collective-permute-start | bytes 221192 | tf_op jit(solution)/shard_map/ppermute | solution.py:85
  151.6 2.3 collective-permute-done.15
  154.1 6.7 %collective-permute-done.16 = bf16[3,3,2,16,256]{4,3,2,1,0:T(8,128)(2,1)S(1)} collective-permute-done((bf16[3,3,2,16,256]{4,3,2,1,0:T(8,128)(2,1)S(1)}, bf16[3,3,2,16,256]{4,3,2,1,0:T(8,128)(2,1)S(1)}, u32[]{:S(2)}, u32[]{:S(2)}) %collective-permute-start.16) | collective-permute-done | bytes 147488 | tf_op jit(solution)/shard_map/ppermute | solution.py:85
  160.9 3.3 %collective-permute-start.17 = (bf16[3,3,2,2,16,256]{5,4,3,2,1,0:T(8,128)(2,1)S(1)}, bf16[3,3,2,2,16,256]{5,4,3,2,1,0:T(8,128)(2,1)S(1)}, u32[]{:S(2)}, u32[]{:S(2)}) collective-permute-start(bf16[3,3,2,2,16,256]{5,4,3,2,1,0:T(8,128)(2,1)S(1)} %pad_maximum_fusion.3), channel_id=1, source_target_pairs={{0,4},{1,17},{2,6},{3,19},{4,0},{5,21},{6,2},{7,23},{8,12},{9,25},... | collective-permute-start | bytes 884744 | tf_op jit(solution)/shard_map/ppermute | solution.py:85
  166.8 2.5 collective-permute-done.17
  171.1 3.7 %collective-permute-done.21 = bf16[2,8,512]{2,1,0:T(8,128)(2,1)S(1)} collective-permute-done((bf16[2,8,512]{2,1,0:T(8,128)(2,1)S(1)}, bf16[2,8,512]{2,1,0:T(8,128)(2,1)S(1)}, u32[]{:S(2)}, u32[]{:S(2)}) %collective-permute-start.21) | collective-permute-done | bytes 16416 | tf_op jit(solution)/shard_map/ppermute | solution.py:85
  174.8 3.0 %collective-permute-start.22 = (bf16[2,2,8,512]{3,2,1,0:T(8,128)(2,1)S(1)}, bf16[2,2,8,512]{3,2,1,0:T(8,128)(2,1)S(1)}, u32[]{:S(2)}, u32[]{:S(2)}) collective-permute-start(bf16[2,2,8,512]{3,2,1,0:T(8,128)(2,1)S(1)} %pad_maximum_fusion.8), channel_id=1, source_target_pairs={{0,4},{1,17},{2,6},{3,19},{4,0},{5,21},{6,2},{7,23},{8,12},{9,25},... | collective-permute-start | bytes 98312 | tf_op jit(solution)/shard_map/ppermute | solution.py:85
  183.7 2.9 collective-permute-done.23
  215.4 4.5 %collective-permute-done.25 = f32[3,3,2,2,2,2,16,256]{7,6,5,4,3,2,1,0:T(8,128)S(1)} collective-permute-done((f32[3,3,2,2,2,2,16,256]{7,6,5,4,3,2,1,0:T(8,128)S(1)}, f32[3,3,2,2,2,2,16,256]{7,6,5,4,3,2,1,0:T(8,128)S(1)}, u32[]{:S(2)}, u32[]{:S(2)}) %collective-permute-start.25) | collective-permute-done | bytes 2359328 | tf_op jit(solution)/shard_map/ppermute | solution.py:85
  225.8 12.5 %collective-permute-done.31 = f32[2,2,2,8,512]{4,3,2,1,0:T(8,128)S(1)} collective-permute-done((f32[2,2,2,8,512]{4,3,2,1,0:T(8,128)S(1)}, f32[2,2,2,8,512]{4,3,2,1,0:T(8,128)S(1)}, u32[]{:S(2)}, u32[]{:S(2)}) %collective-permute-start.31) | collective-permute-done | bytes 131104 | tf_op jit(solution)/shard_map/ppermute | solution.py:85
  239.9 3.1 %collective-permute-start.27 = (f32[3,3,2,2,16,256]{5,4,3,2,1,0:T(8,128)S(1)}, f32[3,3,2,2,16,256]{5,4,3,2,1,0:T(8,128)S(1)}, u32[]{:S(2)}, u32[]{:S(2)}) collective-permute-start(f32[3,3,2,2,16,256]{5,4,3,2,1,0:T(8,128)S(1)} %dynamic-slice_bitcast_fusion.3), channel_id=1, source_target_pairs={{0,4},{1,17},{2,6},{3,19},{4,0},{5,21},{6,2},{7,23},{8,12},{9,25},... | collective-permute-start | bytes 1769480 | tf_op jit(solution)/shard_map/ppermute | solution.py:85
  243.6 8.5 %collective-permute-done.32 = f32[2,2,8,512]{3,2,1,0:T(8,128)S(1)} collective-permute-done((f32[2,2,8,512]{3,2,1,0:T(8,128)S(1)}, f32[2,2,8,512]{3,2,1,0:T(8,128)S(1)}, u32[]{:S(2)}, u32[]{:S(2)}) %collective-permute-start.32) | collective-permute-done | bytes 65568 | tf_op jit(solution)/shard_map/ppermute | solution.py:85
  259.4 3.2 %collective-permute-start.29 = (f32[3,3,16,256]{3,2,1,0:T(8,128)S(1)}, f32[3,3,16,256]{3,2,1,0:T(8,128)S(1)}, u32[]{:S(2)}, u32[]{:S(2)}) collective-permute-start(f32[3,3,16,256]{3,2,1,0:T(8,128)S(1)} %dynamic-slice_bitcast_fusion.9), channel_id=1, source_target_pairs={{0,16},{1,5},{2,18},{3,7},{4,20},{5,1},{6,22},{7,3},{8,24},{9,13},... | collective-permute-start | bytes 442376 | tf_op jit(solution)/shard_map/ppermute | solution.py:85
  263.8 2.3 collective-permute-done.29
  275.0 3.0 %collective-permute-start.37 = (f32[2]{0:T(128)S(1)}, f32[2]{0:T(128)S(1)}, u32[]{:S(2)}, u32[]{:S(2)}) collective-permute-start(f32[2]{0:T(128)S(1)} %fusion.136), channel_id=1, source_target_pairs={{0,4},{1,5},{2,6},{3,7},{4,0},{5,1},{6,2},{7,3},{8,12},{9,13},{10,... | collective-permute-start | bytes 32 | tf_op jit(solution)/shard_map/ppermute | solution.py:85
  283.6 3.2 %collective-permute-start.39 = (f32[2]{0:T(128)S(1)}, f32[2]{0:T(128)S(1)}, u32[]{:S(2)}, u32[]{:S(2)}) collective-permute-start(f32[2]{0:T(128)S(1)} %add.361), channel_id=1, source_target_pairs={{0,16},{1,17},{2,18},{3,19},{4,20},{5,21},{6,22},{7,23},{8,24},{9,... | collective-permute-start | bytes 32 | tf_op jit(solution)/shard_map/ppermute | solution.py:85
  (265 shorter events, 131.8 us)
Async XLA Ops:
  4.8 9.7 %all-to-all-start.1 = ((bf16[4,2,192]{2,1,0:T(2,128)(2,1)}), bf16[4,2,192]{2,1,0:T(2,128)(2,1)S(1)}, u32[]{:S(2)}, u32[]{:S(2)}) async-start(bf16[4,2,192]{2,1,0:T(2,128)(2,1)} %reshape.166), calls=%async_computation.1 | async-start | bytes 8192 | tf_op jit(solution)/shard_map/all_to_all | solution.py:137
  14.5 23.9 %all-to-all-start = ((bf16[4,6,8,8,512]{4,3,2,1,0:T(8,128)(2,1)}), bf16[4,6,8,8,512]{4,3,2,1,0:T(8,128)(2,1)S(1)}, u32[]{:S(2)}, u32[]{:S(2)}) async-start(bf16[4,6,8,8,512]{4,3,2,1,0:T(8,128)(2,1)} %scatter_fusion), calls=%async_computation | async-start | bytes 3145728 | tf_op jit(solution)/shard_map/all_to_all | solution.py:136
  62.5 4.9 %collective-permute-start = (f32[3,3,2,2,2,2,16,256]{7,6,5,4,3,2,1,0:T(8,128)}, f32[3,3,2,2,2,2,16,256]{7,6,5,4,3,2,1,0:T(8,128)}, u32[]{:S(2)}, u32[]{:S(2)}) collective-permute-start(f32[3,3,2,2,2,2,16,256]{7,6,5,4,3,2,1,0:T(8,128)} %dynamic-slice_bitcast_fusion.1), channel_id=1, source_target_pairs={{0,1},{1,0},{2,3},{3,2},{4,5},{5,4},{6,7},{7,6},{8,9},{9,8},{10,11... | collective-permute-start | bytes 7077896 | tf_op jit(solution)/shard_map/ppermute | solution.py:85
  73.7 17.8 %collective-permute-start.1 = (f32[3,3,2,2,2,16,256]{6,5,3,2,1,0,4:T(8,128)}, f32[3,3,2,2,2,16,256]{6,5,3,2,1,0,4:T(8,128)}, u32[]{:S(2)}, u32[]{:S(2)}) collective-permute-start(f32[3,3,2,2,2,16,256]{6,5,3,2,1,0,4:T(8,128)} %bitcast.446), channel_id=1, source_target_pairs={{0,2},{1,9},{2,0},{3,11},{4,6},{5,13},{6,4},{7,15},{8,10},{9,1},{1... | collective-permute-start | bytes 3538952 | tf_op jit(solution)/shard_map/ppermute | solution.py:85
  77.7 13.8 %collective-permute-start.6 = (f32[2,2,2,8,512]{4,3,1,0,2:T(8,128)S(1)}, f32[2,2,2,8,512]{4,3,1,0,2:T(8,128)S(1)}, u32[]{:S(2)}, u32[]{:S(2)}) collective-permute-start(f32[2,2,2,8,512]{4,3,1,0,2:T(8,128)S(1)} %bitcast.507), channel_id=1, source_target_pairs={{0,2},{1,9},{2,0},{3,11},{4,6},{5,13},{6,4},{7,15},{8,10},{9,1},{1... | collective-permute-start | bytes 393224 | tf_op jit(solution)/shard_map/ppermute | solution.py:85
  94.1 14.2 %collective-permute-start.2 = (f32[3,3,2,2,16,256]{5,4,3,2,1,0:T(8,128)S(1)}, f32[3,3,2,2,16,256]{5,4,3,2,1,0:T(8,128)S(1)}, u32[]{:S(2)}, u32[]{:S(2)}) collective-permute-start(f32[3,3,2,2,16,256]{5,4,3,2,1,0:T(8,128)S(1)} %dynamic-slice_bitcast_fusion.4), channel_id=1, source_target_pairs={{0,4},{1,17},{2,6},{3,19},{4,0},{5,21},{6,2},{7,23},{8,12},{9,25},... | collective-permute-start | bytes 1769480 | tf_op jit(solution)/shard_map/ppermute | solution.py:85
  97.4 8.9 %collective-permute-start.7 = (f32[2,2,8,512]{3,2,1,0:T(8,128)S(1)}, f32[2,2,8,512]{3,2,1,0:T(8,128)S(1)}, u32[]{:S(2)}, u32[]{:S(2)}) collective-permute-start(f32[2,2,8,512]{3,2,1,0:T(8,128)S(1)} %dynamic-slice_bitcast_fusion.13), channel_id=1, source_target_pairs={{0,4},{1,17},{2,6},{3,19},{4,0},{5,21},{6,2},{7,23},{8,12},{9,25},... | collective-permute-start | bytes 196616 | tf_op jit(solution)/shard_map/ppermute | solution.py:85
  106.3 4.0 %collective-permute-start.8 = (f32[2,8,512]{2,1,0:T(8,128)S(1)}, f32[2,8,512]{2,1,0:T(8,128)S(1)}, u32[]{:S(2)}, u32[]{:S(2)}) collective-permute-start(f32[2,8,512]{2,1,0:T(8,128)S(1)} %dynamic-slice_bitcast_fusion.15), channel_id=1, source_target_pairs={{0,8},{1,3},{2,10},{3,1},{4,12},{5,7},{6,14},{7,5},{8,0},{9,11},{1... | collective-permute-start | bytes 98312 | tf_op jit(solution)/shard_map/ppermute | solution.py:85
  109.5 6.8 %collective-permute-start.3 = (f32[3,3,2,16,256]{4,3,2,1,0:T(8,128)S(1)}, f32[3,3,2,16,256]{4,3,2,1,0:T(8,128)S(1)}, u32[]{:S(2)}, u32[]{:S(2)}) collective-permute-start(f32[3,3,2,16,256]{4,3,2,1,0:T(8,128)S(1)} %dynamic-slice_bitcast_fusion.6), channel_id=1, source_target_pairs={{0,8},{1,3},{2,10},{3,1},{4,12},{5,7},{6,14},{7,5},{8,0},{9,11},{1... | collective-permute-start | bytes 884744 | tf_op jit(solution)/shard_map/ppermute | solution.py:85
  110.3 10.3 %collective-permute-start.9 = (f32[8,512]{1,0:T(8,128)S(1)}, f32[8,512]{1,0:T(8,128)S(1)}, u32[]{:S(2)}, u32[]{:S(2)}) collective-permute-start(f32[8,512]{1,0:T(8,128)S(1)} %dynamic-slice_bitcast_fusion.17), channel_id=1, source_target_pairs={{0,16},{1,5},{2,18},{3,7},{4,20},{5,1},{6,22},{7,3},{8,24},{9,13},... | collective-permute-start | bytes 49160 | tf_op jit(solution)/shard_map/ppermute | solution.py:85
  116.4 6.8 %collective-permute-start.4 = (f32[3,3,16,256]{3,2,1,0:T(8,128)S(1)}, f32[3,3,16,256]{3,2,1,0:T(8,128)S(1)}, u32[]{:S(2)}, u32[]{:S(2)}) collective-permute-start(f32[3,3,16,256]{3,2,1,0:T(8,128)S(1)} %dynamic-slice_bitcast_fusion.10), channel_id=1, source_target_pairs={{0,16},{1,5},{2,18},{3,7},{4,20},{5,1},{6,22},{7,3},{8,24},{9,13},... | collective-permute-start | bytes 442376 | tf_op jit(solution)/shard_map/ppermute | solution.py:85
  132.0 5.1 %collective-permute-start.12 = (f32[2]{0:T(128)S(1)}, f32[2]{0:T(128)S(1)}, u32[]{:S(2)}, u32[]{:S(2)}) collective-permute-start(f32[2]{0:T(128)S(1)} %fusion.143), channel_id=1, source_target_pairs={{0,4},{1,5},{2,6},{3,7},{4,0},{5,1},{6,2},{7,3},{8,12},{9,13},{10,... | collective-permute-start | bytes 32 | tf_op jit(solution)/shard_map/ppermute | solution.py:85
  140.7 5.1 %collective-permute-start.14 = (f32[2]{0:T(128)S(1)}, f32[2]{0:T(128)S(1)}, u32[]{:S(2)}, u32[]{:S(2)}) collective-permute-start(f32[2]{0:T(128)S(1)} %add.331), channel_id=1, source_target_pairs={{0,16},{1,17},{2,18},{3,19},{4,20},{5,21},{6,22},{7,23},{8,24},{9,... | collective-permute-start | bytes 32 | tf_op jit(solution)/shard_map/ppermute | solution.py:85
  148.0 5.9 %collective-permute-start.15 = (bf16[3,3,16,256]{3,2,1,0:T(8,128)(2,1)S(1)}, bf16[3,3,16,256]{3,2,1,0:T(8,128)(2,1)S(1)}, u32[]{:S(2)}, u32[]{:S(2)}) collective-permute-start(bf16[3,3,16,256]{3,2,1,0:T(8,128)(2,1)S(1)} %get-tuple-element.7), channel_id=1, source_target_pairs={{0,16},{1,5},{2,18},{3,7},{4,20},{5,1},{6,22},{7,3},{8,24},{9,13},... | collective-permute-start | bytes 221192 | tf_op jit(solution)/shard_map/ppermute | solution.py:85
  154.0 6.8 %collective-permute-start.16 = (bf16[3,3,2,16,256]{4,3,2,1,0:T(8,128)(2,1)S(1)}, bf16[3,3,2,16,256]{4,3,2,1,0:T(8,128)(2,1)S(1)}, u32[]{:S(2)}, u32[]{:S(2)}) collective-permute-start(bf16[3,3,2,16,256]{4,3,2,1,0:T(8,128)(2,1)S(1)} %pad_maximum_fusion.5), channel_id=1, source_target_pairs={{0,8},{1,3},{2,10},{3,1},{4,12},{5,7},{6,14},{7,5},{8,0},{9,11},{1... | collective-permute-start | bytes 442376 | tf_op jit(solution)/shard_map/ppermute | solution.py:85
  160.9 8.5 %collective-permute-start.17 = (bf16[3,3,2,2,16,256]{5,4,3,2,1,0:T(8,128)(2,1)S(1)}, bf16[3,3,2,2,16,256]{5,4,3,2,1,0:T(8,128)(2,1)S(1)}, u32[]{:S(2)}, u32[]{:S(2)}) collective-permute-start(bf16[3,3,2,2,16,256]{5,4,3,2,1,0:T(8,128)(2,1)S(1)} %pad_maximum_fusion.3), channel_id=1, source_target_pairs={{0,4},{1,17},{2,6},{3,19},{4,0},{5,21},{6,2},{7,23},{8,12},{9,25},... | collective-permute-start | bytes 884744 | tf_op jit(solution)/shard_map/ppermute | solution.py:85
  164.9 6.1 %collective-permute-start.20 = (bf16[8,512]{1,0:T(8,128)(2,1)S(1)}, bf16[8,512]{1,0:T(8,128)(2,1)S(1)}, u32[]{:S(2)}, u32[]{:S(2)}) collective-permute-start(bf16[8,512]{1,0:T(8,128)(2,1)S(1)} %get-tuple-element.9), channel_id=1, source_target_pairs={{0,16},{1,5},{2,18},{3,7},{4,20},{5,1},{6,22},{7,3},{8,24},{9,13},... | collective-permute-start | bytes 24584 | tf_op jit(solution)/shard_map/ppermute | solution.py:85
  169.5 10.1 %collective-permute-start.18 = (bf16[3,3,2,2,2,16,256]{6,5,4,3,2,1,0:T(8,128)(2,1)S(1)}, bf16[3,3,2,2,2,16,256]{6,5,4,3,2,1,0:T(8,128)(2,1)}, u32[]{:S(2)}, u32[]{:S(2)}) collective-permute-start(bf16[3,3,2,2,2,16,256]{6,5,4,3,2,1,0:T(8,128)(2,1)S(1)} %pad_maximum_fusion.2), channel_id=1, source_target_pairs={{0,2},{1,9},{2,0},{3,11},{4,6},{5,13},{6,4},{7,15},{8,10},{9,1},{1... | collective-permute-start | bytes 1769480 | tf_op jit(solution)/shard_map/ppermute | solution.py:85
  174.8 7.4 %collective-permute-start.22 = (bf16[2,2,8,512]{3,2,1,0:T(8,128)(2,1)S(1)}, bf16[2,2,8,512]{3,2,1,0:T(8,128)(2,1)S(1)}, u32[]{:S(2)}, u32[]{:S(2)}) collective-permute-start(bf16[2,2,8,512]{3,2,1,0:T(8,128)(2,1)S(1)} %pad_maximum_fusion.8), channel_id=1, source_target_pairs={{0,4},{1,17},{2,6},{3,19},{4,0},{5,21},{6,2},{7,23},{8,12},{9,25},... | collective-permute-start | bytes 98312 | tf_op jit(solution)/shard_map/ppermute | solution.py:85
  182.2 6.1 %collective-permute-start.19 = (bf16[3,3,2,2,2,2,16,256]{7,6,5,4,3,2,1,0:T(8,128)(2,1)}, bf16[3,3,2,2,2,2,16,256]{7,6,5,4,3,2,1,0:T(8,128)(2,1)}, u32[]{:S(2)}, u32[]{:S(2)}) collective-permute-start(bf16[3,3,2,2,2,2,16,256]{7,6,5,4,3,2,1,0:T(8,128)(2,1)} %copy_select_fusion.2), channel_id=1, source_target_pairs={{0,1},{1,0},{2,3},{3,2},{4,5},{5,4},{6,7},{7,6},{8,9},{9,8},{10,11... | collective-permute-start | bytes 3538952 | tf_op jit(solution)/shard_map/ppermute | solution.py:85
  182.2 4.3 %collective-permute-start.23 = (bf16[2,2,2,8,512]{4,3,2,1,0:T(8,128)(2,1)S(1)}, bf16[2,2,2,8,512]{4,3,2,1,0:T(8,128)(2,1)S(1)}, u32[]{:S(2)}, u32[]{:S(2)}) collective-permute-start(bf16[2,2,2,8,512]{4,3,2,1,0:T(8,128)(2,1)S(1)} %pad_maximum_fusion.7), channel_id=1, source_target_pairs={{0,2},{1,9},{2,0},{3,11},{4,6},{5,13},{6,4},{7,15},{8,10},{9,1},{1... | collective-permute-start | bytes 196616 | tf_op jit(solution)/shard_map/ppermute | solution.py:85
  215.2 4.6 %collective-permute-start.25 = (f32[3,3,2,2,2,2,16,256]{7,6,5,4,3,2,1,0:T(8,128)S(1)}, f32[3,3,2,2,2,2,16,256]{7,6,5,4,3,2,1,0:T(8,128)S(1)}, u32[]{:S(2)}, u32[]{:S(2)}) collective-permute-start(f32[3,3,2,2,2,2,16,256]{7,6,5,4,3,2,1,0:T(8,128)S(1)} %dynamic-slice_bitcast_fusion), channel_id=1, source_target_pairs={{0,1},{1,0},{2,3},{3,2},{4,5},{5,4},{6,7},{7,6},{8,9},{9,8},{10,11... | collective-permute-start | bytes 7077896 | tf_op jit(solution)/shard_map/ppermute | solution.py:85
  220.6 17.7 %collective-permute-start.26 = (f32[3,3,2,2,2,16,256]{6,5,4,3,2,1,0:T(8,128)S(1)}, f32[3,3,2,2,2,16,256]{6,5,4,3,2,1,0:T(8,128)S(1)}, u32[]{:S(2)}, u32[]{:S(2)}) collective-permute-start(f32[3,3,2,2,2,16,256]{6,5,4,3,2,1,0:T(8,128)S(1)} %dynamic-slice_bitcast_fusion.2), channel_id=1, source_target_pairs={{0,2},{1,9},{2,0},{3,11},{4,6},{5,13},{6,4},{7,15},{8,10},{9,1},{1... | collective-permute-start | bytes 3538952 | tf_op jit(solution)/shard_map/ppermute | solution.py:85
  224.4 13.9 %collective-permute-start.31 = (f32[2,2,2,8,512]{4,3,2,1,0:T(8,128)S(1)}, f32[2,2,2,8,512]{4,3,2,1,0:T(8,128)S(1)}, u32[]{:S(2)}, u32[]{:S(2)}) collective-permute-start(f32[2,2,2,8,512]{4,3,2,1,0:T(8,128)S(1)} %dynamic-slice_bitcast_fusion.11), channel_id=1, source_target_pairs={{0,2},{1,9},{2,0},{3,11},{4,6},{5,13},{6,4},{7,15},{8,10},{9,1},{1... | collective-permute-start | bytes 393224 | tf_op jit(solution)/shard_map/ppermute | solution.py:85
  239.9 12.3 %collective-permute-start.27 = (f32[3,3,2,2,16,256]{5,4,3,2,1,0:T(8,128)S(1)}, f32[3,3,2,2,16,256]{5,4,3,2,1,0:T(8,128)S(1)}, u32[]{:S(2)}, u32[]{:S(2)}) collective-permute-start(f32[3,3,2,2,16,256]{5,4,3,2,1,0:T(8,128)S(1)} %dynamic-slice_bitcast_fusion.3), channel_id=1, source_target_pairs={{0,4},{1,17},{2,6},{3,19},{4,0},{5,21},{6,2},{7,23},{8,12},{9,25},... | collective-permute-start | bytes 1769480 | tf_op jit(solution)/shard_map/ppermute | solution.py:85
  243.0 9.1 %collective-permute-start.32 = (f32[2,2,8,512]{3,2,1,0:T(8,128)S(1)}, f32[2,2,8,512]{3,2,1,0:T(8,128)S(1)}, u32[]{:S(2)}, u32[]{:S(2)}) collective-permute-start(f32[2,2,8,512]{3,2,1,0:T(8,128)S(1)} %dynamic-slice_bitcast_fusion.12), channel_id=1, source_target_pairs={{0,4},{1,17},{2,6},{3,19},{4,0},{5,21},{6,2},{7,23},{8,12},{9,25},... | collective-permute-start | bytes 196616 | tf_op jit(solution)/shard_map/ppermute | solution.py:85
  252.1 4.0 %collective-permute-start.33 = (f32[2,8,512]{2,1,0:T(8,128)S(1)}, f32[2,8,512]{2,1,0:T(8,128)S(1)}, u32[]{:S(2)}, u32[]{:S(2)}) collective-permute-start(f32[2,8,512]{2,1,0:T(8,128)S(1)} %dynamic-slice_bitcast_fusion.14), channel_id=1, source_target_pairs={{0,8},{1,3},{2,10},{3,1},{4,12},{5,7},{6,14},{7,5},{8,0},{9,11},{1... | collective-permute-start | bytes 98312 | tf_op jit(solution)/shard_map/ppermute | solution.py:85
  252.4 6.9 %collective-permute-start.28 = (f32[3,3,2,16,256]{4,3,2,1,0:T(8,128)S(1)}, f32[3,3,2,16,256]{4,3,2,1,0:T(8,128)S(1)}, u32[]{:S(2)}, u32[]{:S(2)}) collective-permute-start(f32[3,3,2,16,256]{4,3,2,1,0:T(8,128)S(1)} %dynamic-slice_bitcast_fusion.5), channel_id=1, source_target_pairs={{0,8},{1,3},{2,10},{3,1},{4,12},{5,7},{6,14},{7,5},{8,0},{9,11},{1... | collective-permute-start | bytes 884744 | tf_op jit(solution)/shard_map/ppermute | solution.py:85
  256.1 7.1 %collective-permute-start.34 = (f32[8,512]{1,0:T(8,128)S(1)}, f32[8,512]{1,0:T(8,128)S(1)}, u32[]{:S(2)}, u32[]{:S(2)}) collective-permute-start(f32[8,512]{1,0:T(8,128)S(1)} %dynamic-slice_bitcast_fusion.16), channel_id=1, source_target_pairs={{0,16},{1,5},{2,18},{3,7},{4,20},{5,1},{6,22},{7,3},{8,24},{9,13},... | collective-permute-start | bytes 49160 | tf_op jit(solution)/shard_map/ppermute | solution.py:85
  259.4 6.7 %collective-permute-start.29 = (f32[3,3,16,256]{3,2,1,0:T(8,128)S(1)}, f32[3,3,16,256]{3,2,1,0:T(8,128)S(1)}, u32[]{:S(2)}, u32[]{:S(2)}) collective-permute-start(f32[3,3,16,256]{3,2,1,0:T(8,128)S(1)} %dynamic-slice_bitcast_fusion.9), channel_id=1, source_target_pairs={{0,16},{1,5},{2,18},{3,7},{4,20},{5,1},{6,22},{7,3},{8,24},{9,13},... | collective-permute-start | bytes 442376 | tf_op jit(solution)/shard_map/ppermute | solution.py:85
  275.0 5.1 %collective-permute-start.37 = (f32[2]{0:T(128)S(1)}, f32[2]{0:T(128)S(1)}, u32[]{:S(2)}, u32[]{:S(2)}) collective-permute-start(f32[2]{0:T(128)S(1)} %fusion.136), channel_id=1, source_target_pairs={{0,4},{1,5},{2,6},{3,7},{4,0},{5,1},{6,2},{7,3},{8,12},{9,13},{10,... | collective-permute-start | bytes 32 | tf_op jit(solution)/shard_map/ppermute | solution.py:85
  283.6 5.1 %collective-permute-start.39 = (f32[2]{0:T(128)S(1)}, f32[2]{0:T(128)S(1)}, u32[]{:S(2)}, u32[]{:S(2)}) collective-permute-start(f32[2]{0:T(128)S(1)} %add.361), channel_id=1, source_target_pairs={{0,16},{1,17},{2,18},{3,19},{4,20},{5,21},{6,22},{7,23},{8,24},{9,... | collective-permute-start | bytes 32 | tf_op jit(solution)/shard_map/ppermute | solution.py:85
  (39 other events, 239.3 us)

commit v4 on v1

--- a/solution.py
+++ b/solution.py
@@ -81,15 +81,72 @@
     return 0.004 * lax.rsqrt(squares / entries + 1e-06)
 
 
+def partner_swap(value, pairs):
+    return lax.ppermute(value, "ex", perm=pairs)
+
+
+def stage_pairs(bits_of, peers):
+    return [(i, i ^ (1 << bits_of[i % 2])) for i in range(peers)]
+
+
+def swap_bit_axes(value):
+    order = list(range(value.ndim))
+    order[:4] = [2, 3, 0, 1]
+    return jnp.transpose(value, order)
+
+
+STAGE_BITS = ((0, 1, 2, 3, 4), (0, 3, 4, 1, 2))
+
+
+def scatter_sum(packed, place, second_core, levels, peers):
+    for stage in range(levels):
+        if stage == 1:
+            packed = jnp.where(second_core, swap_bit_axes(packed), packed)
+        bits_of = (STAGE_BITS[0][stage], STAGE_BITS[1][stage])
+        bit = jnp.where(second_core, bits_of[1], bits_of[0])
+        mine = (place >> bit) & 1
+        axis = levels - 1 - stage
+        keep = lax.dynamic_index_in_dim(packed, mine, axis, keepdims=False)
+        give = lax.dynamic_index_in_dim(packed, 1 - mine, axis, keepdims=False)
+        packed = keep + partner_swap(give, stage_pairs(bits_of, peers))
+    return packed
+
+
+def gather_all(block, place, second_core, levels, peers):
+    for step_index in range(levels):
+        stage = levels - 1 - step_index
+        if stage == 0:
+            block = jnp.where(second_core, swap_bit_axes(block), block)
+        bits_of = (STAGE_BITS[0][stage], STAGE_BITS[1][stage])
+        bit = jnp.where(second_core, bits_of[1], bits_of[0])
+        mine = (place >> bit) & 1
+        other = partner_swap(block, stage_pairs(bits_of, peers))
+        first = jnp.where(mine == 0, block, other)
+        second = jnp.where(mine == 0, other, block)
+        block = jnp.stack([first, second], axis=step_index)
+    return block
+
+
+def pack_grads(grad_down, grad_up, peers, spare):
+    lanes = 128
+    down_rows = grad_down.reshape(3, 3, peers, -1, grad_down.shape[3])
+    down_rows = jnp.transpose(down_rows, (2, 0, 1, 3, 4)).reshape(peers, -1, lanes)
+    up_rows = grad_up.reshape(peers, -1, lanes)
+    parts = [down_rows, up_rows]
+    if spare is not None:
+        parts.append(spare)
+    return jnp.concatenate(parts, axis=1)
+
+
 def shards(feats, targets, task_of, counts, down_w, up_w, head):
     groups = lax.axis_size("task")
     peers = lax.axis_size("ex")
+    levels = peers.bit_length() - 1
     sources = feats.shape[0]
     side = feats.shape[1]
     chans = feats.shape[3]
     cells = side * side
     bucket = (2 * sources + groups - 1) // groups
-    holding = 2 * sources
     order = jnp.arange(sources, dtype=jnp.int32)
     earlier = (task_of[:, None] == task_of[None, :]) & (order[None, :] < order[:, None])
     position = jnp.sum(earlier.astype(jnp.int32), axis=1)
@@ -111,30 +168,56 @@
     held_labels = come_labels.reshape(groups * bucket, cells).astype(jnp.int32)
     count = counts[0].astype(jnp.float32)
     entries = 10.0 * CHANNELS * INNER
-    ex_place = lax.axis_index("ex")
+    place = lax.axis_index("ex")
     part_chans = down_w.shape[3] // peers
     part_inner = up_w.shape[1] // peers
-    collected = []
-    down_low = down_w[0].astype(jnp.bfloat16)
-    upper_low = up_w[0].astype(jnp.bfloat16)
-    down_own = lax.dynamic_slice_in_dim(down_w[0], ex_place * part_chans, part_chans, 2)
-    up_own = lax.dynamic_slice_in_dim(up_w[0], ex_place * part_inner, part_inner, 0)
-    for update_round in range(TRAIN_STEPS):
-        loss_sum, grad_down, grad_up = train_pass(
-            held_feats, held_labels, down_low, upper_low, head, count
-        )
-        grad_down = lax.psum_scatter(grad_down, "ex", scatter_dimension=2, tiled=True)
-        grad_up = lax.psum_scatter(grad_up, "ex", scatter_dimension=0, tiled=True)
-        squares = jnp.sum(grad_down * grad_down) + jnp.sum(grad_up * grad_up)
-        totals = lax.psum(jnp.stack([squares, loss_sum]), "ex")
-        scale = step_scale(totals[0], entries)
-        down_own = down_own - scale * grad_down
-        up_own = up_own - scale * grad_up
-        collected.append(totals[1] / (count * cells))
-        if update_round + 1 < TRAIN_STEPS:
-            down_low = lax.all_gather(down_own.astype(jnp.bfloat16), "ex", axis=2, tiled=True)
-            upper_low = lax.all_gather(up_own.astype(jnp.bfloat16), "ex", axis=0, tiled=True)
-    return (down_own[None], up_own[None], jnp.stack(collected)[None])
+    inner = down_w.shape[4]
+    outer = up_w.shape[2]
+    lanes = 128
+    down_span = 9 * part_chans * inner // lanes
+    up_span = part_inner * outer // lanes
+    second_core = (place % 2) == 1
+    bits_shape = (2,) * levels
+    spare_rows = 8
+
+    loss_sum, grad_down, grad_up = train_pass(
+        held_feats, held_labels, down_w[0].astype(jnp.bfloat16), up_w[0].astype(jnp.bfloat16), head, count
+    )
+    row_ids = lax.broadcasted_iota(jnp.int32, (peers, spare_rows, lanes), 0)
+    col_ids = lax.broadcasted_iota(jnp.int32, (peers, spare_rows, lanes), 2)
+    first_cell = (row_ids == 0) & (col_ids == 0)
+    spare = jnp.where(first_cell & (lax.broadcasted_iota(jnp.int32, (peers, spare_rows, lanes), 1) == 0), loss_sum, 0.0)
+    packed = pack_grads(grad_down, grad_up, peers, spare)
+    packed = packed.reshape(bits_shape + packed.shape[1:])
+    block = scatter_sum(packed, place, second_core, levels, peers)
+    full = gather_all(block, place, second_core, levels, peers).reshape((peers,) + block.shape)
+    full_down = full[:, :down_span].reshape(peers, 3, 3, part_chans, inner)
+    full_down = jnp.transpose(full_down, (1, 2, 0, 3, 4)).reshape(down_w.shape[1:])
+    full_up = full[:, down_span : down_span + up_span].reshape(up_w.shape[1:])
+    loss_first = full[0, down_span + up_span, 0]
+    squares = jnp.sum(full_down * full_down) + jnp.sum(full_up * full_up)
+    scale = step_scale(squares, entries)
+    down_next = down_w[0] - scale * full_down
+    up_next = up_w[0] - scale * full_up
+    down_own = lax.dynamic_slice_in_dim(down_next, place * part_chans, part_chans, 2)
+    up_own = lax.dynamic_slice_in_dim(up_next, place * part_inner, part_inner, 0)
+
+    loss_sum, grad_down, grad_up = train_pass(
+        held_feats, held_labels, down_next.astype(jnp.bfloat16), up_next.astype(jnp.bfloat16), head, count
+    )
+    packed = pack_grads(grad_down, grad_up, peers, None)
+    packed = packed.reshape(bits_shape + packed.shape[1:])
+    block = scatter_sum(packed, place, second_core, levels, peers)
+    shard_down = block[:down_span].reshape(down_own.shape)
+    shard_up = block[down_span:].reshape(up_own.shape)
+    totals = jnp.stack([jnp.sum(shard_down * shard_down) + jnp.sum(shard_up * shard_up), loss_sum])
+    for bit in range(levels):
+        totals = totals + partner_swap(totals, stage_pairs((bit, bit), peers))
+    scale = step_scale(totals[0], entries)
+    down_own = down_own - scale * shard_down
+    up_own = up_own - scale * shard_up
+    losses = jnp.stack([loss_first, totals[1]]) / (count * cells)
+    return (down_own[None], up_own[None], losses[None])
 
 
 def solution(mesh):

time: 619 us -> 370 us (0.60); the launches traced: 607 us -> 365 us
  waiting for transfers between devices: 332 us -> 141 us
  blocking collectives: 148 us -> 0 us
  local copies, waits for them, and re-layouts: 25.1 us -> 73.5 us
  starting transfers between devices: 8.84 us -> 52.5 us
  other arithmetic: 22.3 us -> 53 us
  between operations: 20.5 us -> 5.9 us
  matrix products: 50.6 us -> 39.3 us
    reduce_scatter x4 -> x0, waiting for transfers between devices: 297 us -> none  [the longest x2 172 us: shards(): lax.psum_scatter(grad_down, 'ex', scatter_dimension=2, tiled=True)]
    psum x2 -> x0, blocking collectives: 126 us -> none  [shards(): totals = lax.psum(jnp.stack([squares, loss_sum]), 'ex')]
    ppermute x0 -> x20, waiting for transfers between devices: none -> 125 us  [partner_swap(): return lax.ppermute(value, 'ex', perm=pairs)]
    ppermute x0 -> x20, starting transfers between devices: none -> 44.3 us  [partner_swap(): return lax.ppermute(value, 'ex', perm=pairs)]
    all_gather x1 -> x0, blocking collectives: 21.9 us -> none  [shards(): lax.all_gather(up_own.astype(jnp.bfloat16), 'ex', axis=0, tiled=True)]
    all_gather x1 -> x0, waiting for transfers between devices: 18.9 us -> none  [shards(): lax.all_gather(down_own.astype(jnp.bfloat16), 'ex', axis=2, tiled=True)]
    concatenate x0 -> x5, local copies, waits for them, and re-layouts: none -> 15.3 us  [pack_grads(): return jnp.concatenate(parts, axis=1)]
    mul x0 -> x5, local copies, waits for them, and re-layouts: none -> 11.9 us  [the longest x2 11.7 us: shards(): down_next = down_w[0] - scale * full_down]
  transfers between devices with their start and end apart: 7 -> 22, of which waited for: 7 -> 22; matrix products, arithmetic and copies ran while one was open for 6% -> 3% of each run, Pallas kernels for 0% -> 0%
where the time goes in v4:
time: 370 us; the launch traced here: 365 us
  waiting for transfers between devices  141 us (38%)
  local copies, waits for them, and re-layouts  73.5 us (20%)
  other arithmetic  53 us (14%)
  starting transfers between devices  52.5 us (14%)
  matrix products  39.3 us (11%)
  between operations  5.9 us (2%)
    ppermute x20, waiting for transfers between devices, partner_swap(): return lax.ppermute(value, 'ex', perm=pairs)  125 us
    ppermute x20, starting transfers between devices, partner_swap(): return lax.ppermute(value, 'ex', perm=pairs)  44.3 us
    unnamed x97, local copies, waits for them, and re-layouts  25.5 us
    dot_general x20, matrix products, contract_rows(): lax.dot_general(left, right, (((0,), (0,)), ((), ())), preferred_element_...  18.1 us
    concatenate x5, local copies, waits for them, and re-layouts, pack_grads(): return jnp.concatenate(parts, axis=1)  15.3 us
    all_to_all x1, waiting for transfers between devices, shards(): lax.all_to_all(send_feats, 'task', split_axis=0, concat_axis=0, tiled=True)  15.2 us
    mul x2, local copies, waits for them, and re-layouts, shards(): down_next = down_w[0] - scale * full_down  11.7 us
    dot_general x18, matrix products, train_pass(): jnp.dot(windows[offset_index], down_low[offset_index // 3, offset_index %...  10.3 us
  transfers between devices with their start and end apart: 22, of which 22 were waited for; matrix products, arithmetic and copies ran while one was open for 3% of the time, Pallas kernels for 0%

profile of v4, /device:TPU:0, one launch (start us, length us, event | category | flops | bytes accessed | tf_op | source)
XLA Modules:
  0.0 365.5 jit_solution(1524885261904399939)
XLA Ops:
  4.8 4.4 %all-to-all-start.1 = ((bf16[4,2,192]{2,1,0:T(2,128)(2,1)}), bf16[4,2,192]{2,1,0:T(2,128)(2,1)S(1)}, u32[]{:S(2)}, u32[]{:S(2)}) async-start(bf16[4,2,192]{2,1,0:T(2,128)(2,1)} %reshape.206), calls=%async_computation.1 | async-start | bytes 8192 | tf_op jit(solution)/shard_map/all_to_all | solution.py:165
  14.5 3.8 %all-to-all-start = ((bf16[4,6,8,8,512]{4,3,2,1,0:T(8,128)(2,1)}), bf16[4,6,8,8,512]{4,3,2,1,0:T(8,128)(2,1)S(1)}, u32[]{:S(2)}, u32[]{:S(2)}) async-start(bf16[4,6,8,8,512]{4,3,2,1,0:T(8,128)(2,1)} %scatter_fusion), calls=%async_computation | async-start | bytes 3145728 | tf_op jit(solution)/shard_map/all_to_all | solution.py:164
  19.0 4.0 %bitcast_convert_fusion = bf16[3,3,512,256]{3,2,1,0:T(8,128)(2,1)} fusion(f32[1,3,3,512,256]{4,3,2,1,0:T(8,128)} %param.11), kind=kLoop, calls=%fused_computation.13 | loop fusion | flops 1179648 | bytes 7077888 | tf_op jit(solution)/shard_map/convert_element_type | solution.py:184
  23.2 15.2 %all-to-all-done = bf16[4,6,8,8,512]{4,3,2,1,0:T(8,128)(2,1)S(1)} async-done(((bf16[4,6,8,8,512]{4,3,2,1,0:T(8,128)(2,1)}), bf16[4,6,8,8,512]{4,3,2,1,0:T(8,128)(2,1)S(1)}, u32[]{:S(2)}, u32[]{:S(2)}) %all-to-all-start) | async-done | bytes 1572896 | tf_op jit(solution)/shard_map/all_to_all | solution.py:164
  73.9 5.8 %concatenate.28 = f32[2,2,2,2,2,288,128]{6,5,4,3,2,1,0:T(8,128)} reshape(f32[32,3,3,16,256]{4,3,2,1,0:T(8,128)} %bitcast.351) | data formatting | bytes 9437184 | tf_op jit(solution)/shard_map/concatenate | solution.py:138
  86.7 5.3 %collective-permute-done = f32[2,2,2,2,328,128]{5,4,3,2,1,0:T(8,128)} collective-permute-done((f32[2,2,2,2,328,128]{5,4,3,2,1,0:T(8,128)}, f32[2,2,2,2,328,128]{5,4,3,2,1,0:T(8,128)}, u32[]{:S(2)}, u32[]{:S(2)}) %collective-permute-start) | collective-permute-done | bytes 2687008 | tf_op jit(solution)/shard_map/ppermute | solution.py:85
  98.4 16.4 %collective-permute-done.1 = f32[2,2,2,328,128]{4,3,2,1,0:T(8,128)} collective-permute-done((f32[2,2,2,328,128]{4,3,2,1,0:T(8,128)S(1)}, f32[2,2,2,328,128]{4,3,2,1,0:T(8,128)}, u32[]{:S(2)}, u32[]{:S(2)}) %collective-permute-start.1) | collective-permute-done | bytes 1343520 | tf_op jit(solution)/shard_map/ppermute | solution.py:85
  117.6 3.2 collective-permute-start.2
  120.8 9.4 %collective-permute-done.2 = f32[2,2,328,128]{3,2,1,0:T(8,128)} collective-permute-done((f32[2,2,328,128]{3,2,1,0:T(8,128)}, f32[2,2,328,128]{3,2,1,0:T(8,128)}, u32[]{:S(2)}, u32[]{:S(2)}) %collective-permute-start.2) | collective-permute-done | bytes 671776 | tf_op jit(solution)/shard_map/ppermute | solution.py:85
  134.2 5.2 %collective-permute-done.3 = f32[2,328,128]{2,1,0:T(8,128)S(1)} collective-permute-done((f32[2,328,128]{2,1,0:T(8,128)S(1)}, f32[2,328,128]{2,1,0:T(8,128)S(1)}, u32[]{:S(2)}, u32[]{:S(2)}) %collective-permute-start.3) | collective-permute-done | bytes 335904 | tf_op jit(solution)/shard_map/ppermute | solution.py:85
  140.5 4.0 %collective-permute-start.4 = (f32[328,128]{1,0:T(8,128)S(1)}, f32[328,128]{1,0:T(8,128)S(1)}, u32[]{:S(2)}, u32[]{:S(2)}) collective-permute-start(f32[328,128]{1,0:T(8,128)S(1)} %dynamic-slice_bitcast_fusion.8), channel_id=1, source_target_pairs={{0,16},{1,5},{2,18},{3,7},{4,20},{5,1},{6,22},{7,3},{8,24},{9,13},... | collective-permute-start | bytes 503816 | tf_op jit(solution)/shard_map/ppermute | solution.py:85
  144.5 3.3 collective-permute-done.4
  147.8 3.6 collective-permute-start.5
  151.4 3.3 collective-permute-done.5
  156.5 5.6 %collective-permute-done.6 = f32[2,328,128]{2,1,0:T(8,128)S(1)} collective-permute-done((f32[2,328,128]{2,1,0:T(8,128)S(1)}, f32[2,328,128]{2,1,0:T(8,128)S(1)}, u32[]{:S(2)}, u32[]{:S(2)}) %collective-permute-start.6) | collective-permute-done | bytes 335904 | tf_op jit(solution)/shard_map/ppermute | solution.py:85
  163.0 3.3 collective-permute-start.7
  166.3 9.2 %collective-permute-done.7 = f32[2,2,328,128]{3,2,1,0:T(8,128)S(1)} collective-permute-done((f32[2,2,328,128]{3,2,1,0:T(8,128)}, f32[2,2,328,128]{3,2,1,0:T(8,128)S(1)}, u32[]{:S(2)}, u32[]{:S(2)}) %collective-permute-start.7) | collective-permute-done | bytes 671776 | tf_op jit(solution)/shard_map/ppermute | solution.py:85
  178.3 16.4 %collective-permute-done.8 = f32[2,2,2,328,128]{4,3,2,1,0:T(8,128)} collective-permute-done((f32[2,2,2,328,128]{4,3,2,1,0:T(8,128)S(1)}, f32[2,2,2,328,128]{4,3,2,1,0:T(8,128)}, u32[]{:S(2)}, u32[]{:S(2)}) %collective-permute-start.8) | collective-permute-done | bytes 1343520 | tf_op jit(solution)/shard_map/ppermute | solution.py:85
  198.6 5.3 %collective-permute-done.9 = f32[2,2,2,2,328,128]{5,4,3,2,1,0:T(8,128)} collective-permute-done((f32[2,2,2,2,328,128]{5,4,3,2,1,0:T(8,128)}, f32[2,2,2,2,328,128]{5,4,3,2,1,0:T(8,128)}, u32[]{:S(2)}, u32[]{:S(2)}) %collective-permute-start.9) | collective-permute-done | bytes 2687008 | tf_op jit(solution)/shard_map/ppermute | solution.py:85
  214.4 4.9 %slice_multiply_fusion = f32[32,288,128]{2,1,0:T(8,128)} fusion(f32[32,328,128]{2,1,0:T(8,128)} %bitcast.343, f32[]{:T(128)S(6)} %mul.202), kind=kLoop, calls=%fused_computation.17 | loop fusion | flops 1179648 | bytes 9437188 | tf_op jit(solution)/shard_map/mul | solution.py:200
  219.2 6.4 %mul.205 = f32[32,3,3,16,256]{4,3,2,1,0:T(8,128)} reshape(f32[32,288,128]{2,1,0:T(8,128)} %slice_multiply_fusion) | data formatting | bytes 9437184 | tf_op jit(solution)/shard_map/mul | solution.py:200
  225.7 5.3 %copy.84 = f32[3,3,32,16,256]{4,3,2,1,0:T(8,128)} copy(f32[3,3,32,16,256]{4,3,1,0,2:T(8,128)} %bitcast.352) | data formatting | bytes 9437184 | tf_op jit(solution)/shard_map/mul | solution.py:200
  231.2 6.9 %fusion.61 = (bf16[3,3,512,256]{3,2,1,0:T(8,128)(2,1)S(1)}, f32[3,3,512,256]{3,2,1,0:T(8,128)}) fusion(f32[3,3,32,16,256]{4,3,2,1,0:T(8,128)} %copy.84, f32[1,3,3,512,256]{4,3,2,1,0:T(8,128)} %param.11), kind=kLoop, calls=%fused_computation.220 | loop fusion | flops 2359296 | bytes 16515072 | tf_op jit(solution)/shard_map/convert_element_type | solution.py:206
  273.8 5.8 %concatenate.31 = f32[2,2,2,2,2,288,128]{6,5,4,3,2,1,0:T(8,128)} reshape(f32[32,3,3,16,256]{4,3,2,1,0:T(8,128)} %bitcast.353) | data formatting | bytes 9437184 | tf_op jit(solution)/shard_map/concatenate | solution.py:138
  282.8 4.8 %collective-permute-done.10 = f32[2,2,2,2,320,128]{5,4,3,2,1,0:T(8,128)S(1)} collective-permute-done((f32[2,2,2,2,320,128]{5,4,3,2,1,0:T(8,128)S(1)}, f32[2,2,2,2,320,128]{5,4,3,2,1,0:T(8,128)S(1)}, u32[]{:S(2)}, u32[]{:S(2)}) %collective-permute-start.10) | collective-permute-done | bytes 2621472 | tf_op jit(solution)/shard_map/ppermute | solution.py:85
  290.0 16.0 %collective-permute-done.11 = f32[2,2,2,320,128]{4,3,2,1,0:T(8,128)S(1)} collective-permute-done((f32[2,2,2,320,128]{4,3,2,1,0:T(8,128)S(1)}, f32[2,2,2,320,128]{4,3,2,1,0:T(8,128)S(1)}, u32[]{:S(2)}, u32[]{:S(2)}) %collective-permute-start.11) | collective-permute-done | bytes 1310752 | tf_op jit(solution)/shard_map/ppermute | solution.py:85
  306.2 3.3 collective-permute-start.12
  309.6 8.8 %collective-permute-done.12 = f32[2,2,320,128]{3,2,1,0:T(8,128)S(1)} collective-permute-done((f32[2,2,320,128]{3,2,1,0:T(8,128)S(1)}, f32[2,2,320,128]{3,2,1,0:T(8,128)S(1)}, u32[]{:S(2)}, u32[]{:S(2)}) %collective-permute-start.12) | collective-permute-done | bytes 655392 | tf_op jit(solution)/shard_map/ppermute | solution.py:85
  320.3 5.3 %collective-permute-done.13 = f32[2,320,128]{2,1,0:T(8,128)S(1)} collective-permute-done((f32[2,320,128]{2,1,0:T(8,128)S(1)}, f32[2,320,128]{2,1,0:T(8,128)S(1)}, u32[]{:S(2)}, u32[]{:S(2)}) %collective-permute-start.13) | collective-permute-done | bytes 327712 | tf_op jit(solution)/shard_map/ppermute | solution.py:85
  325.8 6.8 %collective-permute-start.14 = (f32[320,128]{1,0:T(8,128)S(1)}, f32[320,128]{1,0:T(8,128)S(1)}, u32[]{:S(2)}, u32[]{:S(2)}) collective-permute-start(f32[320,128]{1,0:T(8,128)S(1)} %dynamic-slice_bitcast_fusion.9), channel_id=1, source_target_pairs={{0,16},{1,5},{2,18},{3,7},{4,20},{5,1},{6,22},{7,3},{8,24},{9,13},... | collective-permute-start | bytes 491528 | tf_op jit(solution)/shard_map/ppermute | solution.py:85
  345.4 3.0 collective-permute-start.17
  354.0 3.5 collective-permute-start.19
  (252 shorter events, 151.7 us)
Async XLA Ops:
  0.6 49.9 %copy-start = (bf16[512,10]{0,1:T(8,128)(2,1)S(1)}, bf16[512,10]{0,1:T(8,128)(2,1)}, u32[]{:S(2)}) copy-start(bf16[512,10]{0,1:T(8,128)(2,1)} %param.13) | copy-start | bytes 30724
  0.6 9.9 %copy-start.41 = (bf16[12,8,8,512]{3,2,1,0:T(8,128)(2,1)S(1)}, bf16[12,8,8,512]{3,2,1,0:T(8,128)(2,1)}, u32[]{:S(2)}) copy-start(bf16[12,8,8,512]{3,2,1,0:T(8,128)(2,1)} %param.7) | copy-start | bytes 2359300
  4.8 9.7 %all-to-all-start.1 = ((bf16[4,2,192]{2,1,0:T(2,128)(2,1)}), bf16[4,2,192]{2,1,0:T(2,128)(2,1)S(1)}, u32[]{:S(2)}, u32[]{:S(2)}) async-start(bf16[4,2,192]{2,1,0:T(2,128)(2,1)} %reshape.206), calls=%async_computation.1 | async-start | bytes 8192 | tf_op jit(solution)/shard_map/all_to_all | solution.py:165
  14.5 23.9 %all-to-all-start = ((bf16[4,6,8,8,512]{4,3,2,1,0:T(8,128)(2,1)}), bf16[4,6,8,8,512]{4,3,2,1,0:T(8,128)(2,1)S(1)}, u32[]{:S(2)}, u32[]{:S(2)}) async-start(bf16[4,6,8,8,512]{4,3,2,1,0:T(8,128)(2,1)} %scatter_fusion), calls=%async_computation | async-start | bytes 3145728 | tf_op jit(solution)/shard_map/all_to_all | solution.py:164
  42.6 3.8 %copy-start.14 = (bf16[24,8,8,512]{3,2,1,0:T(8,128)(2,1)}, bf16[24,8,8,512]{3,2,1,0:T(8,128)(2,1)S(1)}, u32[]{:S(2)}) copy-start(bf16[24,8,8,512]{3,2,1,0:T(8,128)(2,1)S(1)} %get-tuple-element.17) | copy-start | bytes 4718596
  42.6 4.3 %copy-start.10 = (bf16[24,8,8,512]{3,2,1,0:T(8,128)(2,1)}, bf16[24,8,8,512]{3,2,1,0:T(8,128)(2,1)S(1)}, u32[]{:S(2)}) copy-start(bf16[24,8,8,512]{3,2,1,0:T(8,128)(2,1)S(1)} %get-tuple-element.18) | copy-start | bytes 4718596
  42.6 4.9 %copy-start.6 = (bf16[24,8,8,512]{3,2,1,0:T(8,128)(2,1)}, bf16[24,8,8,512]{3,2,1,0:T(8,128)(2,1)S(1)}, u32[]{:S(2)}) copy-start(bf16[24,8,8,512]{3,2,1,0:T(8,128)(2,1)S(1)} %get-tuple-element.19) | copy-start | bytes 4718596
  42.6 28.0 %copy-start.4 = (bf16[24,8,8,512]{3,2,1,0:T(8,128)(2,1)}, bf16[24,8,8,512]{3,2,1,0:T(8,128)(2,1)S(1)}, u32[]{:S(2)}) copy-start(bf16[24,8,8,512]{3,2,1,0:T(8,128)(2,1)S(1)} %get-tuple-element.13) | copy-start | bytes 4718596
  73.9 6.6 %copy-start.38 = (f32[2,2,2,2,2,32,128]{6,5,4,3,2,1,0:T(8,128)S(1)}, f32[2,2,2,2,2,32,128]{6,5,4,3,2,1,0:T(8,128)}, u32[]{:S(2)}) copy-start(f32[2,2,2,2,2,32,128]{6,5,4,3,2,1,0:T(8,128)} %concatenate.29) | copy-start | bytes 1572868
  86.7 5.3 %collective-permute-start = (f32[2,2,2,2,328,128]{5,4,3,2,1,0:T(8,128)}, f32[2,2,2,2,328,128]{5,4,3,2,1,0:T(8,128)}, u32[]{:S(2)}, u32[]{:S(2)}) collective-permute-start(f32[2,2,2,2,328,128]{5,4,3,2,1,0:T(8,128)} %dynamic-slice_bitcast_fusion), channel_id=1, source_target_pairs={{0,1},{1,0},{2,3},{3,2},{4,5},{5,4},{6,7},{7,6},{8,9},{9,8},{10,11... | collective-permute-start | bytes 8060936 | tf_op jit(solution)/shard_map/ppermute | solution.py:85
  96.7 18.1 %collective-permute-start.1 = (f32[2,2,2,328,128]{4,3,2,1,0:T(8,128)S(1)}, f32[2,2,2,328,128]{4,3,2,1,0:T(8,128)}, u32[]{:S(2)}, u32[]{:S(2)}) collective-permute-start(f32[2,2,2,328,128]{4,3,2,1,0:T(8,128)S(1)} %dynamic-slice_bitcast_fusion.2), channel_id=1, source_target_pairs={{0,2},{1,9},{2,0},{3,11},{4,6},{5,13},{6,4},{7,15},{8,10},{9,1},{1... | collective-permute-start | bytes 4030472 | tf_op jit(solution)/shard_map/ppermute | solution.py:85
  117.6 12.6 %collective-permute-start.2 = (f32[2,2,328,128]{3,2,1,0:T(8,128)}, f32[2,2,328,128]{3,2,1,0:T(8,128)}, u32[]{:S(2)}, u32[]{:S(2)}) collective-permute-start(f32[2,2,328,128]{3,2,1,0:T(8,128)} %dynamic-slice_bitcast_fusion.4), channel_id=1, source_target_pairs={{0,4},{1,17},{2,6},{3,19},{4,0},{5,21},{6,2},{7,23},{8,12},{9,25},... | collective-permute-start | bytes 2015240 | tf_op jit(solution)/shard_map/ppermute | solution.py:85
  132.2 7.2 %collective-permute-start.3 = (f32[2,328,128]{2,1,0:T(8,128)S(1)}, f32[2,328,128]{2,1,0:T(8,128)S(1)}, u32[]{:S(2)}, u32[]{:S(2)}) collective-permute-start(f32[2,328,128]{2,1,0:T(8,128)S(1)} %dynamic-slice_bitcast_fusion.6), channel_id=1, source_target_pairs={{0,8},{1,3},{2,10},{3,1},{4,12},{5,7},{6,14},{7,5},{8,0},{9,11},{1... | collective-permute-start | bytes 1007624 | tf_op jit(solution)/shard_map/ppermute | solution.py:85
  140.5 7.3 %collective-permute-start.4 = (f32[328,128]{1,0:T(8,128)S(1)}, f32[328,128]{1,0:T(8,128)S(1)}, u32[]{:S(2)}, u32[]{:S(2)}) collective-permute-start(f32[328,128]{1,0:T(8,128)S(1)} %dynamic-slice_bitcast_fusion.8), channel_id=1, source_target_pairs={{0,16},{1,5},{2,18},{3,7},{4,20},{5,1},{6,22},{7,3},{8,24},{9,13},... | collective-permute-start | bytes 503816 | tf_op jit(solution)/shard_map/ppermute | solution.py:85
  147.8 6.9 %collective-permute-start.5 = (f32[328,128]{1,0:T(8,128)S(1)}, f32[328,128]{1,0:T(8,128)S(1)}, u32[]{:S(2)}, u32[]{:S(2)}) collective-permute-start(f32[328,128]{1,0:T(8,128)S(1)} %bitcast_add_fusion.8), channel_id=1, source_target_pairs={{0,16},{1,5},{2,18},{3,7},{4,20},{5,1},{6,22},{7,3},{8,24},{9,13},... | collective-permute-start | bytes 503816 | tf_op jit(solution)/shard_map/ppermute | solution.py:85
  154.9 7.2 %collective-permute-start.6 = (f32[2,328,128]{2,1,0:T(8,128)S(1)}, f32[2,328,128]{2,1,0:T(8,128)S(1)}, u32[]{:S(2)}, u32[]{:S(2)}) collective-permute-start(f32[2,328,128]{2,1,0:T(8,128)S(1)} %pad_maximum_fusion.5), channel_id=1, source_target_pairs={{0,8},{1,3},{2,10},{3,1},{4,12},{5,7},{6,14},{7,5},{8,0},{9,11},{1... | collective-permute-start | bytes 1007624 | tf_op jit(solution)/shard_map/ppermute | solution.py:85
  163.0 12.5 %collective-permute-start.7 = (f32[2,2,328,128]{3,2,1,0:T(8,128)}, f32[2,2,328,128]{3,2,1,0:T(8,128)S(1)}, u32[]{:S(2)}, u32[]{:S(2)}) collective-permute-start(f32[2,2,328,128]{3,2,1,0:T(8,128)} %pad_maximum_fusion.4), channel_id=1, source_target_pairs={{0,4},{1,17},{2,6},{3,19},{4,0},{5,21},{6,2},{7,23},{8,12},{9,25},... | collective-permute-start | bytes 2015240 | tf_op jit(solution)/shard_map/ppermute | solution.py:85
  176.7 18.1 %collective-permute-start.8 = (f32[2,2,2,328,128]{4,3,2,1,0:T(8,128)S(1)}, f32[2,2,2,328,128]{4,3,2,1,0:T(8,128)}, u32[]{:S(2)}, u32[]{:S(2)}) collective-permute-start(f32[2,2,2,328,128]{4,3,2,1,0:T(8,128)S(1)} %pad_maximum_fusion.3), channel_id=1, source_target_pairs={{0,2},{1,9},{2,0},{3,11},{4,6},{5,13},{6,4},{7,15},{8,10},{9,1},{1... | collective-permute-start | bytes 4030472 | tf_op jit(solution)/shard_map/ppermute | solution.py:85
  198.6 5.3 %collective-permute-start.9 = (f32[2,2,2,2,328,128]{5,4,3,2,1,0:T(8,128)}, f32[2,2,2,2,328,128]{5,4,3,2,1,0:T(8,128)}, u32[]{:S(2)}, u32[]{:S(2)}) collective-permute-start(f32[2,2,2,2,328,128]{5,4,3,2,1,0:T(8,128)} %copy_select_fusion), channel_id=1, source_target_pairs={{0,1},{1,0},{2,3},{3,2},{4,5},{5,4},{6,7},{7,6},{8,9},{9,8},{10,11... | collective-permute-start | bytes 8060936 | tf_op jit(solution)/shard_map/ppermute | solution.py:85
  225.7 5.4 %copy-start.44 = (f32[1,256,512]{2,1,0:T(8,128)S(1)}, f32[1,256,512]{2,1,0:T(8,128)}, u32[]{:S(2)}) copy-start(f32[1,256,512]{2,1,0:T(8,128)} %param.12) | copy-start | bytes 1572868
  231.2 24.8 %copy-start.42 = (f32[256,512]{1,0:T(8,128)}, f32[256,512]{1,0:T(8,128)S(1)}, u32[]{:S(2)}) copy-start(f32[256,512]{1,0:T(8,128)S(1)} %bitcast_subtract_fusion.1) | copy-start | bytes 1572868
  231.2 6.9 %copy-start.31 = (bf16[24,8,8,512]{3,2,1,0:T(8,128)(2,1)S(1)}, bf16[24,8,8,512]{3,2,1,0:T(8,128)(2,1)}, u32[]{:S(2)}) copy-start(bf16[24,8,8,512]{3,2,1,0:T(8,128)(2,1)} %copy-done.30) | copy-start | bytes 4718596
  282.6 5.0 %collective-permute-start.10 = (f32[2,2,2,2,320,128]{5,4,3,2,1,0:T(8,128)S(1)}, f32[2,2,2,2,320,128]{5,4,3,2,1,0:T(8,128)S(1)}, u32[]{:S(2)}, u32[]{:S(2)}) collective-permute-start(f32[2,2,2,2,320,128]{5,4,3,2,1,0:T(8,128)S(1)} %dynamic-slice_bitcast_fusion.1), channel_id=1, source_target_pairs={{0,1},{1,0},{2,3},{3,2},{4,5},{5,4},{6,7},{7,6},{8,9},{9,8},{10,11... | collective-permute-start | bytes 7864328 | tf_op jit(solution)/shard_map/ppermute | solution.py:85
  288.3 17.7 %collective-permute-start.11 = (f32[2,2,2,320,128]{4,3,2,1,0:T(8,128)S(1)}, f32[2,2,2,320,128]{4,3,2,1,0:T(8,128)S(1)}, u32[]{:S(2)}, u32[]{:S(2)}) collective-permute-start(f32[2,2,2,320,128]{4,3,2,1,0:T(8,128)S(1)} %dynamic-slice_bitcast_fusion.3), channel_id=1, source_target_pairs={{0,2},{1,9},{2,0},{3,11},{4,6},{5,13},{6,4},{7,15},{8,10},{9,1},{1... | collective-permute-start | bytes 3932168 | tf_op jit(solution)/shard_map/ppermute | solution.py:85
  306.2 12.2 %collective-permute-start.12 = (f32[2,2,320,128]{3,2,1,0:T(8,128)S(1)}, f32[2,2,320,128]{3,2,1,0:T(8,128)S(1)}, u32[]{:S(2)}, u32[]{:S(2)}) collective-permute-start(f32[2,2,320,128]{3,2,1,0:T(8,128)S(1)} %dynamic-slice_bitcast_fusion.5), channel_id=1, source_target_pairs={{0,4},{1,17},{2,6},{3,19},{4,0},{5,21},{6,2},{7,23},{8,12},{9,25},... | collective-permute-start | bytes 1966088 | tf_op jit(solution)/shard_map/ppermute | solution.py:85
  318.5 7.2 %collective-permute-start.13 = (f32[2,320,128]{2,1,0:T(8,128)S(1)}, f32[2,320,128]{2,1,0:T(8,128)S(1)}, u32[]{:S(2)}, u32[]{:S(2)}) collective-permute-start(f32[2,320,128]{2,1,0:T(8,128)S(1)} %dynamic-slice_bitcast_fusion.7), channel_id=1, source_target_pairs={{0,8},{1,3},{2,10},{3,1},{4,12},{5,7},{6,14},{7,5},{8,0},{9,11},{1... | collective-permute-start | bytes 983048 | tf_op jit(solution)/shard_map/ppermute | solution.py:85
  325.8 10.1 %collective-permute-start.14 = (f32[320,128]{1,0:T(8,128)S(1)}, f32[320,128]{1,0:T(8,128)S(1)}, u32[]{:S(2)}, u32[]{:S(2)}) collective-permute-start(f32[320,128]{1,0:T(8,128)S(1)} %dynamic-slice_bitcast_fusion.9), channel_id=1, source_target_pairs={{0,16},{1,5},{2,18},{3,7},{4,20},{5,1},{6,22},{7,3},{8,24},{9,13},... | collective-permute-start | bytes 491528 | tf_op jit(solution)/shard_map/ppermute | solution.py:85
  339.1 1.2 collective-permute-start.15
  341.0 3.6 collective-permute-start.16
  345.4 5.1 %collective-permute-start.17 = (f32[2]{0:T(128)S(1)}, f32[2]{0:T(128)S(1)}, u32[]{:S(2)}, u32[]{:S(2)}) collective-permute-start(f32[2]{0:T(128)S(1)} %fusion.132), channel_id=1, source_target_pairs={{0,4},{1,5},{2,6},{3,7},{4,0},{5,1},{6,2},{7,3},{8,12},{9,13},{10,... | collective-permute-start | bytes 32 | tf_op jit(solution)/shard_map/ppermute | solution.py:85
  350.5 3.6 collective-permute-start.18
  354.0 5.1 %collective-permute-start.19 = (f32[2]{0:T(128)S(1)}, f32[2]{0:T(128)S(1)}, u32[]{:S(2)}, u32[]{:S(2)}) collective-permute-start(f32[2]{0:T(128)S(1)} %add.283), channel_id=1, source_target_pairs={{0,16},{1,17},{2,18},{3,19},{4,20},{5,21},{6,22},{7,23},{8,24},{9,... | collective-permute-start | bytes 32 | tf_op jit(solution)/shard_map/ppermute | solution.py:85
  (37 other events, 63.9 us)

commit v5 on v3

--- a/solution.py
+++ b/solution.py
@@ -170,8 +170,8 @@
             grad_up = halve_sum(grad_up, levels - 1 - stage, bit, pairs, place)
         squares = jnp.sum(grad_down * grad_down) + jnp.sum(grad_up * grad_up)
         totals = jnp.stack([squares, loss_sum])
-        for bit in range(levels):
-            totals = totals + partner_swap(totals, stage_pairs((bit, bit), peers))
+        spread = jnp.broadcast_to(totals[None, :], (peers, totals.shape[0]))
+        totals = jnp.sum(lax.all_to_all(spread, "ex", 0, 0, tiled=True), axis=0)
         scale = step_scale(totals[0], entries)
         down_own = down_own - scale * grad_down
         up_own = up_own - scale * grad_up

time: 297 us -> 283 us (0.953)
  starting transfers between devices: 71.5 us -> 57.8 us
  other arithmetic: 35 us -> 31.2 us
    ppermute x40 -> x30, starting transfers between devices: 63.4 us -> 37.5 us  [partner_swap(): return lax.ppermute(value, 'ex', perm=pairs)]
    all_to_all x0 -> x2, waiting for transfers between devices: none -> 14 us  [shards(): totals = jnp.sum(lax.all_to_all(spread, 'ex', 0, 0, tiled=True), axis=0)]
    all_to_all x0 -> x2, starting transfers between devices: none -> 12.1 us  [shards(): totals = jnp.sum(lax.all_to_all(spread, 'ex', 0, 0, tiled=True), axis=0)]
    ppermute x40 -> x30, waiting for transfers between devices: 104 us -> 92.2 us  [partner_swap(): return lax.ppermute(value, 'ex', perm=pairs)]
    unnamed x60 -> x58, local copies, waits for them, and re-layouts: 11.5 us -> 11.4 us
  transfers between devices with their start and end apart: 42 -> 34, of which waited for: 33 -> 25; matrix products, arithmetic and copies ran while one was open for 6% -> 6% of each run, Pallas kernels for 0% -> 0%
where the time goes in v5:
time: 283 us; the launch traced here: 279 us
  waiting for transfers between devices  122 us (43%)
  starting transfers between devices  57.8 us (20%)
  matrix products  32.7 us (12%)
  other arithmetic  31.2 us (11%)
  local copies, waits for them, and re-layouts  26.8 us (9%)
  between operations  7.71 us (3%)
    ppermute x30, waiting for transfers between devices, partner_swap(): return lax.ppermute(value, 'ex', perm=pairs)  92.2 us
    ppermute x30, starting transfers between devices, partner_swap(): return lax.ppermute(value, 'ex', perm=pairs)  37.5 us
    all_to_all x1, waiting for transfers between devices, shards(): lax.all_to_all(send_feats, 'task', split_axis=0, concat_axis=0, tiled=True)  15.3 us
    all_to_all x2, waiting for transfers between devices, shards(): totals = jnp.sum(lax.all_to_all(spread, 'ex', 0, 0, tiled=True), axis=0)  14 us
    dot_general x20, matrix products, contract_rows(): lax.dot_general(left, right, (((0,), (0,)), ((), ())), preferred_element_...  13 us
    all_to_all x2, starting transfers between devices, shards(): totals = jnp.sum(lax.all_to_all(spread, 'ex', 0, 0, tiled=True), axis=0)  12.1 us
    unnamed x58, local copies, waits for them, and re-layouts  11.4 us
    dot_general x18, matrix products, train_pass(): jnp.dot(windows[offset_index], down_low[offset_index // 3, offset_index %...  10.3 us
  transfers between devices with their start and end apart: 34, of which 25 were waited for; matrix products, arithmetic and copies ran while one was open for 6% of the time, Pallas kernels for 0%

profile of v5, /device:TPU:0, one launch (start us, length us, event | category | flops | bytes accessed | tf_op | source)
XLA Modules:
  0.0 278.6 jit_solution(17582653170110332309)
XLA Ops:
  4.8 4.4 %all-to-all-start.1 = ((bf16[4,2,192]{2,1,0:T(2,128)(2,1)}), bf16[4,2,192]{2,1,0:T(2,128)(2,1)S(1)}, u32[]{:S(2)}, u32[]{:S(2)}) async-start(bf16[4,2,192]{2,1,0:T(2,128)(2,1)} %reshape.178), calls=%async_computation.1 | async-start | bytes 8192 | tf_op jit(solution)/shard_map/all_to_all | solution.py:137
  10.5 2.9 %scatter_fusion = bf16[4,6,8,8,512]{4,3,2,1,0:T(8,128)(2,1)} fusion(bf16[4,6,8,8,512]{4,3,2,1,0:T(8,128)(2,1)} %broadcast_in_dim.16, s32[12]{0:T(128)S(1)} %fusion.63, bf16[12,8,8,512]{3,2,1,0:T(8,128)(2,1)S(1)} %copy-done.26), kind=kCustom, calls=%fused_computation | custom fusion | bytes 2359392 | tf_op jit(solution)/shard_map/scatter | solution.py:128
  14.5 3.8 %all-to-all-start = ((bf16[4,6,8,8,512]{4,3,2,1,0:T(8,128)(2,1)}), bf16[4,6,8,8,512]{4,3,2,1,0:T(8,128)(2,1)S(1)}, u32[]{:S(2)}, u32[]{:S(2)}) async-start(bf16[4,6,8,8,512]{4,3,2,1,0:T(8,128)(2,1)} %scatter_fusion), calls=%async_computation | async-start | bytes 3145728 | tf_op jit(solution)/shard_map/all_to_all | solution.py:136
  19.0 4.0 %convert_bitcast_fusion = bf16[3,3,512,256]{3,2,1,0:T(8,128)(2,1)} fusion(f32[1,3,3,512,256]{4,3,2,1,0:T(8,128)} %param.11), kind=kLoop, calls=%fused_computation.51 | loop fusion | flops 1179648 | bytes 7077888 | tf_op jit(solution)/shard_map/convert_element_type | solution.py:148
  23.1 15.3 %all-to-all-done = bf16[4,6,8,8,512]{4,3,2,1,0:T(8,128)(2,1)S(1)} async-done(((bf16[4,6,8,8,512]{4,3,2,1,0:T(8,128)(2,1)}), bf16[4,6,8,8,512]{4,3,2,1,0:T(8,128)(2,1)S(1)}, u32[]{:S(2)}, u32[]{:S(2)}) %all-to-all-start) | async-done | bytes 1572896 | tf_op jit(solution)/shard_map/all_to_all | solution.py:136
  39.1 2.6 pad_slice_fusion
  62.5 4.9 %collective-permute-done = f32[3,3,2,2,2,2,16,256]{7,6,5,4,3,2,1,0:T(8,128)} collective-permute-done((f32[3,3,2,2,2,2,16,256]{7,6,5,4,3,2,1,0:T(8,128)}, f32[3,3,2,2,2,2,16,256]{7,6,5,4,3,2,1,0:T(8,128)}, u32[]{:S(2)}, u32[]{:S(2)}) %collective-permute-start) | collective-permute-done | bytes 2359328 | tf_op jit(solution)/shard_map/ppermute | solution.py:85
  67.4 5.0 %copy_select_fusion.1 = f32[3,3,2,2,2,2,16,256]{7,6,5,4,3,2,1,0:T(8,128)S(1)} fusion(pred[]{:T(512)S(6)} %eq.26, f32[3,3,2,2,2,2,16,256]{7,6,5,4,3,2,1,0:T(8,128)} %collective-permute-done, f32[3,3,2,2,2,2,2,16,256]{8,7,6,5,4,3,2,1,0:T(8,128)} %bitcast.491, s32[]{:T(128)S(6)} %select_n.279), kind=kLoop, calls=%fused_computation.48 | loop fusion | flops 1769472 | bytes 11798016 | tf_op jit(solution)/shard_map/jit(_where)/select_n | solution.py:164
  79.2 12.3 %collective-permute-done.6 = f32[2,2,2,8,512]{4,3,1,0,2:T(8,128)S(1)} collective-permute-done((f32[2,2,2,8,512]{4,3,1,0,2:T(8,128)S(1)}, f32[2,2,2,8,512]{4,3,1,0,2:T(8,128)S(1)}, u32[]{:S(2)}, u32[]{:S(2)}) %collective-permute-start.6) | collective-permute-done | bytes 131104 | tf_op jit(solution)/shard_map/ppermute | solution.py:85
  94.2 3.3 %collective-permute-start.2 = (f32[3,3,2,2,16,256]{5,4,3,2,1,0:T(8,128)S(1)}, f32[3,3,2,2,16,256]{5,4,3,2,1,0:T(8,128)S(1)}, u32[]{:S(2)}, u32[]{:S(2)}) collective-permute-start(f32[3,3,2,2,16,256]{5,4,3,2,1,0:T(8,128)S(1)} %dynamic-slice_bitcast_fusion.4), channel_id=1, source_target_pairs={{0,4},{1,17},{2,6},{3,19},{4,0},{5,21},{6,2},{7,23},{8,12},{9,25},... | collective-permute-start | bytes 1769480 | tf_op jit(solution)/shard_map/ppermute | solution.py:85
  97.9 8.5 %collective-permute-done.7 = f32[2,2,8,512]{3,2,1,0:T(8,128)S(1)} collective-permute-done((f32[2,2,8,512]{3,2,1,0:T(8,128)S(1)}, f32[2,2,8,512]{3,2,1,0:T(8,128)S(1)}, u32[]{:S(2)}, u32[]{:S(2)}) %collective-permute-start.7) | collective-permute-done | bytes 65568 | tf_op jit(solution)/shard_map/ppermute | solution.py:85
  110.4 4.0 %collective-permute-start.9 = (f32[8,512]{1,0:T(8,128)S(1)}, f32[8,512]{1,0:T(8,128)S(1)}, u32[]{:S(2)}, u32[]{:S(2)}) collective-permute-start(f32[8,512]{1,0:T(8,128)S(1)} %dynamic-slice_bitcast_fusion.17), channel_id=1, source_target_pairs={{0,16},{1,5},{2,18},{3,7},{4,20},{5,1},{6,22},{7,3},{8,24},{9,13},... | collective-permute-start | bytes 49160 | tf_op jit(solution)/shard_map/ppermute | solution.py:85
  114.5 2.0 collective-permute-done.3
  116.5 3.7 %collective-permute-start.4 = (f32[3,3,16,256]{3,2,1,0:T(8,128)S(1)}, f32[3,3,16,256]{3,2,1,0:T(8,128)S(1)}, u32[]{:S(2)}, u32[]{:S(2)}) collective-permute-start(f32[3,3,16,256]{3,2,1,0:T(8,128)S(1)} %dynamic-slice_bitcast_fusion.10), channel_id=1, source_target_pairs={{0,16},{1,5},{2,18},{3,7},{4,20},{5,1},{6,22},{7,3},{8,24},{9,13},... | collective-permute-start | bytes 442376 | tf_op jit(solution)/shard_map/ppermute | solution.py:85
  126.6 7.9 %all-to-all-start.2 = ((f32[32,1,2]{2,1,0:T(1,128)}), f32[32,1,2]{2,1,0:T(1,128)S(1)}, u32[]{:S(2)}, u32[]{:S(2)}) async-start(f32[32,1,2]{2,1,0:T(1,128)} %broadcast_in_dim.19), calls=%async_computation.2 | async-start | bytes 32768 | tf_op jit(solution)/shard_map/all_to_all | solution.py:174
  134.5 7.3 %all-to-all-done.2 = f32[32,1,2]{2,1,0:T(1,128)S(1)} async-done(((f32[32,1,2]{2,1,0:T(1,128)}), f32[32,1,2]{2,1,0:T(1,128)S(1)}, u32[]{:S(2)}, u32[]{:S(2)}) %all-to-all-start.2) | async-done | bytes 288 | tf_op jit(solution)/shard_map/all_to_all | solution.py:174
  145.4 4.6 %collective-permute-done.10 = bf16[3,3,16,256]{3,2,1,0:T(8,128)(2,1)S(1)} collective-permute-done((bf16[3,3,16,256]{3,2,1,0:T(8,128)(2,1)S(1)}, bf16[3,3,16,256]{3,2,1,0:T(8,128)(2,1)S(1)}, u32[]{:S(2)}, u32[]{:S(2)}) %collective-permute-start.10) | collective-permute-done | bytes 73760 | tf_op jit(solution)/shard_map/ppermute | solution.py:85
  150.7 4.5 %collective-permute-done.11 = bf16[3,3,2,16,256]{4,3,2,1,0:T(8,128)(2,1)S(1)} collective-permute-done((bf16[3,3,2,16,256]{4,3,2,1,0:T(8,128)(2,1)S(1)}, bf16[3,3,2,16,256]{4,3,2,1,0:T(8,128)(2,1)S(1)}, u32[]{:S(2)}, u32[]{:S(2)}) %collective-permute-start.11) | collective-permute-done | bytes 147488 | tf_op jit(solution)/shard_map/ppermute | solution.py:85
  158.5 5.1 %collective-permute-done.12 = bf16[3,3,2,2,16,256]{5,4,3,2,1,0:T(8,128)(2,1)S(1)} collective-permute-done((bf16[3,3,2,2,16,256]{5,4,3,2,1,0:T(8,128)(2,1)S(1)}, bf16[3,3,2,2,16,256]{5,4,3,2,1,0:T(8,128)(2,1)S(1)}, u32[]{:S(2)}, u32[]{:S(2)}) %collective-permute-start.12) | collective-permute-done | bytes 294944 | tf_op jit(solution)/shard_map/ppermute | solution.py:85
  165.1 3.5 %collective-permute-done.16 = bf16[2,8,512]{2,1,0:T(8,128)(2,1)S(1)} collective-permute-done((bf16[2,8,512]{2,1,0:T(8,128)(2,1)S(1)}, bf16[2,8,512]{2,1,0:T(8,128)(2,1)S(1)}, u32[]{:S(2)}, u32[]{:S(2)}) %collective-permute-start.16) | collective-permute-done | bytes 16416 | tf_op jit(solution)/shard_map/ppermute | solution.py:85
  170.6 3.2 %collective-permute-done.13 = bf16[3,3,2,2,2,16,256]{6,5,4,3,2,1,0:T(8,128)(2,1)} collective-permute-done((bf16[3,3,2,2,2,16,256]{6,5,4,3,2,1,0:T(8,128)(2,1)S(1)}, bf16[3,3,2,2,2,16,256]{6,5,4,3,2,1,0:T(8,128)(2,1)}, u32[]{:S(2)}, u32[]{:S(2)}) %collective-permute-start.13) | collective-permute-done | bytes 589856 | tf_op jit(solution)/shard_map/ppermute | solution.py:85
  177.4 3.5 %collective-permute-done.18 = bf16[2,2,2,8,512]{4,3,2,1,0:T(8,128)(2,1)S(1)} collective-permute-done((bf16[2,2,2,8,512]{4,3,2,1,0:T(8,128)(2,1)S(1)}, bf16[2,2,2,8,512]{4,3,2,1,0:T(8,128)(2,1)S(1)}, u32[]{:S(2)}, u32[]{:S(2)}) %collective-permute-start.18) | collective-permute-done | bytes 65568 | tf_op jit(solution)/shard_map/ppermute | solution.py:85
  182.7 2.1 select_bitcast_fusion.1
  209.9 4.4 %collective-permute-done.20 = f32[3,3,2,2,2,2,16,256]{7,6,5,4,3,2,1,0:T(8,128)S(1)} collective-permute-done((f32[3,3,2,2,2,2,16,256]{7,6,5,4,3,2,1,0:T(8,128)S(1)}, f32[3,3,2,2,2,2,16,256]{7,6,5,4,3,2,1,0:T(8,128)S(1)}, u32[]{:S(2)}, u32[]{:S(2)}) %collective-permute-start.20) | collective-permute-done | bytes 2359328 | tf_op jit(solution)/shard_map/ppermute | solution.py:85
  219.6 13.1 %collective-permute-done.26 = f32[2,2,2,8,512]{4,3,2,1,0:T(8,128)S(1)} collective-permute-done((f32[2,2,2,8,512]{4,3,2,1,0:T(8,128)S(1)}, f32[2,2,2,8,512]{4,3,2,1,0:T(8,128)S(1)}, u32[]{:S(2)}, u32[]{:S(2)}) %collective-permute-start.26) | collective-permute-done | bytes 131104 | tf_op jit(solution)/shard_map/ppermute | solution.py:85
  234.3 2.4 collective-permute-start.27
  236.8 8.5 %collective-permute-done.27 = f32[2,2,8,512]{3,2,1,0:T(8,128)S(1)} collective-permute-done((f32[2,2,8,512]{3,2,1,0:T(8,128)S(1)}, f32[2,2,8,512]{3,2,1,0:T(8,128)S(1)}, u32[]{:S(2)}, u32[]{:S(2)}) %collective-permute-start.27) | collective-permute-done | bytes 65568 | tf_op jit(solution)/shard_map/ppermute | solution.py:85
  250.6 2.3 collective-permute-done.23
  253.0 2.1 collective-permute-start.24
  256.3 3.4 %collective-permute-done.24 = f32[3,3,16,256]{3,2,1,0:T(8,128)S(1)} collective-permute-done((f32[3,3,16,256]{3,2,1,0:T(8,128)S(1)}, f32[3,3,16,256]{3,2,1,0:T(8,128)S(1)}, u32[]{:S(2)}, u32[]{:S(2)}) %collective-permute-start.24) | collective-permute-done | bytes 147488 | tf_op jit(solution)/shard_map/ppermute | solution.py:85
  262.9 4.3 %all-to-all-start.3 = ((f32[32,1,2]{2,1,0:T(1,128)}), f32[32,1,2]{2,1,0:T(1,128)S(1)}, u32[]{:S(2)}, u32[]{:S(2)}) async-start(f32[32,1,2]{2,1,0:T(1,128)} %broadcast_in_dim.20), calls=%async_computation.3 | async-start | bytes 32768 | tf_op jit(solution)/shard_map/all_to_all | solution.py:174
  267.8 6.7 %all-to-all-done.3 = f32[32,1,2]{2,1,0:T(1,128)S(1)} async-done(((f32[32,1,2]{2,1,0:T(1,128)}), f32[32,1,2]{2,1,0:T(1,128)S(1)}, u32[]{:S(2)}, u32[]{:S(2)}) %all-to-all-start.3) | async-done | bytes 288 | tf_op jit(solution)/shard_map/all_to_all | solution.py:174
  (241 shorter events, 105.5 us)
Async XLA Ops:
  4.8 9.7 %all-to-all-start.1 = ((bf16[4,2,192]{2,1,0:T(2,128)(2,1)}), bf16[4,2,192]{2,1,0:T(2,128)(2,1)S(1)}, u32[]{:S(2)}, u32[]{:S(2)}) async-start(bf16[4,2,192]{2,1,0:T(2,128)(2,1)} %reshape.178), calls=%async_computation.1 | async-start | bytes 8192 | tf_op jit(solution)/shard_map/all_to_all | solution.py:137
  14.5 23.9 %all-to-all-start = ((bf16[4,6,8,8,512]{4,3,2,1,0:T(8,128)(2,1)}), bf16[4,6,8,8,512]{4,3,2,1,0:T(8,128)(2,1)S(1)}, u32[]{:S(2)}, u32[]{:S(2)}) async-start(bf16[4,6,8,8,512]{4,3,2,1,0:T(8,128)(2,1)} %scatter_fusion), calls=%async_computation | async-start | bytes 3145728 | tf_op jit(solution)/shard_map/all_to_all | solution.py:136
  62.5 4.9 %collective-permute-start = (f32[3,3,2,2,2,2,16,256]{7,6,5,4,3,2,1,0:T(8,128)}, f32[3,3,2,2,2,2,16,256]{7,6,5,4,3,2,1,0:T(8,128)}, u32[]{:S(2)}, u32[]{:S(2)}) collective-permute-start(f32[3,3,2,2,2,2,16,256]{7,6,5,4,3,2,1,0:T(8,128)} %dynamic-slice_bitcast_fusion.1), channel_id=1, source_target_pairs={{0,1},{1,0},{2,3},{3,2},{4,5},{5,4},{6,7},{7,6},{8,9},{9,8},{10,11... | collective-permute-start | bytes 7077896 | tf_op jit(solution)/shard_map/ppermute | solution.py:85
  73.7 17.8 %collective-permute-start.1 = (f32[3,3,2,2,2,16,256]{6,5,3,2,1,0,4:T(8,128)}, f32[3,3,2,2,2,16,256]{6,5,3,2,1,0,4:T(8,128)}, u32[]{:S(2)}, u32[]{:S(2)}) collective-permute-start(f32[3,3,2,2,2,16,256]{6,5,3,2,1,0,4:T(8,128)} %bitcast.446), channel_id=1, source_target_pairs={{0,2},{1,9},{2,0},{3,11},{4,6},{5,13},{6,4},{7,15},{8,10},{9,1},{1... | collective-permute-start | bytes 3538952 | tf_op jit(solution)/shard_map/ppermute | solution.py:85
  77.7 13.8 %collective-permute-start.6 = (f32[2,2,2,8,512]{4,3,1,0,2:T(8,128)S(1)}, f32[2,2,2,8,512]{4,3,1,0,2:T(8,128)S(1)}, u32[]{:S(2)}, u32[]{:S(2)}) collective-permute-start(f32[2,2,2,8,512]{4,3,1,0,2:T(8,128)S(1)} %bitcast.507), channel_id=1, source_target_pairs={{0,2},{1,9},{2,0},{3,11},{4,6},{5,13},{6,4},{7,15},{8,10},{9,1},{1... | collective-permute-start | bytes 393224 | tf_op jit(solution)/shard_map/ppermute | solution.py:85
  94.2 14.2 %collective-permute-start.2 = (f32[3,3,2,2,16,256]{5,4,3,2,1,0:T(8,128)S(1)}, f32[3,3,2,2,16,256]{5,4,3,2,1,0:T(8,128)S(1)}, u32[]{:S(2)}, u32[]{:S(2)}) collective-permute-start(f32[3,3,2,2,16,256]{5,4,3,2,1,0:T(8,128)S(1)} %dynamic-slice_bitcast_fusion.4), channel_id=1, source_target_pairs={{0,4},{1,17},{2,6},{3,19},{4,0},{5,21},{6,2},{7,23},{8,12},{9,25},... | collective-permute-start | bytes 1769480 | tf_op jit(solution)/shard_map/ppermute | solution.py:85
  97.5 8.9 %collective-permute-start.7 = (f32[2,2,8,512]{3,2,1,0:T(8,128)S(1)}, f32[2,2,8,512]{3,2,1,0:T(8,128)S(1)}, u32[]{:S(2)}, u32[]{:S(2)}) collective-permute-start(f32[2,2,8,512]{3,2,1,0:T(8,128)S(1)} %dynamic-slice_bitcast_fusion.13), channel_id=1, source_target_pairs={{0,4},{1,17},{2,6},{3,19},{4,0},{5,21},{6,2},{7,23},{8,12},{9,25},... | collective-permute-start | bytes 196616 | tf_op jit(solution)/shard_map/ppermute | solution.py:85
  106.4 4.0 %collective-permute-start.8 = (f32[2,8,512]{2,1,0:T(8,128)S(1)}, f32[2,8,512]{2,1,0:T(8,128)S(1)}, u32[]{:S(2)}, u32[]{:S(2)}) collective-permute-start(f32[2,8,512]{2,1,0:T(8,128)S(1)} %dynamic-slice_bitcast_fusion.15), channel_id=1, source_target_pairs={{0,8},{1,3},{2,10},{3,1},{4,12},{5,7},{6,14},{7,5},{8,0},{9,11},{1... | collective-permute-start | bytes 98312 | tf_op jit(solution)/shard_map/ppermute | solution.py:85
  109.7 6.8 %collective-permute-start.3 = (f32[3,3,2,16,256]{4,3,2,1,0:T(8,128)S(1)}, f32[3,3,2,16,256]{4,3,2,1,0:T(8,128)S(1)}, u32[]{:S(2)}, u32[]{:S(2)}) collective-permute-start(f32[3,3,2,16,256]{4,3,2,1,0:T(8,128)S(1)} %dynamic-slice_bitcast_fusion.6), channel_id=1, source_target_pairs={{0,8},{1,3},{2,10},{3,1},{4,12},{5,7},{6,14},{7,5},{8,0},{9,11},{1... | collective-permute-start | bytes 884744 | tf_op jit(solution)/shard_map/ppermute | solution.py:85
  110.4 10.4 %collective-permute-start.9 = (f32[8,512]{1,0:T(8,128)S(1)}, f32[8,512]{1,0:T(8,128)S(1)}, u32[]{:S(2)}, u32[]{:S(2)}) collective-permute-start(f32[8,512]{1,0:T(8,128)S(1)} %dynamic-slice_bitcast_fusion.17), channel_id=1, source_target_pairs={{0,16},{1,5},{2,18},{3,7},{4,20},{5,1},{6,22},{7,3},{8,24},{9,13},... | collective-permute-start | bytes 49160 | tf_op jit(solution)/shard_map/ppermute | solution.py:85
  116.5 6.8 %collective-permute-start.4 = (f32[3,3,16,256]{3,2,1,0:T(8,128)S(1)}, f32[3,3,16,256]{3,2,1,0:T(8,128)S(1)}, u32[]{:S(2)}, u32[]{:S(2)}) collective-permute-start(f32[3,3,16,256]{3,2,1,0:T(8,128)S(1)} %dynamic-slice_bitcast_fusion.10), channel_id=1, source_target_pairs={{0,16},{1,5},{2,18},{3,7},{4,20},{5,1},{6,22},{7,3},{8,24},{9,13},... | collective-permute-start | bytes 442376 | tf_op jit(solution)/shard_map/ppermute | solution.py:85
  126.6 15.2 %all-to-all-start.2 = ((f32[32,1,2]{2,1,0:T(1,128)}), f32[32,1,2]{2,1,0:T(1,128)S(1)}, u32[]{:S(2)}, u32[]{:S(2)}) async-start(f32[32,1,2]{2,1,0:T(1,128)} %broadcast_in_dim.19), calls=%async_computation.2 | async-start | bytes 32768 | tf_op jit(solution)/shard_map/all_to_all | solution.py:174
  144.1 5.9 %collective-permute-start.10 = (bf16[3,3,16,256]{3,2,1,0:T(8,128)(2,1)S(1)}, bf16[3,3,16,256]{3,2,1,0:T(8,128)(2,1)S(1)}, u32[]{:S(2)}, u32[]{:S(2)}) collective-permute-start(bf16[3,3,16,256]{3,2,1,0:T(8,128)(2,1)S(1)} %get-tuple-element.7), channel_id=1, source_target_pairs={{0,16},{1,5},{2,18},{3,7},{4,20},{5,1},{6,22},{7,3},{8,24},{9,13},... | collective-permute-start | bytes 221192 | tf_op jit(solution)/shard_map/ppermute | solution.py:85
  150.0 5.2 %collective-permute-start.11 = (bf16[3,3,2,16,256]{4,3,2,1,0:T(8,128)(2,1)S(1)}, bf16[3,3,2,16,256]{4,3,2,1,0:T(8,128)(2,1)S(1)}, u32[]{:S(2)}, u32[]{:S(2)}) collective-permute-start(bf16[3,3,2,16,256]{4,3,2,1,0:T(8,128)(2,1)S(1)} %pad_maximum_fusion.5), channel_id=1, source_target_pairs={{0,8},{1,3},{2,10},{3,1},{4,12},{5,7},{6,14},{7,5},{8,0},{9,11},{1... | collective-permute-start | bytes 442376 | tf_op jit(solution)/shard_map/ppermute | solution.py:85
  155.3 8.3 %collective-permute-start.12 = (bf16[3,3,2,2,16,256]{5,4,3,2,1,0:T(8,128)(2,1)S(1)}, bf16[3,3,2,2,16,256]{5,4,3,2,1,0:T(8,128)(2,1)S(1)}, u32[]{:S(2)}, u32[]{:S(2)}) collective-permute-start(bf16[3,3,2,2,16,256]{5,4,3,2,1,0:T(8,128)(2,1)S(1)} %pad_maximum_fusion.3), channel_id=1, source_target_pairs={{0,4},{1,17},{2,6},{3,19},{4,0},{5,21},{6,2},{7,23},{8,12},{9,25},... | collective-permute-start | bytes 884744 | tf_op jit(solution)/shard_map/ppermute | solution.py:85
  157.3 7.3 %collective-permute-start.15 = (bf16[8,512]{1,0:T(8,128)(2,1)S(1)}, bf16[8,512]{1,0:T(8,128)(2,1)S(1)}, u32[]{:S(2)}, u32[]{:S(2)}) collective-permute-start(bf16[8,512]{1,0:T(8,128)(2,1)S(1)} %get-tuple-element.9), channel_id=1, source_target_pairs={{0,16},{1,5},{2,18},{3,7},{4,20},{5,1},{6,22},{7,3},{8,24},{9,13},... | collective-permute-start | bytes 24584 | tf_op jit(solution)/shard_map/ppermute | solution.py:85
  163.7 10.1 %collective-permute-start.13 = (bf16[3,3,2,2,2,16,256]{6,5,4,3,2,1,0:T(8,128)(2,1)S(1)}, bf16[3,3,2,2,2,16,256]{6,5,4,3,2,1,0:T(8,128)(2,1)}, u32[]{:S(2)}, u32[]{:S(2)}) collective-permute-start(bf16[3,3,2,2,2,16,256]{6,5,4,3,2,1,0:T(8,128)(2,1)S(1)} %pad_maximum_fusion.2), channel_id=1, source_target_pairs={{0,2},{1,9},{2,0},{3,11},{4,6},{5,13},{6,4},{7,15},{8,10},{9,1},{1... | collective-permute-start | bytes 1769480 | tf_op jit(solution)/shard_map/ppermute | solution.py:85
  164.6 4.0 %collective-permute-start.16 = (bf16[2,8,512]{2,1,0:T(8,128)(2,1)S(1)}, bf16[2,8,512]{2,1,0:T(8,128)(2,1)S(1)}, u32[]{:S(2)}, u32[]{:S(2)}) collective-permute-start(bf16[2,8,512]{2,1,0:T(8,128)(2,1)S(1)} %pad_maximum_fusion.9), channel_id=1, source_target_pairs={{0,8},{1,3},{2,10},{3,1},{4,12},{5,7},{6,14},{7,5},{8,0},{9,11},{1... | collective-permute-start | bytes 49160 | tf_op jit(solution)/shard_map/ppermute | solution.py:85
  168.6 7.9 %collective-permute-start.17 = (bf16[2,2,8,512]{3,2,1,0:T(8,128)(2,1)S(1)}, bf16[2,2,8,512]{3,2,1,0:T(8,128)(2,1)S(1)}, u32[]{:S(2)}, u32[]{:S(2)}) collective-permute-start(bf16[2,2,8,512]{3,2,1,0:T(8,128)(2,1)S(1)} %pad_maximum_fusion.8), channel_id=1, source_target_pairs={{0,4},{1,17},{2,6},{3,19},{4,0},{5,21},{6,2},{7,23},{8,12},{9,25},... | collective-permute-start | bytes 98312 | tf_op jit(solution)/shard_map/ppermute | solution.py:85
  176.5 6.1 %collective-permute-start.14 = (bf16[3,3,2,2,2,2,16,256]{7,6,5,4,3,2,1,0:T(8,128)(2,1)}, bf16[3,3,2,2,2,2,16,256]{7,6,5,4,3,2,1,0:T(8,128)(2,1)}, u32[]{:S(2)}, u32[]{:S(2)}) collective-permute-start(bf16[3,3,2,2,2,2,16,256]{7,6,5,4,3,2,1,0:T(8,128)(2,1)} %copy_select_fusion.2), channel_id=1, source_target_pairs={{0,1},{1,0},{2,3},{3,2},{4,5},{5,4},{6,7},{7,6},{8,9},{9,8},{10,11... | collective-permute-start | bytes 3538952 | tf_op jit(solution)/shard_map/ppermute | solution.py:85
  176.5 4.3 %collective-permute-start.18 = (bf16[2,2,2,8,512]{4,3,2,1,0:T(8,128)(2,1)S(1)}, bf16[2,2,2,8,512]{4,3,2,1,0:T(8,128)(2,1)S(1)}, u32[]{:S(2)}, u32[]{:S(2)}) collective-permute-start(bf16[2,2,2,8,512]{4,3,2,1,0:T(8,128)(2,1)S(1)} %pad_maximum_fusion.7), channel_id=1, source_target_pairs={{0,2},{1,9},{2,0},{3,11},{4,6},{5,13},{6,4},{7,15},{8,10},{9,1},{1... | collective-permute-start | bytes 196616 | tf_op jit(solution)/shard_map/ppermute | solution.py:85
  209.6 4.6 %collective-permute-start.20 = (f32[3,3,2,2,2,2,16,256]{7,6,5,4,3,2,1,0:T(8,128)S(1)}, f32[3,3,2,2,2,2,16,256]{7,6,5,4,3,2,1,0:T(8,128)S(1)}, u32[]{:S(2)}, u32[]{:S(2)}) collective-permute-start(f32[3,3,2,2,2,2,16,256]{7,6,5,4,3,2,1,0:T(8,128)S(1)} %dynamic-slice_bitcast_fusion), channel_id=1, source_target_pairs={{0,1},{1,0},{2,3},{3,2},{4,5},{5,4},{6,7},{7,6},{8,9},{9,8},{10,11... | collective-permute-start | bytes 7077896 | tf_op jit(solution)/shard_map/ppermute | solution.py:85
  215.1 17.7 %collective-permute-start.21 = (f32[3,3,2,2,2,16,256]{6,5,4,3,2,1,0:T(8,128)S(1)}, f32[3,3,2,2,2,16,256]{6,5,4,3,2,1,0:T(8,128)S(1)}, u32[]{:S(2)}, u32[]{:S(2)}) collective-permute-start(f32[3,3,2,2,2,16,256]{6,5,4,3,2,1,0:T(8,128)S(1)} %dynamic-slice_bitcast_fusion.2), channel_id=1, source_target_pairs={{0,2},{1,9},{2,0},{3,11},{4,6},{5,13},{6,4},{7,15},{8,10},{9,1},{1... | collective-permute-start | bytes 3538952 | tf_op jit(solution)/shard_map/ppermute | solution.py:85
  216.6 1.6 collective-permute-start.25
  218.2 14.5 %collective-permute-start.26 = (f32[2,2,2,8,512]{4,3,2,1,0:T(8,128)S(1)}, f32[2,2,2,8,512]{4,3,2,1,0:T(8,128)S(1)}, u32[]{:S(2)}, u32[]{:S(2)}) collective-permute-start(f32[2,2,2,8,512]{4,3,2,1,0:T(8,128)S(1)} %dynamic-slice_bitcast_fusion.11), channel_id=1, source_target_pairs={{0,2},{1,9},{2,0},{3,11},{4,6},{5,13},{6,4},{7,15},{8,10},{9,1},{1... | collective-permute-start | bytes 393224 | tf_op jit(solution)/shard_map/ppermute | solution.py:85
  233.1 12.9 %collective-permute-start.22 = (f32[3,3,2,2,16,256]{5,4,3,2,1,0:T(8,128)S(1)}, f32[3,3,2,2,16,256]{5,4,3,2,1,0:T(8,128)S(1)}, u32[]{:S(2)}, u32[]{:S(2)}) collective-permute-start(f32[3,3,2,2,16,256]{5,4,3,2,1,0:T(8,128)S(1)} %dynamic-slice_bitcast_fusion.3), channel_id=1, source_target_pairs={{0,4},{1,17},{2,6},{3,19},{4,0},{5,21},{6,2},{7,23},{8,12},{9,25},... | collective-permute-start | bytes 1769480 | tf_op jit(solution)/shard_map/ppermute | solution.py:85
  234.3 10.9 %collective-permute-start.27 = (f32[2,2,8,512]{3,2,1,0:T(8,128)S(1)}, f32[2,2,8,512]{3,2,1,0:T(8,128)S(1)}, u32[]{:S(2)}, u32[]{:S(2)}) collective-permute-start(f32[2,2,8,512]{3,2,1,0:T(8,128)S(1)} %dynamic-slice_bitcast_fusion.12), channel_id=1, source_target_pairs={{0,4},{1,17},{2,6},{3,19},{4,0},{5,21},{6,2},{7,23},{8,12},{9,25},... | collective-permute-start | bytes 196616 | tf_op jit(solution)/shard_map/ppermute | solution.py:85
  245.3 4.0 %collective-permute-start.28 = (f32[2,8,512]{2,1,0:T(8,128)S(1)}, f32[2,8,512]{2,1,0:T(8,128)S(1)}, u32[]{:S(2)}, u32[]{:S(2)}) collective-permute-start(f32[2,8,512]{2,1,0:T(8,128)S(1)} %dynamic-slice_bitcast_fusion.14), channel_id=1, source_target_pairs={{0,8},{1,3},{2,10},{3,1},{4,12},{5,7},{6,14},{7,5},{8,0},{9,11},{1... | collective-permute-start | bytes 98312 | tf_op jit(solution)/shard_map/ppermute | solution.py:85
  246.1 6.8 %collective-permute-start.23 = (f32[3,3,2,16,256]{4,3,2,1,0:T(8,128)S(1)}, f32[3,3,2,16,256]{4,3,2,1,0:T(8,128)S(1)}, u32[]{:S(2)}, u32[]{:S(2)}) collective-permute-start(f32[3,3,2,16,256]{4,3,2,1,0:T(8,128)S(1)} %dynamic-slice_bitcast_fusion.5), channel_id=1, source_target_pairs={{0,8},{1,3},{2,10},{3,1},{4,12},{5,7},{6,14},{7,5},{8,0},{9,11},{1... | collective-permute-start | bytes 884744 | tf_op jit(solution)/shard_map/ppermute | solution.py:85
  249.3 6.4 %collective-permute-start.29 = (f32[8,512]{1,0:T(8,128)S(1)}, f32[8,512]{1,0:T(8,128)S(1)}, u32[]{:S(2)}, u32[]{:S(2)}) collective-permute-start(f32[8,512]{1,0:T(8,128)S(1)} %dynamic-slice_bitcast_fusion.16), channel_id=1, source_target_pairs={{0,16},{1,5},{2,18},{3,7},{4,20},{5,1},{6,22},{7,3},{8,24},{9,13},... | collective-permute-start | bytes 49160 | tf_op jit(solution)/shard_map/ppermute | solution.py:85
  253.0 6.7 %collective-permute-start.24 = (f32[3,3,16,256]{3,2,1,0:T(8,128)S(1)}, f32[3,3,16,256]{3,2,1,0:T(8,128)S(1)}, u32[]{:S(2)}, u32[]{:S(2)}) collective-permute-start(f32[3,3,16,256]{3,2,1,0:T(8,128)S(1)} %dynamic-slice_bitcast_fusion.9), channel_id=1, source_target_pairs={{0,16},{1,5},{2,18},{3,7},{4,20},{5,1},{6,22},{7,3},{8,24},{9,13},... | collective-permute-start | bytes 442376 | tf_op jit(solution)/shard_map/ppermute | solution.py:85
  262.9 11.6 %all-to-all-start.3 = ((f32[32,1,2]{2,1,0:T(1,128)}), f32[32,1,2]{2,1,0:T(1,128)S(1)}, u32[]{:S(2)}, u32[]{:S(2)}) async-start(f32[32,1,2]{2,1,0:T(1,128)} %broadcast_in_dim.20), calls=%async_computation.3 | async-start | bytes 32768 | tf_op jit(solution)/shard_map/all_to_all | solution.py:174
  (30 other events, 215.7 us)

commit v6 on v5

--- a/solution.py
+++ b/solution.py
@@ -81,8 +81,11 @@
     return 0.004 * lax.rsqrt(squares / entries + 1e-06)
 
 
+EX_AXES = ("z", "y", "core")
+
+
 def partner_swap(value, pairs):
-    return lax.ppermute(value, "ex", perm=pairs)
+    return lax.ppermute(value, EX_AXES, perm=pairs)
 
 
 def stage_pairs(bits_of, peers):
@@ -112,7 +115,7 @@
 
 def shards(feats, targets, task_of, counts, down_w, up_w, head):
     groups = lax.axis_size("task")
-    peers = lax.axis_size("ex")
+    peers = lax.axis_size(EX_AXES)
     levels = peers.bit_length() - 1
     sources = feats.shape[0]
     side = feats.shape[1]
@@ -140,7 +143,7 @@
     held_labels = come_labels.reshape(groups * bucket, cells).astype(jnp.int32)
     count = counts[0].astype(jnp.float32)
     entries = 10.0 * CHANNELS * INNER
-    place = lax.axis_index("ex")
+    place = lax.axis_index(EX_AXES)
     part_chans = down_w.shape[3] // peers
     part_inner = up_w.shape[1] // peers
     inner = down_w.shape[4]
@@ -149,29 +152,29 @@
     upper_low = up_w[0].astype(jnp.bfloat16)
     down_own = lax.dynamic_slice_in_dim(down_w[0], place * part_chans, part_chans, 2)
     up_own = lax.dynamic_slice_in_dim(up_w[0], place * part_inner, part_inner, 0)
-    bits_shape = (2,) * levels
     core = place % 2
-    second_core = core == 1
-    orders = ([0, 1, 2, 3, 4], [0, 3, 4, 1, 2])
+    grid_axes = ("z", "y")
+    plane = peers // 2
+    core_pairs = [(i, i ^ 1) for i in range(peers)]
     for update_round in range(TRAIN_STEPS):
         loss_sum, grad_down, grad_up = train_pass(
             held_feats, held_labels, down_low, upper_low, head, count
         )
-        grad_down = grad_down.reshape((3, 3) + bits_shape + (part_chans, inner))
-        grad_up = grad_up.reshape(bits_shape + (part_inner, up_w.shape[2]))
-        for stage in range(levels):
-            if stage == 1:
-                grad_down = jnp.where(second_core, swap_bit_axes(grad_down, 2, levels), grad_down)
-                grad_up = jnp.where(second_core, swap_bit_axes(grad_up, 0, levels), grad_up)
-            bits_of = (orders[0][stage], orders[1][stage])
-            pairs = stage_pairs(bits_of, peers)
-            bit = jnp.where(second_core, bits_of[1], bits_of[0])
-            grad_down = halve_sum(grad_down, 2 + levels - 1 - stage, bit, pairs, place)
-            grad_up = halve_sum(grad_up, levels - 1 - stage, bit, pairs, place)
+        grad_down = grad_down.reshape(3, 3, plane, 2, part_chans, inner)
+        grad_up = grad_up.reshape(plane, 2, part_inner, up_w.shape[2])
+        keep_down = lax.dynamic_index_in_dim(grad_down, core, 3, keepdims=False)
+        give_down = lax.dynamic_index_in_dim(grad_down, 1 - core, 3, keepdims=False)
+        keep_up = lax.dynamic_index_in_dim(grad_up, core, 1, keepdims=False)
+        give_up = lax.dynamic_index_in_dim(grad_up, 1 - core, 1, keepdims=False)
+        got_down, got_up = lax.ppermute((give_down, give_up), EX_AXES, perm=core_pairs)
+        grad_down = keep_down + got_down
+        grad_up = keep_up + got_up
+        grad_down = jnp.sum(lax.all_to_all(grad_down, grid_axes, 2, 2, tiled=True), axis=2)
+        grad_up = jnp.sum(lax.all_to_all(grad_up, grid_axes, 0, 0, tiled=True), axis=0)
         squares = jnp.sum(grad_down * grad_down) + jnp.sum(grad_up * grad_up)
         totals = jnp.stack([squares, loss_sum])
         spread = jnp.broadcast_to(totals[None, :], (peers, totals.shape[0]))
-        totals = jnp.sum(lax.all_to_all(spread, "ex", 0, 0, tiled=True), axis=0)
+        totals = jnp.sum(lax.all_to_all(spread, EX_AXES, 0, 0, tiled=True), axis=0)
         scale = step_scale(totals[0], entries)
         down_own = down_own - scale * grad_down
         up_own = up_own - scale * grad_up
@@ -179,26 +182,31 @@
         if update_round + 1 < TRAIN_STEPS:
             down_low = down_own.astype(jnp.bfloat16)
             upper_low = up_own.astype(jnp.bfloat16)
-            for step_index in range(levels):
-                stage = levels - 1 - step_index
-                if stage == 0:
-                    down_low = jnp.where(second_core, swap_bit_axes(down_low, 2, levels), down_low)
-                    upper_low = jnp.where(second_core, swap_bit_axes(upper_low, 0, levels), upper_low)
-                bits_of = (orders[0][stage], orders[1][stage])
-                pairs = stage_pairs(bits_of, peers)
-                bit = jnp.where(second_core, bits_of[1], bits_of[0])
-                down_low = double_join(down_low, 2 + step_index, bit, pairs, place)
-                upper_low = double_join(upper_low, step_index, bit, pairs, place)
+            down_low = jnp.broadcast_to(down_low[:, :, None], (3, 3, plane) + down_low.shape[2:])
+            upper_low = jnp.broadcast_to(upper_low[None], (plane,) + upper_low.shape)
+            down_low = lax.all_to_all(down_low, grid_axes, 2, 2, tiled=True)
+            upper_low = lax.all_to_all(upper_low, grid_axes, 0, 0, tiled=True)
+            other_down, other_up = lax.ppermute((down_low, upper_low), EX_AXES, perm=core_pairs)
+            first_core = core == 0
+            down_low = jnp.stack(
+                [jnp.where(first_core, down_low, other_down), jnp.where(first_core, other_down, down_low)], axis=3
+            )
+            upper_low = jnp.stack(
+                [jnp.where(first_core, upper_low, other_up), jnp.where(first_core, other_up, upper_low)], axis=1
+            )
             down_low = down_low.reshape(down_w.shape[1:])
             upper_low = upper_low.reshape(up_w.shape[1:])
     return (down_own[None], up_own[None], jnp.stack(collected)[None])
 
 
 def solution(mesh):
+    grid = mesh.devices.reshape(mesh.devices.shape[0], 4, -1, 2)
+    split_mesh = jax.sharding.Mesh(grid, ("task",) + EX_AXES)
+    rows = ("task",) + EX_AXES
     placed = (
-        P(("task", "ex"), None, None, None),
-        P(("task", "ex"), None),
-        P(("task", "ex")),
+        P(rows, None, None, None),
+        P(rows, None),
+        P(rows),
         P("task"),
         P("task", None, None, None, None),
         P("task", None, None),
@@ -206,8 +214,8 @@
     )
     return jax.shard_map(
         shards,
-        mesh=mesh,
+        mesh=split_mesh,
         in_specs=placed,
-        out_specs=(P("task", None, None, "ex", None), P("task", "ex", None), P("task", None)),
+        out_specs=(P("task", None, None, EX_AXES, None), P("task", EX_AXES, None), P("task", None)),
         check_vma=False,
     )

time: 283 us -> 293 us (1.035)
  blocking collectives: 0 us -> 32.7 us
  starting transfers between devices: 57.8 us -> 36.9 us
  waiting for transfers between devices: 122 us -> 116 us
    ppermute x30 -> x6, waiting for transfers between devices: 92.2 us -> 9.18 us  [the longest x4 7.72 us: shards(): lax.ppermute((give_down, give_up), EX_AXES, perm=core_pairs)]
    all_to_all x2 -> x6, waiting for transfers between devices: 14 us -> 90.7 us  [the longest x2 66.5 us: shards(): lax.all_to_all(grad_down, grid_axes, 2, 2, tiled=True)]
    ppermute x30 -> x6, starting transfers between devices: 37.5 us -> 1.38 us  [the longest x4 1.18 us: shards(): lax.ppermute((give_down, give_up), EX_AXES, perm=core_pairs)]
    all_to_all x0 -> x2, blocking collectives: none -> 32.7 us  [the longest x1 21.6 us: shards(): down_low = lax.all_to_all(down_low, grid_axes, 2, 2, tiled=True)]
    all_to_all x2 -> x6, starting transfers between devices: 12.1 us -> 27.4 us  [the longest x2 11.6 us: shards(): lax.all_to_all(grad_up, grid_axes, 0, 0, tiled=True)]
    select_n x6 -> x0, other arithmetic: 7.26 us -> none  [the longest x2 5.65 us: shards(): jnp.where(second_core, swap_bit_axes(grad_down, 2, levels), grad_down)]
    add x12 -> x4, other arithmetic: 3.3 us -> 9.41 us  [the longest x2 7.91 us: shards(): grad_down = keep_down + got_down]
    dynamic_slice x4, local copies, waits for them, and re-layouts: 1.37 us -> 6.11 us  [the longest x2 3.21 us: shards(): give_down = lax.dynamic_index_in_dim(grad_down, 1 - core, 3, keepdims=False)]
  transfers between devices with their start and end apart: 34 -> 14, of which waited for: 25 -> 11; matrix products, arithmetic and copies ran while one was open for 6% -> 8% of each run, Pallas kernels for 0% -> 0%
where the time goes in v6:
time: 293 us; the launch traced here: 288 us
  waiting for transfers between devices  116 us (40%)
  starting transfers between devices  36.9 us (13%)
  other arithmetic  32.8 us (11%)
  blocking collectives  32.7 us (11%)
  matrix products  32.4 us (11%)
  local copies, waits for them, and re-layouts  29.6 us (10%)
  between operations  7.44 us (3%)
    all_to_all x2, waiting for transfers between devices, shards(): lax.all_to_all(grad_down, grid_axes, 2, 2, tiled=True)  66.5 us
    all_to_all x1, blocking collectives, shards(): down_low = lax.all_to_all(down_low, grid_axes, 2, 2, tiled=True)  21.6 us
    all_to_all x1, waiting for transfers between devices, shards(): lax.all_to_all(send_feats, 'task', split_axis=0, concat_axis=0, tiled=True)  15.3 us
    all_to_all x2, waiting for transfers between devices, shards(): totals = jnp.sum(lax.all_to_all(spread, EX_AXES, 0, 0, tiled=True), axis=0)  14 us
    dot_general x20, matrix products, contract_rows(): lax.dot_general(left, right, (((0,), (0,)), ((), ())), preferred_element_...  12.8 us
    all_to_all x2, starting transfers between devices, shards(): lax.all_to_all(grad_up, grid_axes, 0, 0, tiled=True)  11.6 us
    all_to_all x1, blocking collectives, shards(): upper_low = lax.all_to_all(upper_low, grid_axes, 0, 0, tiled=True)  11.1 us
    dot_general x18, matrix products, train_pass(): jnp.dot(windows[offset_index], down_low[offset_index // 3, offset_index %...  10.3 us
  transfers between devices with their start and end apart: 14, of which 11 were waited for; matrix products, arithmetic and copies ran while one was open for 8% of the time, Pallas kernels for 0%

profile of v6, /device:TPU:0, one launch (start us, length us, event | category | flops | bytes accessed | tf_op | source)
XLA Modules:
  0.0 288.0 jit_solution(11990526512799209835)
XLA Ops:
  4.8 4.4 %all-to-all-start.1 = ((bf16[4,2,192]{2,1,0:T(2,128)(2,1)}), bf16[4,2,192]{2,1,0:T(2,128)(2,1)S(1)}, u32[]{:S(2)}, u32[]{:S(2)}) async-start(bf16[4,2,192]{2,1,0:T(2,128)(2,1)} %reshape.224), calls=%async_computation.1 | async-start | bytes 8192 | tf_op jit(solution)/shard_map/all_to_all | solution.py:140
  10.5 2.9 %scatter_fusion = bf16[4,6,8,8,512]{4,3,2,1,0:T(8,128)(2,1)} fusion(bf16[4,6,8,8,512]{4,3,2,1,0:T(8,128)(2,1)} %broadcast_in_dim.18, s32[12]{0:T(128)S(1)} %fusion.58, bf16[12,8,8,512]{3,2,1,0:T(8,128)(2,1)S(1)} %copy-done.19), kind=kCustom, calls=%fused_computation | custom fusion | bytes 2359392 | tf_op jit(solution)/shard_map/scatter | solution.py:131
  14.5 3.7 %all-to-all-start = ((bf16[4,6,8,8,512]{4,3,2,1,0:T(8,128)(2,1)}), bf16[4,6,8,8,512]{4,3,2,1,0:T(8,128)(2,1)S(1)}, u32[]{:S(2)}, u32[]{:S(2)}) async-start(bf16[4,6,8,8,512]{4,3,2,1,0:T(8,128)(2,1)} %scatter_fusion), calls=%async_computation | async-start | bytes 3145728 | tf_op jit(solution)/shard_map/all_to_all | solution.py:139
  18.9 4.0 %convert_bitcast_fusion = bf16[3,3,512,256]{3,2,1,0:T(8,128)(2,1)} fusion(f32[1,3,3,512,256]{4,3,2,1,0:T(8,128)} %param.11), kind=kLoop, calls=%fused_computation.49 | loop fusion | flops 1179648 | bytes 7077888 | tf_op jit(solution)/shard_map/convert_element_type | solution.py:151
  23.1 15.3 %all-to-all-done = bf16[4,6,8,8,512]{4,3,2,1,0:T(8,128)(2,1)S(1)} async-done(((bf16[4,6,8,8,512]{4,3,2,1,0:T(8,128)(2,1)}), bf16[4,6,8,8,512]{4,3,2,1,0:T(8,128)(2,1)S(1)}, u32[]{:S(2)}, u32[]{:S(2)}) %all-to-all-start) | async-done | bytes 1572896 | tf_op jit(solution)/shard_map/all_to_all | solution.py:139
  38.4 1.6 copy.38
  40.1 2.8 pad_slice_fusion
  51.3 1.6 multiply_reduce_fusion.2
  60.5 2.2 constant_dynamic-slice_fusion.3
  65.6 3.9 %collective-permute-done.1 = f32[16,8,512]{2,1,0:T(8,128)S(1)} collective-permute-done((f32[16,8,512]{2,1,0:T(8,128)S(1)}, f32[16,8,512]{2,1,0:T(8,128)S(1)}, u32[]{:S(2)}, u32[]{:S(2)}) %collective-permute-start.1) | collective-permute-done | bytes 262176 | tf_op jit(solution)/shard_map/ppermute | solution.py:169
  70.2 8.0 %all-to-all-start.3 = ((f32[16,8,512]{2,1,0:T(8,128)}), f32[16,8,512]{2,1,0:T(8,128)S(1)}, u32[]{:S(2)}, u32[]{:S(2)}) async-start(f32[16,8,512]{2,1,0:T(8,128)} %bitcast_add_fusion.3), calls=%async_computation.3 | async-start | bytes 524288 | tf_op jit(solution)/shard_map/all_to_all | solution.py:173
  78.2 4.3 %bitcast_add_fusion.1 = f32[3,3,16,16,256]{4,3,1,0,2:T(8,128)} fusion(f32[3,3,16,16,256]{4,3,1,0,2:T(8,128)} %collective-permute-done, f32[3,3,16,1,16,256]{5,4,3,2,1,0:T(8,128)} %get-tuple-element.9), kind=kLoop, calls=%fused_computation.46 | loop fusion | flops 589824 | bytes 7077888 | tf_op jit(solution)/shard_map/add | solution.py:170
  82.5 4.7 %all-to-all-done.3 = f32[16,8,512]{2,1,0:T(8,128)S(1)} async-done(((f32[16,8,512]{2,1,0:T(8,128)}), f32[16,8,512]{2,1,0:T(8,128)S(1)}, u32[]{:S(2)}, u32[]{:S(2)}) %all-to-all-start.3) | async-done | bytes 262176 | tf_op jit(solution)/shard_map/all_to_all | solution.py:173
  87.2 4.4 %all-to-all-start.2 = ((f32[3,3,16,16,256]{4,3,1,0,2:T(8,128)}), f32[3,3,16,16,256]{4,3,1,0,2:T(8,128)}, u32[]{:S(2)}, u32[]{:S(2)}) async-start(f32[3,3,16,16,256]{4,3,1,0,2:T(8,128)} %bitcast_add_fusion.1), calls=%async_computation.2 | async-start | bytes 4718592 | tf_op jit(solution)/shard_map/all_to_all | solution.py:172
  92.9 32.9 %all-to-all-done.2 = f32[3,3,16,16,256]{4,3,1,0,2:T(8,128)} async-done(((f32[3,3,16,16,256]{4,3,1,0,2:T(8,128)}), f32[3,3,16,16,256]{4,3,1,0,2:T(8,128)}, u32[]{:S(2)}, u32[]{:S(2)}) %all-to-all-start.2) | async-done | bytes 2359328 | tf_op jit(solution)/shard_map/all_to_all | solution.py:172
  125.8 1.9 reduce_sum.196
  130.9 3.8 %all-to-all-start.4 = ((f32[32,1,2]{2,1,0:T(1,128)}), f32[32,1,2]{2,1,0:T(1,128)S(1)}, u32[]{:S(2)}, u32[]{:S(2)}) async-start(f32[32,1,2]{2,1,0:T(1,128)} %broadcast_in_dim.21), calls=%async_computation.4 | async-start | bytes 32768 | tf_op jit(solution)/shard_map/all_to_all | solution.py:177
  134.7 7.3 %all-to-all-done.4 = f32[32,1,2]{2,1,0:T(1,128)S(1)} async-done(((f32[32,1,2]{2,1,0:T(1,128)}), f32[32,1,2]{2,1,0:T(1,128)S(1)}, u32[]{:S(2)}, u32[]{:S(2)}) %all-to-all-start.4) | async-done | bytes 288 | tf_op jit(solution)/shard_map/all_to_all | solution.py:177
  144.4 21.6 %all_to_all.52 = bf16[3,3,16,16,256]{4,3,1,0,2:T(8,128)(2,1)S(1)} all-to-all(bf16[3,3,16,16,256]{4,3,1,0,2:T(8,128)(2,1)S(1)} %broadcast_in_dim.22), channel_id=1, replica_groups=mesh['task'=4,'z'=4,'y'=4,'core'=2] {'z','y'}, dimensions={2} | all-to-all | bytes 2359296 | tf_op jit(solution)/shard_map/all_to_all | solution.py:187
  168.9 11.1 %all_to_all.53 = bf16[16,8,512]{2,1,0:T(8,128)(2,1)S(1)} all-to-all(bf16[16,8,512]{2,1,0:T(8,128)(2,1)S(1)} %broadcast_in_dim.24), channel_id=1, replica_groups=mesh['task'=4,'z'=4,'y'=4,'core'=2] {'z','y'}, dimensions={0} | all-to-all | bytes 262144 | tf_op jit(solution)/shard_map/all_to_all | solution.py:188
  182.6 1.8 select_bitcast_fusion.1
  198.9 1.6 multiply_reduce_fusion
  208.8 1.6 copy.63
  211.6 3.9 %collective-permute-done.5 = f32[16,8,512]{2,1,0:T(8,128)S(1)} collective-permute-done((f32[16,8,512]{2,1,0:T(8,128)S(1)}, f32[16,8,512]{2,1,0:T(8,128)S(1)}, u32[]{:S(2)}, u32[]{:S(2)}) %collective-permute-start.5) | collective-permute-done | bytes 262176 | tf_op jit(solution)/shard_map/ppermute | solution.py:169
  216.2 3.5 %all-to-all-start.8 = ((f32[16,8,512]{2,1,0:T(8,128)}), f32[16,8,512]{2,1,0:T(8,128)S(1)}, u32[]{:S(2)}, u32[]{:S(2)}) async-start(f32[16,8,512]{2,1,0:T(8,128)} %bitcast_add_fusion.2), calls=%async_computation.8 | async-start | bytes 524288 | tf_op jit(solution)/shard_map/all_to_all | solution.py:173
  219.8 3.6 %bitcast_add_fusion = f32[3,3,16,16,256]{4,3,1,0,2:T(8,128)} fusion(f32[3,3,16,16,256]{4,3,1,0,2:T(8,128)} %collective-permute-done.4, f32[3,3,16,1,16,256]{5,4,3,2,1,0:T(8,128)S(1)} %get-tuple-element.7), kind=kLoop, calls=%fused_computation.45 | loop fusion | flops 589824 | bytes 7077888 | tf_op jit(solution)/shard_map/add | solution.py:170
  223.4 5.6 %all-to-all-done.8 = f32[16,8,512]{2,1,0:T(8,128)S(1)} async-done(((f32[16,8,512]{2,1,0:T(8,128)}), f32[16,8,512]{2,1,0:T(8,128)S(1)}, u32[]{:S(2)}, u32[]{:S(2)}) %all-to-all-start.8) | async-done | bytes 262176 | tf_op jit(solution)/shard_map/all_to_all | solution.py:173
  229.0 3.7 %all-to-all-start.7 = ((f32[3,3,16,16,256]{4,3,1,0,2:T(8,128)}), f32[3,3,16,16,256]{4,3,1,0,2:T(8,128)S(1)}, u32[]{:S(2)}, u32[]{:S(2)}) async-start(f32[3,3,16,16,256]{4,3,1,0,2:T(8,128)} %bitcast_add_fusion), calls=%async_computation.7 | async-start | bytes 4718592 | tf_op jit(solution)/shard_map/all_to_all | solution.py:172
  234.0 33.6 %all-to-all-done.7 = f32[3,3,16,16,256]{4,3,1,0,2:T(8,128)S(1)} async-done(((f32[3,3,16,16,256]{4,3,1,0,2:T(8,128)}), f32[3,3,16,16,256]{4,3,1,0,2:T(8,128)S(1)}, u32[]{:S(2)}, u32[]{:S(2)}) %all-to-all-start.7) | async-done | bytes 2359328 | tf_op jit(solution)/shard_map/all_to_all | solution.py:172
  271.1 3.8 %all-to-all-start.9 = ((f32[32,1,2]{2,1,0:T(1,128)}), f32[32,1,2]{2,1,0:T(1,128)S(1)}, u32[]{:S(2)}, u32[]{:S(2)}) async-start(f32[32,1,2]{2,1,0:T(1,128)} %broadcast_in_dim.25), calls=%async_computation.9 | async-start | bytes 32768 | tf_op jit(solution)/shard_map/all_to_all | solution.py:177
  275.6 6.7 %all-to-all-done.9 = f32[32,1,2]{2,1,0:T(1,128)S(1)} async-done(((f32[32,1,2]{2,1,0:T(1,128)}), f32[32,1,2]{2,1,0:T(1,128)S(1)}, u32[]{:S(2)}, u32[]{:S(2)}) %all-to-all-start.9) | async-done | bytes 288 | tf_op jit(solution)/shard_map/all_to_all | solution.py:177
  283.5 1.6 bitcast_subtract_fusion
  (152 shorter events, 66.9 us)
Async XLA Ops:
  0.6 49.5 %copy-start = (bf16[512,10]{0,1:T(8,128)(2,1)S(1)}, bf16[512,10]{0,1:T(8,128)(2,1)}, u32[]{:S(2)}) copy-start(bf16[512,10]{0,1:T(8,128)(2,1)} %param.13) | copy-start | bytes 30724
  0.6 9.9 %copy-start.19 = (bf16[12,8,8,512]{3,2,1,0:T(8,128)(2,1)S(1)}, bf16[12,8,8,512]{3,2,1,0:T(8,128)(2,1)}, u32[]{:S(2)}) copy-start(bf16[12,8,8,512]{3,2,1,0:T(8,128)(2,1)} %param.7) | copy-start | bytes 2359300
  4.8 9.7 %all-to-all-start.1 = ((bf16[4,2,192]{2,1,0:T(2,128)(2,1)}), bf16[4,2,192]{2,1,0:T(2,128)(2,1)S(1)}, u32[]{:S(2)}, u32[]{:S(2)}) async-start(bf16[4,2,192]{2,1,0:T(2,128)(2,1)} %reshape.224), calls=%async_computation.1 | async-start | bytes 8192 | tf_op jit(solution)/shard_map/all_to_all | solution.py:140
  14.5 23.9 %all-to-all-start = ((bf16[4,6,8,8,512]{4,3,2,1,0:T(8,128)(2,1)}), bf16[4,6,8,8,512]{4,3,2,1,0:T(8,128)(2,1)S(1)}, u32[]{:S(2)}, u32[]{:S(2)}) async-start(bf16[4,6,8,8,512]{4,3,2,1,0:T(8,128)(2,1)} %scatter_fusion), calls=%async_computation | async-start | bytes 3145728 | tf_op jit(solution)/shard_map/all_to_all | solution.py:139
  40.1 2.9 %copy-start.16 = (bf16[3,3,512,256]{3,2,1,0:T(8,128)(2,1)S(1)}, bf16[3,3,512,256]{3,2,1,0:T(8,128)(2,1)}, u32[]{:S(2)}) copy-start(bf16[3,3,512,256]{3,2,1,0:T(8,128)(2,1)} %convert_bitcast_fusion) | copy-start | bytes 7077892
  42.9 11.8 %copy-start.13 = (bf16[24,8,8,512]{3,2,1,0:T(8,128)(2,1)}, bf16[24,8,8,512]{3,2,1,0:T(8,128)(2,1)S(1)}, u32[]{:S(2)}) copy-start(bf16[24,8,8,512]{3,2,1,0:T(8,128)(2,1)S(1)} %get-tuple-element.20) | copy-start | bytes 4718596
  42.9 12.4 %copy-start.11 = (bf16[24,8,8,512]{3,2,1,0:T(8,128)(2,1)}, bf16[24,8,8,512]{3,2,1,0:T(8,128)(2,1)S(1)}, u32[]{:S(2)}) copy-start(bf16[24,8,8,512]{3,2,1,0:T(8,128)(2,1)S(1)} %get-tuple-element.14) | copy-start | bytes 4718596
  42.9 13.0 %copy-start.9 = (bf16[24,8,8,512]{3,2,1,0:T(8,128)(2,1)}, bf16[24,8,8,512]{3,2,1,0:T(8,128)(2,1)S(1)}, u32[]{:S(2)}) copy-start(bf16[24,8,8,512]{3,2,1,0:T(8,128)(2,1)S(1)} %get-tuple-element.15) | copy-start | bytes 4718596
  42.9 13.6 %copy-start.7 = (bf16[24,8,8,512]{3,2,1,0:T(8,128)(2,1)}, bf16[24,8,8,512]{3,2,1,0:T(8,128)(2,1)S(1)}, u32[]{:S(2)}) copy-start(bf16[24,8,8,512]{3,2,1,0:T(8,128)(2,1)S(1)} %get-tuple-element.16) | copy-start | bytes 4718596
  42.9 15.1 %copy-start.5 = (bf16[24,8,8,512]{3,2,1,0:T(8,128)(2,1)}, bf16[24,8,8,512]{3,2,1,0:T(8,128)(2,1)S(1)}, u32[]{:S(2)}) copy-start(bf16[24,8,8,512]{3,2,1,0:T(8,128)(2,1)S(1)} %get-tuple-element.17) | copy-start | bytes 4718596
  42.9 15.7 %copy-start.3 = (bf16[24,8,8,512]{3,2,1,0:T(8,128)(2,1)}, bf16[24,8,8,512]{3,2,1,0:T(8,128)(2,1)S(1)}, u32[]{:S(2)}) copy-start(bf16[24,8,8,512]{3,2,1,0:T(8,128)(2,1)S(1)} %get-tuple-element.18) | copy-start | bytes 4718596
  42.9 16.3 %copy-start.1 = (bf16[24,8,8,512]{3,2,1,0:T(8,128)(2,1)}, bf16[24,8,8,512]{3,2,1,0:T(8,128)(2,1)S(1)}, u32[]{:S(2)}) copy-start(bf16[24,8,8,512]{3,2,1,0:T(8,128)(2,1)S(1)} %get-tuple-element.19) | copy-start | bytes 4718596
  47.7 1.4 copy-start.17
  47.7 1.5 copy-start.20
  64.3 13.9 %collective-permute-start = (f32[3,3,16,16,256]{4,3,1,0,2:T(8,128)}, f32[3,3,16,16,256]{4,3,1,0,2:T(8,128)}, u32[]{:S(2)}, u32[]{:S(2)}) collective-permute-start(f32[3,3,16,16,256]{4,3,1,0,2:T(8,128)} %bitcast.289), channel_id=1, source_target_pairs={{0,1},{1,0},{2,3},{3,2},{4,5},{5,4},{6,7},{7,6},{8,9},{9,8},{10,11... | collective-permute-start | bytes 7077896 | tf_op jit(solution)/shard_map/ppermute | solution.py:169
  65.0 4.4 %collective-permute-start.1 = (f32[16,8,512]{2,1,0:T(8,128)S(1)}, f32[16,8,512]{2,1,0:T(8,128)S(1)}, u32[]{:S(2)}, u32[]{:S(2)}) collective-permute-start(f32[16,8,512]{2,1,0:T(8,128)S(1)} %dynamic-slice_bitcast_fusion.1), channel_id=1, source_target_pairs={{0,1},{1,0},{2,3},{3,2},{4,5},{5,4},{6,7},{7,6},{8,9},{9,8},{10,11... | collective-permute-start | bytes 786440 | tf_op jit(solution)/shard_map/ppermute | solution.py:169
  70.2 17.0 %all-to-all-start.3 = ((f32[16,8,512]{2,1,0:T(8,128)}), f32[16,8,512]{2,1,0:T(8,128)S(1)}, u32[]{:S(2)}, u32[]{:S(2)}) async-start(f32[16,8,512]{2,1,0:T(8,128)} %bitcast_add_fusion.3), calls=%async_computation.3 | async-start | bytes 524288 | tf_op jit(solution)/shard_map/all_to_all | solution.py:173
  87.2 38.6 %all-to-all-start.2 = ((f32[3,3,16,16,256]{4,3,1,0,2:T(8,128)}), f32[3,3,16,16,256]{4,3,1,0,2:T(8,128)}, u32[]{:S(2)}, u32[]{:S(2)}) async-start(f32[3,3,16,16,256]{4,3,1,0,2:T(8,128)} %bitcast_add_fusion.1), calls=%async_computation.2 | async-start | bytes 4718592 | tf_op jit(solution)/shard_map/all_to_all | solution.py:172
  130.9 11.1 %all-to-all-start.4 = ((f32[32,1,2]{2,1,0:T(1,128)}), f32[32,1,2]{2,1,0:T(1,128)S(1)}, u32[]{:S(2)}, u32[]{:S(2)}) async-start(f32[32,1,2]{2,1,0:T(1,128)} %broadcast_in_dim.21), calls=%async_computation.4 | async-start | bytes 32768 | tf_op jit(solution)/shard_map/all_to_all | solution.py:177
  168.1 14.4 %collective-permute-start.2 = (bf16[3,3,16,16,256]{4,3,2,1,0:T(8,128)(2,1)}, bf16[3,3,16,16,256]{4,3,2,1,0:T(8,128)(2,1)}, u32[]{:S(2)}, u32[]{:S(2)}) collective-permute-start(bf16[3,3,16,16,256]{4,3,2,1,0:T(8,128)(2,1)} %copy.44), channel_id=1, source_target_pairs={{0,1},{1,0},{2,3},{3,2},{4,5},{5,4},{6,7},{7,6},{8,9},{9,8},{10,11... | collective-permute-start | bytes 3538952 | tf_op jit(solution)/shard_map/ppermute | solution.py:189
  179.9 1.7 collective-permute-start.3
  184.4 1.4 copy-start.14
  185.8 1.4 copy-start.12
  187.2 1.4 copy-start.10
  188.6 1.4 copy-start.8
  190.6 1.4 copy-start.6
  195.4 1.4 copy-start.18
  210.4 9.4 %collective-permute-start.4 = (f32[3,3,16,16,256]{4,3,1,0,2:T(8,128)}, f32[3,3,16,16,256]{4,3,1,0,2:T(8,128)}, u32[]{:S(2)}, u32[]{:S(2)}) collective-permute-start(f32[3,3,16,16,256]{4,3,1,0,2:T(8,128)} %bitcast.288), channel_id=1, source_target_pairs={{0,1},{1,0},{2,3},{3,2},{4,5},{5,4},{6,7},{7,6},{8,9},{9,8},{10,11... | collective-permute-start | bytes 7077896 | tf_op jit(solution)/shard_map/ppermute | solution.py:169
  211.2 4.3 %collective-permute-start.5 = (f32[16,8,512]{2,1,0:T(8,128)S(1)}, f32[16,8,512]{2,1,0:T(8,128)S(1)}, u32[]{:S(2)}, u32[]{:S(2)}) collective-permute-start(f32[16,8,512]{2,1,0:T(8,128)S(1)} %dynamic-slice_bitcast_fusion), channel_id=1, source_target_pairs={{0,1},{1,0},{2,3},{3,2},{4,5},{5,4},{6,7},{7,6},{8,9},{9,8},{10,11... | collective-permute-start | bytes 786440 | tf_op jit(solution)/shard_map/ppermute | solution.py:169
  216.2 12.8 %all-to-all-start.8 = ((f32[16,8,512]{2,1,0:T(8,128)}), f32[16,8,512]{2,1,0:T(8,128)S(1)}, u32[]{:S(2)}, u32[]{:S(2)}) async-start(f32[16,8,512]{2,1,0:T(8,128)} %bitcast_add_fusion.2), calls=%async_computation.8 | async-start | bytes 524288 | tf_op jit(solution)/shard_map/all_to_all | solution.py:173
  229.0 38.6 %all-to-all-start.7 = ((f32[3,3,16,16,256]{4,3,1,0,2:T(8,128)}), f32[3,3,16,16,256]{4,3,1,0,2:T(8,128)S(1)}, u32[]{:S(2)}, u32[]{:S(2)}) async-start(f32[3,3,16,16,256]{4,3,1,0,2:T(8,128)} %bitcast_add_fusion), calls=%async_computation.7 | async-start | bytes 4718592 | tf_op jit(solution)/shard_map/all_to_all | solution.py:172
  271.1 11.1 %all-to-all-start.9 = ((f32[32,1,2]{2,1,0:T(1,128)}), f32[32,1,2]{2,1,0:T(1,128)S(1)}, u32[]{:S(2)}, u32[]{:S(2)}) async-start(f32[32,1,2]{2,1,0:T(1,128)} %broadcast_in_dim.25), calls=%async_computation.9 | async-start | bytes 32768 | tf_op jit(solution)/shard_map/all_to_all | solution.py:177
  (3 other events, 3.8 us)

commit v7 on v6

--- a/solution.py
+++ b/solution.py
@@ -72,8 +72,7 @@
     )
     sigmoid = jax.nn.sigmoid(middle)
     dmiddle = (dactive * sigmoid * (1.0 + middle * (1.0 - sigmoid))).astype(jnp.bfloat16)
-    grad_down = jnp.stack([contract_rows(window, dmiddle) for window in windows])
-    grad_down = grad_down.reshape(3, 3, grids.shape[3], down_low.shape[3])
+    grad_down = jnp.stack([contract_rows(window, dmiddle) for window in windows], axis=1)
     return (loss_sum, grad_down, grad_up)
 
 
@@ -156,46 +155,44 @@
     grid_axes = ("z", "y")
     plane = peers // 2
     core_pairs = [(i, i ^ 1) for i in range(peers)]
+    lanes = 128
+    down_span = 9 * part_chans * inner // lanes
     for update_round in range(TRAIN_STEPS):
         loss_sum, grad_down, grad_up = train_pass(
             held_feats, held_labels, down_low, upper_low, head, count
         )
-        grad_down = grad_down.reshape(3, 3, plane, 2, part_chans, inner)
-        grad_up = grad_up.reshape(plane, 2, part_inner, up_w.shape[2])
-        keep_down = lax.dynamic_index_in_dim(grad_down, core, 3, keepdims=False)
-        give_down = lax.dynamic_index_in_dim(grad_down, 1 - core, 3, keepdims=False)
-        keep_up = lax.dynamic_index_in_dim(grad_up, core, 1, keepdims=False)
-        give_up = lax.dynamic_index_in_dim(grad_up, 1 - core, 1, keepdims=False)
-        got_down, got_up = lax.ppermute((give_down, give_up), EX_AXES, perm=core_pairs)
-        grad_down = keep_down + got_down
-        grad_up = keep_up + got_up
-        grad_down = jnp.sum(lax.all_to_all(grad_down, grid_axes, 2, 2, tiled=True), axis=2)
-        grad_up = jnp.sum(lax.all_to_all(grad_up, grid_axes, 0, 0, tiled=True), axis=0)
-        squares = jnp.sum(grad_down * grad_down) + jnp.sum(grad_up * grad_up)
+        packed = jnp.concatenate(
+            [grad_down.reshape(plane, 2, down_span, lanes), grad_up.reshape(plane, 2, -1, lanes)], axis=2
+        )
+        keep = lax.dynamic_index_in_dim(packed, core, 1, keepdims=False)
+        give = lax.dynamic_index_in_dim(packed, 1 - core, 1, keepdims=False)
+        packed = keep + lax.ppermute(give, EX_AXES, perm=core_pairs)
+        packed = jnp.sum(lax.all_to_all(packed, grid_axes, 0, 0, tiled=True), axis=0)
+        shard_down = packed[:down_span].reshape(part_chans, 3, 3, inner)
+        shard_down = jnp.transpose(shard_down, (1, 2, 0, 3))
+        shard_up = packed[down_span:].reshape(up_own.shape)
+        squares = jnp.sum(shard_down * shard_down) + jnp.sum(shard_up * shard_up)
         totals = jnp.stack([squares, loss_sum])
         spread = jnp.broadcast_to(totals[None, :], (peers, totals.shape[0]))
         totals = jnp.sum(lax.all_to_all(spread, EX_AXES, 0, 0, tiled=True), axis=0)
         scale = step_scale(totals[0], entries)
-        down_own = down_own - scale * grad_down
-        up_own = up_own - scale * grad_up
+        down_own = down_own - scale * shard_down
+        up_own = up_own - scale * shard_up
         collected.append(totals[1] / (count * cells))
         if update_round + 1 < TRAIN_STEPS:
-            down_low = down_own.astype(jnp.bfloat16)
-            upper_low = up_own.astype(jnp.bfloat16)
-            down_low = jnp.broadcast_to(down_low[:, :, None], (3, 3, plane) + down_low.shape[2:])
-            upper_low = jnp.broadcast_to(upper_low[None], (plane,) + upper_low.shape)
-            down_low = lax.all_to_all(down_low, grid_axes, 2, 2, tiled=True)
-            upper_low = lax.all_to_all(upper_low, grid_axes, 0, 0, tiled=True)
-            other_down, other_up = lax.ppermute((down_low, upper_low), EX_AXES, perm=core_pairs)
+            low_down = jnp.transpose(down_own.astype(jnp.bfloat16), (2, 0, 1, 3)).reshape(down_span, lanes)
+            low_up = up_own.astype(jnp.bfloat16).reshape(-1, lanes)
+            block = jnp.concatenate([low_down, low_up], axis=0)
+            block = jnp.broadcast_to(block[None], (plane,) + block.shape)
+            block = lax.all_to_all(block, grid_axes, 0, 0, tiled=True)
+            other = lax.ppermute(block, EX_AXES, perm=core_pairs)
             first_core = core == 0
-            down_low = jnp.stack(
-                [jnp.where(first_core, down_low, other_down), jnp.where(first_core, other_down, down_low)], axis=3
+            block = jnp.stack(
+                [jnp.where(first_core, block, other), jnp.where(first_core, other, block)], axis=1
             )
-            upper_low = jnp.stack(
-                [jnp.where(first_core, upper_low, other_up), jnp.where(first_core, other_up, upper_low)], axis=1
-            )
-            down_low = down_low.reshape(down_w.shape[1:])
-            upper_low = upper_low.reshape(up_w.shape[1:])
+            down_low = block[:, :, :down_span].reshape(down_w.shape[3], 3, 3, inner)
+            down_low = jnp.transpose(down_low, (1, 2, 0, 3))
+            upper_low = block[:, :, down_span:].reshape(up_w.shape[1:])
     return (down_own[None], up_own[None], jnp.stack(collected)[None])
 
 

time: 293 us -> 351 us (1.20)
  local copies, waits for them, and re-layouts: 29.6 us -> 89.7 us
  blocking collectives: 32.7 us -> 23.6 us
  matrix products: 32.4 us -> 39.9 us
  waiting for transfers between devices: 116 us -> 123 us
  starting transfers between devices: 36.9 us -> 30.1 us
    reshape x0 -> x7, local copies, waits for them, and re-layouts: none -> 29.3 us  [the longest x2 14.8 us: shards(): grad_down.reshape(plane, 2, down_span, lanes)]
    unnamed x44 -> x83, local copies, waits for them, and re-layouts: 9.69 us -> 22.9 us
    another operation x0 -> x2, local copies, waits for them, and re-layouts: none -> 12.4 us  [train_pass(): jnp.stack([contract_rows(window, dmiddle) for window in windows], axis=1)]
    all_to_all x2 -> x1, blocking collectives: 32.7 us -> 23.6 us  [shards(): block = lax.all_to_all(block, grid_axes, 0, 0, tiled=True)]
    slice x0 -> x1, local copies, waits for them, and re-layouts: none -> 7.8 us  [train_pass(): down_low[offset_index // 3, offset_index % 3]]
    all_to_all x4 -> x2, starting transfers between devices: 19.7 us -> 12.7 us  [shards(): lax.all_to_all(packed, grid_axes, 0, 0, tiled=True)]
    dot_general x20, matrix products: 12.8 us -> 18.1 us  [contract_rows(): lax.dot_general(left, right, (((0,), (0,)), ((), ())), preferred_element_...]
    dynamic_slice x4 -> x3, local copies, waits for them, and re-layouts: 6.11 us -> 1.66 us  [the longest x1 0.93 us: shards(): lax.dynamic_slice_in_dim(down_w[0], place * part_chans, part_chans, 2)]
  transfers between devices with their start and end apart: 14 -> 9, of which waited for: 11 -> 9; matrix products, arithmetic and copies ran while one was open for 8% -> 3% of each run, Pallas kernels for 0% -> 0%
where the time goes in v7:
time: 351 us; the launch traced here: 345 us
  waiting for transfers between devices  123 us (35%)
  local copies, waits for them, and re-layouts  89.7 us (26%)
  matrix products  39.9 us (11%)
  other arithmetic  31.9 us (9%)
  starting transfers between devices  30.1 us (9%)
  blocking collectives  23.6 us (7%)
  between operations  7.59 us (2%)
    all_to_all x2, waiting for transfers between devices, shards(): lax.all_to_all(packed, grid_axes, 0, 0, tiled=True)  79.6 us
    all_to_all x1, blocking collectives, shards(): block = lax.all_to_all(block, grid_axes, 0, 0, tiled=True)  23.6 us
    unnamed x83, local copies, waits for them, and re-layouts  22.9 us
    dot_general x20, matrix products, contract_rows(): lax.dot_general(left, right, (((0,), (0,)), ((), ())), preferred_element_...  18.1 us
    all_to_all x1, waiting for transfers between devices, shards(): lax.all_to_all(send_feats, 'task', split_axis=0, concat_axis=0, tiled=True)  15.3 us
    reshape x2, local copies, waits for them, and re-layouts, shards(): grad_down.reshape(plane, 2, down_span, lanes)  14.8 us
    all_to_all x2, waiting for transfers between devices, shards(): totals = jnp.sum(lax.all_to_all(spread, EX_AXES, 0, 0, tiled=True), axis=0)  13.2 us
    all_to_all x2, starting transfers between devices, shards(): lax.all_to_all(packed, grid_axes, 0, 0, tiled=True)  12.7 us
  transfers between devices with their start and end apart: 9, of which 9 were waited for; matrix products, arithmetic and copies ran while one was open for 3% of the time, Pallas kernels for 0%

profile of v7, /device:TPU:0, one launch (start us, length us, event | category | flops | bytes accessed | tf_op | source)
XLA Modules:
  0.0 345.4 jit_solution(14325591774066475010)
XLA Ops:
  4.8 4.4 %all-to-all-start.1 = ((bf16[4,2,192]{2,1,0:T(2,128)(2,1)}), bf16[4,2,192]{2,1,0:T(2,128)(2,1)S(1)}, u32[]{:S(2)}, u32[]{:S(2)}) async-start(bf16[4,2,192]{2,1,0:T(2,128)(2,1)} %reshape.227), calls=%async_computation.1 | async-start | bytes 8192 | tf_op jit(solution)/shard_map/all_to_all | solution.py:139
  10.5 2.9 scatter_fusion
  14.5 3.7 %all-to-all-start = ((bf16[4,6,8,8,512]{4,3,2,1,0:T(8,128)(2,1)}), bf16[4,6,8,8,512]{4,3,2,1,0:T(8,128)(2,1)S(1)}, u32[]{:S(2)}, u32[]{:S(2)}) async-start(bf16[4,6,8,8,512]{4,3,2,1,0:T(8,128)(2,1)} %scatter_fusion), calls=%async_computation | async-start | bytes 3145728 | tf_op jit(solution)/shard_map/all_to_all | solution.py:138
  18.9 4.0 %convert_bitcast_fusion = bf16[3,3,512,256]{3,2,1,0:T(8,128)(2,1)} fusion(f32[1,3,3,512,256]{4,3,2,1,0:T(8,128)} %param.11), kind=kLoop, calls=%fused_computation.51 | loop fusion | flops 1179648 | bytes 7077888 | tf_op jit(solution)/shard_map/convert_element_type | solution.py:150
  23.0 15.3 %all-to-all-done = bf16[4,6,8,8,512]{4,3,2,1,0:T(8,128)(2,1)S(1)} async-done(((bf16[4,6,8,8,512]{4,3,2,1,0:T(8,128)(2,1)}), bf16[4,6,8,8,512]{4,3,2,1,0:T(8,128)(2,1)S(1)}, u32[]{:S(2)}, u32[]{:S(2)}) %all-to-all-start) | async-done | bytes 1572896 | tf_op jit(solution)/shard_map/all_to_all | solution.py:138
  40.0 2.5 pad_slice_fusion
  57.3 1.9 reshape.208
  59.2 2.4 fusion.28
  70.5 6.2 %copy.36 = f32[512,9,256]{2,1,0:T(8,128)} copy(f32[512,9,256]{2,0,1:T(8,128)S(1)} %fusion.20) | data formatting | bytes 9437184 | tf_op jit(solution)/shard_map/stack | solution.py:75
  76.7 7.4 %reshape.207 = f32[16,2,288,128]{3,2,1,0:T(8,128)} reshape(f32[512,9,256]{2,1,0:T(8,128)} %copy.36) | data formatting | bytes 9437184 | tf_op jit(solution)/shard_map/reshape | solution.py:165
  84.1 2.8 constant_dynamic-update-slice_fusion.1
  87.0 2.0 dynamic-slice_bitcast_fusion.1
  90.2 5.2 %collective-permute-done = f32[16,320,128]{2,1,0:T(8,128)} collective-permute-done((f32[16,320,128]{2,1,0:T(8,128)}, f32[16,320,128]{2,1,0:T(8,128)}, u32[]{:S(2)}, u32[]{:S(2)}) %collective-permute-start) | collective-permute-done | bytes 2621472 | tf_op jit(solution)/shard_map/ppermute | solution.py:169
  95.4 4.4 %bitcast_add_fusion.1 = f32[16,320,128]{2,1,0:T(8,128)} fusion(f32[16,320,128]{2,1,0:T(8,128)} %collective-permute-done, f32[16,2,320,128]{3,2,1,0:T(8,128)} %copy-done.1, s32[]{:T(128)S(6)} %select_n.53), kind=kLoop, calls=%fused_computation.45 | loop fusion | flops 655360 | bytes 7864324 | tf_op jit(solution)/shard_map/add | solution.py:169
  99.9 8.1 %all-to-all-start.2 = ((f32[16,320,128]{2,1,0:T(8,128)}), f32[16,320,128]{2,1,0:T(8,128)}, u32[]{:S(2)}, u32[]{:S(2)}) async-start(f32[16,320,128]{2,1,0:T(8,128)} %bitcast_add_fusion.1), calls=%async_computation.2 | async-start | bytes 5242880 | tf_op jit(solution)/shard_map/all_to_all | solution.py:170
  109.6 39.1 %all-to-all-done.2 = f32[16,320,128]{2,1,0:T(8,128)} async-done(((f32[16,320,128]{2,1,0:T(8,128)}), f32[16,320,128]{2,1,0:T(8,128)}, u32[]{:S(2)}, u32[]{:S(2)}) %all-to-all-start.2) | async-done | bytes 2621472 | tf_op jit(solution)/shard_map/all_to_all | solution.py:170
  154.3 4.4 %all-to-all-start.3 = ((f32[32,1,2]{2,1,0:T(1,128)}), f32[32,1,2]{2,1,0:T(1,128)S(1)}, u32[]{:S(2)}, u32[]{:S(2)}) async-start(f32[32,1,2]{2,1,0:T(1,128)} %broadcast_in_dim.19), calls=%async_computation.3 | async-start | bytes 32768 | tf_op jit(solution)/shard_map/all_to_all | solution.py:177
  159.4 6.6 %all-to-all-done.3 = f32[32,1,2]{2,1,0:T(1,128)S(1)} async-done(((f32[32,1,2]{2,1,0:T(1,128)}), f32[32,1,2]{2,1,0:T(1,128)S(1)}, u32[]{:S(2)}, u32[]{:S(2)}) %all-to-all-start.3) | async-done | bytes 288 | tf_op jit(solution)/shard_map/all_to_all | solution.py:177
  172.5 23.6 %all_to_all.37 = bf16[16,320,128]{2,1,0:T(8,128)(2,1)} all-to-all(bf16[16,320,128]{2,1,0:T(8,128)(2,1)S(1)} %broadcast_in_dim.20), channel_id=1, replica_groups=mesh['task'=4,'z'=4,'y'=4,'core'=2] {'z','y'}, dimensions={0} | all-to-all | bytes 2621440 | tf_op jit(solution)/shard_map/all_to_all | solution.py:187
  196.1 3.4 collective-permute-done.1
  205.5 7.3 %reshape.210 = bf16[512,3,3,256]{3,2,1,0:T(4,128)(2,1)} reshape(bf16[16,2,288,128]{3,2,1,0:T(8,128)(2,1)} %fusion.8) | data formatting | bytes 4718592 | tf_op jit(solution)/shard_map/reshape | solution.py:193
  212.9 7.8 %fusion.80 = (bf16[1,1,512,256]{3,1,0,2:T(2,128)(2,1)S(1)}, bf16[1,1,512,256]{3,1,0,2:T(2,128)(2,1)S(1)}, bf16[1,1,512,256]{3,1,0,2:T(2,128)(2,1)S(1)}, bf16[1,1...) fusion(bf16[3,3,512,256]{3,1,0,2:T(4,128)(2,1)} %bitcast.281), kind=kLoop, calls=%fused_computation.202 | loop fusion | bytes 4718592 | tf_op jit(solution)/shard_map/slice | solution.py:37
  241.9 2.4 fusion.19
  253.2 6.2 %copy.39 = f32[512,9,256]{2,1,0:T(8,128)} copy(f32[512,9,256]{2,0,1:T(8,128)S(1)} %fusion.11) | data formatting | bytes 9437184 | tf_op jit(solution)/shard_map/stack | solution.py:75
  259.4 7.4 %reshape.212 = f32[16,2,288,128]{3,2,1,0:T(8,128)} reshape(f32[512,9,256]{2,1,0:T(8,128)} %copy.39) | data formatting | bytes 9437184 | tf_op jit(solution)/shard_map/reshape | solution.py:165
  266.8 2.8 constant_dynamic-update-slice_fusion.3
  270.0 4.8 %collective-permute-done.2 = f32[16,320,128]{2,1,0:T(8,128)S(1)} collective-permute-done((f32[16,320,128]{2,1,0:T(8,128)S(1)}, f32[16,320,128]{2,1,0:T(8,128)S(1)}, u32[]{:S(2)}, u32[]{:S(2)}) %collective-permute-start.2) | collective-permute-done | bytes 2621472 | tf_op jit(solution)/shard_map/ppermute | solution.py:169
  274.8 1.9 bitcast_add_fusion
  276.7 4.6 %all-to-all-start.5 = ((f32[16,320,128]{2,1,0:T(8,128)}), f32[16,320,128]{2,1,0:T(8,128)}, u32[]{:S(2)}, u32[]{:S(2)}) async-start(f32[16,320,128]{2,1,0:T(8,128)} %bitcast_add_fusion), calls=%async_computation.5 | async-start | bytes 5242880 | tf_op jit(solution)/shard_map/all_to_all | solution.py:170
  282.0 40.5 %all-to-all-done.5 = f32[16,320,128]{2,1,0:T(8,128)} async-done(((f32[16,320,128]{2,1,0:T(8,128)}), f32[16,320,128]{2,1,0:T(8,128)}, u32[]{:S(2)}, u32[]{:S(2)}) %all-to-all-start.5) | async-done | bytes 2621472 | tf_op jit(solution)/shard_map/all_to_all | solution.py:170
  328.3 4.7 %all-to-all-start.6 = ((f32[32,1,2]{2,1,0:T(1,128)}), f32[32,1,2]{2,1,0:T(1,128)S(1)}, u32[]{:S(2)}, u32[]{:S(2)}) async-start(f32[32,1,2]{2,1,0:T(1,128)} %broadcast_in_dim.21), calls=%async_computation.6 | async-start | bytes 32768 | tf_op jit(solution)/shard_map/all_to_all | solution.py:177
  333.7 6.7 %all-to-all-done.6 = f32[32,1,2]{2,1,0:T(1,128)S(1)} async-done(((f32[32,1,2]{2,1,0:T(1,128)}), f32[32,1,2]{2,1,0:T(1,128)S(1)}, u32[]{:S(2)}, u32[]{:S(2)}) %all-to-all-start.6) | async-done | bytes 288 | tf_op jit(solution)/shard_map/all_to_all | solution.py:177
  (192 shorter events, 90.7 us)
Async XLA Ops:
  0.6 49.8 %copy-start = (bf16[512,10]{0,1:T(8,128)(2,1)S(1)}, bf16[512,10]{0,1:T(8,128)(2,1)}, u32[]{:S(2)}) copy-start(bf16[512,10]{0,1:T(8,128)(2,1)} %param.13) | copy-start | bytes 30724
  0.6 9.9 %copy-start.33 = (bf16[12,8,8,512]{3,2,1,0:T(8,128)(2,1)S(1)}, bf16[12,8,8,512]{3,2,1,0:T(8,128)(2,1)}, u32[]{:S(2)}) copy-start(bf16[12,8,8,512]{3,2,1,0:T(8,128)(2,1)} %param.7) | copy-start | bytes 2359300
  4.8 9.7 %all-to-all-start.1 = ((bf16[4,2,192]{2,1,0:T(2,128)(2,1)}), bf16[4,2,192]{2,1,0:T(2,128)(2,1)S(1)}, u32[]{:S(2)}, u32[]{:S(2)}) async-start(bf16[4,2,192]{2,1,0:T(2,128)(2,1)} %reshape.227), calls=%async_computation.1 | async-start | bytes 8192 | tf_op jit(solution)/shard_map/all_to_all | solution.py:139
  14.5 23.9 %all-to-all-start = ((bf16[4,6,8,8,512]{4,3,2,1,0:T(8,128)(2,1)}), bf16[4,6,8,8,512]{4,3,2,1,0:T(8,128)(2,1)S(1)}, u32[]{:S(2)}, u32[]{:S(2)}) async-start(bf16[4,6,8,8,512]{4,3,2,1,0:T(8,128)(2,1)} %scatter_fusion), calls=%async_computation | async-start | bytes 3145728 | tf_op jit(solution)/shard_map/all_to_all | solution.py:138
  40.0 2.6 copy-start.28
  42.5 1.8 copy-start.22
  42.5 2.1 copy-start.26
  42.5 2.6 copy-start.14
  42.5 3.7 %copy-start.10 = (bf16[24,8,8,512]{3,2,1,0:T(8,128)(2,1)}, bf16[24,8,8,512]{3,2,1,0:T(8,128)(2,1)S(1)}, u32[]{:S(2)}) copy-start(bf16[24,8,8,512]{3,2,1,0:T(8,128)(2,1)S(1)} %get-tuple-element.36) | copy-start | bytes 4718596
  42.6 4.3 %copy-start.6 = (bf16[24,8,8,512]{3,2,1,0:T(8,128)(2,1)}, bf16[24,8,8,512]{3,2,1,0:T(8,128)(2,1)S(1)}, u32[]{:S(2)}) copy-start(bf16[24,8,8,512]{3,2,1,0:T(8,128)(2,1)S(1)} %get-tuple-element.37) | copy-start | bytes 4718596
  42.6 4.9 %copy-start.2 = (bf16[24,8,8,512]{3,2,1,0:T(8,128)(2,1)}, bf16[24,8,8,512]{3,2,1,0:T(8,128)(2,1)S(1)}, u32[]{:S(2)}) copy-start(bf16[24,8,8,512]{3,2,1,0:T(8,128)(2,1)S(1)} %get-tuple-element.38) | copy-start | bytes 4718596
  48.0 1.4 copy-start.31
  48.1 1.5 copy-start.36
  59.2 2.4 copy-start.23
  59.2 2.4 copy-start.38
  84.1 2.8 copy-start.30
  86.9 3.2 copy-start.1
  90.2 5.3 %collective-permute-start = (f32[16,320,128]{2,1,0:T(8,128)}, f32[16,320,128]{2,1,0:T(8,128)}, u32[]{:S(2)}, u32[]{:S(2)}) collective-permute-start(f32[16,320,128]{2,1,0:T(8,128)} %dynamic-slice_bitcast_fusion.1), channel_id=1, source_target_pairs={{0,1},{1,0},{2,3},{3,2},{4,5},{5,4},{6,7},{7,6},{8,9},{9,8},{10,11... | collective-permute-start | bytes 7864328 | tf_op jit(solution)/shard_map/ppermute | solution.py:169
  99.9 48.8 %all-to-all-start.2 = ((f32[16,320,128]{2,1,0:T(8,128)}), f32[16,320,128]{2,1,0:T(8,128)}, u32[]{:S(2)}, u32[]{:S(2)}) async-start(f32[16,320,128]{2,1,0:T(8,128)} %bitcast_add_fusion.1), calls=%async_computation.2 | async-start | bytes 5242880 | tf_op jit(solution)/shard_map/all_to_all | solution.py:170
  154.3 11.7 %all-to-all-start.3 = ((f32[32,1,2]{2,1,0:T(1,128)}), f32[32,1,2]{2,1,0:T(1,128)S(1)}, u32[]{:S(2)}, u32[]{:S(2)}) async-start(f32[32,1,2]{2,1,0:T(1,128)} %broadcast_in_dim.19), calls=%async_computation.3 | async-start | bytes 32768 | tf_op jit(solution)/shard_map/all_to_all | solution.py:177
  196.1 3.4 collective-permute-start.1
  212.9 7.8 %copy-start.27 = (bf16[24,8,8,512]{3,2,1,0:T(8,128)(2,1)S(1)}, bf16[24,8,8,512]{3,2,1,0:T(8,128)(2,1)}, u32[]{:S(2)}) copy-start(bf16[24,8,8,512]{3,2,1,0:T(8,128)(2,1)} %copy-done.26) | copy-start | bytes 4718596
  220.7 1.4 copy-start.24
  225.5 1.4 copy-start.12
  230.3 1.4 copy-start.34
  241.9 2.4 copy-start.25
  241.9 2.4 copy-start.37
  266.8 2.8 copy-start.29
  269.8 5.0 %collective-permute-start.2 = (f32[16,320,128]{2,1,0:T(8,128)S(1)}, f32[16,320,128]{2,1,0:T(8,128)S(1)}, u32[]{:S(2)}, u32[]{:S(2)}) collective-permute-start(f32[16,320,128]{2,1,0:T(8,128)S(1)} %dynamic-slice_bitcast_fusion), channel_id=1, source_target_pairs={{0,1},{1,0},{2,3},{3,2},{4,5},{5,4},{6,7},{7,6},{8,9},{9,8},{10,11... | collective-permute-start | bytes 7864328 | tf_op jit(solution)/shard_map/ppermute | solution.py:169
  276.7 4.6 %copy-start.35 = (f32[1536]{0:T(1024)S(1)}, f32[1536]{0:T(1024)}, u32[]{:S(2)}) copy-start(f32[1536]{0:T(1024)} %get-tuple-element.15) | copy-start | bytes 18436
  276.7 45.8 %all-to-all-start.5 = ((f32[16,320,128]{2,1,0:T(8,128)}), f32[16,320,128]{2,1,0:T(8,128)}, u32[]{:S(2)}, u32[]{:S(2)}) async-start(f32[16,320,128]{2,1,0:T(8,128)} %bitcast_add_fusion), calls=%async_computation.5 | async-start | bytes 5242880 | tf_op jit(solution)/shard_map/all_to_all | solution.py:170
  328.3 12.0 %all-to-all-start.6 = ((f32[32,1,2]{2,1,0:T(1,128)}), f32[32,1,2]{2,1,0:T(1,128)S(1)}, u32[]{:S(2)}, u32[]{:S(2)}) async-start(f32[32,1,2]{2,1,0:T(1,128)} %broadcast_in_dim.21), calls=%async_computation.6 | async-start | bytes 32768 | tf_op jit(solution)/shard_map/all_to_all | solution.py:177
  (16 other events, 22.4 us)

commit v8 on v5

--- a/solution.py
+++ b/solution.py
@@ -93,7 +93,8 @@
     mine = (place >> bit) & 1
     keep = lax.dynamic_index_in_dim(value, mine, axis, keepdims=False)
     give = lax.dynamic_index_in_dim(value, 1 - mine, axis, keepdims=False)
-    return keep + partner_swap(give, pairs)
+    sent = partner_swap(give.astype(jnp.bfloat16), pairs)
+    return keep + sent.astype(jnp.float32)
 
 
 def double_join(value, axis, bit, pairs, place):

time: 283 us -> 250 us (0.88)
  waiting for transfers between devices: 122 us -> 91.2 us
  other arithmetic: 31.2 us -> 25.6 us
  matrix products: 32.7 us -> 36.6 us
    ppermute x30, waiting for transfers between devices: 92.2 us -> 60.9 us  [partner_swap(): return lax.ppermute(value, 'ex', perm=pairs)]
    select_n x2, other arithmetic: 5.65 us -> 0.98 us  [shards(): jnp.where(second_core, swap_bit_axes(grad_down, 2, levels), grad_down)]
    dot_general x20, matrix products: 13 us -> 17.1 us  [contract_rows(): lax.dot_general(left, right, (((0,), (0,)), ((), ())), preferred_element_...]
    unnamed x58 -> x70, local copies, waits for them, and re-layouts: 11.4 us -> 14.1 us
  transfers between devices with their start and end apart: 34 -> 34, of which waited for: 25 -> 20; matrix products, arithmetic and copies ran while one was open for 6% -> 9% of each run, Pallas kernels for 0% -> 0%
where the time goes in v8:
time: 250 us; the launch traced here: 245 us
  waiting for transfers between devices  91.2 us (36%)
  starting transfers between devices  56.3 us (23%)
  matrix products  36.6 us (15%)
  local copies, waits for them, and re-layouts  27.4 us (11%)
  other arithmetic  25.6 us (10%)
  between operations  7.92 us (3%)
    ppermute x30, waiting for transfers between devices, partner_swap(): return lax.ppermute(value, 'ex', perm=pairs)  60.9 us
    ppermute x30, starting transfers between devices, partner_swap(): return lax.ppermute(value, 'ex', perm=pairs)  37.8 us
    dot_general x20, matrix products, contract_rows(): lax.dot_general(left, right, (((0,), (0,)), ((), ())), preferred_element_...  17.1 us
    all_to_all x1, waiting for transfers between devices, shards(): lax.all_to_all(send_feats, 'task', split_axis=0, concat_axis=0, tiled=True)  15.3 us
    unnamed x70, local copies, waits for them, and re-layouts  14.1 us
    all_to_all x2, waiting for transfers between devices, shards(): totals = jnp.sum(lax.all_to_all(spread, 'ex', 0, 0, tiled=True), axis=0)  14 us
    dot_general x18, matrix products, train_pass(): jnp.dot(windows[offset_index], down_low[offset_index // 3, offset_index %...  10.4 us
    all_to_all x2, starting transfers between devices, shards(): totals = jnp.sum(lax.all_to_all(spread, 'ex', 0, 0, tiled=True), axis=0)  10.2 us
  transfers between devices with their start and end apart: 34, of which 20 were waited for; matrix products, arithmetic and copies ran while one was open for 9% of the time, Pallas kernels for 0%

profile of v8, /device:TPU:0, one launch (start us, length us, event | category | flops | bytes accessed | tf_op | source)
XLA Modules:
  0.0 245.0 jit_solution(4400867614063268200)
XLA Ops:
  4.8 4.4 %all-to-all-start.1 = ((bf16[4,2,192]{2,1,0:T(2,128)(2,1)}), bf16[4,2,192]{2,1,0:T(2,128)(2,1)S(1)}, u32[]{:S(2)}, u32[]{:S(2)}) async-start(bf16[4,2,192]{2,1,0:T(2,128)(2,1)} %reshape.198), calls=%async_computation.1 | async-start | bytes 8192 | tf_op jit(solution)/shard_map/all_to_all | solution.py:138
  10.5 3.0 %scatter_fusion = bf16[4,6,8,8,512]{4,3,2,1,0:T(8,128)(2,1)} fusion(bf16[4,6,8,8,512]{4,3,2,1,0:T(8,128)(2,1)} %broadcast_in_dim.16, s32[12]{0:T(128)S(1)} %fusion.83, bf16[12,8,8,512]{3,2,1,0:T(8,128)(2,1)S(1)} %copy-done.28), kind=kCustom, calls=%fused_computation | custom fusion | bytes 2359392 | tf_op jit(solution)/shard_map/scatter | solution.py:129
  14.5 3.8 %all-to-all-start = ((bf16[4,6,8,8,512]{4,3,2,1,0:T(8,128)(2,1)}), bf16[4,6,8,8,512]{4,3,2,1,0:T(8,128)(2,1)S(1)}, u32[]{:S(2)}, u32[]{:S(2)}) async-start(bf16[4,6,8,8,512]{4,3,2,1,0:T(8,128)(2,1)} %scatter_fusion), calls=%async_computation | async-start | bytes 3145728 | tf_op jit(solution)/shard_map/all_to_all | solution.py:137
  19.0 4.0 %convert_bitcast_fusion = bf16[3,3,512,256]{3,2,1,0:T(8,128)(2,1)} fusion(f32[1,3,3,512,256]{4,3,2,1,0:T(8,128)} %param.11), kind=kLoop, calls=%fused_computation.51 | loop fusion | flops 1179648 | bytes 7077888 | tf_op jit(solution)/shard_map/convert_element_type | solution.py:149
  23.2 15.3 %all-to-all-done = bf16[4,6,8,8,512]{4,3,2,1,0:T(8,128)(2,1)S(1)} async-done(((bf16[4,6,8,8,512]{4,3,2,1,0:T(8,128)(2,1)}), bf16[4,6,8,8,512]{4,3,2,1,0:T(8,128)(2,1)S(1)}, u32[]{:S(2)}, u32[]{:S(2)}) %all-to-all-start) | async-done | bytes 1572896 | tf_op jit(solution)/shard_map/all_to_all | solution.py:137
  39.2 2.6 %pad_slice_fusion = (bf16[24,8,8,512]{3,2,1,0:T(8,128)(2,1)S(1)}, bf16[24,8,8,512]{3,2,1,0:T(8,128)(2,1)S(1)}, bf16[24,8,8,512]{3,2,1,0:T(8,128)(2,1)S(1)}, bf16...) fusion(bf16[24,8,8,512]{3,2,1,0:T(8,128)(2,1)S(1)} %bitcast.461), kind=kLoop, calls=%fused_computation.2 | loop fusion | bytes 14155776 | tf_op jit(solution)/shard_map/slice | solution.py:19
  59.6 2.1 copy-done.19
  63.0 2.7 %fusion.86 = f32[256,512]{1,0:T(8,128)S(1)} fusion(bf16[1536,512]{0,1:T(8,128)(2,1)} %copy-done.26, f32[1536,256]{1,0:T(8,128)} %copy-done.22), kind=kOutput, calls=%fused_computation.280 | convolution fusion | flops 404619264 | bytes 3670016 | tf_op jit(solution)/shard_map/dot_general | solution.py:25
  69.7 7.8 %collective-permute-done.6 = bf16[2,2,2,8,512]{4,3,0,1,2:T(8,128)(2,1)S(1)} collective-permute-done((bf16[2,2,2,8,512]{4,3,0,1,2:T(8,128)(2,1)S(1)}, bf16[2,2,2,8,512]{4,3,0,1,2:T(8,128)(2,1)S(1)}, u32[]{:S(2)}, u32[]{:S(2)}) %collective-permute-start.6) | collective-permute-done | bytes 65568 | tf_op jit(solution)/shard_map/ppermute | solution.py:85
  77.6 3.2 %collective-permute-start.7 = (bf16[2,2,8,512]{3,2,0,1:T(8,128)(2,1)S(1)}, bf16[2,2,8,512]{3,2,0,1:T(8,128)(2,1)S(1)}, u32[]{:S(2)}, u32[]{:S(2)}) collective-permute-start(bf16[2,2,8,512]{3,2,0,1:T(8,128)(2,1)S(1)} %fusion.74), channel_id=1, source_target_pairs={{0,4},{1,17},{2,6},{3,19},{4,0},{5,21},{6,2},{7,23},{8,12},{9,25},... | collective-permute-start | bytes 98312 | tf_op jit(solution)/shard_map/ppermute | solution.py:85
  85.1 4.5 %collective-permute-done.2 = bf16[3,3,2,2,16,256]{5,4,1,0,2,3:T(8,128)(2,1)S(1)} collective-permute-done((bf16[3,3,2,2,16,256]{5,4,1,0,2,3:T(8,128)(2,1)S(1)}, bf16[3,3,2,2,16,256]{5,4,1,0,2,3:T(8,128)(2,1)S(1)}, u32[]{:S(2)}, u32[]{:S(2)}) %collective-permute-start.2) | collective-permute-done | bytes 294944 | tf_op jit(solution)/shard_map/ppermute | solution.py:85
  91.8 3.7 %collective-permute-start.9 = (bf16[8,512]{1,0:T(8,128)(2,1)S(1)}, bf16[8,512]{1,0:T(8,128)(2,1)S(1)}, u32[]{:S(2)}, u32[]{:S(2)}) collective-permute-start(bf16[8,512]{1,0:T(8,128)(2,1)S(1)} %fusion.78), channel_id=1, source_target_pairs={{0,16},{1,5},{2,18},{3,7},{4,20},{5,1},{6,22},{7,3},{8,24},{9,13},... | collective-permute-start | bytes 24584 | tf_op jit(solution)/shard_map/ppermute | solution.py:85
  95.5 3.5 %collective-permute-start.4 = (bf16[3,3,16,256]{3,2,1,0:T(8,128)(2,1)S(1)}, bf16[3,3,16,256]{3,2,1,0:T(8,128)(2,1)S(1)}, u32[]{:S(2)}, u32[]{:S(2)}) collective-permute-start(bf16[3,3,16,256]{3,2,1,0:T(8,128)(2,1)S(1)} %fusion.62), channel_id=1, source_target_pairs={{0,16},{1,5},{2,18},{3,7},{4,20},{5,1},{6,22},{7,3},{8,24},{9,13},... | collective-permute-start | bytes 221192 | tf_op jit(solution)/shard_map/ppermute | solution.py:85
  104.7 5.7 %all-to-all-start.2 = ((f32[32,1,2]{2,1,0:T(1,128)}), f32[32,1,2]{2,1,0:T(1,128)S(1)}, u32[]{:S(2)}, u32[]{:S(2)}) async-start(f32[32,1,2]{2,1,0:T(1,128)} %broadcast_in_dim.19), calls=%async_computation.2 | async-start | bytes 32768 | tf_op jit(solution)/shard_map/all_to_all | solution.py:175
  110.4 7.3 %all-to-all-done.2 = f32[32,1,2]{2,1,0:T(1,128)S(1)} async-done(((f32[32,1,2]{2,1,0:T(1,128)}), f32[32,1,2]{2,1,0:T(1,128)S(1)}, u32[]{:S(2)}, u32[]{:S(2)}) %all-to-all-start.2) | async-done | bytes 288 | tf_op jit(solution)/shard_map/all_to_all | solution.py:175
  121.3 4.6 %collective-permute-done.10 = bf16[3,3,16,256]{3,2,1,0:T(8,128)(2,1)S(1)} collective-permute-done((bf16[3,3,16,256]{3,2,1,0:T(8,128)(2,1)S(1)}, bf16[3,3,16,256]{3,2,1,0:T(8,128)(2,1)S(1)}, u32[]{:S(2)}, u32[]{:S(2)}) %collective-permute-start.10) | collective-permute-done | bytes 73760 | tf_op jit(solution)/shard_map/ppermute | solution.py:85
  126.7 4.5 %collective-permute-done.11 = bf16[3,3,2,16,256]{4,3,2,1,0:T(8,128)(2,1)S(1)} collective-permute-done((bf16[3,3,2,16,256]{4,3,2,1,0:T(8,128)(2,1)S(1)}, bf16[3,3,2,16,256]{4,3,2,1,0:T(8,128)(2,1)S(1)}, u32[]{:S(2)}, u32[]{:S(2)}) %collective-permute-start.11) | collective-permute-done | bytes 147488 | tf_op jit(solution)/shard_map/ppermute | solution.py:85
  134.5 5.1 %collective-permute-done.12 = bf16[3,3,2,2,16,256]{5,4,3,2,1,0:T(8,128)(2,1)S(1)} collective-permute-done((bf16[3,3,2,2,16,256]{5,4,3,2,1,0:T(8,128)(2,1)S(1)}, bf16[3,3,2,2,16,256]{5,4,3,2,1,0:T(8,128)(2,1)S(1)}, u32[]{:S(2)}, u32[]{:S(2)}) %collective-permute-start.12) | collective-permute-done | bytes 294944 | tf_op jit(solution)/shard_map/ppermute | solution.py:85
  141.1 3.5 %collective-permute-done.16 = bf16[2,8,512]{2,1,0:T(8,128)(2,1)S(1)} collective-permute-done((bf16[2,8,512]{2,1,0:T(8,128)(2,1)S(1)}, bf16[2,8,512]{2,1,0:T(8,128)(2,1)S(1)}, u32[]{:S(2)}, u32[]{:S(2)}) %collective-permute-start.16) | collective-permute-done | bytes 16416 | tf_op jit(solution)/shard_map/ppermute | solution.py:85
  146.5 3.2 %collective-permute-done.13 = bf16[3,3,2,2,2,16,256]{6,5,4,3,2,1,0:T(8,128)(2,1)} collective-permute-done((bf16[3,3,2,2,2,16,256]{6,5,4,3,2,1,0:T(8,128)(2,1)S(1)}, bf16[3,3,2,2,2,16,256]{6,5,4,3,2,1,0:T(8,128)(2,1)}, u32[]{:S(2)}, u32[]{:S(2)}) %collective-permute-start.13) | collective-permute-done | bytes 589856 | tf_op jit(solution)/shard_map/ppermute | solution.py:85
  153.3 3.5 %collective-permute-done.18 = bf16[2,2,2,8,512]{4,3,2,1,0:T(8,128)(2,1)S(1)} collective-permute-done((bf16[2,2,2,8,512]{4,3,2,1,0:T(8,128)(2,1)S(1)}, bf16[2,2,2,8,512]{4,3,2,1,0:T(8,128)(2,1)S(1)}, u32[]{:S(2)}, u32[]{:S(2)}) %collective-permute-start.18) | collective-permute-done | bytes 65568 | tf_op jit(solution)/shard_map/ppermute | solution.py:85
  158.6 2.1 select_bitcast_fusion.1
  185.6 2.1 copy-done.18
  188.2 2.7 %fusion.87 = f32[256,512]{1,0:T(8,128)S(1)} fusion(bf16[1536,512]{0,1:T(8,128)(2,1)} %copy-done.27, f32[1536,256]{1,0:T(8,128)} %copy-done.23), kind=kOutput, calls=%fused_computation.281 | convolution fusion | flops 404619264 | bytes 3670016 | tf_op jit(solution)/shard_map/dot_general | solution.py:25
  194.9 7.8 %collective-permute-done.26 = bf16[2,2,2,8,512]{4,3,0,1,2:T(8,128)(2,1)S(1)} collective-permute-done((bf16[2,2,2,8,512]{4,3,0,1,2:T(8,128)(2,1)S(1)}, bf16[2,2,2,8,512]{4,3,0,1,2:T(8,128)(2,1)S(1)}, u32[]{:S(2)}, u32[]{:S(2)}) %collective-permute-start.26) | collective-permute-done | bytes 65568 | tf_op jit(solution)/shard_map/ppermute | solution.py:85
  204.3 2.4 collective-permute-start.22
  209.0 3.8 %collective-permute-done.22 = bf16[3,3,2,2,16,256]{5,4,1,0,2,3:T(8,128)(2,1)S(1)} collective-permute-done((bf16[3,3,2,2,16,256]{5,4,1,0,2,3:T(8,128)(2,1)S(1)}, bf16[3,3,2,2,16,256]{5,4,1,0,2,3:T(8,128)(2,1)S(1)}, u32[]{:S(2)}, u32[]{:S(2)}) %collective-permute-start.22) | collective-permute-done | bytes 294944 | tf_op jit(solution)/shard_map/ppermute | solution.py:85
  213.6 2.1 collective-permute-start.29
  215.7 2.4 collective-permute-done.23
  220.1 4.0 %collective-permute-done.24 = bf16[3,3,16,256]{3,2,1,0:T(8,128)(2,1)S(1)} collective-permute-done((bf16[3,3,16,256]{3,2,1,0:T(8,128)(2,1)S(1)}, bf16[3,3,16,256]{3,2,1,0:T(8,128)(2,1)S(1)}, u32[]{:S(2)}, u32[]{:S(2)}) %collective-permute-start.24) | collective-permute-done | bytes 73760 | tf_op jit(solution)/shard_map/ppermute | solution.py:85
  227.4 4.5 %all-to-all-start.3 = ((f32[32,1,2]{2,1,0:T(1,128)}), f32[32,1,2]{2,1,0:T(1,128)S(1)}, u32[]{:S(2)}, u32[]{:S(2)}) async-start(f32[32,1,2]{2,1,0:T(1,128)} %broadcast_in_dim.20), calls=%async_computation.3 | async-start | bytes 32768 | tf_op jit(solution)/shard_map/all_to_all | solution.py:175
  232.6 6.7 %all-to-all-done.3 = f32[32,1,2]{2,1,0:T(1,128)S(1)} async-done(((f32[32,1,2]{2,1,0:T(1,128)}), f32[32,1,2]{2,1,0:T(1,128)S(1)}, u32[]{:S(2)}, u32[]{:S(2)}) %all-to-all-start.3) | async-done | bytes 288 | tf_op jit(solution)/shard_map/all_to_all | solution.py:175
  (253 shorter events, 98.4 us)
Async XLA Ops:
  4.8 9.7 %all-to-all-start.1 = ((bf16[4,2,192]{2,1,0:T(2,128)(2,1)}), bf16[4,2,192]{2,1,0:T(2,128)(2,1)S(1)}, u32[]{:S(2)}, u32[]{:S(2)}) async-start(bf16[4,2,192]{2,1,0:T(2,128)(2,1)} %reshape.198), calls=%async_computation.1 | async-start | bytes 8192 | tf_op jit(solution)/shard_map/all_to_all | solution.py:138
  14.5 24.0 %all-to-all-start = ((bf16[4,6,8,8,512]{4,3,2,1,0:T(8,128)(2,1)}), bf16[4,6,8,8,512]{4,3,2,1,0:T(8,128)(2,1)S(1)}, u32[]{:S(2)}, u32[]{:S(2)}) async-start(bf16[4,6,8,8,512]{4,3,2,1,0:T(8,128)(2,1)} %scatter_fusion), calls=%async_computation | async-start | bytes 3145728 | tf_op jit(solution)/shard_map/all_to_all | solution.py:137
  62.9 3.4 %collective-permute-start = (bf16[3,3,2,2,2,2,16,256]{7,6,1,0,2,3,4,5:T(8,128)(2,1)}, bf16[3,3,2,2,2,2,16,256]{7,6,1,0,2,3,4,5:T(8,128)(2,1)S(1)}, u32[]{:S(2)}, u32[]{:S(2)}) collective-permute-start(bf16[3,3,2,2,2,2,16,256]{7,6,1,0,2,3,4,5:T(8,128)(2,1)} %fusion.30), channel_id=1, source_target_pairs={{0,1},{1,0},{2,3},{3,2},{4,5},{5,4},{6,7},{7,6},{8,9},{9,8},{10,11... | collective-permute-start | bytes 3538952 | tf_op jit(solution)/shard_map/ppermute | solution.py:85
  65.7 2.8 %collective-permute-start.5 = (bf16[2,2,2,2,8,512]{5,4,0,1,2,3:T(8,128)(2,1)S(1)}, bf16[2,2,2,2,8,512]{5,4,0,1,2,3:T(8,128)(2,1)S(1)}, u32[]{:S(2)}, u32[]{:S(2)}) collective-permute-start(bf16[2,2,2,2,8,512]{5,4,0,1,2,3:T(8,128)(2,1)S(1)} %fusion.45), channel_id=1, source_target_pairs={{0,1},{1,0},{2,3},{3,2},{4,5},{5,4},{6,7},{7,6},{8,9},{9,8},{10,11... | collective-permute-start | bytes 393224 | tf_op jit(solution)/shard_map/ppermute | solution.py:85
  66.9 13.9 %collective-permute-start.1 = (bf16[3,3,2,2,2,16,256]{6,5,1,0,2,3,4:T(8,128)(2,1)S(1)}, bf16[3,3,2,2,2,16,256]{6,5,1,0,2,3,4:T(8,128)(2,1)S(1)}, u32[]{:S(2)}, u32[]{:S(2)}) collective-permute-start(bf16[3,3,2,2,2,16,256]{6,5,1,0,2,3,4:T(8,128)(2,1)S(1)} %fusion.33), channel_id=1, source_target_pairs={{0,2},{1,9},{2,0},{3,11},{4,6},{5,13},{6,4},{7,15},{8,10},{9,1},{1... | collective-permute-start | bytes 1769480 | tf_op jit(solution)/shard_map/ppermute | solution.py:85
  68.6 9.0 %collective-permute-start.6 = (bf16[2,2,2,8,512]{4,3,0,1,2:T(8,128)(2,1)S(1)}, bf16[2,2,2,8,512]{4,3,0,1,2:T(8,128)(2,1)S(1)}, u32[]{:S(2)}, u32[]{:S(2)}) collective-permute-start(bf16[2,2,2,8,512]{4,3,0,1,2:T(8,128)(2,1)S(1)} %fusion.64), channel_id=1, source_target_pairs={{0,2},{1,9},{2,0},{3,11},{4,6},{5,13},{6,4},{7,15},{8,10},{9,1},{1... | collective-permute-start | bytes 196616 | tf_op jit(solution)/shard_map/ppermute | solution.py:85
  77.6 5.5 %collective-permute-start.7 = (bf16[2,2,8,512]{3,2,0,1:T(8,128)(2,1)S(1)}, bf16[2,2,8,512]{3,2,0,1:T(8,128)(2,1)S(1)}, u32[]{:S(2)}, u32[]{:S(2)}) collective-permute-start(bf16[2,2,8,512]{3,2,0,1:T(8,128)(2,1)S(1)} %fusion.74), channel_id=1, source_target_pairs={{0,4},{1,17},{2,6},{3,19},{4,0},{5,21},{6,2},{7,23},{8,12},{9,25},... | collective-permute-start | bytes 98312 | tf_op jit(solution)/shard_map/ppermute | solution.py:85
  81.1 8.5 %collective-permute-start.2 = (bf16[3,3,2,2,16,256]{5,4,1,0,2,3:T(8,128)(2,1)S(1)}, bf16[3,3,2,2,16,256]{5,4,1,0,2,3:T(8,128)(2,1)S(1)}, u32[]{:S(2)}, u32[]{:S(2)}) collective-permute-start(bf16[3,3,2,2,16,256]{5,4,1,0,2,3:T(8,128)(2,1)S(1)} %fusion.35), channel_id=1, source_target_pairs={{0,4},{1,17},{2,6},{3,19},{4,0},{5,21},{6,2},{7,23},{8,12},{9,25},... | collective-permute-start | bytes 884744 | tf_op jit(solution)/shard_map/ppermute | solution.py:85
  83.1 8.6 %collective-permute-start.8 = (bf16[2,8,512]{2,1,0:T(8,128)(2,1)S(1)}, bf16[2,8,512]{2,1,0:T(8,128)(2,1)S(1)}, u32[]{:S(2)}, u32[]{:S(2)}) collective-permute-start(bf16[2,8,512]{2,1,0:T(8,128)(2,1)S(1)} %fusion.76), channel_id=1, source_target_pairs={{0,8},{1,3},{2,10},{3,1},{4,12},{5,7},{6,14},{7,5},{8,0},{9,11},{1... | collective-permute-start | bytes 49160 | tf_op jit(solution)/shard_map/ppermute | solution.py:85
  89.7 5.7 %collective-permute-start.3 = (bf16[3,3,2,16,256]{4,3,1,0,2:T(8,128)(2,1)S(1)}, bf16[3,3,2,16,256]{4,3,1,0,2:T(8,128)(2,1)S(1)}, u32[]{:S(2)}, u32[]{:S(2)}) collective-permute-start(bf16[3,3,2,16,256]{4,3,1,0,2:T(8,128)(2,1)S(1)} %fusion.43), channel_id=1, source_target_pairs={{0,8},{1,3},{2,10},{3,1},{4,12},{5,7},{6,14},{7,5},{8,0},{9,11},{1... | collective-permute-start | bytes 442376 | tf_op jit(solution)/shard_map/ppermute | solution.py:85
  91.8 7.2 %collective-permute-start.9 = (bf16[8,512]{1,0:T(8,128)(2,1)S(1)}, bf16[8,512]{1,0:T(8,128)(2,1)S(1)}, u32[]{:S(2)}, u32[]{:S(2)}) collective-permute-start(bf16[8,512]{1,0:T(8,128)(2,1)S(1)} %fusion.78), channel_id=1, source_target_pairs={{0,16},{1,5},{2,18},{3,7},{4,20},{5,1},{6,22},{7,3},{8,24},{9,13},... | collective-permute-start | bytes 24584 | tf_op jit(solution)/shard_map/ppermute | solution.py:85
  95.5 5.9 %collective-permute-start.4 = (bf16[3,3,16,256]{3,2,1,0:T(8,128)(2,1)S(1)}, bf16[3,3,16,256]{3,2,1,0:T(8,128)(2,1)S(1)}, u32[]{:S(2)}, u32[]{:S(2)}) collective-permute-start(bf16[3,3,16,256]{3,2,1,0:T(8,128)(2,1)S(1)} %fusion.62), channel_id=1, source_target_pairs={{0,16},{1,5},{2,18},{3,7},{4,20},{5,1},{6,22},{7,3},{8,24},{9,13},... | collective-permute-start | bytes 221192 | tf_op jit(solution)/shard_map/ppermute | solution.py:85
  104.7 13.0 %all-to-all-start.2 = ((f32[32,1,2]{2,1,0:T(1,128)}), f32[32,1,2]{2,1,0:T(1,128)S(1)}, u32[]{:S(2)}, u32[]{:S(2)}) async-start(f32[32,1,2]{2,1,0:T(1,128)} %broadcast_in_dim.19), calls=%async_computation.2 | async-start | bytes 32768 | tf_op jit(solution)/shard_map/all_to_all | solution.py:175
  120.0 5.9 %collective-permute-start.10 = (bf16[3,3,16,256]{3,2,1,0:T(8,128)(2,1)S(1)}, bf16[3,3,16,256]{3,2,1,0:T(8,128)(2,1)S(1)}, u32[]{:S(2)}, u32[]{:S(2)}) collective-permute-start(bf16[3,3,16,256]{3,2,1,0:T(8,128)(2,1)S(1)} %fusion.85), channel_id=1, source_target_pairs={{0,16},{1,5},{2,18},{3,7},{4,20},{5,1},{6,22},{7,3},{8,24},{9,13},... | collective-permute-start | bytes 221192 | tf_op jit(solution)/shard_map/ppermute | solution.py:85
  126.0 5.2 %collective-permute-start.11 = (bf16[3,3,2,16,256]{4,3,2,1,0:T(8,128)(2,1)S(1)}, bf16[3,3,2,16,256]{4,3,2,1,0:T(8,128)(2,1)S(1)}, u32[]{:S(2)}, u32[]{:S(2)}) collective-permute-start(bf16[3,3,2,16,256]{4,3,2,1,0:T(8,128)(2,1)S(1)} %pad_maximum_fusion.5), channel_id=1, source_target_pairs={{0,8},{1,3},{2,10},{3,1},{4,12},{5,7},{6,14},{7,5},{8,0},{9,11},{1... | collective-permute-start | bytes 442376 | tf_op jit(solution)/shard_map/ppermute | solution.py:85
  131.3 8.3 %collective-permute-start.12 = (bf16[3,3,2,2,16,256]{5,4,3,2,1,0:T(8,128)(2,1)S(1)}, bf16[3,3,2,2,16,256]{5,4,3,2,1,0:T(8,128)(2,1)S(1)}, u32[]{:S(2)}, u32[]{:S(2)}) collective-permute-start(bf16[3,3,2,2,16,256]{5,4,3,2,1,0:T(8,128)(2,1)S(1)} %pad_maximum_fusion.3), channel_id=1, source_target_pairs={{0,4},{1,17},{2,6},{3,19},{4,0},{5,21},{6,2},{7,23},{8,12},{9,25},... | collective-permute-start | bytes 884744 | tf_op jit(solution)/shard_map/ppermute | solution.py:85
  133.2 7.3 %collective-permute-start.15 = (bf16[8,512]{1,0:T(8,128)(2,1)S(1)}, bf16[8,512]{1,0:T(8,128)(2,1)S(1)}, u32[]{:S(2)}, u32[]{:S(2)}) collective-permute-start(bf16[8,512]{1,0:T(8,128)(2,1)S(1)} %fusion.84), channel_id=1, source_target_pairs={{0,16},{1,5},{2,18},{3,7},{4,20},{5,1},{6,22},{7,3},{8,24},{9,13},... | collective-permute-start | bytes 24584 | tf_op jit(solution)/shard_map/ppermute | solution.py:85
  139.7 10.1 %collective-permute-start.13 = (bf16[3,3,2,2,2,16,256]{6,5,4,3,2,1,0:T(8,128)(2,1)S(1)}, bf16[3,3,2,2,2,16,256]{6,5,4,3,2,1,0:T(8,128)(2,1)}, u32[]{:S(2)}, u32[]{:S(2)}) collective-permute-start(bf16[3,3,2,2,2,16,256]{6,5,4,3,2,1,0:T(8,128)(2,1)S(1)} %pad_maximum_fusion.2), channel_id=1, source_target_pairs={{0,2},{1,9},{2,0},{3,11},{4,6},{5,13},{6,4},{7,15},{8,10},{9,1},{1... | collective-permute-start | bytes 1769480 | tf_op jit(solution)/shard_map/ppermute | solution.py:85
  140.5 4.0 %collective-permute-start.16 = (bf16[2,8,512]{2,1,0:T(8,128)(2,1)S(1)}, bf16[2,8,512]{2,1,0:T(8,128)(2,1)S(1)}, u32[]{:S(2)}, u32[]{:S(2)}) collective-permute-start(bf16[2,8,512]{2,1,0:T(8,128)(2,1)S(1)} %pad_maximum_fusion.9), channel_id=1, source_target_pairs={{0,8},{1,3},{2,10},{3,1},{4,12},{5,7},{6,14},{7,5},{8,0},{9,11},{1... | collective-permute-start | bytes 49160 | tf_op jit(solution)/shard_map/ppermute | solution.py:85
  144.6 7.9 %collective-permute-start.17 = (bf16[2,2,8,512]{3,2,1,0:T(8,128)(2,1)S(1)}, bf16[2,2,8,512]{3,2,1,0:T(8,128)(2,1)S(1)}, u32[]{:S(2)}, u32[]{:S(2)}) collective-permute-start(bf16[2,2,8,512]{3,2,1,0:T(8,128)(2,1)S(1)} %pad_maximum_fusion.8), channel_id=1, source_target_pairs={{0,4},{1,17},{2,6},{3,19},{4,0},{5,21},{6,2},{7,23},{8,12},{9,25},... | collective-permute-start | bytes 98312 | tf_op jit(solution)/shard_map/ppermute | solution.py:85
  152.4 6.1 %collective-permute-start.14 = (bf16[3,3,2,2,2,2,16,256]{7,6,5,4,3,2,1,0:T(8,128)(2,1)}, bf16[3,3,2,2,2,2,16,256]{7,6,5,4,3,2,1,0:T(8,128)(2,1)}, u32[]{:S(2)}, u32[]{:S(2)}) collective-permute-start(bf16[3,3,2,2,2,2,16,256]{7,6,5,4,3,2,1,0:T(8,128)(2,1)} %copy_select_fusion.2), channel_id=1, source_target_pairs={{0,1},{1,0},{2,3},{3,2},{4,5},{5,4},{6,7},{7,6},{8,9},{9,8},{10,11... | collective-permute-start | bytes 3538952 | tf_op jit(solution)/shard_map/ppermute | solution.py:85
  152.5 4.3 %collective-permute-start.18 = (bf16[2,2,2,8,512]{4,3,2,1,0:T(8,128)(2,1)S(1)}, bf16[2,2,2,8,512]{4,3,2,1,0:T(8,128)(2,1)S(1)}, u32[]{:S(2)}, u32[]{:S(2)}) collective-permute-start(bf16[2,2,2,8,512]{4,3,2,1,0:T(8,128)(2,1)S(1)} %pad_maximum_fusion.7), channel_id=1, source_target_pairs={{0,2},{1,9},{2,0},{3,11},{4,6},{5,13},{6,4},{7,15},{8,10},{9,1},{1... | collective-permute-start | bytes 196616 | tf_op jit(solution)/shard_map/ppermute | solution.py:85
  187.9 3.5 %collective-permute-start.20 = (bf16[3,3,2,2,2,2,16,256]{7,6,1,0,2,3,4,5:T(8,128)(2,1)S(1)}, bf16[3,3,2,2,2,2,16,256]{7,6,1,0,2,3,4,5:T(8,128)(2,1)S(1)}, u32[]{:S(2)}, u32[]{:S(2)}) collective-permute-start(bf16[3,3,2,2,2,2,16,256]{7,6,1,0,2,3,4,5:T(8,128)(2,1)S(1)} %fusion.31), channel_id=1, source_target_pairs={{0,1},{1,0},{2,3},{3,2},{4,5},{5,4},{6,7},{7,6},{8,9},{9,8},{10,11... | collective-permute-start | bytes 3538952 | tf_op jit(solution)/shard_map/ppermute | solution.py:85
  192.0 12.0 %collective-permute-start.21 = (bf16[3,3,2,2,2,16,256]{6,5,1,0,2,3,4:T(8,128)(2,1)S(1)}, bf16[3,3,2,2,2,16,256]{6,5,1,0,2,3,4:T(8,128)(2,1)S(1)}, u32[]{:S(2)}, u32[]{:S(2)}) collective-permute-start(bf16[3,3,2,2,2,16,256]{6,5,1,0,2,3,4:T(8,128)(2,1)S(1)} %fusion.34), channel_id=1, source_target_pairs={{0,2},{1,9},{2,0},{3,11},{4,6},{5,13},{6,4},{7,15},{8,10},{9,1},{1... | collective-permute-start | bytes 1769480 | tf_op jit(solution)/shard_map/ppermute | solution.py:85
  192.9 9.7 %collective-permute-start.26 = (bf16[2,2,2,8,512]{4,3,0,1,2:T(8,128)(2,1)S(1)}, bf16[2,2,2,8,512]{4,3,0,1,2:T(8,128)(2,1)S(1)}, u32[]{:S(2)}, u32[]{:S(2)}) collective-permute-start(bf16[2,2,2,8,512]{4,3,0,1,2:T(8,128)(2,1)S(1)} %fusion.65), channel_id=1, source_target_pairs={{0,2},{1,9},{2,0},{3,11},{4,6},{5,13},{6,4},{7,15},{8,10},{9,1},{1... | collective-permute-start | bytes 196616 | tf_op jit(solution)/shard_map/ppermute | solution.py:85
  202.7 5.5 %collective-permute-start.27 = (bf16[2,2,8,512]{3,2,0,1:T(8,128)(2,1)S(1)}, bf16[2,2,8,512]{3,2,0,1:T(8,128)(2,1)S(1)}, u32[]{:S(2)}, u32[]{:S(2)}) collective-permute-start(bf16[2,2,8,512]{3,2,0,1:T(8,128)(2,1)S(1)} %fusion.75), channel_id=1, source_target_pairs={{0,4},{1,17},{2,6},{3,19},{4,0},{5,21},{6,2},{7,23},{8,12},{9,25},... | collective-permute-start | bytes 98312 | tf_op jit(solution)/shard_map/ppermute | solution.py:85
  204.3 8.5 %collective-permute-start.22 = (bf16[3,3,2,2,16,256]{5,4,1,0,2,3:T(8,128)(2,1)S(1)}, bf16[3,3,2,2,16,256]{5,4,1,0,2,3:T(8,128)(2,1)S(1)}, u32[]{:S(2)}, u32[]{:S(2)}) collective-permute-start(bf16[3,3,2,2,16,256]{5,4,1,0,2,3:T(8,128)(2,1)S(1)} %fusion.36), channel_id=1, source_target_pairs={{0,4},{1,17},{2,6},{3,19},{4,0},{5,21},{6,2},{7,23},{8,12},{9,25},... | collective-permute-start | bytes 884744 | tf_op jit(solution)/shard_map/ppermute | solution.py:85
  208.3 5.3 %collective-permute-start.28 = (bf16[2,8,512]{2,1,0:T(8,128)(2,1)S(1)}, bf16[2,8,512]{2,1,0:T(8,128)(2,1)S(1)}, u32[]{:S(2)}, u32[]{:S(2)}) collective-permute-start(bf16[2,8,512]{2,1,0:T(8,128)(2,1)S(1)} %fusion.77), channel_id=1, source_target_pairs={{0,8},{1,3},{2,10},{3,1},{4,12},{5,7},{6,14},{7,5},{8,0},{9,11},{1... | collective-permute-start | bytes 49160 | tf_op jit(solution)/shard_map/ppermute | solution.py:85
  212.9 5.2 %collective-permute-start.23 = (bf16[3,3,2,16,256]{4,3,1,0,2:T(8,128)(2,1)S(1)}, bf16[3,3,2,16,256]{4,3,1,0,2:T(8,128)(2,1)S(1)}, u32[]{:S(2)}, u32[]{:S(2)}) collective-permute-start(bf16[3,3,2,16,256]{4,3,1,0,2:T(8,128)(2,1)S(1)} %fusion.44), channel_id=1, source_target_pairs={{0,8},{1,3},{2,10},{3,1},{4,12},{5,7},{6,14},{7,5},{8,0},{9,11},{1... | collective-permute-start | bytes 442376 | tf_op jit(solution)/shard_map/ppermute | solution.py:85
  213.6 5.9 %collective-permute-start.29 = (bf16[8,512]{1,0:T(8,128)(2,1)S(1)}, bf16[8,512]{1,0:T(8,128)(2,1)S(1)}, u32[]{:S(2)}, u32[]{:S(2)}) collective-permute-start(bf16[8,512]{1,0:T(8,128)(2,1)S(1)} %fusion.79), channel_id=1, source_target_pairs={{0,16},{1,5},{2,18},{3,7},{4,20},{5,1},{6,22},{7,3},{8,24},{9,13},... | collective-permute-start | bytes 24584 | tf_op jit(solution)/shard_map/ppermute | solution.py:85
  218.2 5.9 %collective-permute-start.24 = (bf16[3,3,16,256]{3,2,1,0:T(8,128)(2,1)S(1)}, bf16[3,3,16,256]{3,2,1,0:T(8,128)(2,1)S(1)}, u32[]{:S(2)}, u32[]{:S(2)}) collective-permute-start(bf16[3,3,16,256]{3,2,1,0:T(8,128)(2,1)S(1)} %fusion.63), channel_id=1, source_target_pairs={{0,16},{1,5},{2,18},{3,7},{4,20},{5,1},{6,22},{7,3},{8,24},{9,13},... | collective-permute-start | bytes 221192 | tf_op jit(solution)/shard_map/ppermute | solution.py:85
  227.4 11.8 %all-to-all-start.3 = ((f32[32,1,2]{2,1,0:T(1,128)}), f32[32,1,2]{2,1,0:T(1,128)S(1)}, u32[]{:S(2)}, u32[]{:S(2)}) async-start(f32[32,1,2]{2,1,0:T(1,128)} %broadcast_in_dim.20), calls=%async_computation.3 | async-start | bytes 32768 | tf_op jit(solution)/shard_map/all_to_all | solution.py:175
  (36 other events, 307.2 us)

commit v9 on v8

--- a/solution.py
+++ b/solution.py
@@ -178,8 +178,8 @@
         up_own = up_own - scale * grad_up
         collected.append(totals[1] / (count * cells))
         if update_round + 1 < TRAIN_STEPS:
-            down_low = down_own.astype(jnp.bfloat16)
-            upper_low = up_own.astype(jnp.bfloat16)
+            down_low = grad_down.astype(jnp.bfloat16)
+            upper_low = grad_up.astype(jnp.bfloat16)
             for step_index in range(levels):
                 stage = levels - 1 - step_index
                 if stage == 0:
@@ -190,8 +190,10 @@
                 bit = jnp.where(second_core, bits_of[1], bits_of[0])
                 down_low = double_join(down_low, 2 + step_index, bit, pairs, place)
                 upper_low = double_join(upper_low, step_index, bit, pairs, place)
-            down_low = down_low.reshape(down_w.shape[1:])
-            upper_low = upper_low.reshape(up_w.shape[1:])
+            down_low = down_low.reshape(down_w.shape[1:]).astype(jnp.float32)
+            upper_low = upper_low.reshape(up_w.shape[1:]).astype(jnp.float32)
+            down_low = (down_w[0] - scale * down_low).astype(jnp.bfloat16)
+            upper_low = (up_w[0] - scale * upper_low).astype(jnp.bfloat16)
     return (down_own[None], up_own[None], jnp.stack(collected)[None])
 
 

time: 250 us -> 260 us (1.040)
  other arithmetic: 25.6 us -> 36 us
    convert_element_type x2 -> x3, other arithmetic: 1.67 us -> 4.46 us  [the longest x1 3.65 us: shards(): down_low = (down_w[0] - scale * down_low).astype(jnp.bfloat16)]
    unnamed x70 -> x92, local copies, waits for them, and re-layouts: 14.1 us -> 15.2 us
  transfers between devices with their start and end apart: 34 -> 34, of which waited for: 20 -> 22; matrix products, arithmetic and copies ran while one was open for 9% -> 12% of each run, Pallas kernels for 0% -> 0%
where the time goes in v9:
time: 260 us; the launch traced here: 256 us
  waiting for transfers between devices  90.3 us (35%)
  starting transfers between devices  55.8 us (21%)
  other arithmetic  36 us (14%)
  matrix products  35.9 us (14%)
  local copies, waits for them, and re-layouts  29.5 us (11%)
  between operations  8.03 us (3%)
    ppermute x30, waiting for transfers between devices, partner_swap(): return lax.ppermute(value, 'ex', perm=pairs)  61.8 us
    ppermute x30, starting transfers between devices, partner_swap(): return lax.ppermute(value, 'ex', perm=pairs)  37 us
    dot_general x20, matrix products, contract_rows(): lax.dot_general(left, right, (((0,), (0,)), ((), ())), preferred_element_...  16.5 us
    all_to_all x1, waiting for transfers between devices, shards(): lax.all_to_all(send_feats, 'task', split_axis=0, concat_axis=0, tiled=True)  15.3 us
    unnamed x92, local copies, waits for them, and re-layouts  15.2 us
    all_to_all x2, waiting for transfers between devices, shards(): totals = jnp.sum(lax.all_to_all(spread, 'ex', 0, 0, tiled=True), axis=0)  12.2 us
    all_to_all x2, starting transfers between devices, shards(): totals = jnp.sum(lax.all_to_all(spread, 'ex', 0, 0, tiled=True), axis=0)  10.6 us
    dot_general x18, matrix products, train_pass(): jnp.dot(windows[offset_index], down_low[offset_index // 3, offset_index %...  10.2 us
  transfers between devices with their start and end apart: 34, of which 22 were waited for; matrix products, arithmetic and copies ran while one was open for 12% of the time, Pallas kernels for 0%

profile of v9, /device:TPU:0, one launch (start us, length us, event | category | flops | bytes accessed | tf_op | source)
XLA Modules:
  0.0 255.5 jit_solution(2516930391505883595)
XLA Ops:
  4.8 4.4 %all-to-all-start.1 = ((bf16[4,2,192]{2,1,0:T(2,128)(2,1)}), bf16[4,2,192]{2,1,0:T(2,128)(2,1)S(1)}, u32[]{:S(2)}, u32[]{:S(2)}) async-start(bf16[4,2,192]{2,1,0:T(2,128)(2,1)} %reshape.196), calls=%async_computation.1 | async-start | bytes 8192 | tf_op jit(solution)/shard_map/all_to_all | solution.py:138
  10.5 2.9 %scatter_fusion = bf16[4,6,8,8,512]{4,3,2,1,0:T(8,128)(2,1)} fusion(bf16[4,6,8,8,512]{4,3,2,1,0:T(8,128)(2,1)} %broadcast_in_dim.16, s32[12]{0:T(128)S(1)} %fusion.87, bf16[12,8,8,512]{3,2,1,0:T(8,128)(2,1)S(1)} %copy-done.28), kind=kCustom, calls=%fused_computation | custom fusion | bytes 2359392 | tf_op jit(solution)/shard_map/scatter | solution.py:129
  14.5 3.7 %all-to-all-start = ((bf16[4,6,8,8,512]{4,3,2,1,0:T(8,128)(2,1)}), bf16[4,6,8,8,512]{4,3,2,1,0:T(8,128)(2,1)S(1)}, u32[]{:S(2)}, u32[]{:S(2)}) async-start(bf16[4,6,8,8,512]{4,3,2,1,0:T(8,128)(2,1)} %scatter_fusion), calls=%async_computation | async-start | bytes 3145728 | tf_op jit(solution)/shard_map/all_to_all | solution.py:137
  18.9 4.0 %bitcast_convert_fusion = bf16[3,3,512,256]{3,2,1,0:T(8,128)(2,1)} fusion(f32[1,3,3,512,256]{4,3,2,1,0:T(8,128)} %param.11), kind=kLoop, calls=%fused_computation.12 | loop fusion | flops 1179648 | bytes 7077888 | tf_op jit(solution)/shard_map/convert_element_type | solution.py:149
  23.1 15.3 %all-to-all-done = bf16[4,6,8,8,512]{4,3,2,1,0:T(8,128)(2,1)S(1)} async-done(((bf16[4,6,8,8,512]{4,3,2,1,0:T(8,128)(2,1)}), bf16[4,6,8,8,512]{4,3,2,1,0:T(8,128)(2,1)S(1)}, u32[]{:S(2)}, u32[]{:S(2)}) %all-to-all-start) | async-done | bytes 1572896 | tf_op jit(solution)/shard_map/all_to_all | solution.py:137
  39.1 2.6 %pad_slice_fusion = (bf16[24,8,8,512]{3,2,1,0:T(8,128)(2,1)S(1)}, bf16[24,8,8,512]{3,2,1,0:T(8,128)(2,1)S(1)}, bf16[24,8,8,512]{3,2,1,0:T(8,128)(2,1)S(1)}, bf16...) fusion(bf16[24,8,8,512]{3,2,1,0:T(8,128)(2,1)S(1)} %bitcast.480), kind=kLoop, calls=%fused_computation.2 | loop fusion | bytes 14155776 | tf_op jit(solution)/shard_map/slice | solution.py:19
  63.7 2.5 fusion.88
  66.8 3.1 %copy_select_fusion.1 = f32[3,3,2,2,2,2,16,256]{7,6,1,0,2,3,4,5:T(8,128)S(1)} fusion(bf16[3,3,2,2,2,2,16,256]{7,6,1,0,2,3,4,5:T(8,128)(2,1)S(1)} %collective-permute-done, pred[]{:T(512)S(6)} %eq.26, f32[3,3,2,2,2,2,2,16,256]{8,7,6,5,4,3,2,1,0:T(8,128)} %bitcast.522, s32[]{:T(128)S(6)} %select_n.279), kind=kLoop, calls=%fused_computation.53 | loop fusion | flops 2949120 | bytes 9438720 | tf_op jit(solution)/shard_map/jit(_where)/select_n | solution.py:165
  73.6 8.4 %collective-permute-done.6 = bf16[2,2,2,8,512]{4,3,0,1,2:T(8,128)(2,1)S(1)} collective-permute-done((bf16[2,2,2,8,512]{4,3,0,1,2:T(8,128)(2,1)S(1)}, bf16[2,2,2,8,512]{4,3,0,1,2:T(8,128)(2,1)S(1)}, u32[]{:S(2)}, u32[]{:S(2)}) %collective-permute-start.6) | collective-permute-done | bytes 65568 | tf_op jit(solution)/shard_map/ppermute | solution.py:85
  82.1 3.3 %collective-permute-start.7 = (bf16[2,2,8,512]{3,2,0,1:T(8,128)(2,1)S(1)}, bf16[2,2,8,512]{3,2,0,1:T(8,128)(2,1)S(1)}, u32[]{:S(2)}, u32[]{:S(2)}) collective-permute-start(bf16[2,2,8,512]{3,2,0,1:T(8,128)(2,1)S(1)} %fusion.75), channel_id=1, source_target_pairs={{0,4},{1,17},{2,6},{3,19},{4,0},{5,21},{6,2},{7,23},{8,12},{9,25},... | collective-permute-start | bytes 98312 | tf_op jit(solution)/shard_map/ppermute | solution.py:85
  89.6 5.6 %collective-permute-done.2 = bf16[3,3,2,2,16,256]{5,4,1,0,2,3:T(8,128)(2,1)S(1)} collective-permute-done((bf16[3,3,2,2,16,256]{5,4,1,0,2,3:T(8,128)(2,1)S(1)}, bf16[3,3,2,2,16,256]{5,4,1,0,2,3:T(8,128)(2,1)S(1)}, u32[]{:S(2)}, u32[]{:S(2)}) %collective-permute-start.2) | collective-permute-done | bytes 294944 | tf_op jit(solution)/shard_map/ppermute | solution.py:85
  97.4 3.2 %collective-permute-done.3 = bf16[3,3,2,16,256]{4,3,1,0,2:T(8,128)(2,1)S(1)} collective-permute-done((bf16[3,3,2,16,256]{4,3,1,0,2:T(8,128)(2,1)S(1)}, bf16[3,3,2,16,256]{4,3,1,0,2:T(8,128)(2,1)S(1)}, u32[]{:S(2)}, u32[]{:S(2)}) %collective-permute-start.3) | collective-permute-done | bytes 147488 | tf_op jit(solution)/shard_map/ppermute | solution.py:85
  100.7 4.0 %collective-permute-start.4 = (bf16[3,3,16,256]{3,2,1,0:T(8,128)(2,1)S(1)}, bf16[3,3,16,256]{3,2,1,0:T(8,128)(2,1)S(1)}, u32[]{:S(2)}, u32[]{:S(2)}) collective-permute-start(bf16[3,3,16,256]{3,2,1,0:T(8,128)(2,1)S(1)} %fusion.62), channel_id=1, source_target_pairs={{0,16},{1,5},{2,18},{3,7},{4,20},{5,1},{6,22},{7,3},{8,24},{9,13},... | collective-permute-start | bytes 221192 | tf_op jit(solution)/shard_map/ppermute | solution.py:85
  104.8 2.2 collective-permute-done.4
  107.7 3.5 %collective-permute-start.10 = (bf16[3,3,16,256]{3,2,1,0:T(8,128)(2,1)S(1)}, bf16[3,3,16,256]{3,2,1,0:T(8,128)(2,1)S(1)}, u32[]{:S(2)}, u32[]{:S(2)}) collective-permute-start(bf16[3,3,16,256]{3,2,1,0:T(8,128)(2,1)S(1)} %get-tuple-element.21), channel_id=1, source_target_pairs={{0,16},{1,5},{2,18},{3,7},{4,20},{5,1},{6,22},{7,3},{8,24},{9,13},... | collective-permute-start | bytes 221192 | tf_op jit(solution)/shard_map/ppermute | solution.py:85
  117.0 3.1 %collective-permute-done.11 = bf16[3,3,2,16,256]{4,3,2,1,0:T(8,128)(2,1)S(1)} collective-permute-done((bf16[3,3,2,16,256]{4,3,2,1,0:T(8,128)(2,1)S(1)}, bf16[3,3,2,16,256]{4,3,2,1,0:T(8,128)(2,1)S(1)}, u32[]{:S(2)}, u32[]{:S(2)}) %collective-permute-start.11) | collective-permute-done | bytes 147488 | tf_op jit(solution)/shard_map/ppermute | solution.py:85
  124.3 4.1 %collective-permute-done.12 = bf16[3,3,2,2,16,256]{5,4,3,2,1,0:T(8,128)(2,1)S(1)} collective-permute-done((bf16[3,3,2,2,16,256]{5,4,3,2,1,0:T(8,128)(2,1)S(1)}, bf16[3,3,2,2,16,256]{5,4,3,2,1,0:T(8,128)(2,1)S(1)}, u32[]{:S(2)}, u32[]{:S(2)}) %collective-permute-start.12) | collective-permute-done | bytes 294944 | tf_op jit(solution)/shard_map/ppermute | solution.py:85
  129.7 2.6 %collective-permute-start.17 = (bf16[2,2,8,512]{3,2,1,0:T(8,128)(2,1)S(1)}, bf16[2,2,8,512]{3,2,1,0:T(8,128)(2,1)S(1)}, u32[]{:S(2)}, u32[]{:S(2)}) collective-permute-start(bf16[2,2,8,512]{3,2,1,0:T(8,128)(2,1)S(1)} %pad_maximum_fusion.6), channel_id=1, source_target_pairs={{0,4},{1,17},{2,6},{3,19},{4,0},{5,21},{6,2},{7,23},{8,12},{9,25},... | collective-permute-start | bytes 98312 | tf_op jit(solution)/shard_map/ppermute | solution.py:85
  132.4 8.1 %collective-permute-done.17 = bf16[2,2,8,512]{3,2,1,0:T(8,128)(2,1)S(1)} collective-permute-done((bf16[2,2,8,512]{3,2,1,0:T(8,128)(2,1)S(1)}, bf16[2,2,8,512]{3,2,1,0:T(8,128)(2,1)S(1)}, u32[]{:S(2)}, u32[]{:S(2)}) %collective-permute-start.17) | collective-permute-done | bytes 32800 | tf_op jit(solution)/shard_map/ppermute | solution.py:85
  148.8 6.1 %all-to-all-start.2 = ((f32[32,1,2]{2,1,0:T(1,128)}), f32[32,1,2]{2,1,0:T(1,128)}, u32[]{:S(2)}, u32[]{:S(2)}) async-start(f32[32,1,2]{2,1,0:T(1,128)} %broadcast_in_dim.19), calls=%async_computation.2 | async-start | bytes 32768 | tf_op jit(solution)/shard_map/all_to_all | solution.py:175
  156.6 5.5 %all-to-all-done.2 = f32[32,1,2]{2,1,0:T(1,128)} async-done(((f32[32,1,2]{2,1,0:T(1,128)}), f32[32,1,2]{2,1,0:T(1,128)}, u32[]{:S(2)}, u32[]{:S(2)}) %all-to-all-start.2) | async-done | bytes 288 | tf_op jit(solution)/shard_map/all_to_all | solution.py:175
  165.2 2.2 select_bitcast_fusion.1
  168.3 3.6 %fusion = bf16[3,3,512,256]{3,2,1,0:T(8,128)(2,1)S(1)} fusion(f32[3,3,2,2,2,2,2,16,256]{8,7,6,5,4,3,2,1,0:T(8,128)S(1)} %convert_multiply_fusion, f32[1,3,3,512,256]{4,3,2,1,0:T(8,128)} %param.11), kind=kLoop, calls=%fused_computation.11 | loop fusion | flops 2359296 | bytes 11796480 | tf_op jit(solution)/shard_map/convert_element_type | solution.py:195
  198.9 2.2 fusion.89
  205.3 7.8 %collective-permute-done.26 = bf16[2,2,2,8,512]{4,3,0,1,2:T(8,128)(2,1)S(1)} collective-permute-done((bf16[2,2,2,8,512]{4,3,0,1,2:T(8,128)(2,1)S(1)}, bf16[2,2,2,8,512]{4,3,0,1,2:T(8,128)(2,1)S(1)}, u32[]{:S(2)}, u32[]{:S(2)}) %collective-permute-start.26) | collective-permute-done | bytes 65568 | tf_op jit(solution)/shard_map/ppermute | solution.py:85
  214.8 2.3 collective-permute-start.22
  219.5 3.7 %collective-permute-done.22 = bf16[3,3,2,2,16,256]{5,4,1,0,2,3:T(8,128)(2,1)S(1)} collective-permute-done((bf16[3,3,2,2,16,256]{5,4,1,0,2,3:T(8,128)(2,1)S(1)}, bf16[3,3,2,2,16,256]{5,4,1,0,2,3:T(8,128)(2,1)S(1)}, u32[]{:S(2)}, u32[]{:S(2)}) %collective-permute-start.22) | collective-permute-done | bytes 294944 | tf_op jit(solution)/shard_map/ppermute | solution.py:85
  224.0 2.2 collective-permute-start.29
  226.2 2.4 collective-permute-done.23
  230.5 4.2 %collective-permute-done.24 = bf16[3,3,16,256]{3,2,1,0:T(8,128)(2,1)S(1)} collective-permute-done((bf16[3,3,16,256]{3,2,1,0:T(8,128)(2,1)S(1)}, bf16[3,3,16,256]{3,2,1,0:T(8,128)(2,1)S(1)}, u32[]{:S(2)}, u32[]{:S(2)}) %collective-permute-start.24) | collective-permute-done | bytes 73760 | tf_op jit(solution)/shard_map/ppermute | solution.py:85
  237.9 4.5 %all-to-all-start.3 = ((f32[32,1,2]{2,1,0:T(1,128)}), f32[32,1,2]{2,1,0:T(1,128)S(1)}, u32[]{:S(2)}, u32[]{:S(2)}) async-start(f32[32,1,2]{2,1,0:T(1,128)} %broadcast_in_dim.20), calls=%async_computation.3 | async-start | bytes 32768 | tf_op jit(solution)/shard_map/all_to_all | solution.py:175
  243.1 6.7 %all-to-all-done.3 = f32[32,1,2]{2,1,0:T(1,128)S(1)} async-done(((f32[32,1,2]{2,1,0:T(1,128)}), f32[32,1,2]{2,1,0:T(1,128)S(1)}, u32[]{:S(2)}, u32[]{:S(2)}) %all-to-all-start.3) | async-done | bytes 288 | tf_op jit(solution)/shard_map/all_to_all | solution.py:175
  (274 shorter events, 107.3 us)
Async XLA Ops:
  4.8 9.7 %all-to-all-start.1 = ((bf16[4,2,192]{2,1,0:T(2,128)(2,1)}), bf16[4,2,192]{2,1,0:T(2,128)(2,1)S(1)}, u32[]{:S(2)}, u32[]{:S(2)}) async-start(bf16[4,2,192]{2,1,0:T(2,128)(2,1)} %reshape.196), calls=%async_computation.1 | async-start | bytes 8192 | tf_op jit(solution)/shard_map/all_to_all | solution.py:138
  14.5 23.9 %all-to-all-start = ((bf16[4,6,8,8,512]{4,3,2,1,0:T(8,128)(2,1)}), bf16[4,6,8,8,512]{4,3,2,1,0:T(8,128)(2,1)S(1)}, u32[]{:S(2)}, u32[]{:S(2)}) async-start(bf16[4,6,8,8,512]{4,3,2,1,0:T(8,128)(2,1)} %scatter_fusion), calls=%async_computation | async-start | bytes 3145728 | tf_op jit(solution)/shard_map/all_to_all | solution.py:137
  63.7 3.1 %collective-permute-start = (bf16[3,3,2,2,2,2,16,256]{7,6,1,0,2,3,4,5:T(8,128)(2,1)}, bf16[3,3,2,2,2,2,16,256]{7,6,1,0,2,3,4,5:T(8,128)(2,1)S(1)}, u32[]{:S(2)}, u32[]{:S(2)}) collective-permute-start(bf16[3,3,2,2,2,2,16,256]{7,6,1,0,2,3,4,5:T(8,128)(2,1)} %fusion.31), channel_id=1, source_target_pairs={{0,1},{1,0},{2,3},{3,2},{4,5},{5,4},{6,7},{7,6},{8,9},{9,8},{10,11... | collective-permute-start | bytes 3538952 | tf_op jit(solution)/shard_map/ppermute | solution.py:85
  66.2 6.8 %collective-permute-start.5 = (bf16[2,2,2,2,8,512]{5,4,0,1,2,3:T(8,128)(2,1)S(1)}, bf16[2,2,2,2,8,512]{5,4,0,1,2,3:T(8,128)(2,1)S(1)}, u32[]{:S(2)}, u32[]{:S(2)}) collective-permute-start(bf16[2,2,2,2,8,512]{5,4,0,1,2,3:T(8,128)(2,1)S(1)} %fusion.47), channel_id=1, source_target_pairs={{0,1},{1,0},{2,3},{3,2},{4,5},{5,4},{6,7},{7,6},{8,9},{9,8},{10,11... | collective-permute-start | bytes 393224 | tf_op jit(solution)/shard_map/ppermute | solution.py:85
  71.4 14.0 %collective-permute-start.1 = (bf16[3,3,2,2,2,16,256]{6,5,1,0,2,3,4:T(8,128)(2,1)S(1)}, bf16[3,3,2,2,2,16,256]{6,5,1,0,2,3,4:T(8,128)(2,1)S(1)}, u32[]{:S(2)}, u32[]{:S(2)}) collective-permute-start(bf16[3,3,2,2,2,16,256]{6,5,1,0,2,3,4:T(8,128)(2,1)S(1)} %fusion.34), channel_id=1, source_target_pairs={{0,2},{1,9},{2,0},{3,11},{4,6},{5,13},{6,4},{7,15},{8,10},{9,1},{1... | collective-permute-start | bytes 1769480 | tf_op jit(solution)/shard_map/ppermute | solution.py:85
  73.1 8.9 %collective-permute-start.6 = (bf16[2,2,2,8,512]{4,3,0,1,2:T(8,128)(2,1)S(1)}, bf16[2,2,2,8,512]{4,3,0,1,2:T(8,128)(2,1)S(1)}, u32[]{:S(2)}, u32[]{:S(2)}) collective-permute-start(bf16[2,2,2,8,512]{4,3,0,1,2:T(8,128)(2,1)S(1)} %fusion.64), channel_id=1, source_target_pairs={{0,2},{1,9},{2,0},{3,11},{4,6},{5,13},{6,4},{7,15},{8,10},{9,1},{1... | collective-permute-start | bytes 196616 | tf_op jit(solution)/shard_map/ppermute | solution.py:85
  82.1 5.5 %collective-permute-start.7 = (bf16[2,2,8,512]{3,2,0,1:T(8,128)(2,1)S(1)}, bf16[2,2,8,512]{3,2,0,1:T(8,128)(2,1)S(1)}, u32[]{:S(2)}, u32[]{:S(2)}) collective-permute-start(bf16[2,2,8,512]{3,2,0,1:T(8,128)(2,1)S(1)} %fusion.75), channel_id=1, source_target_pairs={{0,4},{1,17},{2,6},{3,19},{4,0},{5,21},{6,2},{7,23},{8,12},{9,25},... | collective-permute-start | bytes 98312 | tf_op jit(solution)/shard_map/ppermute | solution.py:85
  86.9 8.3 %collective-permute-start.2 = (bf16[3,3,2,2,16,256]{5,4,1,0,2,3:T(8,128)(2,1)S(1)}, bf16[3,3,2,2,16,256]{5,4,1,0,2,3:T(8,128)(2,1)S(1)}, u32[]{:S(2)}, u32[]{:S(2)}) collective-permute-start(bf16[3,3,2,2,16,256]{5,4,1,0,2,3:T(8,128)(2,1)S(1)} %fusion.37), channel_id=1, source_target_pairs={{0,4},{1,17},{2,6},{3,19},{4,0},{5,21},{6,2},{7,23},{8,12},{9,25},... | collective-permute-start | bytes 884744 | tf_op jit(solution)/shard_map/ppermute | solution.py:85
  87.6 9.7 %collective-permute-start.8 = (bf16[2,8,512]{2,1,0:T(8,128)(2,1)S(1)}, bf16[2,8,512]{2,1,0:T(8,128)(2,1)S(1)}, u32[]{:S(2)}, u32[]{:S(2)}) collective-permute-start(bf16[2,8,512]{2,1,0:T(8,128)(2,1)S(1)} %fusion.77), channel_id=1, source_target_pairs={{0,8},{1,3},{2,10},{3,1},{4,12},{5,7},{6,14},{7,5},{8,0},{9,11},{1... | collective-permute-start | bytes 49160 | tf_op jit(solution)/shard_map/ppermute | solution.py:85
  95.3 5.2 %collective-permute-start.3 = (bf16[3,3,2,16,256]{4,3,1,0,2:T(8,128)(2,1)S(1)}, bf16[3,3,2,16,256]{4,3,1,0,2:T(8,128)(2,1)S(1)}, u32[]{:S(2)}, u32[]{:S(2)}) collective-permute-start(bf16[3,3,2,16,256]{4,3,1,0,2:T(8,128)(2,1)S(1)} %fusion.43), channel_id=1, source_target_pairs={{0,8},{1,3},{2,10},{3,1},{4,12},{5,7},{6,14},{7,5},{8,0},{9,11},{1... | collective-permute-start | bytes 442376 | tf_op jit(solution)/shard_map/ppermute | solution.py:85
  100.7 6.3 %collective-permute-start.4 = (bf16[3,3,16,256]{3,2,1,0:T(8,128)(2,1)S(1)}, bf16[3,3,16,256]{3,2,1,0:T(8,128)(2,1)S(1)}, u32[]{:S(2)}, u32[]{:S(2)}) collective-permute-start(bf16[3,3,16,256]{3,2,1,0:T(8,128)(2,1)S(1)} %fusion.62), channel_id=1, source_target_pairs={{0,16},{1,5},{2,18},{3,7},{4,20},{5,1},{6,22},{7,3},{8,24},{9,13},... | collective-permute-start | bytes 221192 | tf_op jit(solution)/shard_map/ppermute | solution.py:85
  104.7 6.6 %collective-permute-start.9 = (bf16[8,512]{1,0:T(8,128)(2,1)S(1)}, bf16[8,512]{1,0:T(8,128)(2,1)S(1)}, u32[]{:S(2)}, u32[]{:S(2)}) collective-permute-start(bf16[8,512]{1,0:T(8,128)(2,1)S(1)} %fusion.81), channel_id=1, source_target_pairs={{0,16},{1,5},{2,18},{3,7},{4,20},{5,1},{6,22},{7,3},{8,24},{9,13},... | collective-permute-start | bytes 24584 | tf_op jit(solution)/shard_map/ppermute | solution.py:85
  107.7 5.9 %collective-permute-start.10 = (bf16[3,3,16,256]{3,2,1,0:T(8,128)(2,1)S(1)}, bf16[3,3,16,256]{3,2,1,0:T(8,128)(2,1)S(1)}, u32[]{:S(2)}, u32[]{:S(2)}) collective-permute-start(bf16[3,3,16,256]{3,2,1,0:T(8,128)(2,1)S(1)} %get-tuple-element.21), channel_id=1, source_target_pairs={{0,16},{1,5},{2,18},{3,7},{4,20},{5,1},{6,22},{7,3},{8,24},{9,13},... | collective-permute-start | bytes 221192 | tf_op jit(solution)/shard_map/ppermute | solution.py:85
  111.8 5.2 %collective-permute-start.15 = (bf16[8,512]{1,0:T(8,128)(2,1)S(1)}, bf16[8,512]{1,0:T(8,128)(2,1)S(1)}, u32[]{:S(2)}, u32[]{:S(2)}) collective-permute-start(bf16[8,512]{1,0:T(8,128)(2,1)S(1)} %get-tuple-element.34), channel_id=1, source_target_pairs={{0,16},{1,5},{2,18},{3,7},{4,20},{5,1},{6,22},{7,3},{8,24},{9,13},... | collective-permute-start | bytes 24584 | tf_op jit(solution)/shard_map/ppermute | solution.py:85
  113.6 6.5 %collective-permute-start.11 = (bf16[3,3,2,16,256]{4,3,2,1,0:T(8,128)(2,1)S(1)}, bf16[3,3,2,16,256]{4,3,2,1,0:T(8,128)(2,1)S(1)}, u32[]{:S(2)}, u32[]{:S(2)}) collective-permute-start(bf16[3,3,2,16,256]{4,3,2,1,0:T(8,128)(2,1)S(1)} %pad_maximum_fusion.3), channel_id=1, source_target_pairs={{0,8},{1,3},{2,10},{3,1},{4,12},{5,7},{6,14},{7,5},{8,0},{9,11},{1... | collective-permute-start | bytes 442376 | tf_op jit(solution)/shard_map/ppermute | solution.py:85
  120.1 8.3 %collective-permute-start.12 = (bf16[3,3,2,2,16,256]{5,4,3,2,1,0:T(8,128)(2,1)S(1)}, bf16[3,3,2,2,16,256]{5,4,3,2,1,0:T(8,128)(2,1)S(1)}, u32[]{:S(2)}, u32[]{:S(2)}) collective-permute-start(bf16[3,3,2,2,16,256]{5,4,3,2,1,0:T(8,128)(2,1)S(1)} %pad_maximum_fusion.2), channel_id=1, source_target_pairs={{0,4},{1,17},{2,6},{3,19},{4,0},{5,21},{6,2},{7,23},{8,12},{9,25},... | collective-permute-start | bytes 884744 | tf_op jit(solution)/shard_map/ppermute | solution.py:85
  120.3 4.1 %collective-permute-start.16 = (bf16[2,8,512]{2,1,0:T(8,128)(2,1)S(1)}, bf16[2,8,512]{2,1,0:T(8,128)(2,1)S(1)}, u32[]{:S(2)}, u32[]{:S(2)}) collective-permute-start(bf16[2,8,512]{2,1,0:T(8,128)(2,1)S(1)} %pad_maximum_fusion.7), channel_id=1, source_target_pairs={{0,8},{1,3},{2,10},{3,1},{4,12},{5,7},{6,14},{7,5},{8,0},{9,11},{1... | collective-permute-start | bytes 49160 | tf_op jit(solution)/shard_map/ppermute | solution.py:85
  128.6 12.0 %collective-permute-start.13 = (bf16[3,3,2,2,2,16,256]{6,5,4,3,2,1,0:T(8,128)(2,1)S(1)}, bf16[3,3,2,2,2,16,256]{6,5,4,3,2,1,0:T(8,128)(2,1)}, u32[]{:S(2)}, u32[]{:S(2)}) collective-permute-start(bf16[3,3,2,2,2,16,256]{6,5,4,3,2,1,0:T(8,128)(2,1)S(1)} %pad_maximum_fusion.1), channel_id=1, source_target_pairs={{0,2},{1,9},{2,0},{3,11},{4,6},{5,13},{6,4},{7,15},{8,10},{9,1},{1... | collective-permute-start | bytes 1769480 | tf_op jit(solution)/shard_map/ppermute | solution.py:85
  129.7 10.8 %collective-permute-start.17 = (bf16[2,2,8,512]{3,2,1,0:T(8,128)(2,1)S(1)}, bf16[2,2,8,512]{3,2,1,0:T(8,128)(2,1)S(1)}, u32[]{:S(2)}, u32[]{:S(2)}) collective-permute-start(bf16[2,2,8,512]{3,2,1,0:T(8,128)(2,1)S(1)} %pad_maximum_fusion.6), channel_id=1, source_target_pairs={{0,4},{1,17},{2,6},{3,19},{4,0},{5,21},{6,2},{7,23},{8,12},{9,25},... | collective-permute-start | bytes 98312 | tf_op jit(solution)/shard_map/ppermute | solution.py:85
  140.5 4.3 %collective-permute-start.18 = (bf16[2,2,2,8,512]{4,3,2,1,0:T(8,128)(2,1)S(1)}, bf16[2,2,2,8,512]{4,3,2,1,0:T(8,128)(2,1)S(1)}, u32[]{:S(2)}, u32[]{:S(2)}) collective-permute-start(bf16[2,2,2,8,512]{4,3,2,1,0:T(8,128)(2,1)S(1)} %pad_maximum_fusion.5), channel_id=1, source_target_pairs={{0,2},{1,9},{2,0},{3,11},{4,6},{5,13},{6,4},{7,15},{8,10},{9,1},{1... | collective-permute-start | bytes 196616 | tf_op jit(solution)/shard_map/ppermute | solution.py:85
  143.3 21.9 %collective-permute-start.14 = (bf16[3,3,2,2,2,2,16,256]{7,6,5,4,3,2,1,0:T(8,128)(2,1)}, bf16[3,3,2,2,2,2,16,256]{7,6,5,4,3,2,1,0:T(8,128)(2,1)}, u32[]{:S(2)}, u32[]{:S(2)}) collective-permute-start(bf16[3,3,2,2,2,2,16,256]{7,6,5,4,3,2,1,0:T(8,128)(2,1)} %copy_select_fusion.2), channel_id=1, source_target_pairs={{0,1},{1,0},{2,3},{3,2},{4,5},{5,4},{6,7},{7,6},{8,9},{9,8},{10,11... | collective-permute-start | bytes 3538952 | tf_op jit(solution)/shard_map/ppermute | solution.py:85
  145.5 9.4 %collective-permute-start.19 = (bf16[2,2,2,2,8,512]{5,4,3,2,1,0:T(8,128)(2,1)}, bf16[2,2,2,2,8,512]{5,4,3,2,1,0:T(8,128)(2,1)}, u32[]{:S(2)}, u32[]{:S(2)}) collective-permute-start(bf16[2,2,2,2,8,512]{5,4,3,2,1,0:T(8,128)(2,1)} %copy_select_fusion.5), channel_id=1, source_target_pairs={{0,1},{1,0},{2,3},{3,2},{4,5},{5,4},{6,7},{7,6},{8,9},{9,8},{10,11... | collective-permute-start | bytes 393224 | tf_op jit(solution)/shard_map/ppermute | solution.py:85
  148.8 13.3 %all-to-all-start.2 = ((f32[32,1,2]{2,1,0:T(1,128)}), f32[32,1,2]{2,1,0:T(1,128)}, u32[]{:S(2)}, u32[]{:S(2)}) async-start(f32[32,1,2]{2,1,0:T(1,128)} %broadcast_in_dim.19), calls=%async_computation.2 | async-start | bytes 32768 | tf_op jit(solution)/shard_map/all_to_all | solution.py:175
  202.4 12.1 %collective-permute-start.21 = (bf16[3,3,2,2,2,16,256]{6,5,1,0,2,3,4:T(8,128)(2,1)S(1)}, bf16[3,3,2,2,2,16,256]{6,5,1,0,2,3,4:T(8,128)(2,1)S(1)}, u32[]{:S(2)}, u32[]{:S(2)}) collective-permute-start(bf16[3,3,2,2,2,16,256]{6,5,1,0,2,3,4:T(8,128)(2,1)S(1)} %fusion.35), channel_id=1, source_target_pairs={{0,2},{1,9},{2,0},{3,11},{4,6},{5,13},{6,4},{7,15},{8,10},{9,1},{1... | collective-permute-start | bytes 1769480 | tf_op jit(solution)/shard_map/ppermute | solution.py:85
  203.3 9.8 %collective-permute-start.26 = (bf16[2,2,2,8,512]{4,3,0,1,2:T(8,128)(2,1)S(1)}, bf16[2,2,2,8,512]{4,3,0,1,2:T(8,128)(2,1)S(1)}, u32[]{:S(2)}, u32[]{:S(2)}) collective-permute-start(bf16[2,2,2,8,512]{4,3,0,1,2:T(8,128)(2,1)S(1)} %fusion.65), channel_id=1, source_target_pairs={{0,2},{1,9},{2,0},{3,11},{4,6},{5,13},{6,4},{7,15},{8,10},{9,1},{1... | collective-permute-start | bytes 196616 | tf_op jit(solution)/shard_map/ppermute | solution.py:85
  213.1 5.5 %collective-permute-start.27 = (bf16[2,2,8,512]{3,2,0,1:T(8,128)(2,1)S(1)}, bf16[2,2,8,512]{3,2,0,1:T(8,128)(2,1)S(1)}, u32[]{:S(2)}, u32[]{:S(2)}) collective-permute-start(bf16[2,2,8,512]{3,2,0,1:T(8,128)(2,1)S(1)} %fusion.76), channel_id=1, source_target_pairs={{0,4},{1,17},{2,6},{3,19},{4,0},{5,21},{6,2},{7,23},{8,12},{9,25},... | collective-permute-start | bytes 98312 | tf_op jit(solution)/shard_map/ppermute | solution.py:85
  214.8 8.5 %collective-permute-start.22 = (bf16[3,3,2,2,16,256]{5,4,1,0,2,3:T(8,128)(2,1)S(1)}, bf16[3,3,2,2,16,256]{5,4,1,0,2,3:T(8,128)(2,1)S(1)}, u32[]{:S(2)}, u32[]{:S(2)}) collective-permute-start(bf16[3,3,2,2,16,256]{5,4,1,0,2,3:T(8,128)(2,1)S(1)} %fusion.38), channel_id=1, source_target_pairs={{0,4},{1,17},{2,6},{3,19},{4,0},{5,21},{6,2},{7,23},{8,12},{9,25},... | collective-permute-start | bytes 884744 | tf_op jit(solution)/shard_map/ppermute | solution.py:85
  218.7 5.3 %collective-permute-start.28 = (bf16[2,8,512]{2,1,0:T(8,128)(2,1)S(1)}, bf16[2,8,512]{2,1,0:T(8,128)(2,1)S(1)}, u32[]{:S(2)}, u32[]{:S(2)}) collective-permute-start(bf16[2,8,512]{2,1,0:T(8,128)(2,1)S(1)} %fusion.78), channel_id=1, source_target_pairs={{0,8},{1,3},{2,10},{3,1},{4,12},{5,7},{6,14},{7,5},{8,0},{9,11},{1... | collective-permute-start | bytes 49160 | tf_op jit(solution)/shard_map/ppermute | solution.py:85
  223.4 5.2 %collective-permute-start.23 = (bf16[3,3,2,16,256]{4,3,1,0,2:T(8,128)(2,1)S(1)}, bf16[3,3,2,16,256]{4,3,1,0,2:T(8,128)(2,1)S(1)}, u32[]{:S(2)}, u32[]{:S(2)}) collective-permute-start(bf16[3,3,2,16,256]{4,3,1,0,2:T(8,128)(2,1)S(1)} %fusion.44), channel_id=1, source_target_pairs={{0,8},{1,3},{2,10},{3,1},{4,12},{5,7},{6,14},{7,5},{8,0},{9,11},{1... | collective-permute-start | bytes 442376 | tf_op jit(solution)/shard_map/ppermute | solution.py:85
  224.0 5.9 %collective-permute-start.29 = (bf16[8,512]{1,0:T(8,128)(2,1)S(1)}, bf16[8,512]{1,0:T(8,128)(2,1)S(1)}, u32[]{:S(2)}, u32[]{:S(2)}) collective-permute-start(bf16[8,512]{1,0:T(8,128)(2,1)S(1)} %fusion.82), channel_id=1, source_target_pairs={{0,16},{1,5},{2,18},{3,7},{4,20},{5,1},{6,22},{7,3},{8,24},{9,13},... | collective-permute-start | bytes 24584 | tf_op jit(solution)/shard_map/ppermute | solution.py:85
  228.7 5.9 %collective-permute-start.24 = (bf16[3,3,16,256]{3,2,1,0:T(8,128)(2,1)S(1)}, bf16[3,3,16,256]{3,2,1,0:T(8,128)(2,1)S(1)}, u32[]{:S(2)}, u32[]{:S(2)}) collective-permute-start(bf16[3,3,16,256]{3,2,1,0:T(8,128)(2,1)S(1)} %fusion.63), channel_id=1, source_target_pairs={{0,16},{1,5},{2,18},{3,7},{4,20},{5,1},{6,22},{7,3},{8,24},{9,13},... | collective-permute-start | bytes 221192 | tf_op jit(solution)/shard_map/ppermute | solution.py:85
  237.9 11.8 %all-to-all-start.3 = ((f32[32,1,2]{2,1,0:T(1,128)}), f32[32,1,2]{2,1,0:T(1,128)S(1)}, u32[]{:S(2)}, u32[]{:S(2)}) async-start(f32[32,1,2]{2,1,0:T(1,128)} %broadcast_in_dim.20), calls=%async_computation.3 | async-start | bytes 32768 | tf_op jit(solution)/shard_map/all_to_all | solution.py:175
  (47 other events, 615.4 us)

commit v10 on v8

--- a/solution.py
+++ b/solution.py
@@ -123,22 +123,21 @@
     order = jnp.arange(sources, dtype=jnp.int32)
     earlier = (task_of[:, None] == task_of[None, :]) & (order[None, :] < order[:, None])
     position = jnp.sum(earlier.astype(jnp.int32), axis=1)
+    label_row = jnp.zeros((sources, 1, side, chans), jnp.bfloat16)
+    label_row = label_row.at[:, 0, 0, :cells].set(targets.astype(jnp.bfloat16))
+    empty_row = jnp.zeros((1, side, chans), jnp.bfloat16).at[0, 0, :cells].set(-1.0)
     send_feats = (
-        jnp.zeros((groups, bucket, side, side, chans), jnp.bfloat16)
+        jnp.broadcast_to(
+            jnp.concatenate([jnp.zeros((side, side, chans), jnp.bfloat16), empty_row], axis=0),
+            (groups, bucket, side + 1, side, chans),
+        )
         .at[task_of, position]
-        .set(feats)
-    )
-    send_labels = (
-        jnp.full((groups, bucket, cells), -1.0, jnp.bfloat16)
-        .at[task_of, position]
-        .set(targets.astype(jnp.bfloat16))
-    )
-    come_feats, come_labels = (
-        lax.all_to_all(send_feats, "task", split_axis=0, concat_axis=0, tiled=True),
-        lax.all_to_all(send_labels, "task", split_axis=0, concat_axis=0, tiled=True),
-    )
-    held_feats = come_feats.reshape(groups * bucket, side, side, chans)
-    held_labels = come_labels.reshape(groups * bucket, cells).astype(jnp.int32)
+        .set(jnp.concatenate([feats, label_row], axis=1))
+    )
+    come_feats = lax.all_to_all(send_feats, "task", split_axis=0, concat_axis=0, tiled=True)
+    come_feats = come_feats.reshape(groups * bucket, side + 1, side, chans)
+    held_feats = come_feats[:, :side]
+    held_labels = come_feats[:, side, 0, :cells].astype(jnp.int32)
     count = counts[0].astype(jnp.float32)
     entries = 10.0 * CHANNELS * INNER
     place = lax.axis_index("ex")

time: 250 us -> 259 us (1.036)
  local copies, waits for them, and re-layouts: 27.4 us -> 35 us
  starting transfers between devices: 56.3 us -> 52.4 us
  other arithmetic: 25.6 us -> 28.4 us
    unnamed x70 -> x69, local copies, waits for them, and re-layouts: 14.1 us -> 19.5 us
    all_to_all x1 -> x0, starting transfers between devices: 4.4 us -> none  [shards(): lax.all_to_all(send_labels, 'task', split_axis=0, concat_axis=0, tiled=True)]
    all_to_all x1, waiting for transfers between devices: 15.3 us -> 18.2 us  [shards(): lax.all_to_all(send_feats, 'task', split_axis=0, concat_axis=0, tiled=True)]
  transfers between devices with their start and end apart: 34 -> 33, of which waited for: 20 -> 19; matrix products, arithmetic and copies ran while one was open for 9% -> 8% of each run, Pallas kernels for 0% -> 0%
where the time goes in v10:
time: 259 us; the launch traced here: 254 us
  waiting for transfers between devices  91.4 us (35%)
  starting transfers between devices  52.4 us (20%)
  matrix products  39.1 us (15%)
  local copies, waits for them, and re-layouts  35 us (14%)
  other arithmetic  28.4 us (11%)
  between operations  7.88 us (3%)
    ppermute x30, waiting for transfers between devices, partner_swap(): return lax.ppermute(value, 'ex', perm=pairs)  59.3 us
    ppermute x30, starting transfers between devices, partner_swap(): return lax.ppermute(value, 'ex', perm=pairs)  37.8 us
    unnamed x69, local copies, waits for them, and re-layouts  19.5 us
    all_to_all x1, waiting for transfers between devices, shards(): lax.all_to_all(send_feats, 'task', split_axis=0, concat_axis=0, tiled=True)  18.2 us
    dot_general x20, matrix products, contract_rows(): lax.dot_general(left, right, (((0,), (0,)), ((), ())), preferred_element_...  17.1 us
    all_to_all x2, waiting for transfers between devices, shards(): totals = jnp.sum(lax.all_to_all(spread, 'ex', 0, 0, tiled=True), axis=0)  14 us
    dot_general x18, matrix products, train_pass(): jnp.dot(windows[offset_index], down_low[offset_index // 3, offset_index %...  12.9 us
    all_to_all x2, starting transfers between devices, shards(): totals = jnp.sum(lax.all_to_all(spread, 'ex', 0, 0, tiled=True), axis=0)  10.2 us
  transfers between devices with their start and end apart: 33, of which 19 were waited for; matrix products, arithmetic and copies ran while one was open for 8% of the time, Pallas kernels for 0%

profile of v10, /device:TPU:0, one launch (start us, length us, event | category | flops | bytes accessed | tf_op | source)
XLA Modules:
  0.0 254.3 jit_solution(10112837087341073032)
XLA Ops:
  5.6 3.0 %scatter_fusion = bf16[4,6,9,8,512]{4,3,2,1,0:T(8,128)(2,1)} fusion(bf16[4,6,9,8,512]{4,3,2,1,0:T(8,128)(2,1)} %broadcast_in_dim.14, s32[12]{0:T(128)S(1)} %fusion.88, bf16[12,9,8,512]{3,2,1,0:T(8,128)(2,1)S(1)} %fusion.33), kind=kCustom, calls=%fused_computation | custom fusion | bytes 2654304 | tf_op jit(solution)/shard_map/scatter | solution.py:135
  8.6 4.4 %all-to-all-start = ((bf16[4,6,9,8,512]{4,3,2,1,0:T(8,128)(2,1)}), bf16[4,6,9,8,512]{4,3,2,1,0:T(8,128)(2,1)S(1)}, u32[]{:S(2)}, u32[]{:S(2)}) async-start(bf16[4,6,9,8,512]{4,3,2,1,0:T(8,128)(2,1)} %scatter_fusion), calls=%async_computation | async-start | bytes 3538944 | tf_op jit(solution)/shard_map/all_to_all | solution.py:137
  13.7 4.0 %convert_bitcast_fusion = bf16[3,3,512,256]{3,2,1,0:T(8,128)(2,1)} fusion(f32[1,3,3,512,256]{4,3,2,1,0:T(8,128)} %param.15), kind=kLoop, calls=%fused_computation.50 | loop fusion | flops 1179648 | bytes 7077888 | tf_op jit(solution)/shard_map/convert_element_type | solution.py:148
  17.7 18.2 %all-to-all-done = bf16[4,6,9,8,512]{4,3,2,1,0:T(8,128)(2,1)S(1)} async-done(((bf16[4,6,9,8,512]{4,3,2,1,0:T(8,128)(2,1)}), bf16[4,6,9,8,512]{4,3,2,1,0:T(8,128)(2,1)S(1)}, u32[]{:S(2)}, u32[]{:S(2)}) %all-to-all-start) | async-done | bytes 1769504 | tf_op jit(solution)/shard_map/all_to_all | solution.py:137
  37.2 4.5 %pad_slice_fusion = (bf16[24,8,8,512]{3,2,1,0:T(8,128)(2,1)S(1)}, bf16[24,8,8,512]{3,2,1,0:T(8,128)(2,1)}, bf16[24,8,8,512]{3,2,1,0:T(8,128)(2,1)}, bf16[24,8,8,...) fusion(bf16[24,8,8,512]{3,2,1,0:T(8,128)(2,1)S(1)} %slice.189), kind=kLoop, calls=%fused_computation.1 | loop fusion | bytes 14155776 | tf_op jit(solution)/shard_map/slice | solution.py:19
  43.5 2.1 fusion.40
  68.8 2.1 copy-done.19
  72.3 2.7 %fusion.91 = f32[256,512]{1,0:T(8,128)S(1)} fusion(bf16[1536,512]{0,1:T(8,128)(2,1)} %copy-done.27, f32[1536,256]{1,0:T(8,128)} %copy-done.23), kind=kOutput, calls=%fused_computation.287 | convolution fusion | flops 404619264 | bytes 3670016 | tf_op jit(solution)/shard_map/dot_general | solution.py:25
  79.9 7.0 %collective-permute-done.6 = bf16[2,2,2,8,512]{4,3,0,1,2:T(8,128)(2,1)S(1)} collective-permute-done((bf16[2,2,2,8,512]{4,3,0,1,2:T(8,128)(2,1)S(1)}, bf16[2,2,2,8,512]{4,3,0,1,2:T(8,128)(2,1)S(1)}, u32[]{:S(2)}, u32[]{:S(2)}) %collective-permute-start.6) | collective-permute-done | bytes 65568 | tf_op jit(solution)/shard_map/ppermute | solution.py:85
  86.9 3.3 %collective-permute-start.7 = (bf16[2,2,8,512]{3,2,0,1:T(8,128)(2,1)S(1)}, bf16[2,2,8,512]{3,2,0,1:T(8,128)(2,1)S(1)}, u32[]{:S(2)}, u32[]{:S(2)}) collective-permute-start(bf16[2,2,8,512]{3,2,0,1:T(8,128)(2,1)S(1)} %fusion.76), channel_id=1, source_target_pairs={{0,4},{1,17},{2,6},{3,19},{4,0},{5,21},{6,2},{7,23},{8,12},{9,25},... | collective-permute-start | bytes 98312 | tf_op jit(solution)/shard_map/ppermute | solution.py:85
  94.4 4.5 %collective-permute-done.2 = bf16[3,3,2,2,16,256]{5,4,1,0,2,3:T(8,128)(2,1)S(1)} collective-permute-done((bf16[3,3,2,2,16,256]{5,4,1,0,2,3:T(8,128)(2,1)S(1)}, bf16[3,3,2,2,16,256]{5,4,1,0,2,3:T(8,128)(2,1)S(1)}, u32[]{:S(2)}, u32[]{:S(2)}) %collective-permute-start.2) | collective-permute-done | bytes 294944 | tf_op jit(solution)/shard_map/ppermute | solution.py:85
  101.1 3.7 %collective-permute-start.9 = (bf16[8,512]{1,0:T(8,128)(2,1)S(1)}, bf16[8,512]{1,0:T(8,128)(2,1)S(1)}, u32[]{:S(2)}, u32[]{:S(2)}) collective-permute-start(bf16[8,512]{1,0:T(8,128)(2,1)S(1)} %fusion.82), channel_id=1, source_target_pairs={{0,16},{1,5},{2,18},{3,7},{4,20},{5,1},{6,22},{7,3},{8,24},{9,13},... | collective-permute-start | bytes 24584 | tf_op jit(solution)/shard_map/ppermute | solution.py:85
  104.8 3.5 %collective-permute-start.4 = (bf16[3,3,16,256]{3,2,1,0:T(8,128)(2,1)S(1)}, bf16[3,3,16,256]{3,2,1,0:T(8,128)(2,1)S(1)}, u32[]{:S(2)}, u32[]{:S(2)}) collective-permute-start(bf16[3,3,16,256]{3,2,1,0:T(8,128)(2,1)S(1)} %fusion.64), channel_id=1, source_target_pairs={{0,16},{1,5},{2,18},{3,7},{4,20},{5,1},{6,22},{7,3},{8,24},{9,13},... | collective-permute-start | bytes 221192 | tf_op jit(solution)/shard_map/ppermute | solution.py:85
  114.1 5.7 %all-to-all-start.1 = ((f32[32,1,2]{2,1,0:T(1,128)}), f32[32,1,2]{2,1,0:T(1,128)S(1)}, u32[]{:S(2)}, u32[]{:S(2)}) async-start(f32[32,1,2]{2,1,0:T(1,128)} %broadcast_in_dim.16), calls=%async_computation.1 | async-start | bytes 32768 | tf_op jit(solution)/shard_map/all_to_all | solution.py:174
  119.8 7.3 %all-to-all-done.1 = f32[32,1,2]{2,1,0:T(1,128)S(1)} async-done(((f32[32,1,2]{2,1,0:T(1,128)}), f32[32,1,2]{2,1,0:T(1,128)S(1)}, u32[]{:S(2)}, u32[]{:S(2)}) %all-to-all-start.1) | async-done | bytes 288 | tf_op jit(solution)/shard_map/all_to_all | solution.py:174
  130.7 4.6 %collective-permute-done.10 = bf16[3,3,16,256]{3,2,1,0:T(8,128)(2,1)S(1)} collective-permute-done((bf16[3,3,16,256]{3,2,1,0:T(8,128)(2,1)S(1)}, bf16[3,3,16,256]{3,2,1,0:T(8,128)(2,1)S(1)}, u32[]{:S(2)}, u32[]{:S(2)}) %collective-permute-start.10) | collective-permute-done | bytes 73760 | tf_op jit(solution)/shard_map/ppermute | solution.py:85
  136.1 4.5 %collective-permute-done.11 = bf16[3,3,2,16,256]{4,3,2,1,0:T(8,128)(2,1)S(1)} collective-permute-done((bf16[3,3,2,16,256]{4,3,2,1,0:T(8,128)(2,1)S(1)}, bf16[3,3,2,16,256]{4,3,2,1,0:T(8,128)(2,1)S(1)}, u32[]{:S(2)}, u32[]{:S(2)}) %collective-permute-start.11) | collective-permute-done | bytes 147488 | tf_op jit(solution)/shard_map/ppermute | solution.py:85
  143.8 5.1 %collective-permute-done.12 = bf16[3,3,2,2,16,256]{5,4,3,2,1,0:T(8,128)(2,1)S(1)} collective-permute-done((bf16[3,3,2,2,16,256]{5,4,3,2,1,0:T(8,128)(2,1)S(1)}, bf16[3,3,2,2,16,256]{5,4,3,2,1,0:T(8,128)(2,1)S(1)}, u32[]{:S(2)}, u32[]{:S(2)}) %collective-permute-start.12) | collective-permute-done | bytes 294944 | tf_op jit(solution)/shard_map/ppermute | solution.py:85
  150.5 3.5 %collective-permute-done.16 = bf16[2,8,512]{2,1,0:T(8,128)(2,1)S(1)} collective-permute-done((bf16[2,8,512]{2,1,0:T(8,128)(2,1)S(1)}, bf16[2,8,512]{2,1,0:T(8,128)(2,1)S(1)}, u32[]{:S(2)}, u32[]{:S(2)}) %collective-permute-start.16) | collective-permute-done | bytes 16416 | tf_op jit(solution)/shard_map/ppermute | solution.py:85
  155.9 3.2 %collective-permute-done.13 = bf16[3,3,2,2,2,16,256]{6,5,4,3,2,1,0:T(8,128)(2,1)} collective-permute-done((bf16[3,3,2,2,2,16,256]{6,5,4,3,2,1,0:T(8,128)(2,1)S(1)}, bf16[3,3,2,2,2,16,256]{6,5,4,3,2,1,0:T(8,128)(2,1)}, u32[]{:S(2)}, u32[]{:S(2)}) %collective-permute-start.13) | collective-permute-done | bytes 589856 | tf_op jit(solution)/shard_map/ppermute | solution.py:85
  162.7 3.5 %collective-permute-done.18 = bf16[2,2,2,8,512]{4,3,2,1,0:T(8,128)(2,1)S(1)} collective-permute-done((bf16[2,2,2,8,512]{4,3,2,1,0:T(8,128)(2,1)S(1)}, bf16[2,2,2,8,512]{4,3,2,1,0:T(8,128)(2,1)S(1)}, u32[]{:S(2)}, u32[]{:S(2)}) %collective-permute-start.18) | collective-permute-done | bytes 65568 | tf_op jit(solution)/shard_map/ppermute | solution.py:85
  167.9 2.1 select_bitcast_fusion.1
  194.9 2.1 copy-done.18
  197.6 2.7 %fusion.92 = f32[256,512]{1,0:T(8,128)S(1)} fusion(bf16[1536,512]{0,1:T(8,128)(2,1)} %copy-done.28, f32[1536,256]{1,0:T(8,128)} %copy-done.24), kind=kOutput, calls=%fused_computation.288 | convolution fusion | flops 404619264 | bytes 3670016 | tf_op jit(solution)/shard_map/dot_general | solution.py:25
  205.1 7.0 %collective-permute-done.26 = bf16[2,2,2,8,512]{4,3,0,1,2:T(8,128)(2,1)S(1)} collective-permute-done((bf16[2,2,2,8,512]{4,3,0,1,2:T(8,128)(2,1)S(1)}, bf16[2,2,2,8,512]{4,3,0,1,2:T(8,128)(2,1)S(1)}, u32[]{:S(2)}, u32[]{:S(2)}) %collective-permute-start.26) | collective-permute-done | bytes 65568 | tf_op jit(solution)/shard_map/ppermute | solution.py:85
  213.6 2.4 collective-permute-start.22
  218.3 3.8 %collective-permute-done.22 = bf16[3,3,2,2,16,256]{5,4,1,0,2,3:T(8,128)(2,1)S(1)} collective-permute-done((bf16[3,3,2,2,16,256]{5,4,1,0,2,3:T(8,128)(2,1)S(1)}, bf16[3,3,2,2,16,256]{5,4,1,0,2,3:T(8,128)(2,1)S(1)}, u32[]{:S(2)}, u32[]{:S(2)}) %collective-permute-start.22) | collective-permute-done | bytes 294944 | tf_op jit(solution)/shard_map/ppermute | solution.py:85
  223.0 2.1 collective-permute-start.29
  225.0 2.4 collective-permute-done.23
  229.5 4.0 %collective-permute-done.24 = bf16[3,3,16,256]{3,2,1,0:T(8,128)(2,1)S(1)} collective-permute-done((bf16[3,3,16,256]{3,2,1,0:T(8,128)(2,1)S(1)}, bf16[3,3,16,256]{3,2,1,0:T(8,128)(2,1)S(1)}, u32[]{:S(2)}, u32[]{:S(2)}) %collective-permute-start.24) | collective-permute-done | bytes 73760 | tf_op jit(solution)/shard_map/ppermute | solution.py:85
  236.7 4.5 %all-to-all-start.2 = ((f32[32,1,2]{2,1,0:T(1,128)}), f32[32,1,2]{2,1,0:T(1,128)S(1)}, u32[]{:S(2)}, u32[]{:S(2)}) async-start(f32[32,1,2]{2,1,0:T(1,128)} %broadcast_in_dim.17), calls=%async_computation.2 | async-start | bytes 32768 | tf_op jit(solution)/shard_map/all_to_all | solution.py:174
  241.9 6.7 %all-to-all-done.2 = f32[32,1,2]{2,1,0:T(1,128)S(1)} async-done(((f32[32,1,2]{2,1,0:T(1,128)}), f32[32,1,2]{2,1,0:T(1,128)S(1)}, u32[]{:S(2)}, u32[]{:S(2)}) %all-to-all-start.2) | async-done | bytes 288 | tf_op jit(solution)/shard_map/all_to_all | solution.py:174
  (252 shorter events, 106.3 us)
Async XLA Ops:
  8.6 27.3 %all-to-all-start = ((bf16[4,6,9,8,512]{4,3,2,1,0:T(8,128)(2,1)}), bf16[4,6,9,8,512]{4,3,2,1,0:T(8,128)(2,1)S(1)}, u32[]{:S(2)}, u32[]{:S(2)}) async-start(bf16[4,6,9,8,512]{4,3,2,1,0:T(8,128)(2,1)} %scatter_fusion), calls=%async_computation | async-start | bytes 3538944 | tf_op jit(solution)/shard_map/all_to_all | solution.py:137
  72.2 3.4 %collective-permute-start = (bf16[3,3,2,2,2,2,16,256]{7,6,1,0,2,3,4,5:T(8,128)(2,1)}, bf16[3,3,2,2,2,2,16,256]{7,6,1,0,2,3,4,5:T(8,128)(2,1)S(1)}, u32[]{:S(2)}, u32[]{:S(2)}) collective-permute-start(bf16[3,3,2,2,2,2,16,256]{7,6,1,0,2,3,4,5:T(8,128)(2,1)} %fusion.31), channel_id=1, source_target_pairs={{0,1},{1,0},{2,3},{3,2},{4,5},{5,4},{6,7},{7,6},{8,9},{9,8},{10,11... | collective-permute-start | bytes 3538952 | tf_op jit(solution)/shard_map/ppermute | solution.py:85
  75.0 2.8 %collective-permute-start.5 = (bf16[2,2,2,2,8,512]{5,4,0,1,2,3:T(8,128)(2,1)S(1)}, bf16[2,2,2,2,8,512]{5,4,0,1,2,3:T(8,128)(2,1)S(1)}, u32[]{:S(2)}, u32[]{:S(2)}) collective-permute-start(bf16[2,2,2,2,8,512]{5,4,0,1,2,3:T(8,128)(2,1)S(1)} %fusion.47), channel_id=1, source_target_pairs={{0,1},{1,0},{2,3},{3,2},{4,5},{5,4},{6,7},{7,6},{8,9},{9,8},{10,11... | collective-permute-start | bytes 393224 | tf_op jit(solution)/shard_map/ppermute | solution.py:85
  76.2 14.0 %collective-permute-start.1 = (bf16[3,3,2,2,2,16,256]{6,5,1,0,2,3,4:T(8,128)(2,1)S(1)}, bf16[3,3,2,2,2,16,256]{6,5,1,0,2,3,4:T(8,128)(2,1)S(1)}, u32[]{:S(2)}, u32[]{:S(2)}) collective-permute-start(bf16[3,3,2,2,2,16,256]{6,5,1,0,2,3,4:T(8,128)(2,1)S(1)} %fusion.35), channel_id=1, source_target_pairs={{0,2},{1,9},{2,0},{3,11},{4,6},{5,13},{6,4},{7,15},{8,10},{9,1},{1... | collective-permute-start | bytes 1769480 | tf_op jit(solution)/shard_map/ppermute | solution.py:85
  77.9 9.0 %collective-permute-start.6 = (bf16[2,2,2,8,512]{4,3,0,1,2:T(8,128)(2,1)S(1)}, bf16[2,2,2,8,512]{4,3,0,1,2:T(8,128)(2,1)S(1)}, u32[]{:S(2)}, u32[]{:S(2)}) collective-permute-start(bf16[2,2,2,8,512]{4,3,0,1,2:T(8,128)(2,1)S(1)} %fusion.66), channel_id=1, source_target_pairs={{0,2},{1,9},{2,0},{3,11},{4,6},{5,13},{6,4},{7,15},{8,10},{9,1},{1... | collective-permute-start | bytes 196616 | tf_op jit(solution)/shard_map/ppermute | solution.py:85
  86.9 5.5 %collective-permute-start.7 = (bf16[2,2,8,512]{3,2,0,1:T(8,128)(2,1)S(1)}, bf16[2,2,8,512]{3,2,0,1:T(8,128)(2,1)S(1)}, u32[]{:S(2)}, u32[]{:S(2)}) collective-permute-start(bf16[2,2,8,512]{3,2,0,1:T(8,128)(2,1)S(1)} %fusion.76), channel_id=1, source_target_pairs={{0,4},{1,17},{2,6},{3,19},{4,0},{5,21},{6,2},{7,23},{8,12},{9,25},... | collective-permute-start | bytes 98312 | tf_op jit(solution)/shard_map/ppermute | solution.py:85
  90.5 8.5 %collective-permute-start.2 = (bf16[3,3,2,2,16,256]{5,4,1,0,2,3:T(8,128)(2,1)S(1)}, bf16[3,3,2,2,16,256]{5,4,1,0,2,3:T(8,128)(2,1)S(1)}, u32[]{:S(2)}, u32[]{:S(2)}) collective-permute-start(bf16[3,3,2,2,16,256]{5,4,1,0,2,3:T(8,128)(2,1)S(1)} %fusion.37), channel_id=1, source_target_pairs={{0,4},{1,17},{2,6},{3,19},{4,0},{5,21},{6,2},{7,23},{8,12},{9,25},... | collective-permute-start | bytes 884744 | tf_op jit(solution)/shard_map/ppermute | solution.py:85
  92.5 8.6 %collective-permute-start.8 = (bf16[2,8,512]{2,1,0:T(8,128)(2,1)S(1)}, bf16[2,8,512]{2,1,0:T(8,128)(2,1)S(1)}, u32[]{:S(2)}, u32[]{:S(2)}) collective-permute-start(bf16[2,8,512]{2,1,0:T(8,128)(2,1)S(1)} %fusion.78), channel_id=1, source_target_pairs={{0,8},{1,3},{2,10},{3,1},{4,12},{5,7},{6,14},{7,5},{8,0},{9,11},{1... | collective-permute-start | bytes 49160 | tf_op jit(solution)/shard_map/ppermute | solution.py:85
  99.1 5.7 %collective-permute-start.3 = (bf16[3,3,2,16,256]{4,3,1,0,2:T(8,128)(2,1)S(1)}, bf16[3,3,2,16,256]{4,3,1,0,2:T(8,128)(2,1)S(1)}, u32[]{:S(2)}, u32[]{:S(2)}) collective-permute-start(bf16[3,3,2,16,256]{4,3,1,0,2:T(8,128)(2,1)S(1)} %fusion.45), channel_id=1, source_target_pairs={{0,8},{1,3},{2,10},{3,1},{4,12},{5,7},{6,14},{7,5},{8,0},{9,11},{1... | collective-permute-start | bytes 442376 | tf_op jit(solution)/shard_map/ppermute | solution.py:85
  101.1 7.2 %collective-permute-start.9 = (bf16[8,512]{1,0:T(8,128)(2,1)S(1)}, bf16[8,512]{1,0:T(8,128)(2,1)S(1)}, u32[]{:S(2)}, u32[]{:S(2)}) collective-permute-start(bf16[8,512]{1,0:T(8,128)(2,1)S(1)} %fusion.82), channel_id=1, source_target_pairs={{0,16},{1,5},{2,18},{3,7},{4,20},{5,1},{6,22},{7,3},{8,24},{9,13},... | collective-permute-start | bytes 24584 | tf_op jit(solution)/shard_map/ppermute | solution.py:85
  104.8 5.9 %collective-permute-start.4 = (bf16[3,3,16,256]{3,2,1,0:T(8,128)(2,1)S(1)}, bf16[3,3,16,256]{3,2,1,0:T(8,128)(2,1)S(1)}, u32[]{:S(2)}, u32[]{:S(2)}) collective-permute-start(bf16[3,3,16,256]{3,2,1,0:T(8,128)(2,1)S(1)} %fusion.64), channel_id=1, source_target_pairs={{0,16},{1,5},{2,18},{3,7},{4,20},{5,1},{6,22},{7,3},{8,24},{9,13},... | collective-permute-start | bytes 221192 | tf_op jit(solution)/shard_map/ppermute | solution.py:85
  114.1 13.0 %all-to-all-start.1 = ((f32[32,1,2]{2,1,0:T(1,128)}), f32[32,1,2]{2,1,0:T(1,128)S(1)}, u32[]{:S(2)}, u32[]{:S(2)}) async-start(f32[32,1,2]{2,1,0:T(1,128)} %broadcast_in_dim.16), calls=%async_computation.1 | async-start | bytes 32768 | tf_op jit(solution)/shard_map/all_to_all | solution.py:174
  129.4 5.9 %collective-permute-start.10 = (bf16[3,3,16,256]{3,2,1,0:T(8,128)(2,1)S(1)}, bf16[3,3,16,256]{3,2,1,0:T(8,128)(2,1)S(1)}, u32[]{:S(2)}, u32[]{:S(2)}) collective-permute-start(bf16[3,3,16,256]{3,2,1,0:T(8,128)(2,1)S(1)} %fusion.90), channel_id=1, source_target_pairs={{0,16},{1,5},{2,18},{3,7},{4,20},{5,1},{6,22},{7,3},{8,24},{9,13},... | collective-permute-start | bytes 221192 | tf_op jit(solution)/shard_map/ppermute | solution.py:85
  135.4 5.2 %collective-permute-start.11 = (bf16[3,3,2,16,256]{4,3,2,1,0:T(8,128)(2,1)S(1)}, bf16[3,3,2,16,256]{4,3,2,1,0:T(8,128)(2,1)S(1)}, u32[]{:S(2)}, u32[]{:S(2)}) collective-permute-start(bf16[3,3,2,16,256]{4,3,2,1,0:T(8,128)(2,1)S(1)} %pad_maximum_fusion.5), channel_id=1, source_target_pairs={{0,8},{1,3},{2,10},{3,1},{4,12},{5,7},{6,14},{7,5},{8,0},{9,11},{1... | collective-permute-start | bytes 442376 | tf_op jit(solution)/shard_map/ppermute | solution.py:85
  140.6 8.3 %collective-permute-start.12 = (bf16[3,3,2,2,16,256]{5,4,3,2,1,0:T(8,128)(2,1)S(1)}, bf16[3,3,2,2,16,256]{5,4,3,2,1,0:T(8,128)(2,1)S(1)}, u32[]{:S(2)}, u32[]{:S(2)}) collective-permute-start(bf16[3,3,2,2,16,256]{5,4,3,2,1,0:T(8,128)(2,1)S(1)} %pad_maximum_fusion.3), channel_id=1, source_target_pairs={{0,4},{1,17},{2,6},{3,19},{4,0},{5,21},{6,2},{7,23},{8,12},{9,25},... | collective-permute-start | bytes 884744 | tf_op jit(solution)/shard_map/ppermute | solution.py:85
  142.6 7.3 %collective-permute-start.15 = (bf16[8,512]{1,0:T(8,128)(2,1)S(1)}, bf16[8,512]{1,0:T(8,128)(2,1)S(1)}, u32[]{:S(2)}, u32[]{:S(2)}) collective-permute-start(bf16[8,512]{1,0:T(8,128)(2,1)S(1)} %fusion.89), channel_id=1, source_target_pairs={{0,16},{1,5},{2,18},{3,7},{4,20},{5,1},{6,22},{7,3},{8,24},{9,13},... | collective-permute-start | bytes 24584 | tf_op jit(solution)/shard_map/ppermute | solution.py:85
  149.1 10.1 %collective-permute-start.13 = (bf16[3,3,2,2,2,16,256]{6,5,4,3,2,1,0:T(8,128)(2,1)S(1)}, bf16[3,3,2,2,2,16,256]{6,5,4,3,2,1,0:T(8,128)(2,1)}, u32[]{:S(2)}, u32[]{:S(2)}) collective-permute-start(bf16[3,3,2,2,2,16,256]{6,5,4,3,2,1,0:T(8,128)(2,1)S(1)} %pad_maximum_fusion.2), channel_id=1, source_target_pairs={{0,2},{1,9},{2,0},{3,11},{4,6},{5,13},{6,4},{7,15},{8,10},{9,1},{1... | collective-permute-start | bytes 1769480 | tf_op jit(solution)/shard_map/ppermute | solution.py:85
  149.9 4.0 %collective-permute-start.16 = (bf16[2,8,512]{2,1,0:T(8,128)(2,1)S(1)}, bf16[2,8,512]{2,1,0:T(8,128)(2,1)S(1)}, u32[]{:S(2)}, u32[]{:S(2)}) collective-permute-start(bf16[2,8,512]{2,1,0:T(8,128)(2,1)S(1)} %pad_maximum_fusion.9), channel_id=1, source_target_pairs={{0,8},{1,3},{2,10},{3,1},{4,12},{5,7},{6,14},{7,5},{8,0},{9,11},{1... | collective-permute-start | bytes 49160 | tf_op jit(solution)/shard_map/ppermute | solution.py:85
  153.9 7.9 %collective-permute-start.17 = (bf16[2,2,8,512]{3,2,1,0:T(8,128)(2,1)S(1)}, bf16[2,2,8,512]{3,2,1,0:T(8,128)(2,1)S(1)}, u32[]{:S(2)}, u32[]{:S(2)}) collective-permute-start(bf16[2,2,8,512]{3,2,1,0:T(8,128)(2,1)S(1)} %pad_maximum_fusion.8), channel_id=1, source_target_pairs={{0,4},{1,17},{2,6},{3,19},{4,0},{5,21},{6,2},{7,23},{8,12},{9,25},... | collective-permute-start | bytes 98312 | tf_op jit(solution)/shard_map/ppermute | solution.py:85
  161.8 6.1 %collective-permute-start.14 = (bf16[3,3,2,2,2,2,16,256]{7,6,5,4,3,2,1,0:T(8,128)(2,1)}, bf16[3,3,2,2,2,2,16,256]{7,6,5,4,3,2,1,0:T(8,128)(2,1)}, u32[]{:S(2)}, u32[]{:S(2)}) collective-permute-start(bf16[3,3,2,2,2,2,16,256]{7,6,5,4,3,2,1,0:T(8,128)(2,1)} %copy_select_fusion.2), channel_id=1, source_target_pairs={{0,1},{1,0},{2,3},{3,2},{4,5},{5,4},{6,7},{7,6},{8,9},{9,8},{10,11... | collective-permute-start | bytes 3538952 | tf_op jit(solution)/shard_map/ppermute | solution.py:85
  161.8 4.3 %collective-permute-start.18 = (bf16[2,2,2,8,512]{4,3,2,1,0:T(8,128)(2,1)S(1)}, bf16[2,2,2,8,512]{4,3,2,1,0:T(8,128)(2,1)S(1)}, u32[]{:S(2)}, u32[]{:S(2)}) collective-permute-start(bf16[2,2,2,8,512]{4,3,2,1,0:T(8,128)(2,1)S(1)} %pad_maximum_fusion.7), channel_id=1, source_target_pairs={{0,2},{1,9},{2,0},{3,11},{4,6},{5,13},{6,4},{7,15},{8,10},{9,1},{1... | collective-permute-start | bytes 196616 | tf_op jit(solution)/shard_map/ppermute | solution.py:85
  197.2 3.5 %collective-permute-start.20 = (bf16[3,3,2,2,2,2,16,256]{7,6,1,0,2,3,4,5:T(8,128)(2,1)S(1)}, bf16[3,3,2,2,2,2,16,256]{7,6,1,0,2,3,4,5:T(8,128)(2,1)S(1)}, u32[]{:S(2)}, u32[]{:S(2)}) collective-permute-start(bf16[3,3,2,2,2,2,16,256]{7,6,1,0,2,3,4,5:T(8,128)(2,1)S(1)} %fusion.32), channel_id=1, source_target_pairs={{0,1},{1,0},{2,3},{3,2},{4,5},{5,4},{6,7},{7,6},{8,9},{9,8},{10,11... | collective-permute-start | bytes 3538952 | tf_op jit(solution)/shard_map/ppermute | solution.py:85
  200.3 2.0 collective-permute-start.25
  201.4 12.0 %collective-permute-start.21 = (bf16[3,3,2,2,2,16,256]{6,5,1,0,2,3,4:T(8,128)(2,1)S(1)}, bf16[3,3,2,2,2,16,256]{6,5,1,0,2,3,4:T(8,128)(2,1)S(1)}, u32[]{:S(2)}, u32[]{:S(2)}) collective-permute-start(bf16[3,3,2,2,2,16,256]{6,5,1,0,2,3,4:T(8,128)(2,1)S(1)} %fusion.36), channel_id=1, source_target_pairs={{0,2},{1,9},{2,0},{3,11},{4,6},{5,13},{6,4},{7,15},{8,10},{9,1},{1... | collective-permute-start | bytes 1769480 | tf_op jit(solution)/shard_map/ppermute | solution.py:85
  202.3 9.8 %collective-permute-start.26 = (bf16[2,2,2,8,512]{4,3,0,1,2:T(8,128)(2,1)S(1)}, bf16[2,2,2,8,512]{4,3,0,1,2:T(8,128)(2,1)S(1)}, u32[]{:S(2)}, u32[]{:S(2)}) collective-permute-start(bf16[2,2,2,8,512]{4,3,0,1,2:T(8,128)(2,1)S(1)} %fusion.67), channel_id=1, source_target_pairs={{0,2},{1,9},{2,0},{3,11},{4,6},{5,13},{6,4},{7,15},{8,10},{9,1},{1... | collective-permute-start | bytes 196616 | tf_op jit(solution)/shard_map/ppermute | solution.py:85
  212.1 5.5 %collective-permute-start.27 = (bf16[2,2,8,512]{3,2,0,1:T(8,128)(2,1)S(1)}, bf16[2,2,8,512]{3,2,0,1:T(8,128)(2,1)S(1)}, u32[]{:S(2)}, u32[]{:S(2)}) collective-permute-start(bf16[2,2,8,512]{3,2,0,1:T(8,128)(2,1)S(1)} %fusion.77), channel_id=1, source_target_pairs={{0,4},{1,17},{2,6},{3,19},{4,0},{5,21},{6,2},{7,23},{8,12},{9,25},... | collective-permute-start | bytes 98312 | tf_op jit(solution)/shard_map/ppermute | solution.py:85
  213.6 8.5 %collective-permute-start.22 = (bf16[3,3,2,2,16,256]{5,4,1,0,2,3:T(8,128)(2,1)S(1)}, bf16[3,3,2,2,16,256]{5,4,1,0,2,3:T(8,128)(2,1)S(1)}, u32[]{:S(2)}, u32[]{:S(2)}) collective-permute-start(bf16[3,3,2,2,16,256]{5,4,1,0,2,3:T(8,128)(2,1)S(1)} %fusion.38), channel_id=1, source_target_pairs={{0,4},{1,17},{2,6},{3,19},{4,0},{5,21},{6,2},{7,23},{8,12},{9,25},... | collective-permute-start | bytes 884744 | tf_op jit(solution)/shard_map/ppermute | solution.py:85
  217.6 5.3 %collective-permute-start.28 = (bf16[2,8,512]{2,1,0:T(8,128)(2,1)S(1)}, bf16[2,8,512]{2,1,0:T(8,128)(2,1)S(1)}, u32[]{:S(2)}, u32[]{:S(2)}) collective-permute-start(bf16[2,8,512]{2,1,0:T(8,128)(2,1)S(1)} %fusion.79), channel_id=1, source_target_pairs={{0,8},{1,3},{2,10},{3,1},{4,12},{5,7},{6,14},{7,5},{8,0},{9,11},{1... | collective-permute-start | bytes 49160 | tf_op jit(solution)/shard_map/ppermute | solution.py:85
  222.2 5.2 %collective-permute-start.23 = (bf16[3,3,2,16,256]{4,3,1,0,2:T(8,128)(2,1)S(1)}, bf16[3,3,2,16,256]{4,3,1,0,2:T(8,128)(2,1)S(1)}, u32[]{:S(2)}, u32[]{:S(2)}) collective-permute-start(bf16[3,3,2,16,256]{4,3,1,0,2:T(8,128)(2,1)S(1)} %fusion.46), channel_id=1, source_target_pairs={{0,8},{1,3},{2,10},{3,1},{4,12},{5,7},{6,14},{7,5},{8,0},{9,11},{1... | collective-permute-start | bytes 442376 | tf_op jit(solution)/shard_map/ppermute | solution.py:85
  223.0 5.9 %collective-permute-start.29 = (bf16[8,512]{1,0:T(8,128)(2,1)S(1)}, bf16[8,512]{1,0:T(8,128)(2,1)S(1)}, u32[]{:S(2)}, u32[]{:S(2)}) collective-permute-start(bf16[8,512]{1,0:T(8,128)(2,1)S(1)} %fusion.83), channel_id=1, source_target_pairs={{0,16},{1,5},{2,18},{3,7},{4,20},{5,1},{6,22},{7,3},{8,24},{9,13},... | collective-permute-start | bytes 24584 | tf_op jit(solution)/shard_map/ppermute | solution.py:85
  227.5 5.9 %collective-permute-start.24 = (bf16[3,3,16,256]{3,2,1,0:T(8,128)(2,1)S(1)}, bf16[3,3,16,256]{3,2,1,0:T(8,128)(2,1)S(1)}, u32[]{:S(2)}, u32[]{:S(2)}) collective-permute-start(bf16[3,3,16,256]{3,2,1,0:T(8,128)(2,1)S(1)} %fusion.65), channel_id=1, source_target_pairs={{0,16},{1,5},{2,18},{3,7},{4,20},{5,1},{6,22},{7,3},{8,24},{9,13},... | collective-permute-start | bytes 221192 | tf_op jit(solution)/shard_map/ppermute | solution.py:85
  236.7 11.8 %all-to-all-start.2 = ((f32[32,1,2]{2,1,0:T(1,128)}), f32[32,1,2]{2,1,0:T(1,128)S(1)}, u32[]{:S(2)}, u32[]{:S(2)}) async-start(f32[32,1,2]{2,1,0:T(1,128)} %broadcast_in_dim.17), calls=%async_computation.2 | async-start | bytes 32768 | tf_op jit(solution)/shard_map/all_to_all | solution.py:174
  (35 other events, 222.5 us)

commit v11 on v8

--- a/solution.py
+++ b/solution.py
@@ -159,16 +159,16 @@
             held_feats, held_labels, down_low, upper_low, head, count
         )
         grad_down = grad_down.reshape((3, 3) + bits_shape + (part_chans, inner))
-        grad_up = grad_up.reshape(bits_shape + (part_inner, up_w.shape[2]))
+        grad_up = grad_up.reshape(peers, part_inner, up_w.shape[2]).astype(jnp.bfloat16)
+        grad_up = lax.all_to_all(grad_up, "ex", 0, 0, tiled=True)
+        grad_up = jnp.sum(grad_up.astype(jnp.float32), axis=0)
         for stage in range(levels):
             if stage == 1:
                 grad_down = jnp.where(second_core, swap_bit_axes(grad_down, 2, levels), grad_down)
-                grad_up = jnp.where(second_core, swap_bit_axes(grad_up, 0, levels), grad_up)
             bits_of = (orders[0][stage], orders[1][stage])
             pairs = stage_pairs(bits_of, peers)
             bit = jnp.where(second_core, bits_of[1], bits_of[0])
             grad_down = halve_sum(grad_down, 2 + levels - 1 - stage, bit, pairs, place)
-            grad_up = halve_sum(grad_up, levels - 1 - stage, bit, pairs, place)
         squares = jnp.sum(grad_down * grad_down) + jnp.sum(grad_up * grad_up)
         totals = jnp.stack([squares, loss_sum])
         spread = jnp.broadcast_to(totals[None, :], (peers, totals.shape[0]))
@@ -180,16 +180,16 @@
         if update_round + 1 < TRAIN_STEPS:
             down_low = down_own.astype(jnp.bfloat16)
             upper_low = up_own.astype(jnp.bfloat16)
+            upper_low = jnp.broadcast_to(upper_low[None], (peers,) + upper_low.shape)
+            upper_low = lax.all_to_all(upper_low, "ex", 0, 0, tiled=True)
             for step_index in range(levels):
                 stage = levels - 1 - step_index
                 if stage == 0:
                     down_low = jnp.where(second_core, swap_bit_axes(down_low, 2, levels), down_low)
-                    upper_low = jnp.where(second_core, swap_bit_axes(upper_low, 0, levels), upper_low)
                 bits_of = (orders[0][stage], orders[1][stage])
                 pairs = stage_pairs(bits_of, peers)
                 bit = jnp.where(second_core, bits_of[1], bits_of[0])
                 down_low = double_join(down_low, 2 + step_index, bit, pairs, place)
-                upper_low = double_join(upper_low, step_index, bit, pairs, place)
             down_low = down_low.reshape(down_w.shape[1:])
             upper_low = upper_low.reshape(up_w.shape[1:])
     return (down_own[None], up_own[None], jnp.stack(collected)[None])

time: 250 us -> 268 us (1.072)
  other arithmetic: 25.6 us -> 32.4 us
  waiting for transfers between devices: 91.2 us -> 96.8 us
  local copies, waits for them, and re-layouts: 27.4 us -> 32.5 us
    ppermute x30 -> x15, starting transfers between devices: 37.8 us -> 21 us  [partner_swap(): return lax.ppermute(value, 'ex', perm=pairs)]
    all_to_all x0 -> x3, starting transfers between devices: none -> 16.6 us  [the longest x2 11.6 us: shards(): grad_up = lax.all_to_all(grad_up, 'ex', 0, 0, tiled=True)]
    all_to_all x0 -> x3, waiting for transfers between devices: none -> 11.4 us  [the longest x2 11.4 us: shards(): grad_up = lax.all_to_all(grad_up, 'ex', 0, 0, tiled=True)]
    ppermute x30 -> x15, waiting for transfers between devices: 60.9 us -> 55.2 us  [partner_swap(): return lax.ppermute(value, 'ex', perm=pairs)]
    unnamed x70 -> x84, local copies, waits for them, and re-layouts: 14.1 us -> 18.7 us
    add x12 -> x6, other arithmetic: 0.73 us -> 4.19 us  [halve_sum(): return keep + sent.astype(jnp.float32)]
    dot_general x20, matrix products: 17.1 us -> 14.2 us  [contract_rows(): lax.dot_general(left, right, (((0,), (0,)), ((), ())), preferred_element_...]
  transfers between devices with their start and end apart: 34 -> 22, of which waited for: 20 -> 16; matrix products, arithmetic and copies ran while one was open for 9% -> 10% of each run, Pallas kernels for 0% -> 0%
where the time goes in v11:
time: 268 us; the launch traced here: 263 us
  waiting for transfers between devices  96.8 us (36%)
  starting transfers between devices  55.3 us (21%)
  matrix products  38 us (14%)
  local copies, waits for them, and re-layouts  32.5 us (12%)
  other arithmetic  32.4 us (12%)
  between operations  7.73 us (3%)
    ppermute x15, waiting for transfers between devices, partner_swap(): return lax.ppermute(value, 'ex', perm=pairs)  55.2 us
    ppermute x15, starting transfers between devices, partner_swap(): return lax.ppermute(value, 'ex', perm=pairs)  21 us
    unnamed x84, local copies, waits for them, and re-layouts  18.7 us
    all_to_all x1, waiting for transfers between devices, shards(): lax.all_to_all(send_feats, 'task', split_axis=0, concat_axis=0, tiled=True)  15.3 us
    dot_general x20, matrix products, contract_rows(): lax.dot_general(left, right, (((0,), (0,)), ((), ())), preferred_element_...  14.2 us
    all_to_all x2, waiting for transfers between devices, shards(): totals = jnp.sum(lax.all_to_all(spread, 'ex', 0, 0, tiled=True), axis=0)  14 us
    all_to_all x2, starting transfers between devices, shards(): grad_up = lax.all_to_all(grad_up, 'ex', 0, 0, tiled=True)  11.6 us
    dot_general x18, matrix products, train_pass(): jnp.dot(windows[offset_index], down_low[offset_index // 3, offset_index %...  11.5 us
  transfers between devices with their start and end apart: 22, of which 16 were waited for; matrix products, arithmetic and copies ran while one was open for 10% of the time, Pallas kernels for 0%

profile of v11, /device:TPU:0, one launch (start us, length us, event | category | flops | bytes accessed | tf_op | source)
XLA Modules:
  0.0 262.7 jit_solution(14493083039334110686)
XLA Ops:
  4.8 4.4 %all-to-all-start.1 = ((bf16[4,2,192]{2,1,0:T(2,128)(2,1)}), bf16[4,2,192]{2,1,0:T(2,128)(2,1)S(1)}, u32[]{:S(2)}, u32[]{:S(2)}) async-start(bf16[4,2,192]{2,1,0:T(2,128)(2,1)} %reshape.203), calls=%async_computation.1 | async-start | bytes 8192 | tf_op jit(solution)/shard_map/all_to_all | solution.py:138
  10.5 2.9 %scatter_fusion = bf16[4,6,8,8,512]{4,3,2,1,0:T(8,128)(2,1)} fusion(bf16[4,6,8,8,512]{4,3,2,1,0:T(8,128)(2,1)} %broadcast_in_dim.18, s32[12]{0:T(128)S(1)} %fusion.74, bf16[12,8,8,512]{3,2,1,0:T(8,128)(2,1)S(1)} %copy-done.39), kind=kCustom, calls=%fused_computation | custom fusion | bytes 2359392 | tf_op jit(solution)/shard_map/scatter | solution.py:129
  14.5 3.8 %all-to-all-start = ((bf16[4,6,8,8,512]{4,3,2,1,0:T(8,128)(2,1)}), bf16[4,6,8,8,512]{4,3,2,1,0:T(8,128)(2,1)S(1)}, u32[]{:S(2)}, u32[]{:S(2)}) async-start(bf16[4,6,8,8,512]{4,3,2,1,0:T(8,128)(2,1)} %scatter_fusion), calls=%async_computation | async-start | bytes 3145728 | tf_op jit(solution)/shard_map/all_to_all | solution.py:137
  18.9 4.0 %convert_bitcast_fusion = bf16[3,3,512,256]{3,2,1,0:T(8,128)(2,1)} fusion(f32[1,3,3,512,256]{4,3,2,1,0:T(8,128)} %param.11), kind=kLoop, calls=%fused_computation.51 | loop fusion | flops 1179648 | bytes 7077888 | tf_op jit(solution)/shard_map/convert_element_type | solution.py:149
  23.1 15.3 %all-to-all-done = bf16[4,6,8,8,512]{4,3,2,1,0:T(8,128)(2,1)S(1)} async-done(((bf16[4,6,8,8,512]{4,3,2,1,0:T(8,128)(2,1)}), bf16[4,6,8,8,512]{4,3,2,1,0:T(8,128)(2,1)S(1)}, u32[]{:S(2)}, u32[]{:S(2)}) %all-to-all-start) | async-done | bytes 1572896 | tf_op jit(solution)/shard_map/all_to_all | solution.py:137
  39.1 2.6 pad_slice_fusion
  59.2 2.1 copy-done.25
  62.6 3.1 %collective-permute-done = bf16[3,3,2,2,2,2,16,256]{7,6,1,0,2,3,4,5:T(8,128)(2,1)S(1)} collective-permute-done((bf16[3,3,2,2,2,2,16,256]{7,6,1,0,2,3,4,5:T(8,128)(2,1)}, bf16[3,3,2,2,2,2,16,256]{7,6,1,0,2,3,4,5:T(8,128)(2,1)S(1)}, u32[]{:S(2)}, u32[]{:S(2)}) %collective-permute-start) | collective-permute-done | bytes 1179680 | tf_op jit(solution)/shard_map/ppermute | solution.py:85
  65.6 3.1 %copy_select_fusion.1 = f32[3,3,2,2,2,2,16,256]{7,6,1,0,2,3,4,5:T(8,128)S(1)} fusion(bf16[3,3,2,2,2,2,16,256]{7,6,1,0,2,3,4,5:T(8,128)(2,1)S(1)} %collective-permute-done, pred[]{:T(512)S(6)} %eq.26, f32[3,3,2,2,2,2,2,16,256]{8,7,6,5,4,3,2,1,0:T(8,128)} %bitcast.418, s32[]{:T(128)S(6)} %select_n.178), kind=kLoop, calls=%fused_computation.50 | loop fusion | flops 2949120 | bytes 9438720 | tf_op jit(solution)/shard_map/jit(_where)/select_n | solution.py:167
  72.0 8.2 %collective-permute-done.1 = bf16[3,3,2,2,2,16,256]{6,5,1,0,2,3,4:T(8,128)(2,1)S(1)} collective-permute-done((bf16[3,3,2,2,2,16,256]{6,5,1,0,2,3,4:T(8,128)(2,1)S(1)}, bf16[3,3,2,2,2,16,256]{6,5,1,0,2,3,4:T(8,128)(2,1)S(1)}, u32[]{:S(2)}, u32[]{:S(2)}) %collective-permute-start.1) | collective-permute-done | bytes 589856 | tf_op jit(solution)/shard_map/ppermute | solution.py:85
  81.7 3.3 %collective-permute-start.2 = (bf16[3,3,2,2,16,256]{5,4,1,0,2,3:T(8,128)(2,1)S(1)}, bf16[3,3,2,2,16,256]{5,4,1,0,2,3:T(8,128)(2,1)}, u32[]{:S(2)}, u32[]{:S(2)}) collective-permute-start(bf16[3,3,2,2,16,256]{5,4,1,0,2,3:T(8,128)(2,1)S(1)} %fusion.37), channel_id=1, source_target_pairs={{0,4},{1,17},{2,6},{3,19},{4,0},{5,21},{6,2},{7,23},{8,12},{9,25},... | collective-permute-start | bytes 884744 | tf_op jit(solution)/shard_map/ppermute | solution.py:85
  86.4 6.3 %all-to-all-start.2 = ((bf16[32,8,512]{2,1,0:T(8,128)(2,1)}), bf16[32,8,512]{2,1,0:T(8,128)(2,1)}, u32[]{:S(2)}, u32[]{:S(2)}) async-start(bf16[32,8,512]{2,1,0:T(8,128)(2,1)} %fusion.32), calls=%async_computation.2 | async-start | bytes 524288 | tf_op jit(solution)/shard_map/all_to_all | solution.py:163
  96.2 5.2 %all-to-all-done.2 = bf16[32,8,512]{2,1,0:T(8,128)(2,1)} async-done(((bf16[32,8,512]{2,1,0:T(8,128)(2,1)}), bf16[32,8,512]{2,1,0:T(8,128)(2,1)}, u32[]{:S(2)}, u32[]{:S(2)}) %all-to-all-start.2) | async-done | bytes 262176 | tf_op jit(solution)/shard_map/all_to_all | solution.py:163
  104.6 3.9 %collective-permute-done.4 = bf16[3,3,16,256]{3,2,1,0:T(8,128)(2,1)S(1)} collective-permute-done((bf16[3,3,16,256]{3,2,1,0:T(8,128)(2,1)S(1)}, bf16[3,3,16,256]{3,2,1,0:T(8,128)(2,1)S(1)}, u32[]{:S(2)}, u32[]{:S(2)}) %collective-permute-start.4) | collective-permute-done | bytes 73760 | tf_op jit(solution)/shard_map/ppermute | solution.py:85
  111.7 4.3 %all-to-all-start.3 = ((f32[32,1,2]{2,1,0:T(1,128)}), f32[32,1,2]{2,1,0:T(1,128)S(1)}, u32[]{:S(2)}, u32[]{:S(2)}) async-start(f32[32,1,2]{2,1,0:T(1,128)} %broadcast_in_dim.21), calls=%async_computation.3 | async-start | bytes 32768 | tf_op jit(solution)/shard_map/all_to_all | solution.py:175
  116.0 7.3 %all-to-all-done.3 = f32[32,1,2]{2,1,0:T(1,128)S(1)} async-done(((f32[32,1,2]{2,1,0:T(1,128)}), f32[32,1,2]{2,1,0:T(1,128)S(1)}, u32[]{:S(2)}, u32[]{:S(2)}) %all-to-all-start.3) | async-done | bytes 288 | tf_op jit(solution)/shard_map/all_to_all | solution.py:175
  126.9 4.6 %collective-permute-done.5 = bf16[3,3,16,256]{3,2,1,0:T(8,128)(2,1)S(1)} collective-permute-done((bf16[3,3,16,256]{3,2,1,0:T(8,128)(2,1)S(1)}, bf16[3,3,16,256]{3,2,1,0:T(8,128)(2,1)S(1)}, u32[]{:S(2)}, u32[]{:S(2)}) %collective-permute-start.5) | collective-permute-done | bytes 73760 | tf_op jit(solution)/shard_map/ppermute | solution.py:85
  132.3 4.5 %collective-permute-done.6 = bf16[3,3,2,16,256]{4,3,2,1,0:T(8,128)(2,1)S(1)} collective-permute-done((bf16[3,3,2,16,256]{4,3,2,1,0:T(8,128)(2,1)S(1)}, bf16[3,3,2,16,256]{4,3,2,1,0:T(8,128)(2,1)S(1)}, u32[]{:S(2)}, u32[]{:S(2)}) %collective-permute-start.6) | collective-permute-done | bytes 147488 | tf_op jit(solution)/shard_map/ppermute | solution.py:85
  138.1 7.1 %collective-permute-done.7 = bf16[3,3,2,2,16,256]{5,4,3,2,1,0:T(8,128)(2,1)S(1)} collective-permute-done((bf16[3,3,2,2,16,256]{5,4,3,2,1,0:T(8,128)(2,1)S(1)}, bf16[3,3,2,2,16,256]{5,4,3,2,1,0:T(8,128)(2,1)S(1)}, u32[]{:S(2)}, u32[]{:S(2)}) %collective-permute-start.7) | collective-permute-done | bytes 294944 | tf_op jit(solution)/shard_map/ppermute | solution.py:85
  146.0 9.4 %collective-permute-done.8 = bf16[3,3,2,2,2,16,256]{6,5,4,3,2,1,0:T(8,128)(2,1)} collective-permute-done((bf16[3,3,2,2,2,16,256]{6,5,4,3,2,1,0:T(8,128)(2,1)S(1)}, bf16[3,3,2,2,2,16,256]{6,5,4,3,2,1,0:T(8,128)(2,1)}, u32[]{:S(2)}, u32[]{:S(2)}) %collective-permute-start.8) | collective-permute-done | bytes 589856 | tf_op jit(solution)/shard_map/ppermute | solution.py:85
  159.5 5.0 %all-to-all-start.4 = ((bf16[32,8,512]{2,1,0:T(8,128)(2,1)}), bf16[32,8,512]{2,1,0:T(8,128)(2,1)}, u32[]{:S(2)}, u32[]{:S(2)}) async-start(bf16[32,8,512]{2,1,0:T(8,128)(2,1)} %broadcast_in_dim.23), calls=%async_computation.4 | async-start | bytes 524288 | tf_op jit(solution)/shard_map/all_to_all | solution.py:184
  164.5 2.1 select_bitcast_fusion.1
  180.2 2.8 %multiply_reduce_fusion.1 = (f32[1536]{0:T(1024)S(1)}, f32[1536,512]{0,1:T(8,128)S(1)}) fusion(bf16[32,8,512]{2,1,0:T(8,128)(2,1)} %all-to-all-done.4, f32[1536,256]{1,0:T(8,128)} %convolution_add_fusion, bf16[1536,512]{0,1:T(8,128)(2,1)} %copy-done.34), kind=kOutput, calls=%fused_computation.14 | convolution fusion | flops 407763456 | bytes 6559744 | tf_op jit(solution)/shard_map/dot_general | solution.py:41
  187.4 2.1 fusion.7
  200.4 2.5 collective-permute-done.10
  206.7 8.2 %collective-permute-done.11 = bf16[3,3,2,2,2,16,256]{6,5,1,0,2,3,4:T(8,128)(2,1)S(1)} collective-permute-done((bf16[3,3,2,2,2,16,256]{6,5,1,0,2,3,4:T(8,128)(2,1)S(1)}, bf16[3,3,2,2,2,16,256]{6,5,1,0,2,3,4:T(8,128)(2,1)S(1)}, u32[]{:S(2)}, u32[]{:S(2)}) %collective-permute-start.11) | collective-permute-done | bytes 589856 | tf_op jit(solution)/shard_map/ppermute | solution.py:85
  216.4 3.2 %collective-permute-start.12 = (bf16[3,3,2,2,16,256]{5,4,1,0,2,3:T(8,128)(2,1)S(1)}, bf16[3,3,2,2,16,256]{5,4,1,0,2,3:T(8,128)(2,1)S(1)}, u32[]{:S(2)}, u32[]{:S(2)}) collective-permute-start(bf16[3,3,2,2,16,256]{5,4,1,0,2,3:T(8,128)(2,1)S(1)} %fusion.38), channel_id=1, source_target_pairs={{0,4},{1,17},{2,6},{3,19},{4,0},{5,21},{6,2},{7,23},{8,12},{9,25},... | collective-permute-start | bytes 884744 | tf_op jit(solution)/shard_map/ppermute | solution.py:85
  221.0 5.3 %all-to-all-start.5 = ((bf16[32,8,512]{2,1,0:T(8,128)(2,1)}), bf16[32,8,512]{2,1,0:T(8,128)(2,1)S(1)}, u32[]{:S(2)}, u32[]{:S(2)}) async-start(bf16[32,8,512]{2,1,0:T(8,128)(2,1)} %fusion.33), calls=%async_computation.5 | async-start | bytes 524288 | tf_op jit(solution)/shard_map/all_to_all | solution.py:163
  229.0 6.1 %all-to-all-done.5 = bf16[32,8,512]{2,1,0:T(8,128)(2,1)S(1)} async-done(((bf16[32,8,512]{2,1,0:T(8,128)(2,1)}), bf16[32,8,512]{2,1,0:T(8,128)(2,1)S(1)}, u32[]{:S(2)}, u32[]{:S(2)}) %all-to-all-start.5) | async-done | bytes 262176 | tf_op jit(solution)/shard_map/all_to_all | solution.py:163
  237.6 3.6 %collective-permute-done.14 = bf16[3,3,16,256]{3,2,1,0:T(8,128)(2,1)S(1)} collective-permute-done((bf16[3,3,16,256]{3,2,1,0:T(8,128)(2,1)S(1)}, bf16[3,3,16,256]{3,2,1,0:T(8,128)(2,1)S(1)}, u32[]{:S(2)}, u32[]{:S(2)}) %collective-permute-start.14) | collective-permute-done | bytes 73760 | tf_op jit(solution)/shard_map/ppermute | solution.py:85
  244.5 5.2 %all-to-all-start.6 = ((f32[32,1,2]{2,1,0:T(1,128)}), f32[32,1,2]{2,1,0:T(1,128)S(1)}, u32[]{:S(2)}, u32[]{:S(2)}) async-start(f32[32,1,2]{2,1,0:T(1,128)} %broadcast_in_dim.24), calls=%async_computation.6 | async-start | bytes 32768 | tf_op jit(solution)/shard_map/all_to_all | solution.py:175
  250.4 6.7 %all-to-all-done.6 = f32[32,1,2]{2,1,0:T(1,128)S(1)} async-done(((f32[32,1,2]{2,1,0:T(1,128)}), f32[32,1,2]{2,1,0:T(1,128)S(1)}, u32[]{:S(2)}, u32[]{:S(2)}) %all-to-all-start.6) | async-done | bytes 288 | tf_op jit(solution)/shard_map/all_to_all | solution.py:175
  (216 shorter events, 96.7 us)
Async XLA Ops:
  0.6 47.8 %copy-start = (bf16[512,10]{0,1:T(8,128)(2,1)S(1)}, bf16[512,10]{0,1:T(8,128)(2,1)}, u32[]{:S(2)}) copy-start(bf16[512,10]{0,1:T(8,128)(2,1)} %param.13) | copy-start | bytes 30724
  4.8 9.7 %all-to-all-start.1 = ((bf16[4,2,192]{2,1,0:T(2,128)(2,1)}), bf16[4,2,192]{2,1,0:T(2,128)(2,1)S(1)}, u32[]{:S(2)}, u32[]{:S(2)}) async-start(bf16[4,2,192]{2,1,0:T(2,128)(2,1)} %reshape.203), calls=%async_computation.1 | async-start | bytes 8192 | tf_op jit(solution)/shard_map/all_to_all | solution.py:138
  14.5 23.9 %all-to-all-start = ((bf16[4,6,8,8,512]{4,3,2,1,0:T(8,128)(2,1)}), bf16[4,6,8,8,512]{4,3,2,1,0:T(8,128)(2,1)S(1)}, u32[]{:S(2)}, u32[]{:S(2)}) async-start(bf16[4,6,8,8,512]{4,3,2,1,0:T(8,128)(2,1)} %scatter_fusion), calls=%async_computation | async-start | bytes 3145728 | tf_op jit(solution)/shard_map/all_to_all | solution.py:137
  41.8 13.4 %copy-start.12 = (bf16[24,8,8,512]{3,2,1,0:T(8,128)(2,1)}, bf16[24,8,8,512]{3,2,1,0:T(8,128)(2,1)S(1)}, u32[]{:S(2)}) copy-start(bf16[24,8,8,512]{3,2,1,0:T(8,128)(2,1)S(1)} %get-tuple-element.12) | copy-start | bytes 4718596
  41.8 14.9 %copy-start.9 = (bf16[24,8,8,512]{3,2,1,0:T(8,128)(2,1)}, bf16[24,8,8,512]{3,2,1,0:T(8,128)(2,1)S(1)}, u32[]{:S(2)}) copy-start(bf16[24,8,8,512]{3,2,1,0:T(8,128)(2,1)S(1)} %get-tuple-element.13) | copy-start | bytes 4718596
  41.8 15.5 %copy-start.6 = (bf16[24,8,8,512]{3,2,1,0:T(8,128)(2,1)}, bf16[24,8,8,512]{3,2,1,0:T(8,128)(2,1)S(1)}, u32[]{:S(2)}) copy-start(bf16[24,8,8,512]{3,2,1,0:T(8,128)(2,1)S(1)} %get-tuple-element.14) | copy-start | bytes 4718596
  41.8 16.2 %copy-start.3 = (bf16[24,8,8,512]{3,2,1,0:T(8,128)(2,1)}, bf16[24,8,8,512]{3,2,1,0:T(8,128)(2,1)S(1)}, u32[]{:S(2)}) copy-start(bf16[24,8,8,512]{3,2,1,0:T(8,128)(2,1)S(1)} %get-tuple-element.15) | copy-start | bytes 4718596
  41.8 16.8 %copy-start.1 = (bf16[24,8,8,512]{3,2,1,0:T(8,128)(2,1)}, bf16[24,8,8,512]{3,2,1,0:T(8,128)(2,1)S(1)}, u32[]{:S(2)}) copy-start(bf16[24,8,8,512]{3,2,1,0:T(8,128)(2,1)S(1)} %get-tuple-element.9) | copy-start | bytes 4718596
  62.6 3.1 %collective-permute-start = (bf16[3,3,2,2,2,2,16,256]{7,6,1,0,2,3,4,5:T(8,128)(2,1)}, bf16[3,3,2,2,2,2,16,256]{7,6,1,0,2,3,4,5:T(8,128)(2,1)S(1)}, u32[]{:S(2)}, u32[]{:S(2)}) collective-permute-start(bf16[3,3,2,2,2,2,16,256]{7,6,1,0,2,3,4,5:T(8,128)(2,1)} %fusion.30), channel_id=1, source_target_pairs={{0,1},{1,0},{2,3},{3,2},{4,5},{5,4},{6,7},{7,6},{8,9},{9,8},{10,11... | collective-permute-start | bytes 3538952 | tf_op jit(solution)/shard_map/ppermute | solution.py:85
  70.2 10.0 %collective-permute-start.1 = (bf16[3,3,2,2,2,16,256]{6,5,1,0,2,3,4:T(8,128)(2,1)S(1)}, bf16[3,3,2,2,2,16,256]{6,5,1,0,2,3,4:T(8,128)(2,1)S(1)}, u32[]{:S(2)}, u32[]{:S(2)}) collective-permute-start(bf16[3,3,2,2,2,16,256]{6,5,1,0,2,3,4:T(8,128)(2,1)S(1)} %fusion.35), channel_id=1, source_target_pairs={{0,2},{1,9},{2,0},{3,11},{4,6},{5,13},{6,4},{7,15},{8,10},{9,1},{1... | collective-permute-start | bytes 1769480 | tf_op jit(solution)/shard_map/ppermute | solution.py:85
  72.0 13.1 %copy-start.31 = (f32[1536,256]{1,0:T(8,128)S(1)}, f32[1536,256]{1,0:T(8,128)}, u32[]{:S(2)}) copy-start(f32[1536,256]{1,0:T(8,128)} %copy-done.30) | copy-start | bytes 4718596
  72.0 13.1 %copy-start.36 = (bf16[1536,512]{0,1:T(8,128)(2,1)S(1)}, bf16[1536,512]{0,1:T(8,128)(2,1)}, u32[]{:S(2)}) copy-start(bf16[1536,512]{0,1:T(8,128)(2,1)} %copy-done.35) | copy-start | bytes 4718596
  81.7 11.0 %collective-permute-start.2 = (bf16[3,3,2,2,16,256]{5,4,1,0,2,3:T(8,128)(2,1)S(1)}, bf16[3,3,2,2,16,256]{5,4,1,0,2,3:T(8,128)(2,1)}, u32[]{:S(2)}, u32[]{:S(2)}) collective-permute-start(bf16[3,3,2,2,16,256]{5,4,1,0,2,3:T(8,128)(2,1)S(1)} %fusion.37), channel_id=1, source_target_pairs={{0,4},{1,17},{2,6},{3,19},{4,0},{5,21},{6,2},{7,23},{8,12},{9,25},... | collective-permute-start | bytes 884744 | tf_op jit(solution)/shard_map/ppermute | solution.py:85
  86.4 15.1 %all-to-all-start.2 = ((bf16[32,8,512]{2,1,0:T(8,128)(2,1)}), bf16[32,8,512]{2,1,0:T(8,128)(2,1)}, u32[]{:S(2)}, u32[]{:S(2)}) async-start(bf16[32,8,512]{2,1,0:T(8,128)(2,1)} %fusion.32), calls=%async_computation.2 | async-start | bytes 524288 | tf_op jit(solution)/shard_map/all_to_all | solution.py:163
  93.8 8.7 %collective-permute-start.3 = (bf16[3,3,2,16,256]{4,3,1,0,2:T(8,128)(2,1)S(1)}, bf16[3,3,2,16,256]{4,3,1,0,2:T(8,128)(2,1)S(1)}, u32[]{:S(2)}, u32[]{:S(2)}) collective-permute-start(bf16[3,3,2,16,256]{4,3,1,0,2:T(8,128)(2,1)S(1)} %fusion.45), channel_id=1, source_target_pairs={{0,8},{1,3},{2,10},{3,1},{4,12},{5,7},{6,14},{7,5},{8,0},{9,11},{1... | collective-permute-start | bytes 442376 | tf_op jit(solution)/shard_map/ppermute | solution.py:85
  102.5 42.7 %copy-start.28 = (f32[3,3,2,16,256]{4,3,1,0,2:T(8,128)}, f32[3,3,2,16,256]{4,3,1,0,2:T(8,128)S(1)}, u32[]{:S(2)}) copy-start(f32[3,3,2,16,256]{4,3,1,0,2:T(8,128)S(1)} %bitcast_add_fusion.7) | copy-start | bytes 884740
  102.5 5.9 %collective-permute-start.4 = (bf16[3,3,16,256]{3,2,1,0:T(8,128)(2,1)S(1)}, bf16[3,3,16,256]{3,2,1,0:T(8,128)(2,1)S(1)}, u32[]{:S(2)}, u32[]{:S(2)}) collective-permute-start(bf16[3,3,16,256]{3,2,1,0:T(8,128)(2,1)S(1)} %fusion.61), channel_id=1, source_target_pairs={{0,16},{1,5},{2,18},{3,7},{4,20},{5,1},{6,22},{7,3},{8,24},{9,13},... | collective-permute-start | bytes 221192 | tf_op jit(solution)/shard_map/ppermute | solution.py:85
  111.7 11.6 %all-to-all-start.3 = ((f32[32,1,2]{2,1,0:T(1,128)}), f32[32,1,2]{2,1,0:T(1,128)S(1)}, u32[]{:S(2)}, u32[]{:S(2)}) async-start(f32[32,1,2]{2,1,0:T(1,128)} %broadcast_in_dim.21), calls=%async_computation.3 | async-start | bytes 32768 | tf_op jit(solution)/shard_map/all_to_all | solution.py:175
  125.6 5.9 %collective-permute-start.5 = (bf16[3,3,16,256]{3,2,1,0:T(8,128)(2,1)S(1)}, bf16[3,3,16,256]{3,2,1,0:T(8,128)(2,1)S(1)}, u32[]{:S(2)}, u32[]{:S(2)}) collective-permute-start(bf16[3,3,16,256]{3,2,1,0:T(8,128)(2,1)S(1)} %fusion.75), channel_id=1, source_target_pairs={{0,16},{1,5},{2,18},{3,7},{4,20},{5,1},{6,22},{7,3},{8,24},{9,13},... | collective-permute-start | bytes 221192 | tf_op jit(solution)/shard_map/ppermute | solution.py:85
  131.6 5.2 %collective-permute-start.6 = (bf16[3,3,2,16,256]{4,3,2,1,0:T(8,128)(2,1)S(1)}, bf16[3,3,2,16,256]{4,3,2,1,0:T(8,128)(2,1)S(1)}, u32[]{:S(2)}, u32[]{:S(2)}) collective-permute-start(bf16[3,3,2,16,256]{4,3,2,1,0:T(8,128)(2,1)S(1)} %pad_maximum_fusion.4), channel_id=1, source_target_pairs={{0,8},{1,3},{2,10},{3,1},{4,12},{5,7},{6,14},{7,5},{8,0},{9,11},{1... | collective-permute-start | bytes 442376 | tf_op jit(solution)/shard_map/ppermute | solution.py:85
  136.9 8.3 %collective-permute-start.7 = (bf16[3,3,2,2,16,256]{5,4,3,2,1,0:T(8,128)(2,1)S(1)}, bf16[3,3,2,2,16,256]{5,4,3,2,1,0:T(8,128)(2,1)S(1)}, u32[]{:S(2)}, u32[]{:S(2)}) collective-permute-start(bf16[3,3,2,2,16,256]{5,4,3,2,1,0:T(8,128)(2,1)S(1)} %pad_maximum_fusion.3), channel_id=1, source_target_pairs={{0,4},{1,17},{2,6},{3,19},{4,0},{5,21},{6,2},{7,23},{8,12},{9,25},... | collective-permute-start | bytes 884744 | tf_op jit(solution)/shard_map/ppermute | solution.py:85
  145.3 10.1 %collective-permute-start.8 = (bf16[3,3,2,2,2,16,256]{6,5,4,3,2,1,0:T(8,128)(2,1)S(1)}, bf16[3,3,2,2,2,16,256]{6,5,4,3,2,1,0:T(8,128)(2,1)}, u32[]{:S(2)}, u32[]{:S(2)}) collective-permute-start(bf16[3,3,2,2,2,16,256]{6,5,4,3,2,1,0:T(8,128)(2,1)S(1)} %pad_maximum_fusion.2), channel_id=1, source_target_pairs={{0,2},{1,9},{2,0},{3,11},{4,6},{5,13},{6,4},{7,15},{8,10},{9,1},{1... | collective-permute-start | bytes 1769480 | tf_op jit(solution)/shard_map/ppermute | solution.py:85
  158.0 6.5 %collective-permute-start.9 = (bf16[3,3,2,2,2,2,16,256]{7,6,5,4,3,2,1,0:T(8,128)(2,1)}, bf16[3,3,2,2,2,2,16,256]{7,6,5,4,3,2,1,0:T(8,128)(2,1)}, u32[]{:S(2)}, u32[]{:S(2)}) collective-permute-start(bf16[3,3,2,2,2,2,16,256]{7,6,5,4,3,2,1,0:T(8,128)(2,1)} %copy_select_fusion.2), channel_id=1, source_target_pairs={{0,1},{1,0},{2,3},{3,2},{4,5},{5,4},{6,7},{7,6},{8,9},{9,8},{10,11... | collective-permute-start | bytes 3538952 | tf_op jit(solution)/shard_map/ppermute | solution.py:85
  159.5 20.7 %all-to-all-start.4 = ((bf16[32,8,512]{2,1,0:T(8,128)(2,1)}), bf16[32,8,512]{2,1,0:T(8,128)(2,1)}, u32[]{:S(2)}, u32[]{:S(2)}) async-start(bf16[32,8,512]{2,1,0:T(8,128)(2,1)} %broadcast_in_dim.23), calls=%async_computation.4 | async-start | bytes 524288 | tf_op jit(solution)/shard_map/all_to_all | solution.py:184
  200.0 2.9 %collective-permute-start.10 = (bf16[3,3,2,2,2,2,16,256]{7,6,1,0,2,3,4,5:T(8,128)(2,1)S(1)}, bf16[3,3,2,2,2,2,16,256]{7,6,1,0,2,3,4,5:T(8,128)(2,1)S(1)}, u32[]{:S(2)}, u32[]{:S(2)}) collective-permute-start(bf16[3,3,2,2,2,2,16,256]{7,6,1,0,2,3,4,5:T(8,128)(2,1)S(1)} %fusion.31), channel_id=1, source_target_pairs={{0,1},{1,0},{2,3},{3,2},{4,5},{5,4},{6,7},{7,6},{8,9},{9,8},{10,11... | collective-permute-start | bytes 3538952 | tf_op jit(solution)/shard_map/ppermute | solution.py:85
  204.9 10.0 %collective-permute-start.11 = (bf16[3,3,2,2,2,16,256]{6,5,1,0,2,3,4:T(8,128)(2,1)S(1)}, bf16[3,3,2,2,2,16,256]{6,5,1,0,2,3,4:T(8,128)(2,1)S(1)}, u32[]{:S(2)}, u32[]{:S(2)}) collective-permute-start(bf16[3,3,2,2,2,16,256]{6,5,1,0,2,3,4:T(8,128)(2,1)S(1)} %fusion.36), channel_id=1, source_target_pairs={{0,2},{1,9},{2,0},{3,11},{4,6},{5,13},{6,4},{7,15},{8,10},{9,1},{1... | collective-permute-start | bytes 1769480 | tf_op jit(solution)/shard_map/ppermute | solution.py:85
  216.4 9.9 %collective-permute-start.12 = (bf16[3,3,2,2,16,256]{5,4,1,0,2,3:T(8,128)(2,1)S(1)}, bf16[3,3,2,2,16,256]{5,4,1,0,2,3:T(8,128)(2,1)S(1)}, u32[]{:S(2)}, u32[]{:S(2)}) collective-permute-start(bf16[3,3,2,2,16,256]{5,4,1,0,2,3:T(8,128)(2,1)S(1)} %fusion.38), channel_id=1, source_target_pairs={{0,4},{1,17},{2,6},{3,19},{4,0},{5,21},{6,2},{7,23},{8,12},{9,25},... | collective-permute-start | bytes 884744 | tf_op jit(solution)/shard_map/ppermute | solution.py:85
  221.0 14.1 %all-to-all-start.5 = ((bf16[32,8,512]{2,1,0:T(8,128)(2,1)}), bf16[32,8,512]{2,1,0:T(8,128)(2,1)S(1)}, u32[]{:S(2)}, u32[]{:S(2)}) async-start(bf16[32,8,512]{2,1,0:T(8,128)(2,1)} %fusion.33), calls=%async_computation.5 | async-start | bytes 524288 | tf_op jit(solution)/shard_map/all_to_all | solution.py:163
  226.4 34.6 %copy-start.29 = (f32[3,3,2,16,256]{4,3,1,0,2:T(8,128)S(1)}, f32[3,3,2,16,256]{4,3,1,0,2:T(8,128)}, u32[]{:S(2)}) copy-start(f32[3,3,2,16,256]{4,3,1,0,2:T(8,128)} %copy-done.28) | copy-start | bytes 884740
  226.5 8.7 %collective-permute-start.13 = (bf16[3,3,2,16,256]{4,3,1,0,2:T(8,128)(2,1)S(1)}, bf16[3,3,2,16,256]{4,3,1,0,2:T(8,128)(2,1)S(1)}, u32[]{:S(2)}, u32[]{:S(2)}) collective-permute-start(bf16[3,3,2,16,256]{4,3,1,0,2:T(8,128)(2,1)S(1)} %fusion.46), channel_id=1, source_target_pairs={{0,8},{1,3},{2,10},{3,1},{4,12},{5,7},{6,14},{7,5},{8,0},{9,11},{1... | collective-permute-start | bytes 442376 | tf_op jit(solution)/shard_map/ppermute | solution.py:85
  235.3 5.9 %collective-permute-start.14 = (bf16[3,3,16,256]{3,2,1,0:T(8,128)(2,1)S(1)}, bf16[3,3,16,256]{3,2,1,0:T(8,128)(2,1)S(1)}, u32[]{:S(2)}, u32[]{:S(2)}) collective-permute-start(bf16[3,3,16,256]{3,2,1,0:T(8,128)(2,1)S(1)} %fusion.62), channel_id=1, source_target_pairs={{0,16},{1,5},{2,18},{3,7},{4,20},{5,1},{6,22},{7,3},{8,24},{9,13},... | collective-permute-start | bytes 221192 | tf_op jit(solution)/shard_map/ppermute | solution.py:85
  244.5 12.5 %all-to-all-start.6 = ((f32[32,1,2]{2,1,0:T(1,128)}), f32[32,1,2]{2,1,0:T(1,128)S(1)}, u32[]{:S(2)}, u32[]{:S(2)}) async-start(f32[32,1,2]{2,1,0:T(1,128)} %broadcast_in_dim.24), calls=%async_computation.6 | async-start | bytes 32768 | tf_op jit(solution)/shard_map/all_to_all | solution.py:175
  (31 other events, 119.9 us)

commit v12 on v8

--- a/solution.py
+++ b/solution.py
@@ -85,20 +85,35 @@
     return lax.ppermute(value, "ex", perm=pairs)
 
 
+STAGE_MASKS = (1, 2, 6, 8, 24)
+
+
 def stage_pairs(bits_of, peers):
-    return [(i, i ^ (1 << bits_of[i % 2])) for i in range(peers)]
-
-
-def halve_sum(value, axis, bit, pairs, place):
-    mine = (place >> bit) & 1
+    return [(i, i ^ STAGE_MASKS[bits_of[i % 2]]) for i in range(peers)]
+
+
+def stage_side(bit, place):
+    if bit in (1, 3):
+        return ((place >> bit) ^ (place >> (bit + 1))) & 1
+    return (place >> bit) & 1
+
+
+def gray_rows(value, lead):
+    for high in (lead, lead + 2):
+        low_half = lax.index_in_dim(value, 0, high, keepdims=True)
+        high_half = jnp.flip(lax.index_in_dim(value, 1, high, keepdims=True), axis=high + 1)
+        value = jnp.concatenate([low_half, high_half], axis=high)
+    return value
+
+
+def halve_sum(value, axis, mine, pairs, place):
     keep = lax.dynamic_index_in_dim(value, mine, axis, keepdims=False)
     give = lax.dynamic_index_in_dim(value, 1 - mine, axis, keepdims=False)
     sent = partner_swap(give.astype(jnp.bfloat16), pairs)
     return keep + sent.astype(jnp.float32)
 
 
-def double_join(value, axis, bit, pairs, place):
-    mine = (place >> bit) & 1
+def double_join(value, axis, mine, pairs, place):
     other = partner_swap(value, pairs)
     first = jnp.where(mine == 0, value, other)
     second = jnp.where(mine == 0, other, value)
@@ -162,11 +177,13 @@
         grad_up = grad_up.reshape(bits_shape + (part_inner, up_w.shape[2]))
         for stage in range(levels):
             if stage == 1:
+                grad_down = gray_rows(grad_down, 2)
+                grad_up = gray_rows(grad_up, 0)
                 grad_down = jnp.where(second_core, swap_bit_axes(grad_down, 2, levels), grad_down)
                 grad_up = jnp.where(second_core, swap_bit_axes(grad_up, 0, levels), grad_up)
             bits_of = (orders[0][stage], orders[1][stage])
             pairs = stage_pairs(bits_of, peers)
-            bit = jnp.where(second_core, bits_of[1], bits_of[0])
+            bit = jnp.where(second_core, stage_side(bits_of[1], place), stage_side(bits_of[0], place))
             grad_down = halve_sum(grad_down, 2 + levels - 1 - stage, bit, pairs, place)
             grad_up = halve_sum(grad_up, levels - 1 - stage, bit, pairs, place)
         squares = jnp.sum(grad_down * grad_down) + jnp.sum(grad_up * grad_up)
@@ -185,9 +202,11 @@
                 if stage == 0:
                     down_low = jnp.where(second_core, swap_bit_axes(down_low, 2, levels), down_low)
                     upper_low = jnp.where(second_core, swap_bit_axes(upper_low, 0, levels), upper_low)
+                    down_low = gray_rows(down_low, 2)
+                    upper_low = gray_rows(upper_low, 0)
                 bits_of = (orders[0][stage], orders[1][stage])
                 pairs = stage_pairs(bits_of, peers)
-                bit = jnp.where(second_core, bits_of[1], bits_of[0])
+                bit = jnp.where(second_core, stage_side(bits_of[1], place), stage_side(bits_of[0], place))
                 down_low = double_join(down_low, 2 + step_index, bit, pairs, place)
                 upper_low = double_join(upper_low, step_index, bit, pairs, place)
             down_low = down_low.reshape(down_w.shape[1:])

time: 250 us -> 281 us (1.12)
  other arithmetic: 25.6 us -> 51 us
  local copies, waits for them, and re-layouts: 27.4 us -> 44.1 us
  starting transfers between devices: 56.3 us -> 49 us
  matrix products: 36.6 us -> 32.6 us
    concatenate x0 -> x8, other arithmetic: none -> 11.7 us  [gray_rows(): value = jnp.concatenate([low_half, high_half], axis=high)]
    rev x0 -> x12, local copies, waits for them, and re-layouts: none -> 11.5 us  [gray_rows(): jnp.flip(lax.index_in_dim(value, 1, high, keepdims=True), axis=high + 1)]
    ppermute x30, starting transfers between devices: 37.8 us -> 31.6 us  [partner_swap(): return lax.ppermute(value, 'ex', perm=pairs)]
    add x12 -> x16, other arithmetic: 0.73 us -> 6.66 us  [halve_sum(): return keep + sent.astype(jnp.float32)]
    slice x0 -> x6, local copies, waits for them, and re-layouts: none -> 5.23 us  [gray_rows(): low_half = lax.index_in_dim(value, 0, high, keepdims=True)]
    another operation x18, other arithmetic: 3.79 us -> 8.98 us  [double_join(): return jnp.stack([first, second], axis=axis)]
    dot_general x20, matrix products: 17.1 us -> 13 us  [contract_rows(): lax.dot_general(left, right, (((0,), (0,)), ((), ())), preferred_element_...]
    unnamed x70 -> x86, local copies, waits for them, and re-layouts: 14.1 us -> 12.6 us
  transfers between devices with their start and end apart: 34 -> 34, of which waited for: 20 -> 22; matrix products, arithmetic and copies ran while one was open for 9% -> 12% of each run, Pallas kernels for 0% -> 0%
where the time goes in v12:
time: 281 us; the launch traced here: 275 us
  waiting for transfers between devices  90.6 us (32%)
  other arithmetic  51 us (18%)
  starting transfers between devices  49 us (17%)
  local copies, waits for them, and re-layouts  44.1 us (16%)
  matrix products  32.6 us (12%)
  between operations  8.22 us (3%)
    ppermute x30, waiting for transfers between devices, partner_swap(): return lax.ppermute(value, 'ex', perm=pairs)  60.4 us
    ppermute x30, starting transfers between devices, partner_swap(): return lax.ppermute(value, 'ex', perm=pairs)  31.6 us
    all_to_all x1, waiting for transfers between devices, shards(): lax.all_to_all(send_feats, 'task', split_axis=0, concat_axis=0, tiled=True)  15.3 us
    all_to_all x2, waiting for transfers between devices, shards(): totals = jnp.sum(lax.all_to_all(spread, 'ex', 0, 0, tiled=True), axis=0)  13.8 us
    dot_general x20, matrix products, contract_rows(): lax.dot_general(left, right, (((0,), (0,)), ((), ())), preferred_element_...  13 us
    unnamed x86, local copies, waits for them, and re-layouts  12.6 us
    concatenate x8, other arithmetic, gray_rows(): value = jnp.concatenate([low_half, high_half], axis=high)  11.7 us
    rev x12, local copies, waits for them, and re-layouts, gray_rows(): jnp.flip(lax.index_in_dim(value, 1, high, keepdims=True), axis=high + 1)  11.5 us
  transfers between devices with their start and end apart: 34, of which 22 were waited for; matrix products, arithmetic and copies ran while one was open for 12% of the time, Pallas kernels for 0%

profile of v12, /device:TPU:0, one launch (start us, length us, event | category | flops | bytes accessed | tf_op | source)
XLA Modules:
  0.0 275.4 jit_solution(7879482500087660561)
XLA Ops:
  4.8 4.4 %all-to-all-start.1 = ((bf16[4,2,192]{2,1,0:T(2,128)(2,1)}), bf16[4,2,192]{2,1,0:T(2,128)(2,1)S(1)}, u32[]{:S(2)}, u32[]{:S(2)}) async-start(bf16[4,2,192]{2,1,0:T(2,128)(2,1)} %reshape.198), calls=%async_computation.1 | async-start | bytes 8192 | tf_op jit(solution)/shard_map/all_to_all | solution.py:153
  10.5 2.9 %scatter_fusion = bf16[4,6,8,8,512]{4,3,2,1,0:T(8,128)(2,1)} fusion(bf16[4,6,8,8,512]{4,3,2,1,0:T(8,128)(2,1)} %broadcast_in_dim.16, s32[12]{0:T(128)S(1)} %fusion.89, bf16[12,8,8,512]{3,2,1,0:T(8,128)(2,1)S(1)} %copy-done.23), kind=kCustom, calls=%fused_computation | custom fusion | bytes 2359392 | tf_op jit(solution)/shard_map/scatter | solution.py:144
  14.5 3.8 %all-to-all-start = ((bf16[4,6,8,8,512]{4,3,2,1,0:T(8,128)(2,1)}), bf16[4,6,8,8,512]{4,3,2,1,0:T(8,128)(2,1)S(1)}, u32[]{:S(2)}, u32[]{:S(2)}) async-start(bf16[4,6,8,8,512]{4,3,2,1,0:T(8,128)(2,1)} %scatter_fusion), calls=%async_computation | async-start | bytes 3145728 | tf_op jit(solution)/shard_map/all_to_all | solution.py:152
  18.9 4.0 %convert_bitcast_fusion = bf16[3,3,512,256]{3,2,1,0:T(8,128)(2,1)} fusion(f32[1,3,3,512,256]{4,3,2,1,0:T(8,128)} %param.11), kind=kLoop, calls=%fused_computation.57 | loop fusion | flops 1179648 | bytes 7077888 | tf_op jit(solution)/shard_map/convert_element_type | solution.py:164
  23.1 15.3 %all-to-all-done = bf16[4,6,8,8,512]{4,3,2,1,0:T(8,128)(2,1)S(1)} async-done(((bf16[4,6,8,8,512]{4,3,2,1,0:T(8,128)(2,1)}), bf16[4,6,8,8,512]{4,3,2,1,0:T(8,128)(2,1)S(1)}, u32[]{:S(2)}, u32[]{:S(2)}) %all-to-all-start) | async-done | bytes 1572896 | tf_op jit(solution)/shard_map/all_to_all | solution.py:152
  40.0 2.5 pad_slice_fusion
  67.8 2.4 bitcast_add_fusion.1
  71.9 2.4 rev.44
  74.3 3.4 %fusion.33 = (f32[3,3,2,2,1,2,16,256]{7,6,1,0,2,3,4,5:T(8,128)}, f32[3,3,2,2,1,2,16,256]{7,6,1,0,2,3,4,5:T(8,128)}) fusion(f32[3,3,1,2,2,2,16,256]{7,6,1,0,2,3,4,5:T(8,128)} %get-tuple-element.15, f32[3,3,1,2,2,2,16,256]{7,6,1,0,2,3,4,5:T(8,128)} %rev.44), kind=kLoop, calls=%fused_computation.105 | loop fusion | flops 589824 | bytes 4718592 | tf_op jit(solution)/shard_map/concatenate | solution.py:105
  77.7 2.4 rev.45
  80.1 2.9 %copy_select_fusion.1 = f32[3,3,2,2,2,2,16,256]{7,6,1,0,2,3,4,5:T(8,128)S(1)} fusion(f32[3,3,2,2,1,2,16,256]{7,6,1,0,2,3,4,5:T(8,128)} %rev.45, f32[3,3,2,2,1,2,16,256]{7,6,1,0,2,3,4,5:T(8,128)} %get-tuple-element.13, pred[]{:T(512)S(6)} %eq.26), kind=kLoop, calls=%fused_computation.56 | loop fusion | flops 1769472 | bytes 4718593 | tf_op jit(solution)/shard_map/jit(_where)/select_n | solution.py:182
  86.0 7.8 %collective-permute-done.6 = bf16[2,2,2,8,512]{4,3,0,1,2:T(8,128)(2,1)S(1)} collective-permute-done((bf16[2,2,2,8,512]{4,3,0,1,2:T(8,128)(2,1)S(1)}, bf16[2,2,2,8,512]{4,3,0,1,2:T(8,128)(2,1)S(1)}, u32[]{:S(2)}, u32[]{:S(2)}) %collective-permute-start.6) | collective-permute-done | bytes 65568 | tf_op jit(solution)/shard_map/ppermute | solution.py:85
  93.8 3.1 %collective-permute-start.7 = (bf16[2,2,8,512]{3,2,0,1:T(8,128)(2,1)S(1)}, bf16[2,2,8,512]{3,2,0,1:T(8,128)(2,1)S(1)}, u32[]{:S(2)}, u32[]{:S(2)}) collective-permute-start(bf16[2,2,8,512]{3,2,0,1:T(8,128)(2,1)S(1)} %fusion.80), channel_id=1, source_target_pairs={{0,6},{1,25},{2,4},{3,27},{4,2},{5,29},{6,0},{7,31},{8,14},{9,17},... | collective-permute-start | bytes 98312 | tf_op jit(solution)/shard_map/ppermute | solution.py:85
  101.1 4.1 %collective-permute-done.2 = bf16[3,3,2,2,16,256]{5,4,1,0,2,3:T(8,128)(2,1)S(1)} collective-permute-done((bf16[3,3,2,2,16,256]{5,4,1,0,2,3:T(8,128)(2,1)S(1)}, bf16[3,3,2,2,16,256]{5,4,1,0,2,3:T(8,128)(2,1)S(1)}, u32[]{:S(2)}, u32[]{:S(2)}) %collective-permute-start.2) | collective-permute-done | bytes 294944 | tf_op jit(solution)/shard_map/ppermute | solution.py:85
  107.4 2.7 collective-permute-start.9
  110.6 4.1 %collective-permute-start.4 = (bf16[3,3,16,256]{3,2,1,0:T(8,128)(2,1)S(1)}, bf16[3,3,16,256]{3,2,1,0:T(8,128)(2,1)S(1)}, u32[]{:S(2)}, u32[]{:S(2)}) collective-permute-start(bf16[3,3,16,256]{3,2,1,0:T(8,128)(2,1)S(1)} %fusion.67), channel_id=1, source_target_pairs={{0,24},{1,7},{2,26},{3,5},{4,28},{5,3},{6,30},{7,1},{8,16},{9,15},... | collective-permute-start | bytes 221192 | tf_op jit(solution)/shard_map/ppermute | solution.py:85
  120.4 5.0 %all-to-all-start.2 = ((f32[32,1,2]{2,1,0:T(1,128)}), f32[32,1,2]{2,1,0:T(1,128)}, u32[]{:S(2)}, u32[]{:S(2)}) async-start(f32[32,1,2]{2,1,0:T(1,128)} %broadcast_in_dim.19), calls=%async_computation.2 | async-start | bytes 32768 | tf_op jit(solution)/shard_map/all_to_all | solution.py:192
  125.5 7.1 %all-to-all-done.2 = f32[32,1,2]{2,1,0:T(1,128)} async-done(((f32[32,1,2]{2,1,0:T(1,128)}), f32[32,1,2]{2,1,0:T(1,128)}, u32[]{:S(2)}, u32[]{:S(2)}) %all-to-all-start.2) | async-done | bytes 288 | tf_op jit(solution)/shard_map/all_to_all | solution.py:192
  137.4 4.7 %collective-permute-done.10 = bf16[3,3,16,256]{3,2,1,0:T(8,128)(2,1)} collective-permute-done((bf16[3,3,16,256]{3,2,1,0:T(8,128)(2,1)}, bf16[3,3,16,256]{3,2,1,0:T(8,128)(2,1)}, u32[]{:S(2)}, u32[]{:S(2)}) %collective-permute-start.10) | collective-permute-done | bytes 73760 | tf_op jit(solution)/shard_map/ppermute | solution.py:85
  145.1 3.2 %collective-permute-done.11 = bf16[3,3,2,16,256]{4,3,2,1,0:T(8,128)(2,1)S(1)} collective-permute-done((bf16[3,3,2,16,256]{4,3,2,1,0:T(8,128)(2,1)S(1)}, bf16[3,3,2,16,256]{4,3,2,1,0:T(8,128)(2,1)S(1)}, u32[]{:S(2)}, u32[]{:S(2)}) %collective-permute-start.11) | collective-permute-done | bytes 147488 | tf_op jit(solution)/shard_map/ppermute | solution.py:85
  149.9 6.5 %collective-permute-done.12 = bf16[3,3,2,2,16,256]{5,4,3,2,1,0:T(8,128)(2,1)S(1)} collective-permute-done((bf16[3,3,2,2,16,256]{5,4,3,2,1,0:T(8,128)(2,1)S(1)}, bf16[3,3,2,2,16,256]{5,4,3,2,1,0:T(8,128)(2,1)S(1)}, u32[]{:S(2)}, u32[]{:S(2)}) %collective-permute-start.12) | collective-permute-done | bytes 294944 | tf_op jit(solution)/shard_map/ppermute | solution.py:85
  160.8 4.1 %collective-permute-done.17 = bf16[2,2,8,512]{3,2,1,0:T(8,128)(2,1)} collective-permute-done((bf16[2,2,8,512]{3,2,1,0:T(8,128)(2,1)}, bf16[2,2,8,512]{3,2,1,0:T(8,128)(2,1)}, u32[]{:S(2)}, u32[]{:S(2)}) %collective-permute-start.17) | collective-permute-done | bytes 32800 | tf_op jit(solution)/shard_map/ppermute | solution.py:85
  173.1 2.5 fusion.37
  177.5 2.4 pad_maximum_fusion.6
  213.4 2.5 bitcast_add_fusion
  219.0 2.6 fusion.32
  226.2 7.8 %collective-permute-done.26 = bf16[2,2,2,8,512]{4,3,0,1,2:T(8,128)(2,1)S(1)} collective-permute-done((bf16[2,2,2,8,512]{4,3,0,1,2:T(8,128)(2,1)S(1)}, bf16[2,2,2,8,512]{4,3,0,1,2:T(8,128)(2,1)S(1)}, u32[]{:S(2)}, u32[]{:S(2)}) %collective-permute-start.26) | collective-permute-done | bytes 65568 | tf_op jit(solution)/shard_map/ppermute | solution.py:85
  239.5 4.3 %collective-permute-done.22 = bf16[3,3,2,2,16,256]{5,4,1,0,2,3:T(8,128)(2,1)S(1)} collective-permute-done((bf16[3,3,2,2,16,256]{5,4,1,0,2,3:T(8,128)(2,1)S(1)}, bf16[3,3,2,2,16,256]{5,4,1,0,2,3:T(8,128)(2,1)S(1)}, u32[]{:S(2)}, u32[]{:S(2)}) %collective-permute-start.22) | collective-permute-done | bytes 294944 | tf_op jit(solution)/shard_map/ppermute | solution.py:85
  245.1 4.0 %collective-permute-done.23 = bf16[3,3,2,16,256]{4,3,1,0,2:T(8,128)(2,1)S(1)} collective-permute-done((bf16[3,3,2,16,256]{4,3,1,0,2:T(8,128)(2,1)S(1)}, bf16[3,3,2,16,256]{4,3,1,0,2:T(8,128)(2,1)S(1)}, u32[]{:S(2)}, u32[]{:S(2)}) %collective-permute-start.23) | collective-permute-done | bytes 147488 | tf_op jit(solution)/shard_map/ppermute | solution.py:85
  251.0 3.9 %collective-permute-done.24 = bf16[3,3,16,256]{3,2,1,0:T(8,128)(2,1)S(1)} collective-permute-done((bf16[3,3,16,256]{3,2,1,0:T(8,128)(2,1)S(1)}, bf16[3,3,16,256]{3,2,1,0:T(8,128)(2,1)S(1)}, u32[]{:S(2)}, u32[]{:S(2)}) %collective-permute-start.24) | collective-permute-done | bytes 73760 | tf_op jit(solution)/shard_map/ppermute | solution.py:85
  258.2 4.2 %all-to-all-start.3 = ((f32[32,1,2]{2,1,0:T(1,128)}), f32[32,1,2]{2,1,0:T(1,128)S(1)}, u32[]{:S(2)}, u32[]{:S(2)}) async-start(f32[32,1,2]{2,1,0:T(1,128)} %broadcast_in_dim.20), calls=%async_computation.3 | async-start | bytes 32768 | tf_op jit(solution)/shard_map/all_to_all | solution.py:192
  263.0 6.7 %all-to-all-done.3 = f32[32,1,2]{2,1,0:T(1,128)S(1)} async-done(((f32[32,1,2]{2,1,0:T(1,128)}), f32[32,1,2]{2,1,0:T(1,128)S(1)}, u32[]{:S(2)}, u32[]{:S(2)}) %all-to-all-start.3) | async-done | bytes 288 | tf_op jit(solution)/shard_map/all_to_all | solution.py:192
  (297 shorter events, 127.4 us)
Async XLA Ops:
  4.8 9.7 %all-to-all-start.1 = ((bf16[4,2,192]{2,1,0:T(2,128)(2,1)}), bf16[4,2,192]{2,1,0:T(2,128)(2,1)S(1)}, u32[]{:S(2)}, u32[]{:S(2)}) async-start(bf16[4,2,192]{2,1,0:T(2,128)(2,1)} %reshape.198), calls=%async_computation.1 | async-start | bytes 8192 | tf_op jit(solution)/shard_map/all_to_all | solution.py:153
  14.5 23.9 %all-to-all-start = ((bf16[4,6,8,8,512]{4,3,2,1,0:T(8,128)(2,1)}), bf16[4,6,8,8,512]{4,3,2,1,0:T(8,128)(2,1)S(1)}, u32[]{:S(2)}, u32[]{:S(2)}) async-start(bf16[4,6,8,8,512]{4,3,2,1,0:T(8,128)(2,1)} %scatter_fusion), calls=%async_computation | async-start | bytes 3145728 | tf_op jit(solution)/shard_map/all_to_all | solution.py:152
  61.8 6.0 %collective-permute-start = (bf16[3,3,2,2,2,2,16,256]{7,6,1,0,2,3,4,5:T(8,128)(2,1)}, bf16[3,3,2,2,2,2,16,256]{7,6,1,0,2,3,4,5:T(8,128)(2,1)}, u32[]{:S(2)}, u32[]{:S(2)}) collective-permute-start(bf16[3,3,2,2,2,2,16,256]{7,6,1,0,2,3,4,5:T(8,128)(2,1)} %fusion.30), channel_id=1, source_target_pairs={{0,1},{1,0},{2,3},{3,2},{4,5},{5,4},{6,7},{7,6},{8,9},{9,8},{10,11... | collective-permute-start | bytes 3538952 | tf_op jit(solution)/shard_map/ppermute | solution.py:85
  83.1 13.8 %collective-permute-start.1 = (bf16[3,3,2,2,2,16,256]{6,5,1,0,2,3,4:T(8,128)(2,1)S(1)}, bf16[3,3,2,2,2,16,256]{6,5,1,0,2,3,4:T(8,128)(2,1)S(1)}, u32[]{:S(2)}, u32[]{:S(2)}) collective-permute-start(bf16[3,3,2,2,2,16,256]{6,5,1,0,2,3,4:T(8,128)(2,1)S(1)} %fusion.35), channel_id=1, source_target_pairs={{0,2},{1,9},{2,0},{3,11},{4,6},{5,13},{6,4},{7,15},{8,10},{9,1},{1... | collective-permute-start | bytes 1769480 | tf_op jit(solution)/shard_map/ppermute | solution.py:85
  84.8 9.0 %collective-permute-start.6 = (bf16[2,2,2,8,512]{4,3,0,1,2:T(8,128)(2,1)S(1)}, bf16[2,2,2,8,512]{4,3,0,1,2:T(8,128)(2,1)S(1)}, u32[]{:S(2)}, u32[]{:S(2)}) collective-permute-start(bf16[2,2,2,8,512]{4,3,0,1,2:T(8,128)(2,1)S(1)} %fusion.69), channel_id=1, source_target_pairs={{0,2},{1,9},{2,0},{3,11},{4,6},{5,13},{6,4},{7,15},{8,10},{9,1},{1... | collective-permute-start | bytes 196616 | tf_op jit(solution)/shard_map/ppermute | solution.py:85
  93.8 5.2 %collective-permute-start.7 = (bf16[2,2,8,512]{3,2,0,1:T(8,128)(2,1)S(1)}, bf16[2,2,8,512]{3,2,0,1:T(8,128)(2,1)S(1)}, u32[]{:S(2)}, u32[]{:S(2)}) collective-permute-start(bf16[2,2,8,512]{3,2,0,1:T(8,128)(2,1)S(1)} %fusion.80), channel_id=1, source_target_pairs={{0,6},{1,25},{2,4},{3,27},{4,2},{5,29},{6,0},{7,31},{8,14},{9,17},... | collective-permute-start | bytes 98312 | tf_op jit(solution)/shard_map/ppermute | solution.py:85
  97.2 8.0 %collective-permute-start.2 = (bf16[3,3,2,2,16,256]{5,4,1,0,2,3:T(8,128)(2,1)S(1)}, bf16[3,3,2,2,16,256]{5,4,1,0,2,3:T(8,128)(2,1)S(1)}, u32[]{:S(2)}, u32[]{:S(2)}) collective-permute-start(bf16[3,3,2,2,16,256]{5,4,1,0,2,3:T(8,128)(2,1)S(1)} %fusion.38), channel_id=1, source_target_pairs={{0,6},{1,25},{2,4},{3,27},{4,2},{5,29},{6,0},{7,31},{8,14},{9,17},... | collective-permute-start | bytes 884744 | tf_op jit(solution)/shard_map/ppermute | solution.py:85
  99.1 8.3 %collective-permute-start.8 = (bf16[2,8,512]{2,1,0:T(8,128)(2,1)S(1)}, bf16[2,8,512]{2,1,0:T(8,128)(2,1)S(1)}, u32[]{:S(2)}, u32[]{:S(2)}) collective-permute-start(bf16[2,8,512]{2,1,0:T(8,128)(2,1)S(1)} %fusion.82), channel_id=1, source_target_pairs={{0,8},{1,3},{2,10},{3,1},{4,12},{5,7},{6,14},{7,5},{8,0},{9,11},{1... | collective-permute-start | bytes 49160 | tf_op jit(solution)/shard_map/ppermute | solution.py:85
  105.3 5.2 %collective-permute-start.3 = (bf16[3,3,2,16,256]{4,3,1,0,2:T(8,128)(2,1)S(1)}, bf16[3,3,2,16,256]{4,3,1,0,2:T(8,128)(2,1)S(1)}, u32[]{:S(2)}, u32[]{:S(2)}) collective-permute-start(bf16[3,3,2,16,256]{4,3,1,0,2:T(8,128)(2,1)S(1)} %fusion.46), channel_id=1, source_target_pairs={{0,8},{1,3},{2,10},{3,1},{4,12},{5,7},{6,14},{7,5},{8,0},{9,11},{1... | collective-permute-start | bytes 442376 | tf_op jit(solution)/shard_map/ppermute | solution.py:85
  107.4 7.4 %collective-permute-start.9 = (bf16[8,512]{1,0:T(8,128)(2,1)S(1)}, bf16[8,512]{1,0:T(8,128)(2,1)S(1)}, u32[]{:S(2)}, u32[]{:S(2)}) collective-permute-start(bf16[8,512]{1,0:T(8,128)(2,1)S(1)} %fusion.84), channel_id=1, source_target_pairs={{0,24},{1,7},{2,26},{3,5},{4,28},{5,3},{6,30},{7,1},{8,16},{9,15},... | collective-permute-start | bytes 24584 | tf_op jit(solution)/shard_map/ppermute | solution.py:85
  110.6 6.5 %collective-permute-start.4 = (bf16[3,3,16,256]{3,2,1,0:T(8,128)(2,1)S(1)}, bf16[3,3,16,256]{3,2,1,0:T(8,128)(2,1)S(1)}, u32[]{:S(2)}, u32[]{:S(2)}) collective-permute-start(bf16[3,3,16,256]{3,2,1,0:T(8,128)(2,1)S(1)} %fusion.67), channel_id=1, source_target_pairs={{0,24},{1,7},{2,26},{3,5},{4,28},{5,3},{6,30},{7,1},{8,16},{9,15},... | collective-permute-start | bytes 221192 | tf_op jit(solution)/shard_map/ppermute | solution.py:85
  120.4 12.2 %all-to-all-start.2 = ((f32[32,1,2]{2,1,0:T(1,128)}), f32[32,1,2]{2,1,0:T(1,128)}, u32[]{:S(2)}, u32[]{:S(2)}) async-start(f32[32,1,2]{2,1,0:T(1,128)} %broadcast_in_dim.19), calls=%async_computation.2 | async-start | bytes 32768 | tf_op jit(solution)/shard_map/all_to_all | solution.py:192
  136.2 5.9 %collective-permute-start.10 = (bf16[3,3,16,256]{3,2,1,0:T(8,128)(2,1)}, bf16[3,3,16,256]{3,2,1,0:T(8,128)(2,1)}, u32[]{:S(2)}, u32[]{:S(2)}) collective-permute-start(bf16[3,3,16,256]{3,2,1,0:T(8,128)(2,1)} %fusion.91), channel_id=1, source_target_pairs={{0,24},{1,7},{2,26},{3,5},{4,28},{5,3},{6,30},{7,1},{8,16},{9,15},... | collective-permute-start | bytes 221192 | tf_op jit(solution)/shard_map/ppermute | solution.py:85
  143.1 5.2 %collective-permute-start.11 = (bf16[3,3,2,16,256]{4,3,2,1,0:T(8,128)(2,1)S(1)}, bf16[3,3,2,16,256]{4,3,2,1,0:T(8,128)(2,1)S(1)}, u32[]{:S(2)}, u32[]{:S(2)}) collective-permute-start(bf16[3,3,2,16,256]{4,3,2,1,0:T(8,128)(2,1)S(1)} %pad_maximum_fusion.13), channel_id=1, source_target_pairs={{0,8},{1,3},{2,10},{3,1},{4,12},{5,7},{6,14},{7,5},{8,0},{9,11},{1... | collective-permute-start | bytes 442376 | tf_op jit(solution)/shard_map/ppermute | solution.py:85
  143.9 5.9 %collective-permute-start.15 = (bf16[8,512]{1,0:T(8,128)(2,1)S(1)}, bf16[8,512]{1,0:T(8,128)(2,1)S(1)}, u32[]{:S(2)}, u32[]{:S(2)}) collective-permute-start(bf16[8,512]{1,0:T(8,128)(2,1)S(1)} %fusion.90), channel_id=1, source_target_pairs={{0,24},{1,7},{2,26},{3,5},{4,28},{5,3},{6,30},{7,1},{8,16},{9,15},... | collective-permute-start | bytes 24584 | tf_op jit(solution)/shard_map/ppermute | solution.py:85
  148.4 8.0 %collective-permute-start.12 = (bf16[3,3,2,2,16,256]{5,4,3,2,1,0:T(8,128)(2,1)S(1)}, bf16[3,3,2,2,16,256]{5,4,3,2,1,0:T(8,128)(2,1)S(1)}, u32[]{:S(2)}, u32[]{:S(2)}) collective-permute-start(bf16[3,3,2,2,16,256]{5,4,3,2,1,0:T(8,128)(2,1)S(1)} %pad_maximum_fusion.9), channel_id=1, source_target_pairs={{0,6},{1,25},{2,4},{3,27},{4,2},{5,29},{6,0},{7,31},{8,14},{9,17},... | collective-permute-start | bytes 884744 | tf_op jit(solution)/shard_map/ppermute | solution.py:85
  149.8 8.3 %collective-permute-start.16 = (bf16[2,8,512]{2,1,0:T(8,128)(2,1)S(1)}, bf16[2,8,512]{2,1,0:T(8,128)(2,1)S(1)}, u32[]{:S(2)}, u32[]{:S(2)}) collective-permute-start(bf16[2,8,512]{2,1,0:T(8,128)(2,1)S(1)} %pad_maximum_fusion.21), channel_id=1, source_target_pairs={{0,8},{1,3},{2,10},{3,1},{4,12},{5,7},{6,14},{7,5},{8,0},{9,11},{1... | collective-permute-start | bytes 49160 | tf_op jit(solution)/shard_map/ppermute | solution.py:85
  158.0 10.2 %collective-permute-start.13 = (bf16[3,3,2,2,2,16,256]{6,5,4,3,2,1,0:T(8,128)(2,1)}, bf16[3,3,2,2,2,16,256]{6,5,4,3,2,1,0:T(8,128)(2,1)}, u32[]{:S(2)}, u32[]{:S(2)}) collective-permute-start(bf16[3,3,2,2,2,16,256]{6,5,4,3,2,1,0:T(8,128)(2,1)} %pad_maximum_fusion.8), channel_id=1, source_target_pairs={{0,2},{1,9},{2,0},{3,11},{4,6},{5,13},{6,4},{7,15},{8,10},{9,1},{1... | collective-permute-start | bytes 1769480 | tf_op jit(solution)/shard_map/ppermute | solution.py:85
  159.3 5.6 %collective-permute-start.17 = (bf16[2,2,8,512]{3,2,1,0:T(8,128)(2,1)}, bf16[2,2,8,512]{3,2,1,0:T(8,128)(2,1)}, u32[]{:S(2)}, u32[]{:S(2)}) collective-permute-start(bf16[2,2,8,512]{3,2,1,0:T(8,128)(2,1)} %pad_maximum_fusion.20), channel_id=1, source_target_pairs={{0,6},{1,25},{2,4},{3,27},{4,2},{5,29},{6,0},{7,31},{8,14},{9,17},... | collective-permute-start | bytes 98312 | tf_op jit(solution)/shard_map/ppermute | solution.py:85
  166.3 13.6 %collective-permute-start.18 = (bf16[2,2,2,8,512]{4,3,2,1,0:T(8,128)(2,1)}, bf16[2,2,2,8,512]{4,3,2,1,0:T(8,128)(2,1)}, u32[]{:S(2)}, u32[]{:S(2)}) collective-permute-start(bf16[2,2,2,8,512]{4,3,2,1,0:T(8,128)(2,1)} %pad_maximum_fusion.19), channel_id=1, source_target_pairs={{0,2},{1,9},{2,0},{3,11},{4,6},{5,13},{6,4},{7,15},{8,10},{9,1},{1... | collective-permute-start | bytes 196616 | tf_op jit(solution)/shard_map/ppermute | solution.py:85
  179.9 4.3 %collective-permute-start.14 = (bf16[3,3,2,2,2,2,16,256]{7,6,5,4,3,2,1,0:T(8,128)(2,1)}, bf16[3,3,2,2,2,2,16,256]{7,6,5,4,3,2,1,0:T(8,128)(2,1)}, u32[]{:S(2)}, u32[]{:S(2)}) collective-permute-start(bf16[3,3,2,2,2,2,16,256]{7,6,5,4,3,2,1,0:T(8,128)(2,1)} %pad_maximum_fusion.6), channel_id=1, source_target_pairs={{0,1},{1,0},{2,3},{3,2},{4,5},{5,4},{6,7},{7,6},{8,9},{9,8},{10,11... | collective-permute-start | bytes 3538952 | tf_op jit(solution)/shard_map/ppermute | solution.py:85
  180.9 2.4 collective-permute-start.19
  209.8 3.6 %collective-permute-start.20 = (bf16[3,3,2,2,2,2,16,256]{7,6,1,0,2,3,4,5:T(8,128)(2,1)S(1)}, bf16[3,3,2,2,2,2,16,256]{7,6,1,0,2,3,4,5:T(8,128)(2,1)}, u32[]{:S(2)}, u32[]{:S(2)}) collective-permute-start(bf16[3,3,2,2,2,2,16,256]{7,6,1,0,2,3,4,5:T(8,128)(2,1)S(1)} %fusion.31), channel_id=1, source_target_pairs={{0,1},{1,0},{2,3},{3,2},{4,5},{5,4},{6,7},{7,6},{8,9},{9,8},{10,11... | collective-permute-start | bytes 3538952 | tf_op jit(solution)/shard_map/ppermute | solution.py:85
  223.4 12.1 %collective-permute-start.21 = (bf16[3,3,2,2,2,16,256]{6,5,1,0,2,3,4:T(8,128)(2,1)S(1)}, bf16[3,3,2,2,2,16,256]{6,5,1,0,2,3,4:T(8,128)(2,1)S(1)}, u32[]{:S(2)}, u32[]{:S(2)}) collective-permute-start(bf16[3,3,2,2,2,16,256]{6,5,1,0,2,3,4:T(8,128)(2,1)S(1)} %fusion.36), channel_id=1, source_target_pairs={{0,2},{1,9},{2,0},{3,11},{4,6},{5,13},{6,4},{7,15},{8,10},{9,1},{1... | collective-permute-start | bytes 1769480 | tf_op jit(solution)/shard_map/ppermute | solution.py:85
  223.6 10.4 %collective-permute-start.26 = (bf16[2,2,2,8,512]{4,3,0,1,2:T(8,128)(2,1)S(1)}, bf16[2,2,2,8,512]{4,3,0,1,2:T(8,128)(2,1)S(1)}, u32[]{:S(2)}, u32[]{:S(2)}) collective-permute-start(bf16[2,2,2,8,512]{4,3,0,1,2:T(8,128)(2,1)S(1)} %fusion.70), channel_id=1, source_target_pairs={{0,2},{1,9},{2,0},{3,11},{4,6},{5,13},{6,4},{7,15},{8,10},{9,1},{1... | collective-permute-start | bytes 196616 | tf_op jit(solution)/shard_map/ppermute | solution.py:85
  234.1 5.2 %collective-permute-start.27 = (bf16[2,2,8,512]{3,2,0,1:T(8,128)(2,1)S(1)}, bf16[2,2,8,512]{3,2,0,1:T(8,128)(2,1)S(1)}, u32[]{:S(2)}, u32[]{:S(2)}) collective-permute-start(bf16[2,2,8,512]{3,2,0,1:T(8,128)(2,1)S(1)} %fusion.81), channel_id=1, source_target_pairs={{0,6},{1,25},{2,4},{3,27},{4,2},{5,29},{6,0},{7,31},{8,14},{9,17},... | collective-permute-start | bytes 98312 | tf_op jit(solution)/shard_map/ppermute | solution.py:85
  235.8 8.0 %collective-permute-start.22 = (bf16[3,3,2,2,16,256]{5,4,1,0,2,3:T(8,128)(2,1)S(1)}, bf16[3,3,2,2,16,256]{5,4,1,0,2,3:T(8,128)(2,1)S(1)}, u32[]{:S(2)}, u32[]{:S(2)}) collective-permute-start(bf16[3,3,2,2,16,256]{5,4,1,0,2,3:T(8,128)(2,1)S(1)} %fusion.39), channel_id=1, source_target_pairs={{0,6},{1,25},{2,4},{3,27},{4,2},{5,29},{6,0},{7,31},{8,14},{9,17},... | collective-permute-start | bytes 884744 | tf_op jit(solution)/shard_map/ppermute | solution.py:85
  239.4 4.6 %collective-permute-start.28 = (bf16[2,8,512]{2,1,0:T(8,128)(2,1)S(1)}, bf16[2,8,512]{2,1,0:T(8,128)(2,1)S(1)}, u32[]{:S(2)}, u32[]{:S(2)}) collective-permute-start(bf16[2,8,512]{2,1,0:T(8,128)(2,1)S(1)} %fusion.83), channel_id=1, source_target_pairs={{0,8},{1,3},{2,10},{3,1},{4,12},{5,7},{6,14},{7,5},{8,0},{9,11},{1... | collective-permute-start | bytes 49160 | tf_op jit(solution)/shard_map/ppermute | solution.py:85
  243.9 5.2 %collective-permute-start.23 = (bf16[3,3,2,16,256]{4,3,1,0,2:T(8,128)(2,1)S(1)}, bf16[3,3,2,16,256]{4,3,1,0,2:T(8,128)(2,1)S(1)}, u32[]{:S(2)}, u32[]{:S(2)}) collective-permute-start(bf16[3,3,2,16,256]{4,3,1,0,2:T(8,128)(2,1)S(1)} %fusion.47), channel_id=1, source_target_pairs={{0,8},{1,3},{2,10},{3,1},{4,12},{5,7},{6,14},{7,5},{8,0},{9,11},{1... | collective-permute-start | bytes 442376 | tf_op jit(solution)/shard_map/ppermute | solution.py:85
  244.1 6.2 %collective-permute-start.29 = (bf16[8,512]{1,0:T(8,128)(2,1)S(1)}, bf16[8,512]{1,0:T(8,128)(2,1)S(1)}, u32[]{:S(2)}, u32[]{:S(2)}) collective-permute-start(bf16[8,512]{1,0:T(8,128)(2,1)S(1)} %fusion.85), channel_id=1, source_target_pairs={{0,24},{1,7},{2,26},{3,5},{4,28},{5,3},{6,30},{7,1},{8,16},{9,15},... | collective-permute-start | bytes 24584 | tf_op jit(solution)/shard_map/ppermute | solution.py:85
  249.2 5.6 %collective-permute-start.24 = (bf16[3,3,16,256]{3,2,1,0:T(8,128)(2,1)S(1)}, bf16[3,3,16,256]{3,2,1,0:T(8,128)(2,1)S(1)}, u32[]{:S(2)}, u32[]{:S(2)}) collective-permute-start(bf16[3,3,16,256]{3,2,1,0:T(8,128)(2,1)S(1)} %fusion.68), channel_id=1, source_target_pairs={{0,24},{1,7},{2,26},{3,5},{4,28},{5,3},{6,30},{7,1},{8,16},{9,15},... | collective-permute-start | bytes 221192 | tf_op jit(solution)/shard_map/ppermute | solution.py:85
  258.2 11.5 %all-to-all-start.3 = ((f32[32,1,2]{2,1,0:T(1,128)}), f32[32,1,2]{2,1,0:T(1,128)S(1)}, u32[]{:S(2)}, u32[]{:S(2)}) async-start(f32[32,1,2]{2,1,0:T(1,128)} %broadcast_in_dim.20), calls=%async_computation.3 | async-start | bytes 32768 | tf_op jit(solution)/shard_map/all_to_all | solution.py:192
  (44 other events, 467.9 us)

commit v13 on v8

--- a/solution.py
+++ b/solution.py
@@ -162,8 +162,8 @@
         grad_up = grad_up.reshape(bits_shape + (part_inner, up_w.shape[2]))
         for stage in range(levels):
             if stage == 1:
-                grad_down = jnp.where(second_core, swap_bit_axes(grad_down, 2, levels), grad_down)
-                grad_up = jnp.where(second_core, swap_bit_axes(grad_up, 0, levels), grad_up)
+                grad_down = lax.cond(second_core, lambda v: swap_bit_axes(v, 2, levels), lambda v: v, grad_down)
+                grad_up = lax.cond(second_core, lambda v: swap_bit_axes(v, 0, levels), lambda v: v, grad_up)
             bits_of = (orders[0][stage], orders[1][stage])
             pairs = stage_pairs(bits_of, peers)
             bit = jnp.where(second_core, bits_of[1], bits_of[0])
@@ -183,8 +183,8 @@
             for step_index in range(levels):
                 stage = levels - 1 - step_index
                 if stage == 0:
-                    down_low = jnp.where(second_core, swap_bit_axes(down_low, 2, levels), down_low)
-                    upper_low = jnp.where(second_core, swap_bit_axes(upper_low, 0, levels), upper_low)
+                    down_low = lax.cond(second_core, lambda v: swap_bit_axes(v, 2, levels), lambda v: v, down_low)
+                    upper_low = lax.cond(second_core, lambda v: swap_bit_axes(v, 0, levels), lambda v: v, upper_low)
                 bits_of = (orders[0][stage], orders[1][stage])
                 pairs = stage_pairs(bits_of, peers)
                 bit = jnp.where(second_core, bits_of[1], bits_of[0])

time: 250 us -> 273 us (1.092)
  local copies, waits for them, and re-layouts: 27.4 us -> 41.2 us
  other arithmetic: 25.6 us -> 39.2 us
  waiting for transfers between devices: 91.2 us -> 88 us
    another operation x18 -> x20, other arithmetic: 3.79 us -> 10.9 us  [double_join(): return jnp.stack([first, second], axis=axis)]
    add x12 -> x16, other arithmetic: 0.73 us -> 5.75 us  [halve_sum(): return keep + sent.astype(jnp.float32)]
    convert_element_type x20, local copies, waits for them, and re-layouts: 1.9 us -> 6.9 us  [halve_sum(): sent = partner_swap(give.astype(jnp.bfloat16), pairs)]
    add x0 -> x4, local copies, waits for them, and re-layouts: none -> 4 us
    ppermute x30, waiting for transfers between devices: 60.9 us -> 57.8 us  [partner_swap(): return lax.ppermute(value, 'ex', perm=pairs)]
    squeeze x0 -> x4, local copies, waits for them, and re-layouts: none -> 3.1 us  [halve_sum(): keep = lax.dynamic_index_in_dim(value, mine, axis, keepdims=False)]
    convert_element_type x0 -> x4, other arithmetic: none -> 2.84 us  [halve_sum(): return keep + sent.astype(jnp.float32)]
    unnamed x70 -> x88, local copies, waits for them, and re-layouts: 14.1 us -> 13.9 us
  transfers between devices with their start and end apart: 34 -> 34, of which waited for: 20 -> 21; matrix products, arithmetic and copies ran while one was open for 9% -> 16% of each run, Pallas kernels for 0% -> 0%
where the time goes in v13:
time: 273 us; the launch traced here: 268 us
  waiting for transfers between devices  88 us (32%)
  starting transfers between devices  56.9 us (21%)
  local copies, waits for them, and re-layouts  41.2 us (15%)
  other arithmetic  39.2 us (14%)
  matrix products  34.4 us (13%)
  between operations  7.96 us (3%)
    ppermute x30, waiting for transfers between devices, partner_swap(): return lax.ppermute(value, 'ex', perm=pairs)  57.8 us
    ppermute x30, starting transfers between devices, partner_swap(): return lax.ppermute(value, 'ex', perm=pairs)  37.6 us
    all_to_all x1, waiting for transfers between devices, shards(): lax.all_to_all(send_feats, 'task', split_axis=0, concat_axis=0, tiled=True)  15.3 us
    dot_general x20, matrix products, contract_rows(): lax.dot_general(left, right, (((0,), (0,)), ((), ())), preferred_element_...  14.9 us
    all_to_all x2, waiting for transfers between devices, shards(): totals = jnp.sum(lax.all_to_all(spread, 'ex', 0, 0, tiled=True), axis=0)  13.9 us
    unnamed x88, local copies, waits for them, and re-layouts  13.9 us
    all_to_all x2, starting transfers between devices, shards(): totals = jnp.sum(lax.all_to_all(spread, 'ex', 0, 0, tiled=True), axis=0)  11.2 us
    another operation x20, other arithmetic, double_join(): return jnp.stack([first, second], axis=axis)  10.9 us
  transfers between devices with their start and end apart: 34, of which 21 were waited for; matrix products, arithmetic and copies ran while one was open for 16% of the time, Pallas kernels for 0%

profile of v13, /device:TPU:0, one launch (start us, length us, event | category | flops | bytes accessed | tf_op | source)
XLA Modules:
  0.0 267.8 jit_solution(16277230876347109319)
XLA Ops:
  4.8 4.4 %all-to-all-start.1 = ((bf16[4,2,192]{2,1,0:T(2,128)(2,1)}), bf16[4,2,192]{2,1,0:T(2,128)(2,1)S(1)}, u32[]{:S(2)}, u32[]{:S(2)}) async-start(bf16[4,2,192]{2,1,0:T(2,128)(2,1)} %reshape.198), calls=%async_computation.1 | async-start | bytes 8192 | tf_op jit(solution)/shard_map/all_to_all | solution.py:138
  10.5 2.9 %scatter_fusion = bf16[4,6,8,8,512]{4,3,2,1,0:T(8,128)(2,1)} fusion(bf16[4,6,8,8,512]{4,3,2,1,0:T(8,128)(2,1)} %broadcast_in_dim.16, s32[12]{0:T(128)S(1)} %fusion.77, bf16[12,8,8,512]{3,2,1,0:T(8,128)(2,1)S(1)} %copy-done.26), kind=kCustom, calls=%fused_computation | custom fusion | bytes 2359392 | tf_op jit(solution)/shard_map/scatter | solution.py:129
  14.5 3.7 %all-to-all-start = ((bf16[4,6,8,8,512]{4,3,2,1,0:T(8,128)(2,1)}), bf16[4,6,8,8,512]{4,3,2,1,0:T(8,128)(2,1)S(1)}, u32[]{:S(2)}, u32[]{:S(2)}) async-start(bf16[4,6,8,8,512]{4,3,2,1,0:T(8,128)(2,1)} %scatter_fusion), calls=%async_computation | async-start | bytes 3145728 | tf_op jit(solution)/shard_map/all_to_all | solution.py:137
  18.9 4.0 %convert_bitcast_fusion = bf16[3,3,512,256]{3,2,1,0:T(8,128)(2,1)} fusion(f32[1,3,3,512,256]{4,3,2,1,0:T(8,128)} %param.23), kind=kLoop, calls=%fused_computation.53 | loop fusion | flops 1179648 | bytes 7077888 | tf_op jit(solution)/shard_map/convert_element_type | solution.py:149
  23.1 15.3 %all-to-all-done = bf16[4,6,8,8,512]{4,3,2,1,0:T(8,128)(2,1)S(1)} async-done(((bf16[4,6,8,8,512]{4,3,2,1,0:T(8,128)(2,1)}), bf16[4,6,8,8,512]{4,3,2,1,0:T(8,128)(2,1)S(1)}, u32[]{:S(2)}, u32[]{:S(2)}) %all-to-all-start) | async-done | bytes 1572896 | tf_op jit(solution)/shard_map/all_to_all | solution.py:137
  40.0 2.5 pad_slice_fusion
  60.6 2.2 copy-done.16
  64.0 2.5 fusion.80
  71.4 2.4 conditional.6
  73.9 2.2 fusion.30
  82.4 4.4 %collective-permute-done.6 = bf16[2,2,2,8,512]{4,3,0,1,2:T(8,128)(2,1)S(1)} collective-permute-done((bf16[2,2,2,8,512]{4,3,0,1,2:T(8,128)(2,1)S(1)}, bf16[2,2,2,8,512]{4,3,0,1,2:T(8,128)(2,1)S(1)}, u32[]{:S(2)}, u32[]{:S(2)}) %collective-permute-start.6) | collective-permute-done | bytes 65568 | tf_op jit(solution)/shard_map/ppermute | solution.py:85
  87.8 3.3 %collective-permute-start.7 = (bf16[2,2,8,512]{3,2,0,1:T(8,128)(2,1)S(1)}, bf16[2,2,8,512]{3,2,0,1:T(8,128)(2,1)S(1)}, u32[]{:S(2)}, u32[]{:S(2)}) collective-permute-start(bf16[2,2,8,512]{3,2,0,1:T(8,128)(2,1)S(1)} %fusion.68), channel_id=1, source_target_pairs={{0,4},{1,17},{2,6},{3,19},{4,0},{5,21},{6,2},{7,23},{8,12},{9,25},... | collective-permute-start | bytes 98312 | tf_op jit(solution)/shard_map/ppermute | solution.py:85
  93.3 2.0 collective-permute-start.8
  95.3 5.8 %collective-permute-done.2 = bf16[3,3,2,2,16,256]{5,4,1,0,2,3:T(8,128)(2,1)S(1)} collective-permute-done((bf16[3,3,2,2,16,256]{5,4,1,0,2,3:T(8,128)(2,1)S(1)}, bf16[3,3,2,2,16,256]{5,4,1,0,2,3:T(8,128)(2,1)S(1)}, u32[]{:S(2)}, u32[]{:S(2)}) %collective-permute-start.2) | collective-permute-done | bytes 294944 | tf_op jit(solution)/shard_map/ppermute | solution.py:85
  101.2 2.0 collective-permute-start.3
  103.3 3.6 %collective-permute-start.9 = (bf16[8,512]{1,0:T(8,128)(2,1)S(1)}, bf16[8,512]{1,0:T(8,128)(2,1)S(1)}, u32[]{:S(2)}, u32[]{:S(2)}) collective-permute-start(bf16[8,512]{1,0:T(8,128)(2,1)S(1)} %fusion.72), channel_id=1, source_target_pairs={{0,16},{1,5},{2,18},{3,7},{4,20},{5,1},{6,22},{7,3},{8,24},{9,13},... | collective-permute-start | bytes 24584 | tf_op jit(solution)/shard_map/ppermute | solution.py:85
  107.0 3.7 %collective-permute-start.4 = (bf16[3,3,16,256]{3,2,1,0:T(8,128)(2,1)S(1)}, bf16[3,3,16,256]{3,2,1,0:T(8,128)(2,1)S(1)}, u32[]{:S(2)}, u32[]{:S(2)}) collective-permute-start(bf16[3,3,16,256]{3,2,1,0:T(8,128)(2,1)S(1)} %fusion.56), channel_id=1, source_target_pairs={{0,16},{1,5},{2,18},{3,7},{4,20},{5,1},{6,22},{7,3},{8,24},{9,13},... | collective-permute-start | bytes 221192 | tf_op jit(solution)/shard_map/ppermute | solution.py:85
  116.2 6.7 %all-to-all-start.2 = ((f32[32,1,2]{2,1,0:T(1,128)}), f32[32,1,2]{2,1,0:T(1,128)}, u32[]{:S(2)}, u32[]{:S(2)}) async-start(f32[32,1,2]{2,1,0:T(1,128)} %broadcast_in_dim.19), calls=%async_computation.2 | async-start | bytes 32768 | tf_op jit(solution)/shard_map/all_to_all | solution.py:175
  122.9 7.3 %all-to-all-done.2 = f32[32,1,2]{2,1,0:T(1,128)} async-done(((f32[32,1,2]{2,1,0:T(1,128)}), f32[32,1,2]{2,1,0:T(1,128)}, u32[]{:S(2)}, u32[]{:S(2)}) %all-to-all-start.2) | async-done | bytes 288 | tf_op jit(solution)/shard_map/all_to_all | solution.py:175
  135.1 4.9 %collective-permute-done.10 = bf16[3,3,16,256]{3,2,1,0:T(8,128)(2,1)} collective-permute-done((bf16[3,3,16,256]{3,2,1,0:T(8,128)(2,1)}, bf16[3,3,16,256]{3,2,1,0:T(8,128)(2,1)}, u32[]{:S(2)}, u32[]{:S(2)}) %collective-permute-start.10) | collective-permute-done | bytes 73760 | tf_op jit(solution)/shard_map/ppermute | solution.py:85
  142.9 4.8 %collective-permute-done.11 = bf16[3,3,2,16,256]{4,3,1,0,2:T(8,128)(2,1)} collective-permute-done((bf16[3,3,2,16,256]{4,3,1,0,2:T(8,128)(2,1)}, bf16[3,3,2,16,256]{4,3,1,0,2:T(8,128)(2,1)}, u32[]{:S(2)}, u32[]{:S(2)}) %collective-permute-start.11) | collective-permute-done | bytes 147488 | tf_op jit(solution)/shard_map/ppermute | solution.py:85
  153.2 5.6 %collective-permute-done.12 = bf16[3,3,2,2,16,256]{5,4,1,0,2,3:T(8,128)(2,1)} collective-permute-done((bf16[3,3,2,2,16,256]{5,4,1,0,2,3:T(8,128)(2,1)}, bf16[3,3,2,2,16,256]{5,4,1,0,2,3:T(8,128)(2,1)}, u32[]{:S(2)}, u32[]{:S(2)}) %collective-permute-start.12) | collective-permute-done | bytes 294944 | tf_op jit(solution)/shard_map/ppermute | solution.py:85
  163.3 3.5 %collective-permute-done.16 = bf16[2,8,512]{2,1,0:T(8,128)(2,1)} collective-permute-done((bf16[2,8,512]{2,1,0:T(8,128)(2,1)S(1)}, bf16[2,8,512]{2,1,0:T(8,128)(2,1)}, u32[]{:S(2)}, u32[]{:S(2)}) %collective-permute-start.16) | collective-permute-done | bytes 16416 | tf_op jit(solution)/shard_map/ppermute | solution.py:85
  176.1 3.3 %collective-permute-done.18 = bf16[2,2,2,8,512]{4,3,0,1,2:T(8,128)(2,1)S(1)} collective-permute-done((bf16[2,2,2,8,512]{4,3,0,1,2:T(8,128)(2,1)S(1)}, bf16[2,2,2,8,512]{4,3,0,1,2:T(8,128)(2,1)S(1)}, u32[]{:S(2)}, u32[]{:S(2)}) %collective-permute-start.18) | collective-permute-done | bytes 65568 | tf_op jit(solution)/shard_map/ppermute | solution.py:85
  209.8 2.2 conditional.10
  216.4 7.6 %collective-permute-done.26 = bf16[2,2,2,8,512]{4,3,0,1,2:T(8,128)(2,1)S(1)} collective-permute-done((bf16[2,2,2,8,512]{4,3,0,1,2:T(8,128)(2,1)S(1)}, bf16[2,2,2,8,512]{4,3,0,1,2:T(8,128)(2,1)S(1)}, u32[]{:S(2)}, u32[]{:S(2)}) %collective-permute-start.26) | collective-permute-done | bytes 65568 | tf_op jit(solution)/shard_map/ppermute | solution.py:85
  227.2 2.1 collective-permute-start.22
  230.4 5.2 %collective-permute-done.22 = bf16[3,3,2,2,16,256]{5,4,1,0,2,3:T(8,128)(2,1)S(1)} collective-permute-done((bf16[3,3,2,2,16,256]{5,4,1,0,2,3:T(8,128)(2,1)S(1)}, bf16[3,3,2,2,16,256]{5,4,1,0,2,3:T(8,128)(2,1)S(1)}, u32[]{:S(2)}, u32[]{:S(2)}) %collective-permute-start.22) | collective-permute-done | bytes 294944 | tf_op jit(solution)/shard_map/ppermute | solution.py:85
  238.6 2.3 collective-permute-done.23
  243.0 3.9 %collective-permute-done.24 = bf16[3,3,16,256]{3,2,1,0:T(8,128)(2,1)S(1)} collective-permute-done((bf16[3,3,16,256]{3,2,1,0:T(8,128)(2,1)S(1)}, bf16[3,3,16,256]{3,2,1,0:T(8,128)(2,1)S(1)}, u32[]{:S(2)}, u32[]{:S(2)}) %collective-permute-start.24) | collective-permute-done | bytes 73760 | tf_op jit(solution)/shard_map/ppermute | solution.py:85
  250.2 4.5 %all-to-all-start.3 = ((f32[32,1,2]{2,1,0:T(1,128)}), f32[32,1,2]{2,1,0:T(1,128)S(1)}, u32[]{:S(2)}, u32[]{:S(2)}) async-start(f32[32,1,2]{2,1,0:T(1,128)} %broadcast_in_dim.20), calls=%async_computation.3 | async-start | bytes 32768 | tf_op jit(solution)/shard_map/all_to_all | solution.py:175
  255.4 6.6 %all-to-all-done.3 = f32[32,1,2]{2,1,0:T(1,128)S(1)} async-done(((f32[32,1,2]{2,1,0:T(1,128)}), f32[32,1,2]{2,1,0:T(1,128)S(1)}, u32[]{:S(2)}, u32[]{:S(2)}) %all-to-all-start.3) | async-done | bytes 288 | tf_op jit(solution)/shard_map/all_to_all | solution.py:175
  (289 shorter events, 129.0 us)
Async XLA Ops:
  4.8 9.7 %all-to-all-start.1 = ((bf16[4,2,192]{2,1,0:T(2,128)(2,1)}), bf16[4,2,192]{2,1,0:T(2,128)(2,1)S(1)}, u32[]{:S(2)}, u32[]{:S(2)}) async-start(bf16[4,2,192]{2,1,0:T(2,128)(2,1)} %reshape.198), calls=%async_computation.1 | async-start | bytes 8192 | tf_op jit(solution)/shard_map/all_to_all | solution.py:138
  14.5 23.9 %all-to-all-start = ((bf16[4,6,8,8,512]{4,3,2,1,0:T(8,128)(2,1)}), bf16[4,6,8,8,512]{4,3,2,1,0:T(8,128)(2,1)S(1)}, u32[]{:S(2)}, u32[]{:S(2)}) async-start(bf16[4,6,8,8,512]{4,3,2,1,0:T(8,128)(2,1)} %scatter_fusion), calls=%async_computation | async-start | bytes 3145728 | tf_op jit(solution)/shard_map/all_to_all | solution.py:137
  64.0 5.8 %collective-permute-start = (bf16[3,3,2,2,2,2,16,256]{7,6,5,4,3,2,1,0:T(8,128)(2,1)}, bf16[3,3,2,2,2,2,16,256]{7,6,5,4,3,2,1,0:T(8,128)(2,1)}, u32[]{:S(2)}, u32[]{:S(2)}) collective-permute-start(bf16[3,3,2,2,2,2,16,256]{7,6,5,4,3,2,1,0:T(8,128)(2,1)} %fusion.28), channel_id=1, source_target_pairs={{0,1},{1,0},{2,3},{3,2},{4,5},{5,4},{6,7},{7,6},{8,9},{9,8},{10,11... | collective-permute-start | bytes 3538952 | tf_op jit(solution)/shard_map/ppermute | solution.py:85
  67.4 11.3 %collective-permute-start.5 = (bf16[2,2,2,2,8,512]{5,4,3,2,1,0:T(8,128)(2,1)}, bf16[2,2,2,2,8,512]{5,4,3,2,1,0:T(8,128)(2,1)}, u32[]{:S(2)}, u32[]{:S(2)}) collective-permute-start(bf16[2,2,2,2,8,512]{5,4,3,2,1,0:T(8,128)(2,1)} %fusion.40), channel_id=1, source_target_pairs={{0,1},{1,0},{2,3},{3,2},{4,5},{5,4},{6,7},{7,6},{8,9},{9,8},{10,11... | collective-permute-start | bytes 393224 | tf_op jit(solution)/shard_map/ppermute | solution.py:85
  76.0 15.0 %collective-permute-start.1 = (bf16[3,3,2,2,2,16,256]{6,5,1,0,2,3,4:T(8,128)(2,1)}, bf16[3,3,2,2,2,16,256]{6,5,1,0,2,3,4:T(8,128)(2,1)}, u32[]{:S(2)}, u32[]{:S(2)}) collective-permute-start(bf16[3,3,2,2,2,16,256]{6,5,1,0,2,3,4:T(8,128)(2,1)} %fusion.30), channel_id=1, source_target_pairs={{0,2},{1,9},{2,0},{3,11},{4,6},{5,13},{6,4},{7,15},{8,10},{9,1},{1... | collective-permute-start | bytes 1769480 | tf_op jit(solution)/shard_map/ppermute | solution.py:85
  81.3 5.5 %collective-permute-start.6 = (bf16[2,2,2,8,512]{4,3,0,1,2:T(8,128)(2,1)S(1)}, bf16[2,2,2,8,512]{4,3,0,1,2:T(8,128)(2,1)S(1)}, u32[]{:S(2)}, u32[]{:S(2)}) collective-permute-start(bf16[2,2,2,8,512]{4,3,0,1,2:T(8,128)(2,1)S(1)} %fusion.58), channel_id=1, source_target_pairs={{0,2},{1,9},{2,0},{3,11},{4,6},{5,13},{6,4},{7,15},{8,10},{9,1},{1... | collective-permute-start | bytes 196616 | tf_op jit(solution)/shard_map/ppermute | solution.py:85
  87.8 5.5 %collective-permute-start.7 = (bf16[2,2,8,512]{3,2,0,1:T(8,128)(2,1)S(1)}, bf16[2,2,8,512]{3,2,0,1:T(8,128)(2,1)S(1)}, u32[]{:S(2)}, u32[]{:S(2)}) collective-permute-start(bf16[2,2,8,512]{3,2,0,1:T(8,128)(2,1)S(1)} %fusion.68), channel_id=1, source_target_pairs={{0,4},{1,17},{2,6},{3,19},{4,0},{5,21},{6,2},{7,23},{8,12},{9,25},... | collective-permute-start | bytes 98312 | tf_op jit(solution)/shard_map/ppermute | solution.py:85
  92.8 8.3 %collective-permute-start.2 = (bf16[3,3,2,2,16,256]{5,4,1,0,2,3:T(8,128)(2,1)S(1)}, bf16[3,3,2,2,16,256]{5,4,1,0,2,3:T(8,128)(2,1)S(1)}, u32[]{:S(2)}, u32[]{:S(2)}) collective-permute-start(bf16[3,3,2,2,16,256]{5,4,1,0,2,3:T(8,128)(2,1)S(1)} %fusion.32), channel_id=1, source_target_pairs={{0,4},{1,17},{2,6},{3,19},{4,0},{5,21},{6,2},{7,23},{8,12},{9,25},... | collective-permute-start | bytes 884744 | tf_op jit(solution)/shard_map/ppermute | solution.py:85
  93.3 9.9 %collective-permute-start.8 = (bf16[2,8,512]{2,1,0:T(8,128)(2,1)S(1)}, bf16[2,8,512]{2,1,0:T(8,128)(2,1)S(1)}, u32[]{:S(2)}, u32[]{:S(2)}) collective-permute-start(bf16[2,8,512]{2,1,0:T(8,128)(2,1)S(1)} %fusion.70), channel_id=1, source_target_pairs={{0,8},{1,3},{2,10},{3,1},{4,12},{5,7},{6,14},{7,5},{8,0},{9,11},{1... | collective-permute-start | bytes 49160 | tf_op jit(solution)/shard_map/ppermute | solution.py:85
  101.2 5.7 %collective-permute-start.3 = (bf16[3,3,2,16,256]{4,3,1,0,2:T(8,128)(2,1)S(1)}, bf16[3,3,2,16,256]{4,3,1,0,2:T(8,128)(2,1)S(1)}, u32[]{:S(2)}, u32[]{:S(2)}) collective-permute-start(bf16[3,3,2,16,256]{4,3,1,0,2:T(8,128)(2,1)S(1)} %fusion.38), channel_id=1, source_target_pairs={{0,8},{1,3},{2,10},{3,1},{4,12},{5,7},{6,14},{7,5},{8,0},{9,11},{1... | collective-permute-start | bytes 442376 | tf_op jit(solution)/shard_map/ppermute | solution.py:85
  103.3 7.4 %collective-permute-start.9 = (bf16[8,512]{1,0:T(8,128)(2,1)S(1)}, bf16[8,512]{1,0:T(8,128)(2,1)S(1)}, u32[]{:S(2)}, u32[]{:S(2)}) collective-permute-start(bf16[8,512]{1,0:T(8,128)(2,1)S(1)} %fusion.72), channel_id=1, source_target_pairs={{0,16},{1,5},{2,18},{3,7},{4,20},{5,1},{6,22},{7,3},{8,24},{9,13},... | collective-permute-start | bytes 24584 | tf_op jit(solution)/shard_map/ppermute | solution.py:85
  107.0 6.1 %collective-permute-start.4 = (bf16[3,3,16,256]{3,2,1,0:T(8,128)(2,1)S(1)}, bf16[3,3,16,256]{3,2,1,0:T(8,128)(2,1)S(1)}, u32[]{:S(2)}, u32[]{:S(2)}) collective-permute-start(bf16[3,3,16,256]{3,2,1,0:T(8,128)(2,1)S(1)} %fusion.56), channel_id=1, source_target_pairs={{0,16},{1,5},{2,18},{3,7},{4,20},{5,1},{6,22},{7,3},{8,24},{9,13},... | collective-permute-start | bytes 221192 | tf_op jit(solution)/shard_map/ppermute | solution.py:85
  116.2 13.9 %all-to-all-start.2 = ((f32[32,1,2]{2,1,0:T(1,128)}), f32[32,1,2]{2,1,0:T(1,128)}, u32[]{:S(2)}, u32[]{:S(2)}) async-start(f32[32,1,2]{2,1,0:T(1,128)} %broadcast_in_dim.19), calls=%async_computation.2 | async-start | bytes 32768 | tf_op jit(solution)/shard_map/all_to_all | solution.py:175
  133.9 6.2 %collective-permute-start.10 = (bf16[3,3,16,256]{3,2,1,0:T(8,128)(2,1)}, bf16[3,3,16,256]{3,2,1,0:T(8,128)(2,1)}, u32[]{:S(2)}, u32[]{:S(2)}) collective-permute-start(bf16[3,3,16,256]{3,2,1,0:T(8,128)(2,1)} %fusion.79), channel_id=1, source_target_pairs={{0,16},{1,5},{2,18},{3,7},{4,20},{5,1},{6,22},{7,3},{8,24},{9,13},... | collective-permute-start | bytes 221192 | tf_op jit(solution)/shard_map/ppermute | solution.py:85
  142.3 5.5 %collective-permute-start.11 = (bf16[3,3,2,16,256]{4,3,1,0,2:T(8,128)(2,1)}, bf16[3,3,2,16,256]{4,3,1,0,2:T(8,128)(2,1)}, u32[]{:S(2)}, u32[]{:S(2)}) collective-permute-start(bf16[3,3,2,16,256]{4,3,1,0,2:T(8,128)(2,1)} %pad_maximum_fusion.5), channel_id=1, source_target_pairs={{0,8},{1,3},{2,10},{3,1},{4,12},{5,7},{6,14},{7,5},{8,0},{9,11},{1... | collective-permute-start | bytes 442376 | tf_op jit(solution)/shard_map/ppermute | solution.py:85
  150.2 8.5 %collective-permute-start.12 = (bf16[3,3,2,2,16,256]{5,4,1,0,2,3:T(8,128)(2,1)}, bf16[3,3,2,2,16,256]{5,4,1,0,2,3:T(8,128)(2,1)}, u32[]{:S(2)}, u32[]{:S(2)}) collective-permute-start(bf16[3,3,2,2,16,256]{5,4,1,0,2,3:T(8,128)(2,1)} %pad_maximum_fusion.3), channel_id=1, source_target_pairs={{0,4},{1,17},{2,6},{3,19},{4,0},{5,21},{6,2},{7,23},{8,12},{9,25},... | collective-permute-start | bytes 884744 | tf_op jit(solution)/shard_map/ppermute | solution.py:85
  152.1 10.0 %collective-permute-start.15 = (bf16[8,512]{1,0:T(8,128)(2,1)S(1)}, bf16[8,512]{1,0:T(8,128)(2,1)S(1)}, u32[]{:S(2)}, u32[]{:S(2)}) collective-permute-start(bf16[8,512]{1,0:T(8,128)(2,1)S(1)} %fusion.78), channel_id=1, source_target_pairs={{0,16},{1,5},{2,18},{3,7},{4,20},{5,1},{6,22},{7,3},{8,24},{9,13},... | collective-permute-start | bytes 24584 | tf_op jit(solution)/shard_map/ppermute | solution.py:85
  161.5 10.2 %collective-permute-start.13 = (bf16[3,3,2,2,2,16,256]{6,5,1,0,2,3,4:T(8,128)(2,1)}, bf16[3,3,2,2,2,16,256]{6,5,1,0,2,3,4:T(8,128)(2,1)}, u32[]{:S(2)}, u32[]{:S(2)}) collective-permute-start(bf16[3,3,2,2,2,16,256]{6,5,1,0,2,3,4:T(8,128)(2,1)} %pad_maximum_fusion.2), channel_id=1, source_target_pairs={{0,2},{1,9},{2,0},{3,11},{4,6},{5,13},{6,4},{7,15},{8,10},{9,1},{1... | collective-permute-start | bytes 1769480 | tf_op jit(solution)/shard_map/ppermute | solution.py:85
  162.7 4.2 %collective-permute-start.16 = (bf16[2,8,512]{2,1,0:T(8,128)(2,1)S(1)}, bf16[2,8,512]{2,1,0:T(8,128)(2,1)}, u32[]{:S(2)}, u32[]{:S(2)}) collective-permute-start(bf16[2,8,512]{2,1,0:T(8,128)(2,1)S(1)} %pad_maximum_fusion.9), channel_id=1, source_target_pairs={{0,8},{1,3},{2,10},{3,1},{4,12},{5,7},{6,14},{7,5},{8,0},{9,11},{1... | collective-permute-start | bytes 49160 | tf_op jit(solution)/shard_map/ppermute | solution.py:85
  168.2 6.0 %collective-permute-start.17 = (bf16[2,2,8,512]{3,2,0,1:T(8,128)(2,1)}, bf16[2,2,8,512]{3,2,0,1:T(8,128)(2,1)}, u32[]{:S(2)}, u32[]{:S(2)}) collective-permute-start(bf16[2,2,8,512]{3,2,0,1:T(8,128)(2,1)} %pad_maximum_fusion.8), channel_id=1, source_target_pairs={{0,4},{1,17},{2,6},{3,19},{4,0},{5,21},{6,2},{7,23},{8,12},{9,25},... | collective-permute-start | bytes 98312 | tf_op jit(solution)/shard_map/ppermute | solution.py:85
  174.2 6.7 %collective-permute-start.14 = (bf16[3,3,2,2,2,2,16,256]{7,6,5,4,3,2,1,0:T(8,128)(2,1)}, bf16[3,3,2,2,2,2,16,256]{7,6,5,4,3,2,1,0:T(8,128)(2,1)}, u32[]{:S(2)}, u32[]{:S(2)}) collective-permute-start(bf16[3,3,2,2,2,2,16,256]{7,6,5,4,3,2,1,0:T(8,128)(2,1)} %get-tuple-element.41), channel_id=1, source_target_pairs={{0,1},{1,0},{2,3},{3,2},{4,5},{5,4},{6,7},{7,6},{8,9},{9,8},{10,11... | collective-permute-start | bytes 3538952 | tf_op jit(solution)/shard_map/ppermute | solution.py:85
  175.0 4.3 %collective-permute-start.18 = (bf16[2,2,2,8,512]{4,3,0,1,2:T(8,128)(2,1)S(1)}, bf16[2,2,2,8,512]{4,3,0,1,2:T(8,128)(2,1)S(1)}, u32[]{:S(2)}, u32[]{:S(2)}) collective-permute-start(bf16[2,2,2,8,512]{4,3,0,1,2:T(8,128)(2,1)S(1)} %pad_maximum_fusion.7), channel_id=1, source_target_pairs={{0,2},{1,9},{2,0},{3,11},{4,6},{5,13},{6,4},{7,15},{8,10},{9,1},{1... | collective-permute-start | bytes 196616 | tf_op jit(solution)/shard_map/ppermute | solution.py:85
  207.5 7.1 %collective-permute-start.25 = (bf16[2,2,2,2,8,512]{5,4,3,2,1,0:T(8,128)(2,1)S(1)}, bf16[2,2,2,2,8,512]{5,4,3,2,1,0:T(8,128)(2,1)S(1)}, u32[]{:S(2)}, u32[]{:S(2)}) collective-permute-start(bf16[2,2,2,2,8,512]{5,4,3,2,1,0:T(8,128)(2,1)S(1)} %fusion.41), channel_id=1, source_target_pairs={{0,1},{1,0},{2,3},{3,2},{4,5},{5,4},{6,7},{7,6},{8,9},{9,8},{10,11... | collective-permute-start | bytes 393224 | tf_op jit(solution)/shard_map/ppermute | solution.py:85
  213.4 12.3 %collective-permute-start.21 = (bf16[3,3,2,2,2,16,256]{6,5,1,0,2,3,4:T(8,128)(2,1)S(1)}, bf16[3,3,2,2,2,16,256]{6,5,1,0,2,3,4:T(8,128)(2,1)S(1)}, u32[]{:S(2)}, u32[]{:S(2)}) collective-permute-start(bf16[3,3,2,2,2,16,256]{6,5,1,0,2,3,4:T(8,128)(2,1)S(1)} %fusion.31), channel_id=1, source_target_pairs={{0,2},{1,9},{2,0},{3,11},{4,6},{5,13},{6,4},{7,15},{8,10},{9,1},{1... | collective-permute-start | bytes 1769480 | tf_op jit(solution)/shard_map/ppermute | solution.py:85
  214.7 9.4 %collective-permute-start.26 = (bf16[2,2,2,8,512]{4,3,0,1,2:T(8,128)(2,1)S(1)}, bf16[2,2,2,8,512]{4,3,0,1,2:T(8,128)(2,1)S(1)}, u32[]{:S(2)}, u32[]{:S(2)}) collective-permute-start(bf16[2,2,2,8,512]{4,3,0,1,2:T(8,128)(2,1)S(1)} %fusion.59), channel_id=1, source_target_pairs={{0,2},{1,9},{2,0},{3,11},{4,6},{5,13},{6,4},{7,15},{8,10},{9,1},{1... | collective-permute-start | bytes 196616 | tf_op jit(solution)/shard_map/ppermute | solution.py:85
  224.1 5.5 %collective-permute-start.27 = (bf16[2,2,8,512]{3,2,0,1:T(8,128)(2,1)S(1)}, bf16[2,2,8,512]{3,2,0,1:T(8,128)(2,1)S(1)}, u32[]{:S(2)}, u32[]{:S(2)}) collective-permute-start(bf16[2,2,8,512]{3,2,0,1:T(8,128)(2,1)S(1)} %fusion.69), channel_id=1, source_target_pairs={{0,4},{1,17},{2,6},{3,19},{4,0},{5,21},{6,2},{7,23},{8,12},{9,25},... | collective-permute-start | bytes 98312 | tf_op jit(solution)/shard_map/ppermute | solution.py:85
  227.2 8.3 %collective-permute-start.22 = (bf16[3,3,2,2,16,256]{5,4,1,0,2,3:T(8,128)(2,1)S(1)}, bf16[3,3,2,2,16,256]{5,4,1,0,2,3:T(8,128)(2,1)S(1)}, u32[]{:S(2)}, u32[]{:S(2)}) collective-permute-start(bf16[3,3,2,2,16,256]{5,4,1,0,2,3:T(8,128)(2,1)S(1)} %fusion.33), channel_id=1, source_target_pairs={{0,4},{1,17},{2,6},{3,19},{4,0},{5,21},{6,2},{7,23},{8,12},{9,25},... | collective-permute-start | bytes 884744 | tf_op jit(solution)/shard_map/ppermute | solution.py:85
  229.7 7.0 %collective-permute-start.28 = (bf16[2,8,512]{2,1,0:T(8,128)(2,1)S(1)}, bf16[2,8,512]{2,1,0:T(8,128)(2,1)S(1)}, u32[]{:S(2)}, u32[]{:S(2)}) collective-permute-start(bf16[2,8,512]{2,1,0:T(8,128)(2,1)S(1)} %fusion.71), channel_id=1, source_target_pairs={{0,8},{1,3},{2,10},{3,1},{4,12},{5,7},{6,14},{7,5},{8,0},{9,11},{1... | collective-permute-start | bytes 49160 | tf_op jit(solution)/shard_map/ppermute | solution.py:85
  235.7 5.2 %collective-permute-start.23 = (bf16[3,3,2,16,256]{4,3,1,0,2:T(8,128)(2,1)S(1)}, bf16[3,3,2,16,256]{4,3,1,0,2:T(8,128)(2,1)S(1)}, u32[]{:S(2)}, u32[]{:S(2)}) collective-permute-start(bf16[3,3,2,16,256]{4,3,1,0,2:T(8,128)(2,1)S(1)} %fusion.39), channel_id=1, source_target_pairs={{0,8},{1,3},{2,10},{3,1},{4,12},{5,7},{6,14},{7,5},{8,0},{9,11},{1... | collective-permute-start | bytes 442376 | tf_op jit(solution)/shard_map/ppermute | solution.py:85
  236.7 5.8 %collective-permute-start.29 = (bf16[8,512]{1,0:T(8,128)(2,1)S(1)}, bf16[8,512]{1,0:T(8,128)(2,1)S(1)}, u32[]{:S(2)}, u32[]{:S(2)}) collective-permute-start(bf16[8,512]{1,0:T(8,128)(2,1)S(1)} %fusion.73), channel_id=1, source_target_pairs={{0,16},{1,5},{2,18},{3,7},{4,20},{5,1},{6,22},{7,3},{8,24},{9,13},... | collective-permute-start | bytes 24584 | tf_op jit(solution)/shard_map/ppermute | solution.py:85
  241.0 5.9 %collective-permute-start.24 = (bf16[3,3,16,256]{3,2,1,0:T(8,128)(2,1)S(1)}, bf16[3,3,16,256]{3,2,1,0:T(8,128)(2,1)S(1)}, u32[]{:S(2)}, u32[]{:S(2)}) collective-permute-start(bf16[3,3,16,256]{3,2,1,0:T(8,128)(2,1)S(1)} %fusion.57), channel_id=1, source_target_pairs={{0,16},{1,5},{2,18},{3,7},{4,20},{5,1},{6,22},{7,3},{8,24},{9,13},... | collective-permute-start | bytes 221192 | tf_op jit(solution)/shard_map/ppermute | solution.py:85
  250.2 11.8 %all-to-all-start.3 = ((f32[32,1,2]{2,1,0:T(1,128)}), f32[32,1,2]{2,1,0:T(1,128)S(1)}, u32[]{:S(2)}, u32[]{:S(2)}) async-start(f32[32,1,2]{2,1,0:T(1,128)} %broadcast_in_dim.20), calls=%async_computation.3 | async-start | bytes 32768 | tf_op jit(solution)/shard_map/all_to_all | solution.py:175
  (45 other events, 502.1 us)

commit v14 on v8

--- a/solution.py
+++ b/solution.py
@@ -123,22 +123,22 @@
     order = jnp.arange(sources, dtype=jnp.int32)
     earlier = (task_of[:, None] == task_of[None, :]) & (order[None, :] < order[:, None])
     position = jnp.sum(earlier.astype(jnp.int32), axis=1)
-    send_feats = (
-        jnp.zeros((groups, bucket, side, side, chans), jnp.bfloat16)
-        .at[task_of, position]
-        .set(feats)
-    )
     send_labels = (
         jnp.full((groups, bucket, cells), -1.0, jnp.bfloat16)
         .at[task_of, position]
         .set(targets.astype(jnp.bfloat16))
     )
-    come_feats, come_labels = (
-        lax.all_to_all(send_feats, "task", split_axis=0, concat_axis=0, tiled=True),
-        lax.all_to_all(send_labels, "task", split_axis=0, concat_axis=0, tiled=True),
-    )
-    held_feats = come_feats.reshape(groups * bucket, side, side, chans)
-    held_labels = come_labels.reshape(groups * bucket, cells).astype(jnp.int32)
+    send_feats = (
+        jnp.zeros((groups, bucket + 1, side, side, chans), jnp.bfloat16)
+        .at[task_of, position]
+        .set(feats)
+        .at[:, bucket, 0, 0, : bucket * cells]
+        .set(send_labels.reshape(groups, bucket * cells))
+    )
+    come_feats = lax.all_to_all(send_feats, "task", split_axis=0, concat_axis=0, tiled=True)
+    held_feats = come_feats[:, :bucket].reshape(groups * bucket, side, side, chans)
+    held_labels = come_feats[:, bucket, 0, 0, : bucket * cells]
+    held_labels = held_labels.reshape(groups * bucket, cells).astype(jnp.int32)
     count = counts[0].astype(jnp.float32)
     entries = 10.0 * CHANNELS * INNER
     place = lax.axis_index("ex")

time: 250 us -> 251 us (level)
  starting transfers between devices: 56.3 us -> 52.4 us
    all_to_all x1 -> x0, starting transfers between devices: 4.4 us -> none  [shards(): lax.all_to_all(send_labels, 'task', split_axis=0, concat_axis=0, tiled=True)]
    all_to_all x1, waiting for transfers between devices: 15.3 us -> 18.9 us  [shards(): lax.all_to_all(send_feats, 'task', split_axis=0, concat_axis=0, tiled=True)]
  transfers between devices with their start and end apart: 34 -> 33, of which waited for: 20 -> 19; matrix products, arithmetic and copies ran while one was open for 9% -> 8% of each run, Pallas kernels for 0% -> 0%
where the time goes in v14:
time: 251 us; the launch traced here: 246 us
  waiting for transfers between devices  92.2 us (37%)
  starting transfers between devices  52.4 us (21%)
  matrix products  36.6 us (15%)
  local copies, waits for them, and re-layouts  29.4 us (12%)
  other arithmetic  27.1 us (11%)
  between operations  8 us (3%)
    ppermute x30, waiting for transfers between devices, partner_swap(): return lax.ppermute(value, 'ex', perm=pairs)  59.4 us
    ppermute x30, starting transfers between devices, partner_swap(): return lax.ppermute(value, 'ex', perm=pairs)  37.8 us
    all_to_all x1, waiting for transfers between devices, shards(): lax.all_to_all(send_feats, 'task', split_axis=0, concat_axis=0, tiled=True)  18.9 us
    dot_general x20, matrix products, contract_rows(): lax.dot_general(left, right, (((0,), (0,)), ((), ())), preferred_element_...  17.1 us
    unnamed x70, local copies, waits for them, and re-layouts  14.5 us
    all_to_all x2, waiting for transfers between devices, shards(): totals = jnp.sum(lax.all_to_all(spread, 'ex', 0, 0, tiled=True), axis=0)  14 us
    dot_general x18, matrix products, train_pass(): jnp.dot(windows[offset_index], down_low[offset_index // 3, offset_index %...  10.4 us
    all_to_all x2, starting transfers between devices, shards(): totals = jnp.sum(lax.all_to_all(spread, 'ex', 0, 0, tiled=True), axis=0)  10.2 us
  transfers between devices with their start and end apart: 33, of which 19 were waited for; matrix products, arithmetic and copies ran while one was open for 8% of the time, Pallas kernels for 0%

profile of v14, /device:TPU:0, one launch (start us, length us, event | category | flops | bytes accessed | tf_op | source)
XLA Modules:
  0.0 245.8 jit_solution(17173738577941735833)
XLA Ops:
  5.7 2.9 %scatter_fusion = bf16[4,7,8,8,512]{4,3,2,1,0:T(8,128)(2,1)} fusion(bf16[4,7,8,8,512]{4,3,2,1,0:T(8,128)(2,1)} %broadcast_in_dim.16, s32[12]{0:T(128)S(1)} %get-tuple-element.48, bf16[12,8,8,512]{3,2,1,0:T(8,128)(2,1)S(1)} %copy-done.29), kind=kCustom, calls=%fused_computation | custom fusion | bytes 2359392 | tf_op jit(solution)/shard_map/scatter | solution.py:134
  10.1 4.4 %all-to-all-start = ((bf16[4,7,8,8,512]{4,3,2,1,0:T(8,128)(2,1)}), bf16[4,7,8,8,512]{4,3,2,1,0:T(8,128)(2,1)S(1)}, u32[]{:S(2)}, u32[]{:S(2)}) async-start(bf16[4,7,8,8,512]{4,3,2,1,0:T(8,128)(2,1)} %scatter.21), calls=%async_computation | async-start | bytes 3670016 | tf_op jit(solution)/shard_map/all_to_all | solution.py:138
  15.1 4.0 %convert_bitcast_fusion = bf16[3,3,512,256]{3,2,1,0:T(8,128)(2,1)} fusion(f32[1,3,3,512,256]{4,3,2,1,0:T(8,128)} %param.13), kind=kLoop, calls=%fused_computation.51 | loop fusion | flops 1179648 | bytes 7077888 | tf_op jit(solution)/shard_map/convert_element_type | solution.py:149
  19.1 18.9 %all-to-all-done = bf16[4,7,8,8,512]{4,3,2,1,0:T(8,128)(2,1)S(1)} async-done(((bf16[4,7,8,8,512]{4,3,2,1,0:T(8,128)(2,1)}), bf16[4,7,8,8,512]{4,3,2,1,0:T(8,128)(2,1)S(1)}, u32[]{:S(2)}, u32[]{:S(2)}) %all-to-all-start) | async-done | bytes 1835040 | tf_op jit(solution)/shard_map/all_to_all | solution.py:138
  40.0 2.6 %pad_slice_fusion = (bf16[24,8,8,512]{3,2,1,0:T(8,128)(2,1)S(1)}, bf16[24,8,8,512]{3,2,1,0:T(8,128)(2,1)S(1)}, bf16[24,8,8,512]{3,2,1,0:T(8,128)(2,1)S(1)}, bf16...) fusion(bf16[24,8,8,512]{3,2,1,0:T(8,128)(2,1)S(1)} %bitcast.466), kind=kLoop, calls=%fused_computation.2 | loop fusion | bytes 14155776 | tf_op jit(solution)/shard_map/slice | solution.py:19
  60.3 2.1 copy-done.19
  63.8 2.7 %fusion.91 = f32[256,512]{1,0:T(8,128)S(1)} fusion(bf16[1536,512]{0,1:T(8,128)(2,1)} %copy-done.27, f32[1536,256]{1,0:T(8,128)} %copy-done.23), kind=kOutput, calls=%fused_computation.289 | convolution fusion | flops 404619264 | bytes 3670016 | tf_op jit(solution)/shard_map/dot_general | solution.py:25
  71.3 7.1 %collective-permute-done.6 = bf16[2,2,2,8,512]{4,3,0,1,2:T(8,128)(2,1)S(1)} collective-permute-done((bf16[2,2,2,8,512]{4,3,0,1,2:T(8,128)(2,1)S(1)}, bf16[2,2,2,8,512]{4,3,0,1,2:T(8,128)(2,1)S(1)}, u32[]{:S(2)}, u32[]{:S(2)}) %collective-permute-start.6) | collective-permute-done | bytes 65568 | tf_op jit(solution)/shard_map/ppermute | solution.py:85
  78.4 3.3 %collective-permute-start.7 = (bf16[2,2,8,512]{3,2,0,1:T(8,128)(2,1)S(1)}, bf16[2,2,8,512]{3,2,0,1:T(8,128)(2,1)S(1)}, u32[]{:S(2)}, u32[]{:S(2)}) collective-permute-start(bf16[2,2,8,512]{3,2,0,1:T(8,128)(2,1)S(1)} %fusion.74), channel_id=1, source_target_pairs={{0,4},{1,17},{2,6},{3,19},{4,0},{5,21},{6,2},{7,23},{8,12},{9,25},... | collective-permute-start | bytes 98312 | tf_op jit(solution)/shard_map/ppermute | solution.py:85
  83.9 2.0 collective-permute-start.8
  86.0 4.5 %collective-permute-done.2 = bf16[3,3,2,2,16,256]{5,4,1,0,2,3:T(8,128)(2,1)S(1)} collective-permute-done((bf16[3,3,2,2,16,256]{5,4,1,0,2,3:T(8,128)(2,1)S(1)}, bf16[3,3,2,2,16,256]{5,4,1,0,2,3:T(8,128)(2,1)S(1)}, u32[]{:S(2)}, u32[]{:S(2)}) %collective-permute-start.2) | collective-permute-done | bytes 294944 | tf_op jit(solution)/shard_map/ppermute | solution.py:85
  92.6 3.6 %collective-permute-start.9 = (bf16[8,512]{1,0:T(8,128)(2,1)S(1)}, bf16[8,512]{1,0:T(8,128)(2,1)S(1)}, u32[]{:S(2)}, u32[]{:S(2)}) collective-permute-start(bf16[8,512]{1,0:T(8,128)(2,1)S(1)} %fusion.78), channel_id=1, source_target_pairs={{0,16},{1,5},{2,18},{3,7},{4,20},{5,1},{6,22},{7,3},{8,24},{9,13},... | collective-permute-start | bytes 24584 | tf_op jit(solution)/shard_map/ppermute | solution.py:85
  96.3 3.5 %collective-permute-start.4 = (bf16[3,3,16,256]{3,2,1,0:T(8,128)(2,1)S(1)}, bf16[3,3,16,256]{3,2,1,0:T(8,128)(2,1)S(1)}, u32[]{:S(2)}, u32[]{:S(2)}) collective-permute-start(bf16[3,3,16,256]{3,2,1,0:T(8,128)(2,1)S(1)} %fusion.62), channel_id=1, source_target_pairs={{0,16},{1,5},{2,18},{3,7},{4,20},{5,1},{6,22},{7,3},{8,24},{9,13},... | collective-permute-start | bytes 221192 | tf_op jit(solution)/shard_map/ppermute | solution.py:85
  105.6 5.7 %all-to-all-start.1 = ((f32[32,1,2]{2,1,0:T(1,128)}), f32[32,1,2]{2,1,0:T(1,128)S(1)}, u32[]{:S(2)}, u32[]{:S(2)}) async-start(f32[32,1,2]{2,1,0:T(1,128)} %broadcast_in_dim.19), calls=%async_computation.1 | async-start | bytes 32768 | tf_op jit(solution)/shard_map/all_to_all | solution.py:175
  111.3 7.3 %all-to-all-done.1 = f32[32,1,2]{2,1,0:T(1,128)S(1)} async-done(((f32[32,1,2]{2,1,0:T(1,128)}), f32[32,1,2]{2,1,0:T(1,128)S(1)}, u32[]{:S(2)}, u32[]{:S(2)}) %all-to-all-start.1) | async-done | bytes 288 | tf_op jit(solution)/shard_map/all_to_all | solution.py:175
  122.2 4.6 %collective-permute-done.10 = bf16[3,3,16,256]{3,2,1,0:T(8,128)(2,1)S(1)} collective-permute-done((bf16[3,3,16,256]{3,2,1,0:T(8,128)(2,1)S(1)}, bf16[3,3,16,256]{3,2,1,0:T(8,128)(2,1)S(1)}, u32[]{:S(2)}, u32[]{:S(2)}) %collective-permute-start.10) | collective-permute-done | bytes 73760 | tf_op jit(solution)/shard_map/ppermute | solution.py:85
  127.6 4.5 %collective-permute-done.11 = bf16[3,3,2,16,256]{4,3,2,1,0:T(8,128)(2,1)S(1)} collective-permute-done((bf16[3,3,2,16,256]{4,3,2,1,0:T(8,128)(2,1)S(1)}, bf16[3,3,2,16,256]{4,3,2,1,0:T(8,128)(2,1)S(1)}, u32[]{:S(2)}, u32[]{:S(2)}) %collective-permute-start.11) | collective-permute-done | bytes 147488 | tf_op jit(solution)/shard_map/ppermute | solution.py:85
  135.4 5.1 %collective-permute-done.12 = bf16[3,3,2,2,16,256]{5,4,3,2,1,0:T(8,128)(2,1)S(1)} collective-permute-done((bf16[3,3,2,2,16,256]{5,4,3,2,1,0:T(8,128)(2,1)S(1)}, bf16[3,3,2,2,16,256]{5,4,3,2,1,0:T(8,128)(2,1)S(1)}, u32[]{:S(2)}, u32[]{:S(2)}) %collective-permute-start.12) | collective-permute-done | bytes 294944 | tf_op jit(solution)/shard_map/ppermute | solution.py:85
  142.0 3.5 %collective-permute-done.16 = bf16[2,8,512]{2,1,0:T(8,128)(2,1)S(1)} collective-permute-done((bf16[2,8,512]{2,1,0:T(8,128)(2,1)S(1)}, bf16[2,8,512]{2,1,0:T(8,128)(2,1)S(1)}, u32[]{:S(2)}, u32[]{:S(2)}) %collective-permute-start.16) | collective-permute-done | bytes 16416 | tf_op jit(solution)/shard_map/ppermute | solution.py:85
  147.4 3.2 %collective-permute-done.13 = bf16[3,3,2,2,2,16,256]{6,5,4,3,2,1,0:T(8,128)(2,1)} collective-permute-done((bf16[3,3,2,2,2,16,256]{6,5,4,3,2,1,0:T(8,128)(2,1)S(1)}, bf16[3,3,2,2,2,16,256]{6,5,4,3,2,1,0:T(8,128)(2,1)}, u32[]{:S(2)}, u32[]{:S(2)}) %collective-permute-start.13) | collective-permute-done | bytes 589856 | tf_op jit(solution)/shard_map/ppermute | solution.py:85
  154.2 3.5 %collective-permute-done.18 = bf16[2,2,2,8,512]{4,3,2,1,0:T(8,128)(2,1)S(1)} collective-permute-done((bf16[2,2,2,8,512]{4,3,2,1,0:T(8,128)(2,1)S(1)}, bf16[2,2,2,8,512]{4,3,2,1,0:T(8,128)(2,1)S(1)}, u32[]{:S(2)}, u32[]{:S(2)}) %collective-permute-start.18) | collective-permute-done | bytes 65568 | tf_op jit(solution)/shard_map/ppermute | solution.py:85
  159.5 2.1 select_bitcast_fusion.1
  186.5 2.1 copy-done.18
  189.0 2.7 %fusion.92 = f32[256,512]{1,0:T(8,128)S(1)} fusion(bf16[1536,512]{0,1:T(8,128)(2,1)} %copy-done.28, f32[1536,256]{1,0:T(8,128)} %copy-done.24), kind=kOutput, calls=%fused_computation.290 | convolution fusion | flops 404619264 | bytes 3670016 | tf_op jit(solution)/shard_map/dot_general | solution.py:25
  196.5 7.1 %collective-permute-done.26 = bf16[2,2,2,8,512]{4,3,0,1,2:T(8,128)(2,1)S(1)} collective-permute-done((bf16[2,2,2,8,512]{4,3,0,1,2:T(8,128)(2,1)S(1)}, bf16[2,2,2,8,512]{4,3,0,1,2:T(8,128)(2,1)S(1)}, u32[]{:S(2)}, u32[]{:S(2)}) %collective-permute-start.26) | collective-permute-done | bytes 65568 | tf_op jit(solution)/shard_map/ppermute | solution.py:85
  205.1 2.4 collective-permute-start.22
  209.9 3.8 %collective-permute-done.22 = bf16[3,3,2,2,16,256]{5,4,1,0,2,3:T(8,128)(2,1)S(1)} collective-permute-done((bf16[3,3,2,2,16,256]{5,4,1,0,2,3:T(8,128)(2,1)S(1)}, bf16[3,3,2,2,16,256]{5,4,1,0,2,3:T(8,128)(2,1)S(1)}, u32[]{:S(2)}, u32[]{:S(2)}) %collective-permute-start.22) | collective-permute-done | bytes 294944 | tf_op jit(solution)/shard_map/ppermute | solution.py:85
  214.5 2.1 collective-permute-start.29
  216.6 2.4 collective-permute-done.23
  221.0 4.0 %collective-permute-done.24 = bf16[3,3,16,256]{3,2,1,0:T(8,128)(2,1)S(1)} collective-permute-done((bf16[3,3,16,256]{3,2,1,0:T(8,128)(2,1)S(1)}, bf16[3,3,16,256]{3,2,1,0:T(8,128)(2,1)S(1)}, u32[]{:S(2)}, u32[]{:S(2)}) %collective-permute-start.24) | collective-permute-done | bytes 73760 | tf_op jit(solution)/shard_map/ppermute | solution.py:85
  228.2 4.5 %all-to-all-start.2 = ((f32[32,1,2]{2,1,0:T(1,128)}), f32[32,1,2]{2,1,0:T(1,128)S(1)}, u32[]{:S(2)}, u32[]{:S(2)}) async-start(f32[32,1,2]{2,1,0:T(1,128)} %broadcast_in_dim.20), calls=%async_computation.2 | async-start | bytes 32768 | tf_op jit(solution)/shard_map/all_to_all | solution.py:175
  233.4 6.7 %all-to-all-done.2 = f32[32,1,2]{2,1,0:T(1,128)S(1)} async-done(((f32[32,1,2]{2,1,0:T(1,128)}), f32[32,1,2]{2,1,0:T(1,128)S(1)}, u32[]{:S(2)}, u32[]{:S(2)}) %all-to-all-start.2) | async-done | bytes 288 | tf_op jit(solution)/shard_map/all_to_all | solution.py:175
  (254 shorter events, 99.0 us)
Async XLA Ops:
  10.1 27.9 %all-to-all-start = ((bf16[4,7,8,8,512]{4,3,2,1,0:T(8,128)(2,1)}), bf16[4,7,8,8,512]{4,3,2,1,0:T(8,128)(2,1)S(1)}, u32[]{:S(2)}, u32[]{:S(2)}) async-start(bf16[4,7,8,8,512]{4,3,2,1,0:T(8,128)(2,1)} %scatter.21), calls=%async_computation | async-start | bytes 3670016 | tf_op jit(solution)/shard_map/all_to_all | solution.py:138
  63.8 3.3 %collective-permute-start = (bf16[3,3,2,2,2,2,16,256]{7,6,1,0,2,3,4,5:T(8,128)(2,1)}, bf16[3,3,2,2,2,2,16,256]{7,6,1,0,2,3,4,5:T(8,128)(2,1)S(1)}, u32[]{:S(2)}, u32[]{:S(2)}) collective-permute-start(bf16[3,3,2,2,2,2,16,256]{7,6,1,0,2,3,4,5:T(8,128)(2,1)} %fusion.30), channel_id=1, source_target_pairs={{0,1},{1,0},{2,3},{3,2},{4,5},{5,4},{6,7},{7,6},{8,9},{9,8},{10,11... | collective-permute-start | bytes 3538952 | tf_op jit(solution)/shard_map/ppermute | solution.py:85
  66.5 2.8 %collective-permute-start.5 = (bf16[2,2,2,2,8,512]{5,4,0,1,2,3:T(8,128)(2,1)S(1)}, bf16[2,2,2,2,8,512]{5,4,0,1,2,3:T(8,128)(2,1)S(1)}, u32[]{:S(2)}, u32[]{:S(2)}) collective-permute-start(bf16[2,2,2,2,8,512]{5,4,0,1,2,3:T(8,128)(2,1)S(1)} %fusion.45), channel_id=1, source_target_pairs={{0,1},{1,0},{2,3},{3,2},{4,5},{5,4},{6,7},{7,6},{8,9},{9,8},{10,11... | collective-permute-start | bytes 393224 | tf_op jit(solution)/shard_map/ppermute | solution.py:85
  67.7 14.0 %collective-permute-start.1 = (bf16[3,3,2,2,2,16,256]{6,5,1,0,2,3,4:T(8,128)(2,1)S(1)}, bf16[3,3,2,2,2,16,256]{6,5,1,0,2,3,4:T(8,128)(2,1)S(1)}, u32[]{:S(2)}, u32[]{:S(2)}) collective-permute-start(bf16[3,3,2,2,2,16,256]{6,5,1,0,2,3,4:T(8,128)(2,1)S(1)} %fusion.33), channel_id=1, source_target_pairs={{0,2},{1,9},{2,0},{3,11},{4,6},{5,13},{6,4},{7,15},{8,10},{9,1},{1... | collective-permute-start | bytes 1769480 | tf_op jit(solution)/shard_map/ppermute | solution.py:85
  69.4 9.0 %collective-permute-start.6 = (bf16[2,2,2,8,512]{4,3,0,1,2:T(8,128)(2,1)S(1)}, bf16[2,2,2,8,512]{4,3,0,1,2:T(8,128)(2,1)S(1)}, u32[]{:S(2)}, u32[]{:S(2)}) collective-permute-start(bf16[2,2,2,8,512]{4,3,0,1,2:T(8,128)(2,1)S(1)} %fusion.64), channel_id=1, source_target_pairs={{0,2},{1,9},{2,0},{3,11},{4,6},{5,13},{6,4},{7,15},{8,10},{9,1},{1... | collective-permute-start | bytes 196616 | tf_op jit(solution)/shard_map/ppermute | solution.py:85
  78.4 5.5 %collective-permute-start.7 = (bf16[2,2,8,512]{3,2,0,1:T(8,128)(2,1)S(1)}, bf16[2,2,8,512]{3,2,0,1:T(8,128)(2,1)S(1)}, u32[]{:S(2)}, u32[]{:S(2)}) collective-permute-start(bf16[2,2,8,512]{3,2,0,1:T(8,128)(2,1)S(1)} %fusion.74), channel_id=1, source_target_pairs={{0,4},{1,17},{2,6},{3,19},{4,0},{5,21},{6,2},{7,23},{8,12},{9,25},... | collective-permute-start | bytes 98312 | tf_op jit(solution)/shard_map/ppermute | solution.py:85
  82.0 8.5 %collective-permute-start.2 = (bf16[3,3,2,2,16,256]{5,4,1,0,2,3:T(8,128)(2,1)S(1)}, bf16[3,3,2,2,16,256]{5,4,1,0,2,3:T(8,128)(2,1)S(1)}, u32[]{:S(2)}, u32[]{:S(2)}) collective-permute-start(bf16[3,3,2,2,16,256]{5,4,1,0,2,3:T(8,128)(2,1)S(1)} %fusion.35), channel_id=1, source_target_pairs={{0,4},{1,17},{2,6},{3,19},{4,0},{5,21},{6,2},{7,23},{8,12},{9,25},... | collective-permute-start | bytes 884744 | tf_op jit(solution)/shard_map/ppermute | solution.py:85
  83.9 8.6 %collective-permute-start.8 = (bf16[2,8,512]{2,1,0:T(8,128)(2,1)S(1)}, bf16[2,8,512]{2,1,0:T(8,128)(2,1)S(1)}, u32[]{:S(2)}, u32[]{:S(2)}) collective-permute-start(bf16[2,8,512]{2,1,0:T(8,128)(2,1)S(1)} %fusion.76), channel_id=1, source_target_pairs={{0,8},{1,3},{2,10},{3,1},{4,12},{5,7},{6,14},{7,5},{8,0},{9,11},{1... | collective-permute-start | bytes 49160 | tf_op jit(solution)/shard_map/ppermute | solution.py:85
  90.6 5.7 %collective-permute-start.3 = (bf16[3,3,2,16,256]{4,3,1,0,2:T(8,128)(2,1)S(1)}, bf16[3,3,2,16,256]{4,3,1,0,2:T(8,128)(2,1)S(1)}, u32[]{:S(2)}, u32[]{:S(2)}) collective-permute-start(bf16[3,3,2,16,256]{4,3,1,0,2:T(8,128)(2,1)S(1)} %fusion.43), channel_id=1, source_target_pairs={{0,8},{1,3},{2,10},{3,1},{4,12},{5,7},{6,14},{7,5},{8,0},{9,11},{1... | collective-permute-start | bytes 442376 | tf_op jit(solution)/shard_map/ppermute | solution.py:85
  92.6 7.2 %collective-permute-start.9 = (bf16[8,512]{1,0:T(8,128)(2,1)S(1)}, bf16[8,512]{1,0:T(8,128)(2,1)S(1)}, u32[]{:S(2)}, u32[]{:S(2)}) collective-permute-start(bf16[8,512]{1,0:T(8,128)(2,1)S(1)} %fusion.78), channel_id=1, source_target_pairs={{0,16},{1,5},{2,18},{3,7},{4,20},{5,1},{6,22},{7,3},{8,24},{9,13},... | collective-permute-start | bytes 24584 | tf_op jit(solution)/shard_map/ppermute | solution.py:85
  96.3 5.9 %collective-permute-start.4 = (bf16[3,3,16,256]{3,2,1,0:T(8,128)(2,1)S(1)}, bf16[3,3,16,256]{3,2,1,0:T(8,128)(2,1)S(1)}, u32[]{:S(2)}, u32[]{:S(2)}) collective-permute-start(bf16[3,3,16,256]{3,2,1,0:T(8,128)(2,1)S(1)} %fusion.62), channel_id=1, source_target_pairs={{0,16},{1,5},{2,18},{3,7},{4,20},{5,1},{6,22},{7,3},{8,24},{9,13},... | collective-permute-start | bytes 221192 | tf_op jit(solution)/shard_map/ppermute | solution.py:85
  105.6 13.0 %all-to-all-start.1 = ((f32[32,1,2]{2,1,0:T(1,128)}), f32[32,1,2]{2,1,0:T(1,128)S(1)}, u32[]{:S(2)}, u32[]{:S(2)}) async-start(f32[32,1,2]{2,1,0:T(1,128)} %broadcast_in_dim.19), calls=%async_computation.1 | async-start | bytes 32768 | tf_op jit(solution)/shard_map/all_to_all | solution.py:175
  120.9 5.9 %collective-permute-start.10 = (bf16[3,3,16,256]{3,2,1,0:T(8,128)(2,1)S(1)}, bf16[3,3,16,256]{3,2,1,0:T(8,128)(2,1)S(1)}, u32[]{:S(2)}, u32[]{:S(2)}) collective-permute-start(bf16[3,3,16,256]{3,2,1,0:T(8,128)(2,1)S(1)} %fusion.90), channel_id=1, source_target_pairs={{0,16},{1,5},{2,18},{3,7},{4,20},{5,1},{6,22},{7,3},{8,24},{9,13},... | collective-permute-start | bytes 221192 | tf_op jit(solution)/shard_map/ppermute | solution.py:85
  126.9 5.2 %collective-permute-start.11 = (bf16[3,3,2,16,256]{4,3,2,1,0:T(8,128)(2,1)S(1)}, bf16[3,3,2,16,256]{4,3,2,1,0:T(8,128)(2,1)S(1)}, u32[]{:S(2)}, u32[]{:S(2)}) collective-permute-start(bf16[3,3,2,16,256]{4,3,2,1,0:T(8,128)(2,1)S(1)} %pad_maximum_fusion.5), channel_id=1, source_target_pairs={{0,8},{1,3},{2,10},{3,1},{4,12},{5,7},{6,14},{7,5},{8,0},{9,11},{1... | collective-permute-start | bytes 442376 | tf_op jit(solution)/shard_map/ppermute | solution.py:85
  132.2 8.3 %collective-permute-start.12 = (bf16[3,3,2,2,16,256]{5,4,3,2,1,0:T(8,128)(2,1)S(1)}, bf16[3,3,2,2,16,256]{5,4,3,2,1,0:T(8,128)(2,1)S(1)}, u32[]{:S(2)}, u32[]{:S(2)}) collective-permute-start(bf16[3,3,2,2,16,256]{5,4,3,2,1,0:T(8,128)(2,1)S(1)} %pad_maximum_fusion.3), channel_id=1, source_target_pairs={{0,4},{1,17},{2,6},{3,19},{4,0},{5,21},{6,2},{7,23},{8,12},{9,25},... | collective-permute-start | bytes 884744 | tf_op jit(solution)/shard_map/ppermute | solution.py:85
  134.1 7.3 %collective-permute-start.15 = (bf16[8,512]{1,0:T(8,128)(2,1)S(1)}, bf16[8,512]{1,0:T(8,128)(2,1)S(1)}, u32[]{:S(2)}, u32[]{:S(2)}) collective-permute-start(bf16[8,512]{1,0:T(8,128)(2,1)S(1)} %fusion.89), channel_id=1, source_target_pairs={{0,16},{1,5},{2,18},{3,7},{4,20},{5,1},{6,22},{7,3},{8,24},{9,13},... | collective-permute-start | bytes 24584 | tf_op jit(solution)/shard_map/ppermute | solution.py:85
  140.6 10.1 %collective-permute-start.13 = (bf16[3,3,2,2,2,16,256]{6,5,4,3,2,1,0:T(8,128)(2,1)S(1)}, bf16[3,3,2,2,2,16,256]{6,5,4,3,2,1,0:T(8,128)(2,1)}, u32[]{:S(2)}, u32[]{:S(2)}) collective-permute-start(bf16[3,3,2,2,2,16,256]{6,5,4,3,2,1,0:T(8,128)(2,1)S(1)} %pad_maximum_fusion.2), channel_id=1, source_target_pairs={{0,2},{1,9},{2,0},{3,11},{4,6},{5,13},{6,4},{7,15},{8,10},{9,1},{1... | collective-permute-start | bytes 1769480 | tf_op jit(solution)/shard_map/ppermute | solution.py:85
  141.5 4.0 %collective-permute-start.16 = (bf16[2,8,512]{2,1,0:T(8,128)(2,1)S(1)}, bf16[2,8,512]{2,1,0:T(8,128)(2,1)S(1)}, u32[]{:S(2)}, u32[]{:S(2)}) collective-permute-start(bf16[2,8,512]{2,1,0:T(8,128)(2,1)S(1)} %pad_maximum_fusion.9), channel_id=1, source_target_pairs={{0,8},{1,3},{2,10},{3,1},{4,12},{5,7},{6,14},{7,5},{8,0},{9,11},{1... | collective-permute-start | bytes 49160 | tf_op jit(solution)/shard_map/ppermute | solution.py:85
  145.5 7.9 %collective-permute-start.17 = (bf16[2,2,8,512]{3,2,1,0:T(8,128)(2,1)S(1)}, bf16[2,2,8,512]{3,2,1,0:T(8,128)(2,1)S(1)}, u32[]{:S(2)}, u32[]{:S(2)}) collective-permute-start(bf16[2,2,8,512]{3,2,1,0:T(8,128)(2,1)S(1)} %pad_maximum_fusion.8), channel_id=1, source_target_pairs={{0,4},{1,17},{2,6},{3,19},{4,0},{5,21},{6,2},{7,23},{8,12},{9,25},... | collective-permute-start | bytes 98312 | tf_op jit(solution)/shard_map/ppermute | solution.py:85
  153.3 6.1 %collective-permute-start.14 = (bf16[3,3,2,2,2,2,16,256]{7,6,5,4,3,2,1,0:T(8,128)(2,1)}, bf16[3,3,2,2,2,2,16,256]{7,6,5,4,3,2,1,0:T(8,128)(2,1)}, u32[]{:S(2)}, u32[]{:S(2)}) collective-permute-start(bf16[3,3,2,2,2,2,16,256]{7,6,5,4,3,2,1,0:T(8,128)(2,1)} %copy_select_fusion.2), channel_id=1, source_target_pairs={{0,1},{1,0},{2,3},{3,2},{4,5},{5,4},{6,7},{7,6},{8,9},{9,8},{10,11... | collective-permute-start | bytes 3538952 | tf_op jit(solution)/shard_map/ppermute | solution.py:85
  153.4 4.3 %collective-permute-start.18 = (bf16[2,2,2,8,512]{4,3,2,1,0:T(8,128)(2,1)S(1)}, bf16[2,2,2,8,512]{4,3,2,1,0:T(8,128)(2,1)S(1)}, u32[]{:S(2)}, u32[]{:S(2)}) collective-permute-start(bf16[2,2,2,8,512]{4,3,2,1,0:T(8,128)(2,1)S(1)} %pad_maximum_fusion.7), channel_id=1, source_target_pairs={{0,2},{1,9},{2,0},{3,11},{4,6},{5,13},{6,4},{7,15},{8,10},{9,1},{1... | collective-permute-start | bytes 196616 | tf_op jit(solution)/shard_map/ppermute | solution.py:85
  188.8 3.4 %collective-permute-start.20 = (bf16[3,3,2,2,2,2,16,256]{7,6,1,0,2,3,4,5:T(8,128)(2,1)S(1)}, bf16[3,3,2,2,2,2,16,256]{7,6,1,0,2,3,4,5:T(8,128)(2,1)S(1)}, u32[]{:S(2)}, u32[]{:S(2)}) collective-permute-start(bf16[3,3,2,2,2,2,16,256]{7,6,1,0,2,3,4,5:T(8,128)(2,1)S(1)} %fusion.31), channel_id=1, source_target_pairs={{0,1},{1,0},{2,3},{3,2},{4,5},{5,4},{6,7},{7,6},{8,9},{9,8},{10,11... | collective-permute-start | bytes 3538952 | tf_op jit(solution)/shard_map/ppermute | solution.py:85
  191.7 2.0 collective-permute-start.25
  192.9 12.0 %collective-permute-start.21 = (bf16[3,3,2,2,2,16,256]{6,5,1,0,2,3,4:T(8,128)(2,1)S(1)}, bf16[3,3,2,2,2,16,256]{6,5,1,0,2,3,4:T(8,128)(2,1)S(1)}, u32[]{:S(2)}, u32[]{:S(2)}) collective-permute-start(bf16[3,3,2,2,2,16,256]{6,5,1,0,2,3,4:T(8,128)(2,1)S(1)} %fusion.34), channel_id=1, source_target_pairs={{0,2},{1,9},{2,0},{3,11},{4,6},{5,13},{6,4},{7,15},{8,10},{9,1},{1... | collective-permute-start | bytes 1769480 | tf_op jit(solution)/shard_map/ppermute | solution.py:85
  193.8 9.8 %collective-permute-start.26 = (bf16[2,2,2,8,512]{4,3,0,1,2:T(8,128)(2,1)S(1)}, bf16[2,2,2,8,512]{4,3,0,1,2:T(8,128)(2,1)S(1)}, u32[]{:S(2)}, u32[]{:S(2)}) collective-permute-start(bf16[2,2,2,8,512]{4,3,0,1,2:T(8,128)(2,1)S(1)} %fusion.65), channel_id=1, source_target_pairs={{0,2},{1,9},{2,0},{3,11},{4,6},{5,13},{6,4},{7,15},{8,10},{9,1},{1... | collective-permute-start | bytes 196616 | tf_op jit(solution)/shard_map/ppermute | solution.py:85
  203.6 5.5 %collective-permute-start.27 = (bf16[2,2,8,512]{3,2,0,1:T(8,128)(2,1)S(1)}, bf16[2,2,8,512]{3,2,0,1:T(8,128)(2,1)S(1)}, u32[]{:S(2)}, u32[]{:S(2)}) collective-permute-start(bf16[2,2,8,512]{3,2,0,1:T(8,128)(2,1)S(1)} %fusion.75), channel_id=1, source_target_pairs={{0,4},{1,17},{2,6},{3,19},{4,0},{5,21},{6,2},{7,23},{8,12},{9,25},... | collective-permute-start | bytes 98312 | tf_op jit(solution)/shard_map/ppermute | solution.py:85
  205.1 8.5 %collective-permute-start.22 = (bf16[3,3,2,2,16,256]{5,4,1,0,2,3:T(8,128)(2,1)S(1)}, bf16[3,3,2,2,16,256]{5,4,1,0,2,3:T(8,128)(2,1)S(1)}, u32[]{:S(2)}, u32[]{:S(2)}) collective-permute-start(bf16[3,3,2,2,16,256]{5,4,1,0,2,3:T(8,128)(2,1)S(1)} %fusion.36), channel_id=1, source_target_pairs={{0,4},{1,17},{2,6},{3,19},{4,0},{5,21},{6,2},{7,23},{8,12},{9,25},... | collective-permute-start | bytes 884744 | tf_op jit(solution)/shard_map/ppermute | solution.py:85
  209.2 5.3 %collective-permute-start.28 = (bf16[2,8,512]{2,1,0:T(8,128)(2,1)S(1)}, bf16[2,8,512]{2,1,0:T(8,128)(2,1)S(1)}, u32[]{:S(2)}, u32[]{:S(2)}) collective-permute-start(bf16[2,8,512]{2,1,0:T(8,128)(2,1)S(1)} %fusion.77), channel_id=1, source_target_pairs={{0,8},{1,3},{2,10},{3,1},{4,12},{5,7},{6,14},{7,5},{8,0},{9,11},{1... | collective-permute-start | bytes 49160 | tf_op jit(solution)/shard_map/ppermute | solution.py:85
  213.8 5.2 %collective-permute-start.23 = (bf16[3,3,2,16,256]{4,3,1,0,2:T(8,128)(2,1)S(1)}, bf16[3,3,2,16,256]{4,3,1,0,2:T(8,128)(2,1)S(1)}, u32[]{:S(2)}, u32[]{:S(2)}) collective-permute-start(bf16[3,3,2,16,256]{4,3,1,0,2:T(8,128)(2,1)S(1)} %fusion.44), channel_id=1, source_target_pairs={{0,8},{1,3},{2,10},{3,1},{4,12},{5,7},{6,14},{7,5},{8,0},{9,11},{1... | collective-permute-start | bytes 442376 | tf_op jit(solution)/shard_map/ppermute | solution.py:85
  214.5 5.9 %collective-permute-start.29 = (bf16[8,512]{1,0:T(8,128)(2,1)S(1)}, bf16[8,512]{1,0:T(8,128)(2,1)S(1)}, u32[]{:S(2)}, u32[]{:S(2)}) collective-permute-start(bf16[8,512]{1,0:T(8,128)(2,1)S(1)} %fusion.79), channel_id=1, source_target_pairs={{0,16},{1,5},{2,18},{3,7},{4,20},{5,1},{6,22},{7,3},{8,24},{9,13},... | collective-permute-start | bytes 24584 | tf_op jit(solution)/shard_map/ppermute | solution.py:85
  219.0 5.9 %collective-permute-start.24 = (bf16[3,3,16,256]{3,2,1,0:T(8,128)(2,1)S(1)}, bf16[3,3,16,256]{3,2,1,0:T(8,128)(2,1)S(1)}, u32[]{:S(2)}, u32[]{:S(2)}) collective-permute-start(bf16[3,3,16,256]{3,2,1,0:T(8,128)(2,1)S(1)} %fusion.63), channel_id=1, source_target_pairs={{0,16},{1,5},{2,18},{3,7},{4,20},{5,1},{6,22},{7,3},{8,24},{9,13},... | collective-permute-start | bytes 221192 | tf_op jit(solution)/shard_map/ppermute | solution.py:85
  228.2 11.8 %all-to-all-start.2 = ((f32[32,1,2]{2,1,0:T(1,128)}), f32[32,1,2]{2,1,0:T(1,128)S(1)}, u32[]{:S(2)}, u32[]{:S(2)}) async-start(f32[32,1,2]{2,1,0:T(1,128)} %broadcast_in_dim.20), calls=%async_computation.2 | async-start | bytes 32768 | tf_op jit(solution)/shard_map/all_to_all | solution.py:175
  (36 other events, 302.7 us)

commit v15 on v8

--- a/solution.py
+++ b/solution.py
@@ -100,9 +100,9 @@
 def double_join(value, axis, bit, pairs, place):
     mine = (place >> bit) & 1
     other = partner_swap(value, pairs)
-    first = jnp.where(mine == 0, value, other)
-    second = jnp.where(mine == 0, other, value)
-    return jnp.stack([first, second], axis=axis)
+    joined = jnp.zeros(value.shape[:axis] + (2,) + value.shape[axis:], value.dtype)
+    joined = lax.dynamic_update_slice_in_dim(joined, jnp.expand_dims(value, axis), mine, axis)
+    return lax.dynamic_update_slice_in_dim(joined, jnp.expand_dims(other, axis), 1 - mine, axis)
 
 
 def swap_bit_axes(value, lead, levels):

time: 250 us -> 267 us (1.068)
  local copies, waits for them, and re-layouts: 27.4 us -> 35.9 us
  starting transfers between devices: 56.3 us -> 61.4 us
  other arithmetic: 25.6 us -> 28.9 us
    select_n x2, other arithmetic: 0.98 us -> 7.86 us  [shards(): jnp.where(second_core, swap_bit_axes(grad_down, 2, levels), grad_down)]
    unnamed x70 -> x68, local copies, waits for them, and re-layouts: 14.1 us -> 18 us
    ppermute x30, starting transfers between devices: 37.8 us -> 41.6 us  [partner_swap(): return lax.ppermute(value, 'ex', perm=pairs)]
    another operation x18 -> x0, other arithmetic: 3.79 us -> none  [double_join(): return jnp.stack([first, second], axis=axis)]
  transfers between devices with their start and end apart: 34 -> 34, of which waited for: 20 -> 21; matrix products, arithmetic and copies ran while one was open for 9% -> 10% of each run, Pallas kernels for 0% -> 0%
where the time goes in v15:
time: 267 us; the launch traced here: 262 us
  waiting for transfers between devices  89.4 us (33%)
  starting transfers between devices  61.4 us (23%)
  matrix products  38.3 us (14%)
  local copies, waits for them, and re-layouts  35.9 us (13%)
  other arithmetic  28.9 us (11%)
  between operations  7.87 us (3%)
    ppermute x30, waiting for transfers between devices, partner_swap(): return lax.ppermute(value, 'ex', perm=pairs)  59.1 us
    ppermute x30, starting transfers between devices, partner_swap(): return lax.ppermute(value, 'ex', perm=pairs)  41.6 us
    unnamed x68, local copies, waits for them, and re-layouts  18 us
    dot_general x20, matrix products, contract_rows(): lax.dot_general(left, right, (((0,), (0,)), ((), ())), preferred_element_...  16.3 us
    all_to_all x1, waiting for transfers between devices, shards(): lax.all_to_all(send_feats, 'task', split_axis=0, concat_axis=0, tiled=True)  15.3 us
    all_to_all x2, waiting for transfers between devices, shards(): totals = jnp.sum(lax.all_to_all(spread, 'ex', 0, 0, tiled=True), axis=0)  13.9 us
    dot_general x18, matrix products, train_pass(): jnp.dot(windows[offset_index], down_low[offset_index // 3, offset_index %...  12.9 us
    all_to_all x2, starting transfers between devices, shards(): totals = jnp.sum(lax.all_to_all(spread, 'ex', 0, 0, tiled=True), axis=0)  11.7 us
  transfers between devices with their start and end apart: 34, of which 21 were waited for; matrix products, arithmetic and copies ran while one was open for 10% of the time, Pallas kernels for 0%

profile of v15, /device:TPU:0, one launch (start us, length us, event | category | flops | bytes accessed | tf_op | source)
XLA Modules:
  0.0 261.9 jit_solution(18140934828117763966)
XLA Ops:
  4.8 4.4 %all-to-all-start.1 = ((bf16[4,2,192]{2,1,0:T(2,128)(2,1)}), bf16[4,2,192]{2,1,0:T(2,128)(2,1)S(1)}, u32[]{:S(2)}, u32[]{:S(2)}) async-start(bf16[4,2,192]{2,1,0:T(2,128)(2,1)} %reshape.198), calls=%async_computation.1 | async-start | bytes 8192 | tf_op jit(solution)/shard_map/all_to_all | solution.py:138
  10.5 2.9 %scatter_fusion = bf16[4,6,8,8,512]{4,3,2,1,0:T(8,128)(2,1)} fusion(bf16[4,6,8,8,512]{4,3,2,1,0:T(8,128)(2,1)} %broadcast_in_dim.137, s32[12]{0:T(128)S(1)} %fusion.81, bf16[12,8,8,512]{3,2,1,0:T(8,128)(2,1)S(1)} %copy-done.27), kind=kCustom, calls=%fused_computation | custom fusion | bytes 2359392 | tf_op jit(solution)/shard_map/scatter | solution.py:129
  14.5 3.7 %all-to-all-start = ((bf16[4,6,8,8,512]{4,3,2,1,0:T(8,128)(2,1)}), bf16[4,6,8,8,512]{4,3,2,1,0:T(8,128)(2,1)S(1)}, u32[]{:S(2)}, u32[]{:S(2)}) async-start(bf16[4,6,8,8,512]{4,3,2,1,0:T(8,128)(2,1)} %scatter_fusion), calls=%async_computation | async-start | bytes 3145728 | tf_op jit(solution)/shard_map/all_to_all | solution.py:137
  18.9 4.0 %convert_bitcast_fusion = bf16[3,3,512,256]{3,2,1,0:T(8,128)(2,1)} fusion(f32[1,3,3,512,256]{4,3,2,1,0:T(8,128)} %param.11), kind=kLoop, calls=%fused_computation.50 | loop fusion | flops 1179648 | bytes 7077888 | tf_op jit(solution)/shard_map/convert_element_type | solution.py:149
  23.1 15.3 %all-to-all-done = bf16[4,6,8,8,512]{4,3,2,1,0:T(8,128)(2,1)S(1)} async-done(((bf16[4,6,8,8,512]{4,3,2,1,0:T(8,128)(2,1)}), bf16[4,6,8,8,512]{4,3,2,1,0:T(8,128)(2,1)S(1)}, u32[]{:S(2)}, u32[]{:S(2)}) %all-to-all-start) | async-done | bytes 1572896 | tf_op jit(solution)/shard_map/all_to_all | solution.py:137
  38.4 4.5 %pad_slice_fusion = (bf16[24,8,8,512]{3,2,1,0:T(8,128)(2,1)S(1)}, bf16[24,8,8,512]{3,2,1,0:T(8,128)(2,1)}, bf16[24,8,8,512]{3,2,1,0:T(8,128)(2,1)}, bf16[24,8,8,...) fusion(bf16[24,8,8,512]{3,2,1,0:T(8,128)(2,1)S(1)} %bitcast.460), kind=kLoop, calls=%fused_computation.2 | loop fusion | bytes 14155776 | tf_op jit(solution)/shard_map/slice | solution.py:19
  69.9 2.1 copy-done.17
  73.3 2.5 fusion.84
  77.3 3.9 %copy_select_fusion.1 = f32[3,3,2,2,2,2,16,256]{7,6,1,0,2,3,4,5:T(8,128)S(1)} fusion(bf16[3,3,2,2,2,2,16,256]{7,6,1,0,2,3,4,5:T(8,128)(2,1)} %collective-permute-done, pred[]{:T(512)S(6)} %eq.16, f32[3,3,2,2,2,2,2,16,256]{8,7,6,5,4,3,2,1,0:T(8,128)} %bitcast.510, s32[]{:T(128)S(6)} %select_n.183), kind=kLoop, calls=%fused_computation.49 | loop fusion | flops 2949120 | bytes 9438720 | tf_op jit(solution)/shard_map/jit(_where)/select_n | solution.py:165
  84.2 7.8 %collective-permute-done.6 = bf16[2,2,2,8,512]{4,3,0,1,2:T(8,128)(2,1)S(1)} collective-permute-done((bf16[2,2,2,8,512]{4,3,0,1,2:T(8,128)(2,1)S(1)}, bf16[2,2,2,8,512]{4,3,0,1,2:T(8,128)(2,1)S(1)}, u32[]{:S(2)}, u32[]{:S(2)}) %collective-permute-start.6) | collective-permute-done | bytes 65568 | tf_op jit(solution)/shard_map/ppermute | solution.py:85
  92.1 3.3 %collective-permute-start.7 = (bf16[2,2,8,512]{3,2,0,1:T(8,128)(2,1)S(1)}, bf16[2,2,8,512]{3,2,0,1:T(8,128)(2,1)S(1)}, u32[]{:S(2)}, u32[]{:S(2)}) collective-permute-start(bf16[2,2,8,512]{3,2,0,1:T(8,128)(2,1)S(1)} %fusion.72), channel_id=1, source_target_pairs={{0,4},{1,17},{2,6},{3,19},{4,0},{5,21},{6,2},{7,23},{8,12},{9,25},... | collective-permute-start | bytes 98312 | tf_op jit(solution)/shard_map/ppermute | solution.py:85
  99.6 4.5 %collective-permute-done.2 = bf16[3,3,2,2,16,256]{5,4,1,0,2,3:T(8,128)(2,1)S(1)} collective-permute-done((bf16[3,3,2,2,16,256]{5,4,1,0,2,3:T(8,128)(2,1)S(1)}, bf16[3,3,2,2,16,256]{5,4,1,0,2,3:T(8,128)(2,1)S(1)}, u32[]{:S(2)}, u32[]{:S(2)}) %collective-permute-start.2) | collective-permute-done | bytes 294944 | tf_op jit(solution)/shard_map/ppermute | solution.py:85
  106.2 3.7 %collective-permute-start.9 = (bf16[8,512]{1,0:T(8,128)(2,1)S(1)}, bf16[8,512]{1,0:T(8,128)(2,1)S(1)}, u32[]{:S(2)}, u32[]{:S(2)}) collective-permute-start(bf16[8,512]{1,0:T(8,128)(2,1)S(1)} %fusion.76), channel_id=1, source_target_pairs={{0,16},{1,5},{2,18},{3,7},{4,20},{5,1},{6,22},{7,3},{8,24},{9,13},... | collective-permute-start | bytes 24584 | tf_op jit(solution)/shard_map/ppermute | solution.py:85
  110.0 3.5 %collective-permute-start.4 = (bf16[3,3,16,256]{3,2,1,0:T(8,128)(2,1)S(1)}, bf16[3,3,16,256]{3,2,1,0:T(8,128)(2,1)S(1)}, u32[]{:S(2)}, u32[]{:S(2)}) collective-permute-start(bf16[3,3,16,256]{3,2,1,0:T(8,128)(2,1)S(1)} %fusion.60), channel_id=1, source_target_pairs={{0,16},{1,5},{2,18},{3,7},{4,20},{5,1},{6,22},{7,3},{8,24},{9,13},... | collective-permute-start | bytes 221192 | tf_op jit(solution)/shard_map/ppermute | solution.py:85
  119.2 6.3 %all-to-all-start.2 = ((f32[32,1,2]{2,1,0:T(1,128)}), f32[32,1,2]{2,1,0:T(1,128)}, u32[]{:S(2)}, u32[]{:S(2)}) async-start(f32[32,1,2]{2,1,0:T(1,128)} %broadcast_in_dim.140), calls=%async_computation.2 | async-start | bytes 32768 | tf_op jit(solution)/shard_map/all_to_all | solution.py:175
  125.5 7.3 %all-to-all-done.2 = f32[32,1,2]{2,1,0:T(1,128)} async-done(((f32[32,1,2]{2,1,0:T(1,128)}), f32[32,1,2]{2,1,0:T(1,128)}, u32[]{:S(2)}, u32[]{:S(2)}) %all-to-all-start.2) | async-done | bytes 288 | tf_op jit(solution)/shard_map/all_to_all | solution.py:175
  138.9 2.5 collective-permute-start.10
  142.5 2.4 collective-permute-done.10
  145.9 4.2 %collective-permute-done.11 = bf16[3,3,2,16,256]{4,3,2,1,0:T(8,128)(2,1)S(1)} collective-permute-done((bf16[3,3,2,16,256]{4,3,2,1,0:T(8,128)(2,1)S(1)}, bf16[3,3,2,16,256]{4,3,2,1,0:T(8,128)(2,1)S(1)}, u32[]{:S(2)}, u32[]{:S(2)}) %collective-permute-start.11) | collective-permute-done | bytes 147488 | tf_op jit(solution)/shard_map/ppermute | solution.py:85
  151.6 6.8 %collective-permute-done.12 = bf16[3,3,2,2,16,256]{5,4,3,2,1,0:T(8,128)(2,1)S(1)} collective-permute-done((bf16[3,3,2,2,16,256]{5,4,3,2,1,0:T(8,128)(2,1)S(1)}, bf16[3,3,2,2,16,256]{5,4,3,2,1,0:T(8,128)(2,1)S(1)}, u32[]{:S(2)}, u32[]{:S(2)}) %collective-permute-start.12) | collective-permute-done | bytes 294944 | tf_op jit(solution)/shard_map/ppermute | solution.py:85
  161.4 7.0 %collective-permute-done.13 = bf16[3,3,2,2,2,16,256]{6,5,4,3,2,1,0:T(8,128)(2,1)S(1)} collective-permute-done((bf16[3,3,2,2,2,16,256]{6,5,4,3,2,1,0:T(8,128)(2,1)S(1)}, bf16[3,3,2,2,2,16,256]{6,5,4,3,2,1,0:T(8,128)(2,1)S(1)}, u32[]{:S(2)}, u32[]{:S(2)}) %collective-permute-start.13) | collective-permute-done | bytes 589856 | tf_op jit(solution)/shard_map/ppermute | solution.py:85
  170.3 3.5 %collective-permute-done.18 = bf16[2,2,2,8,512]{4,3,2,1,0:T(8,128)(2,1)S(1)} collective-permute-done((bf16[2,2,2,8,512]{4,3,2,1,0:T(8,128)(2,1)S(1)}, bf16[2,2,2,8,512]{4,3,2,1,0:T(8,128)(2,1)S(1)}, u32[]{:S(2)}, u32[]{:S(2)}) %collective-permute-start.18) | collective-permute-done | bytes 65568 | tf_op jit(solution)/shard_map/ppermute | solution.py:85
  198.3 2.1 copy-done.16
  203.7 3.9 %copy_select_fusion = f32[3,3,2,2,2,2,16,256]{7,6,1,0,2,3,4,5:T(8,128)S(1)} fusion(bf16[3,3,2,2,2,2,16,256]{7,6,1,0,2,3,4,5:T(8,128)(2,1)} %collective-permute-done.20, pred[]{:T(512)S(6)} %eq.16, f32[3,3,2,2,2,2,2,16,256]{8,7,6,5,4,3,2,1,0:T(8,128)} %bitcast.508, s32[]{:T(128)S(6)} %select_n.183), kind=kLoop, calls=%fused_computation.48 | loop fusion | flops 2949120 | bytes 9438720 | tf_op jit(solution)/shard_map/jit(_where)/select_n | solution.py:165
  210.6 7.8 %collective-permute-done.26 = bf16[2,2,2,8,512]{4,3,0,1,2:T(8,128)(2,1)S(1)} collective-permute-done((bf16[2,2,2,8,512]{4,3,0,1,2:T(8,128)(2,1)S(1)}, bf16[2,2,2,8,512]{4,3,0,1,2:T(8,128)(2,1)S(1)}, u32[]{:S(2)}, u32[]{:S(2)}) %collective-permute-start.26) | collective-permute-done | bytes 65568 | tf_op jit(solution)/shard_map/ppermute | solution.py:85
  220.3 2.1 collective-permute-start.22
  225.0 3.8 %collective-permute-done.22 = bf16[3,3,2,2,16,256]{5,4,1,0,2,3:T(8,128)(2,1)S(1)} collective-permute-done((bf16[3,3,2,2,16,256]{5,4,1,0,2,3:T(8,128)(2,1)S(1)}, bf16[3,3,2,2,16,256]{5,4,1,0,2,3:T(8,128)(2,1)S(1)}, u32[]{:S(2)}, u32[]{:S(2)}) %collective-permute-start.22) | collective-permute-done | bytes 294944 | tf_op jit(solution)/shard_map/ppermute | solution.py:85
  229.8 2.8 %collective-permute-start.29 = (bf16[8,512]{1,0:T(8,128)(2,1)S(1)}, bf16[8,512]{1,0:T(8,128)(2,1)S(1)}, u32[]{:S(2)}, u32[]{:S(2)}) collective-permute-start(bf16[8,512]{1,0:T(8,128)(2,1)S(1)} %fusion.77), channel_id=1, source_target_pairs={{0,16},{1,5},{2,18},{3,7},{4,20},{5,1},{6,22},{7,3},{8,24},{9,13},... | collective-permute-start | bytes 24584 | tf_op jit(solution)/shard_map/ppermute | solution.py:85
  234.2 2.4 collective-permute-start.24
  237.2 2.9 %collective-permute-done.24 = bf16[3,3,16,256]{3,2,1,0:T(8,128)(2,1)S(1)} collective-permute-done((bf16[3,3,16,256]{3,2,1,0:T(8,128)(2,1)S(1)}, bf16[3,3,16,256]{3,2,1,0:T(8,128)(2,1)S(1)}, u32[]{:S(2)}, u32[]{:S(2)}) %collective-permute-start.24) | collective-permute-done | bytes 73760 | tf_op jit(solution)/shard_map/ppermute | solution.py:85
  243.4 5.4 %all-to-all-start.3 = ((f32[32,1,2]{2,1,0:T(1,128)}), f32[32,1,2]{2,1,0:T(1,128)S(1)}, u32[]{:S(2)}, u32[]{:S(2)}) async-start(f32[32,1,2]{2,1,0:T(1,128)} %broadcast_in_dim.171), calls=%async_computation.3 | async-start | bytes 32768 | tf_op jit(solution)/shard_map/all_to_all | solution.py:175
  249.5 6.7 %all-to-all-done.3 = f32[32,1,2]{2,1,0:T(1,128)S(1)} async-done(((f32[32,1,2]{2,1,0:T(1,128)}), f32[32,1,2]{2,1,0:T(1,128)S(1)}, u32[]{:S(2)}, u32[]{:S(2)}) %all-to-all-start.3) | async-done | bytes 288 | tf_op jit(solution)/shard_map/all_to_all | solution.py:175
  (257 shorter events, 108.0 us)
Async XLA Ops:
  4.8 9.7 %all-to-all-start.1 = ((bf16[4,2,192]{2,1,0:T(2,128)(2,1)}), bf16[4,2,192]{2,1,0:T(2,128)(2,1)S(1)}, u32[]{:S(2)}, u32[]{:S(2)}) async-start(bf16[4,2,192]{2,1,0:T(2,128)(2,1)} %reshape.198), calls=%async_computation.1 | async-start | bytes 8192 | tf_op jit(solution)/shard_map/all_to_all | solution.py:138
  14.5 23.9 %all-to-all-start = ((bf16[4,6,8,8,512]{4,3,2,1,0:T(8,128)(2,1)}), bf16[4,6,8,8,512]{4,3,2,1,0:T(8,128)(2,1)S(1)}, u32[]{:S(2)}, u32[]{:S(2)}) async-start(bf16[4,6,8,8,512]{4,3,2,1,0:T(8,128)(2,1)} %scatter_fusion), calls=%async_computation | async-start | bytes 3145728 | tf_op jit(solution)/shard_map/all_to_all | solution.py:137
  73.3 4.0 %collective-permute-start = (bf16[3,3,2,2,2,2,16,256]{7,6,1,0,2,3,4,5:T(8,128)(2,1)}, bf16[3,3,2,2,2,2,16,256]{7,6,1,0,2,3,4,5:T(8,128)(2,1)}, u32[]{:S(2)}, u32[]{:S(2)}) collective-permute-start(bf16[3,3,2,2,2,2,16,256]{7,6,1,0,2,3,4,5:T(8,128)(2,1)} %fusion.30), channel_id=1, source_target_pairs={{0,1},{1,0},{2,3},{3,2},{4,5},{5,4},{6,7},{7,6},{8,9},{9,8},{10,11... | collective-permute-start | bytes 3538952 | tf_op jit(solution)/shard_map/ppermute | solution.py:85
  76.7 6.4 %collective-permute-start.5 = (bf16[2,2,2,2,8,512]{5,4,0,1,2,3:T(8,128)(2,1)S(1)}, bf16[2,2,2,2,8,512]{5,4,0,1,2,3:T(8,128)(2,1)S(1)}, u32[]{:S(2)}, u32[]{:S(2)}) collective-permute-start(bf16[2,2,2,2,8,512]{5,4,0,1,2,3:T(8,128)(2,1)S(1)} %fusion.44), channel_id=1, source_target_pairs={{0,1},{1,0},{2,3},{3,2},{4,5},{5,4},{6,7},{7,6},{8,9},{9,8},{10,11... | collective-permute-start | bytes 393224 | tf_op jit(solution)/shard_map/ppermute | solution.py:85
  81.4 14.0 %collective-permute-start.1 = (bf16[3,3,2,2,2,16,256]{6,5,1,0,2,3,4:T(8,128)(2,1)S(1)}, bf16[3,3,2,2,2,16,256]{6,5,1,0,2,3,4:T(8,128)(2,1)S(1)}, u32[]{:S(2)}, u32[]{:S(2)}) collective-permute-start(bf16[3,3,2,2,2,16,256]{6,5,1,0,2,3,4:T(8,128)(2,1)S(1)} %fusion.32), channel_id=1, source_target_pairs={{0,2},{1,9},{2,0},{3,11},{4,6},{5,13},{6,4},{7,15},{8,10},{9,1},{1... | collective-permute-start | bytes 1769480 | tf_op jit(solution)/shard_map/ppermute | solution.py:85
  83.1 8.9 %collective-permute-start.6 = (bf16[2,2,2,8,512]{4,3,0,1,2:T(8,128)(2,1)S(1)}, bf16[2,2,2,8,512]{4,3,0,1,2:T(8,128)(2,1)S(1)}, u32[]{:S(2)}, u32[]{:S(2)}) collective-permute-start(bf16[2,2,2,8,512]{4,3,0,1,2:T(8,128)(2,1)S(1)} %fusion.62), channel_id=1, source_target_pairs={{0,2},{1,9},{2,0},{3,11},{4,6},{5,13},{6,4},{7,15},{8,10},{9,1},{1... | collective-permute-start | bytes 196616 | tf_op jit(solution)/shard_map/ppermute | solution.py:85
  92.1 5.5 %collective-permute-start.7 = (bf16[2,2,8,512]{3,2,0,1:T(8,128)(2,1)S(1)}, bf16[2,2,8,512]{3,2,0,1:T(8,128)(2,1)S(1)}, u32[]{:S(2)}, u32[]{:S(2)}) collective-permute-start(bf16[2,2,8,512]{3,2,0,1:T(8,128)(2,1)S(1)} %fusion.72), channel_id=1, source_target_pairs={{0,4},{1,17},{2,6},{3,19},{4,0},{5,21},{6,2},{7,23},{8,12},{9,25},... | collective-permute-start | bytes 98312 | tf_op jit(solution)/shard_map/ppermute | solution.py:85
  95.6 8.5 %collective-permute-start.2 = (bf16[3,3,2,2,16,256]{5,4,1,0,2,3:T(8,128)(2,1)S(1)}, bf16[3,3,2,2,16,256]{5,4,1,0,2,3:T(8,128)(2,1)S(1)}, u32[]{:S(2)}, u32[]{:S(2)}) collective-permute-start(bf16[3,3,2,2,16,256]{5,4,1,0,2,3:T(8,128)(2,1)S(1)} %fusion.34), channel_id=1, source_target_pairs={{0,4},{1,17},{2,6},{3,19},{4,0},{5,21},{6,2},{7,23},{8,12},{9,25},... | collective-permute-start | bytes 884744 | tf_op jit(solution)/shard_map/ppermute | solution.py:85
  97.6 8.6 %collective-permute-start.8 = (bf16[2,8,512]{2,1,0:T(8,128)(2,1)S(1)}, bf16[2,8,512]{2,1,0:T(8,128)(2,1)S(1)}, u32[]{:S(2)}, u32[]{:S(2)}) collective-permute-start(bf16[2,8,512]{2,1,0:T(8,128)(2,1)S(1)} %fusion.74), channel_id=1, source_target_pairs={{0,8},{1,3},{2,10},{3,1},{4,12},{5,7},{6,14},{7,5},{8,0},{9,11},{1... | collective-permute-start | bytes 49160 | tf_op jit(solution)/shard_map/ppermute | solution.py:85
  104.2 5.7 %collective-permute-start.3 = (bf16[3,3,2,16,256]{4,3,1,0,2:T(8,128)(2,1)S(1)}, bf16[3,3,2,16,256]{4,3,1,0,2:T(8,128)(2,1)S(1)}, u32[]{:S(2)}, u32[]{:S(2)}) collective-permute-start(bf16[3,3,2,16,256]{4,3,1,0,2:T(8,128)(2,1)S(1)} %fusion.42), channel_id=1, source_target_pairs={{0,8},{1,3},{2,10},{3,1},{4,12},{5,7},{6,14},{7,5},{8,0},{9,11},{1... | collective-permute-start | bytes 442376 | tf_op jit(solution)/shard_map/ppermute | solution.py:85
  106.2 7.3 %collective-permute-start.9 = (bf16[8,512]{1,0:T(8,128)(2,1)S(1)}, bf16[8,512]{1,0:T(8,128)(2,1)S(1)}, u32[]{:S(2)}, u32[]{:S(2)}) collective-permute-start(bf16[8,512]{1,0:T(8,128)(2,1)S(1)} %fusion.76), channel_id=1, source_target_pairs={{0,16},{1,5},{2,18},{3,7},{4,20},{5,1},{6,22},{7,3},{8,24},{9,13},... | collective-permute-start | bytes 24584 | tf_op jit(solution)/shard_map/ppermute | solution.py:85
  110.0 5.9 %collective-permute-start.4 = (bf16[3,3,16,256]{3,2,1,0:T(8,128)(2,1)S(1)}, bf16[3,3,16,256]{3,2,1,0:T(8,128)(2,1)S(1)}, u32[]{:S(2)}, u32[]{:S(2)}) collective-permute-start(bf16[3,3,16,256]{3,2,1,0:T(8,128)(2,1)S(1)} %fusion.60), channel_id=1, source_target_pairs={{0,16},{1,5},{2,18},{3,7},{4,20},{5,1},{6,22},{7,3},{8,24},{9,13},... | collective-permute-start | bytes 221192 | tf_op jit(solution)/shard_map/ppermute | solution.py:85
  119.2 13.6 %all-to-all-start.2 = ((f32[32,1,2]{2,1,0:T(1,128)}), f32[32,1,2]{2,1,0:T(1,128)}, u32[]{:S(2)}, u32[]{:S(2)}) async-start(f32[32,1,2]{2,1,0:T(1,128)} %broadcast_in_dim.140), calls=%async_computation.2 | async-start | bytes 32768 | tf_op jit(solution)/shard_map/all_to_all | solution.py:175
  136.8 5.2 %collective-permute-start.15 = (bf16[8,512]{1,0:T(8,128)(2,1)S(1)}, bf16[8,512]{1,0:T(8,128)(2,1)S(1)}, u32[]{:S(2)}, u32[]{:S(2)}) collective-permute-start(bf16[8,512]{1,0:T(8,128)(2,1)S(1)} %get-tuple-element.14), channel_id=1, source_target_pairs={{0,16},{1,5},{2,18},{3,7},{4,20},{5,1},{6,22},{7,3},{8,24},{9,13},... | collective-permute-start | bytes 24584 | tf_op jit(solution)/shard_map/ppermute | solution.py:85
  138.9 5.9 %collective-permute-start.10 = (bf16[3,3,16,256]{3,2,1,0:T(8,128)(2,1)S(1)}, bf16[3,3,16,256]{3,2,1,0:T(8,128)(2,1)S(1)}, u32[]{:S(2)}, u32[]{:S(2)}) collective-permute-start(bf16[3,3,16,256]{3,2,1,0:T(8,128)(2,1)S(1)} %get-tuple-element.10), channel_id=1, source_target_pairs={{0,16},{1,5},{2,18},{3,7},{4,20},{5,1},{6,22},{7,3},{8,24},{9,13},... | collective-permute-start | bytes 221192 | tf_op jit(solution)/shard_map/ppermute | solution.py:85
  142.0 17.2 %collective-permute-start.16 = (bf16[2,8,512]{2,1,0:T(8,128)(2,1)S(1)}, bf16[2,8,512]{2,1,0:T(8,128)(2,1)S(1)}, u32[]{:S(2)}, u32[]{:S(2)}) collective-permute-start(bf16[2,8,512]{2,1,0:T(8,128)(2,1)S(1)} %constant_dynamic-update-slice_fusion), channel_id=1, source_target_pairs={{0,8},{1,3},{2,10},{3,1},{4,12},{5,7},{6,14},{7,5},{8,0},{9,11},{1... | collective-permute-start | bytes 49160 | tf_op jit(solution)/shard_map/ppermute | solution.py:85
  144.8 5.2 %collective-permute-start.11 = (bf16[3,3,2,16,256]{4,3,2,1,0:T(8,128)(2,1)S(1)}, bf16[3,3,2,16,256]{4,3,2,1,0:T(8,128)(2,1)S(1)}, u32[]{:S(2)}, u32[]{:S(2)}) collective-permute-start(bf16[3,3,2,16,256]{4,3,2,1,0:T(8,128)(2,1)S(1)} %bitcast_dynamic-update-slice_fusion.11), channel_id=1, source_target_pairs={{0,8},{1,3},{2,10},{3,1},{4,12},{5,7},{6,14},{7,5},{8,0},{9,11},{1... | collective-permute-start | bytes 442376 | tf_op jit(solution)/shard_map/ppermute | solution.py:85
  150.1 8.3 %collective-permute-start.12 = (bf16[3,3,2,2,16,256]{5,4,3,2,1,0:T(8,128)(2,1)S(1)}, bf16[3,3,2,2,16,256]{5,4,3,2,1,0:T(8,128)(2,1)S(1)}, u32[]{:S(2)}, u32[]{:S(2)}) collective-permute-start(bf16[3,3,2,2,16,256]{5,4,3,2,1,0:T(8,128)(2,1)S(1)} %bitcast_dynamic-update-slice_fusion.7), channel_id=1, source_target_pairs={{0,4},{1,17},{2,6},{3,19},{4,0},{5,21},{6,2},{7,23},{8,12},{9,25},... | collective-permute-start | bytes 884744 | tf_op jit(solution)/shard_map/ppermute | solution.py:85
  158.4 10.0 %collective-permute-start.13 = (bf16[3,3,2,2,2,16,256]{6,5,4,3,2,1,0:T(8,128)(2,1)S(1)}, bf16[3,3,2,2,2,16,256]{6,5,4,3,2,1,0:T(8,128)(2,1)S(1)}, u32[]{:S(2)}, u32[]{:S(2)}) collective-permute-start(bf16[3,3,2,2,2,16,256]{6,5,4,3,2,1,0:T(8,128)(2,1)S(1)} %bitcast_dynamic-update-slice_fusion.5), channel_id=1, source_target_pairs={{0,2},{1,9},{2,0},{3,11},{4,6},{5,13},{6,4},{7,15},{8,10},{9,1},{1... | collective-permute-start | bytes 1769480 | tf_op jit(solution)/shard_map/ppermute | solution.py:85
  159.2 10.1 %collective-permute-start.17 = (bf16[2,2,8,512]{3,2,1,0:T(8,128)(2,1)S(1)}, bf16[2,2,8,512]{3,2,1,0:T(8,128)(2,1)S(1)}, u32[]{:S(2)}, u32[]{:S(2)}) collective-permute-start(bf16[2,2,8,512]{3,2,1,0:T(8,128)(2,1)S(1)} %bitcast_dynamic-update-slice_fusion.17), channel_id=1, source_target_pairs={{0,4},{1,17},{2,6},{3,19},{4,0},{5,21},{6,2},{7,23},{8,12},{9,25},... | collective-permute-start | bytes 98312 | tf_op jit(solution)/shard_map/ppermute | solution.py:85
  169.3 6.2 %collective-permute-start.14 = (bf16[3,3,2,2,2,2,16,256]{7,6,5,4,3,2,1,0:T(8,128)(2,1)S(1)}, bf16[3,3,2,2,2,2,16,256]{7,6,5,4,3,2,1,0:T(8,128)(2,1)S(1)}, u32[]{:S(2)}, u32[]{:S(2)}) collective-permute-start(bf16[3,3,2,2,2,2,16,256]{7,6,5,4,3,2,1,0:T(8,128)(2,1)S(1)} %get-tuple-element.8), channel_id=1, source_target_pairs={{0,1},{1,0},{2,3},{3,2},{4,5},{5,4},{6,7},{7,6},{8,9},{9,8},{10,11... | collective-permute-start | bytes 3538952 | tf_op jit(solution)/shard_map/ppermute | solution.py:85
  169.4 4.3 %collective-permute-start.18 = (bf16[2,2,2,8,512]{4,3,2,1,0:T(8,128)(2,1)S(1)}, bf16[2,2,2,8,512]{4,3,2,1,0:T(8,128)(2,1)S(1)}, u32[]{:S(2)}, u32[]{:S(2)}) collective-permute-start(bf16[2,2,2,8,512]{4,3,2,1,0:T(8,128)(2,1)S(1)} %bitcast_dynamic-update-slice_fusion.15), channel_id=1, source_target_pairs={{0,2},{1,9},{2,0},{3,11},{4,6},{5,13},{6,4},{7,15},{8,10},{9,1},{1... | collective-permute-start | bytes 196616 | tf_op jit(solution)/shard_map/ppermute | solution.py:85
  203.0 5.5 %collective-permute-start.25 = (bf16[2,2,2,2,8,512]{5,4,0,1,2,3:T(8,128)(2,1)S(1)}, bf16[2,2,2,2,8,512]{5,4,0,1,2,3:T(8,128)(2,1)S(1)}, u32[]{:S(2)}, u32[]{:S(2)}) collective-permute-start(bf16[2,2,2,2,8,512]{5,4,0,1,2,3:T(8,128)(2,1)S(1)} %fusion.45), channel_id=1, source_target_pairs={{0,1},{1,0},{2,3},{3,2},{4,5},{5,4},{6,7},{7,6},{8,9},{9,8},{10,11... | collective-permute-start | bytes 393224 | tf_op jit(solution)/shard_map/ppermute | solution.py:85
  207.7 12.3 %collective-permute-start.21 = (bf16[3,3,2,2,2,16,256]{6,5,1,0,2,3,4:T(8,128)(2,1)S(1)}, bf16[3,3,2,2,2,16,256]{6,5,1,0,2,3,4:T(8,128)(2,1)S(1)}, u32[]{:S(2)}, u32[]{:S(2)}) collective-permute-start(bf16[3,3,2,2,2,16,256]{6,5,1,0,2,3,4:T(8,128)(2,1)S(1)} %fusion.33), channel_id=1, source_target_pairs={{0,2},{1,9},{2,0},{3,11},{4,6},{5,13},{6,4},{7,15},{8,10},{9,1},{1... | collective-permute-start | bytes 1769480 | tf_op jit(solution)/shard_map/ppermute | solution.py:85
  208.6 9.8 %collective-permute-start.26 = (bf16[2,2,2,8,512]{4,3,0,1,2:T(8,128)(2,1)S(1)}, bf16[2,2,2,8,512]{4,3,0,1,2:T(8,128)(2,1)S(1)}, u32[]{:S(2)}, u32[]{:S(2)}) collective-permute-start(bf16[2,2,2,8,512]{4,3,0,1,2:T(8,128)(2,1)S(1)} %fusion.63), channel_id=1, source_target_pairs={{0,2},{1,9},{2,0},{3,11},{4,6},{5,13},{6,4},{7,15},{8,10},{9,1},{1... | collective-permute-start | bytes 196616 | tf_op jit(solution)/shard_map/ppermute | solution.py:85
  218.4 5.5 %collective-permute-start.27 = (bf16[2,2,8,512]{3,2,0,1:T(8,128)(2,1)S(1)}, bf16[2,2,8,512]{3,2,0,1:T(8,128)(2,1)S(1)}, u32[]{:S(2)}, u32[]{:S(2)}) collective-permute-start(bf16[2,2,8,512]{3,2,0,1:T(8,128)(2,1)S(1)} %fusion.73), channel_id=1, source_target_pairs={{0,4},{1,17},{2,6},{3,19},{4,0},{5,21},{6,2},{7,23},{8,12},{9,25},... | collective-permute-start | bytes 98312 | tf_op jit(solution)/shard_map/ppermute | solution.py:85
  220.3 8.5 %collective-permute-start.22 = (bf16[3,3,2,2,16,256]{5,4,1,0,2,3:T(8,128)(2,1)S(1)}, bf16[3,3,2,2,16,256]{5,4,1,0,2,3:T(8,128)(2,1)S(1)}, u32[]{:S(2)}, u32[]{:S(2)}) collective-permute-start(bf16[3,3,2,2,16,256]{5,4,1,0,2,3:T(8,128)(2,1)S(1)} %fusion.35), channel_id=1, source_target_pairs={{0,4},{1,17},{2,6},{3,19},{4,0},{5,21},{6,2},{7,23},{8,12},{9,25},... | collective-permute-start | bytes 884744 | tf_op jit(solution)/shard_map/ppermute | solution.py:85
  224.0 5.8 %collective-permute-start.28 = (bf16[2,8,512]{2,1,0:T(8,128)(2,1)S(1)}, bf16[2,8,512]{2,1,0:T(8,128)(2,1)S(1)}, u32[]{:S(2)}, u32[]{:S(2)}) collective-permute-start(bf16[2,8,512]{2,1,0:T(8,128)(2,1)S(1)} %fusion.75), channel_id=1, source_target_pairs={{0,8},{1,3},{2,10},{3,1},{4,12},{5,7},{6,14},{7,5},{8,0},{9,11},{1... | collective-permute-start | bytes 49160 | tf_op jit(solution)/shard_map/ppermute | solution.py:85
  228.9 5.2 %collective-permute-start.23 = (bf16[3,3,2,16,256]{4,3,1,0,2:T(8,128)(2,1)S(1)}, bf16[3,3,2,16,256]{4,3,1,0,2:T(8,128)(2,1)S(1)}, u32[]{:S(2)}, u32[]{:S(2)}) collective-permute-start(bf16[3,3,2,16,256]{4,3,1,0,2:T(8,128)(2,1)S(1)} %fusion.43), channel_id=1, source_target_pairs={{0,8},{1,3},{2,10},{3,1},{4,12},{5,7},{6,14},{7,5},{8,0},{9,11},{1... | collective-permute-start | bytes 442376 | tf_op jit(solution)/shard_map/ppermute | solution.py:85
  229.8 6.8 %collective-permute-start.29 = (bf16[8,512]{1,0:T(8,128)(2,1)S(1)}, bf16[8,512]{1,0:T(8,128)(2,1)S(1)}, u32[]{:S(2)}, u32[]{:S(2)}) collective-permute-start(bf16[8,512]{1,0:T(8,128)(2,1)S(1)} %fusion.77), channel_id=1, source_target_pairs={{0,16},{1,5},{2,18},{3,7},{4,20},{5,1},{6,22},{7,3},{8,24},{9,13},... | collective-permute-start | bytes 24584 | tf_op jit(solution)/shard_map/ppermute | solution.py:85
  234.2 5.9 %collective-permute-start.24 = (bf16[3,3,16,256]{3,2,1,0:T(8,128)(2,1)S(1)}, bf16[3,3,16,256]{3,2,1,0:T(8,128)(2,1)S(1)}, u32[]{:S(2)}, u32[]{:S(2)}) collective-permute-start(bf16[3,3,16,256]{3,2,1,0:T(8,128)(2,1)S(1)} %fusion.61), channel_id=1, source_target_pairs={{0,16},{1,5},{2,18},{3,7},{4,20},{5,1},{6,22},{7,3},{8,24},{9,13},... | collective-permute-start | bytes 221192 | tf_op jit(solution)/shard_map/ppermute | solution.py:85
  243.4 12.7 %all-to-all-start.3 = ((f32[32,1,2]{2,1,0:T(1,128)}), f32[32,1,2]{2,1,0:T(1,128)S(1)}, u32[]{:S(2)}, u32[]{:S(2)}) async-start(f32[32,1,2]{2,1,0:T(1,128)} %broadcast_in_dim.171), calls=%async_computation.3 | async-start | bytes 32768 | tf_op jit(solution)/shard_map/all_to_all | solution.py:175
  (35 other events, 211.1 us)

commit v16 on v8

--- a/solution.py
+++ b/solution.py
@@ -182,10 +182,7 @@
             upper_low = up_own.astype(jnp.bfloat16)
             for step_index in range(levels):
                 stage = levels - 1 - step_index
-                if stage == 0:
-                    down_low = jnp.where(second_core, swap_bit_axes(down_low, 2, levels), down_low)
-                    upper_low = jnp.where(second_core, swap_bit_axes(upper_low, 0, levels), upper_low)
-                bits_of = (orders[0][stage], orders[1][stage])
+                bits_of = (orders[0][stage], orders[0][stage])
                 pairs = stage_pairs(bits_of, peers)
                 bit = jnp.where(second_core, bits_of[1], bits_of[0])
                 down_low = double_join(down_low, 2 + step_index, bit, pairs, place)

time: 250 us -> 270 us (1.080)
  other arithmetic: 25.6 us -> 41.1 us
  local copies, waits for them, and re-layouts: 27.4 us -> 31 us
    another operation x18 -> x20, other arithmetic: 3.79 us -> 12.2 us  [double_join(): return jnp.stack([first, second], axis=axis)]
    select_n x2, other arithmetic: 0.98 us -> 7.83 us  [shards(): jnp.where(second_core, swap_bit_axes(grad_down, 2, levels), grad_down)]
    unnamed x70 -> x86, local copies, waits for them, and re-layouts: 14.1 us -> 16.2 us
  transfers between devices with their start and end apart: 34 -> 34, of which waited for: 20 -> 21; matrix products, arithmetic and copies ran while one was open for 9% -> 12% of each run, Pallas kernels for 0% -> 0%
where the time goes in v16:
time: 270 us; the launch traced here: 265 us
  waiting for transfers between devices  93.3 us (35%)
  starting transfers between devices  56.3 us (21%)
  other arithmetic  41.1 us (15%)
  matrix products  35.8 us (13%)
  local copies, waits for them, and re-layouts  31 us (11%)
  between operations  7.92 us (3%)
    ppermute x30, waiting for transfers between devices, partner_swap(): return lax.ppermute(value, 'ex', perm=pairs)  63 us
    ppermute x30, starting transfers between devices, partner_swap(): return lax.ppermute(value, 'ex', perm=pairs)  37.5 us
    dot_general x20, matrix products, contract_rows(): lax.dot_general(left, right, (((0,), (0,)), ((), ())), preferred_element_...  16.3 us
    unnamed x86, local copies, waits for them, and re-layouts  16.2 us
    all_to_all x1, waiting for transfers between devices, shards(): lax.all_to_all(send_feats, 'task', split_axis=0, concat_axis=0, tiled=True)  15.3 us
    all_to_all x2, waiting for transfers between devices, shards(): totals = jnp.sum(lax.all_to_all(spread, 'ex', 0, 0, tiled=True), axis=0)  13.9 us
    another operation x20, other arithmetic, double_join(): return jnp.stack([first, second], axis=axis)  12.2 us
    all_to_all x2, starting transfers between devices, shards(): totals = jnp.sum(lax.all_to_all(spread, 'ex', 0, 0, tiled=True), axis=0)  10.7 us
  transfers between devices with their start and end apart: 34, of which 21 were waited for; matrix products, arithmetic and copies ran while one was open for 12% of the time, Pallas kernels for 0%

profile of v16, /device:TPU:0, one launch (start us, length us, event | category | flops | bytes accessed | tf_op | source)
XLA Modules:
  0.0 265.5 jit_solution(7599929744540884429)
XLA Ops:
  4.8 4.4 %all-to-all-start.1 = ((bf16[4,2,192]{2,1,0:T(2,128)(2,1)}), bf16[4,2,192]{2,1,0:T(2,128)(2,1)S(1)}, u32[]{:S(2)}, u32[]{:S(2)}) async-start(bf16[4,2,192]{2,1,0:T(2,128)(2,1)} %reshape.198), calls=%async_computation.1 | async-start | bytes 8192 | tf_op jit(solution)/shard_map/all_to_all | solution.py:138
  10.5 2.9 %scatter_fusion = bf16[4,6,8,8,512]{4,3,2,1,0:T(8,128)(2,1)} fusion(bf16[4,6,8,8,512]{4,3,2,1,0:T(8,128)(2,1)} %broadcast_in_dim.16, s32[12]{0:T(128)S(1)} %fusion.81, bf16[12,8,8,512]{3,2,1,0:T(8,128)(2,1)S(1)} %copy-done.32), kind=kCustom, calls=%fused_computation | custom fusion | bytes 2359392 | tf_op jit(solution)/shard_map/scatter | solution.py:129
  14.5 3.8 %all-to-all-start = ((bf16[4,6,8,8,512]{4,3,2,1,0:T(8,128)(2,1)}), bf16[4,6,8,8,512]{4,3,2,1,0:T(8,128)(2,1)S(1)}, u32[]{:S(2)}, u32[]{:S(2)}) async-start(bf16[4,6,8,8,512]{4,3,2,1,0:T(8,128)(2,1)} %scatter_fusion), calls=%async_computation | async-start | bytes 3145728 | tf_op jit(solution)/shard_map/all_to_all | solution.py:137
  18.9 4.0 %convert_bitcast_fusion = bf16[3,3,512,256]{3,2,1,0:T(8,128)(2,1)} fusion(f32[1,3,3,512,256]{4,3,2,1,0:T(8,128)} %param.11), kind=kLoop, calls=%fused_computation.51 | loop fusion | flops 1179648 | bytes 7077888 | tf_op jit(solution)/shard_map/convert_element_type | solution.py:149
  23.1 15.3 %all-to-all-done = bf16[4,6,8,8,512]{4,3,2,1,0:T(8,128)(2,1)S(1)} async-done(((bf16[4,6,8,8,512]{4,3,2,1,0:T(8,128)(2,1)}), bf16[4,6,8,8,512]{4,3,2,1,0:T(8,128)(2,1)S(1)}, u32[]{:S(2)}, u32[]{:S(2)}) %all-to-all-start) | async-done | bytes 1572896 | tf_op jit(solution)/shard_map/all_to_all | solution.py:137
  40.0 2.5 pad_slice_fusion
  60.7 2.1 copy-done.17
  64.1 2.5 fusion.84
  67.3 3.9 %copy_select_fusion.1 = f32[3,3,2,2,2,2,16,256]{7,6,1,0,2,3,4,5:T(8,128)S(1)} fusion(bf16[3,3,2,2,2,2,16,256]{7,6,1,0,2,3,4,5:T(8,128)(2,1)} %collective-permute-done, pred[]{:T(512)S(6)} %eq.26, f32[3,3,2,2,2,2,2,16,256]{8,7,6,5,4,3,2,1,0:T(8,128)} %bitcast.502, s32[]{:T(128)S(6)} %select_n.271), kind=kLoop, calls=%fused_computation.50 | loop fusion | flops 2949120 | bytes 9438720 | tf_op jit(solution)/shard_map/jit(_where)/select_n | solution.py:165
  74.1 7.8 %collective-permute-done.6 = bf16[2,2,2,8,512]{4,3,0,1,2:T(8,128)(2,1)S(1)} collective-permute-done((bf16[2,2,2,8,512]{4,3,0,1,2:T(8,128)(2,1)S(1)}, bf16[2,2,2,8,512]{4,3,0,1,2:T(8,128)(2,1)S(1)}, u32[]{:S(2)}, u32[]{:S(2)}) %collective-permute-start.6) | collective-permute-done | bytes 65568 | tf_op jit(solution)/shard_map/ppermute | solution.py:85
  82.0 3.3 %collective-permute-start.7 = (bf16[2,2,8,512]{3,2,0,1:T(8,128)(2,1)S(1)}, bf16[2,2,8,512]{3,2,0,1:T(8,128)(2,1)S(1)}, u32[]{:S(2)}, u32[]{:S(2)}) collective-permute-start(bf16[2,2,8,512]{3,2,0,1:T(8,128)(2,1)S(1)} %fusion.72), channel_id=1, source_target_pairs={{0,4},{1,17},{2,6},{3,19},{4,0},{5,21},{6,2},{7,23},{8,12},{9,25},... | collective-permute-start | bytes 98312 | tf_op jit(solution)/shard_map/ppermute | solution.py:85
  89.5 4.5 %collective-permute-done.2 = bf16[3,3,2,2,16,256]{5,4,1,0,2,3:T(8,128)(2,1)S(1)} collective-permute-done((bf16[3,3,2,2,16,256]{5,4,1,0,2,3:T(8,128)(2,1)S(1)}, bf16[3,3,2,2,16,256]{5,4,1,0,2,3:T(8,128)(2,1)S(1)}, u32[]{:S(2)}, u32[]{:S(2)}) %collective-permute-start.2) | collective-permute-done | bytes 294944 | tf_op jit(solution)/shard_map/ppermute | solution.py:85
  96.2 3.7 %collective-permute-start.9 = (bf16[8,512]{1,0:T(8,128)(2,1)S(1)}, bf16[8,512]{1,0:T(8,128)(2,1)S(1)}, u32[]{:S(2)}, u32[]{:S(2)}) collective-permute-start(bf16[8,512]{1,0:T(8,128)(2,1)S(1)} %fusion.76), channel_id=1, source_target_pairs={{0,16},{1,5},{2,18},{3,7},{4,20},{5,1},{6,22},{7,3},{8,24},{9,13},... | collective-permute-start | bytes 24584 | tf_op jit(solution)/shard_map/ppermute | solution.py:85
  99.9 3.4 %collective-permute-start.4 = (bf16[3,3,16,256]{3,2,1,0:T(8,128)(2,1)S(1)}, bf16[3,3,16,256]{3,2,1,0:T(8,128)(2,1)S(1)}, u32[]{:S(2)}, u32[]{:S(2)}) collective-permute-start(bf16[3,3,16,256]{3,2,1,0:T(8,128)(2,1)S(1)} %fusion.60), channel_id=1, source_target_pairs={{0,16},{1,5},{2,18},{3,7},{4,20},{5,1},{6,22},{7,3},{8,24},{9,13},... | collective-permute-start | bytes 221192 | tf_op jit(solution)/shard_map/ppermute | solution.py:85
  109.1 6.1 %all-to-all-start.2 = ((f32[32,1,2]{2,1,0:T(1,128)}), f32[32,1,2]{2,1,0:T(1,128)}, u32[]{:S(2)}, u32[]{:S(2)}) async-start(f32[32,1,2]{2,1,0:T(1,128)} %broadcast_in_dim.19), calls=%async_computation.2 | async-start | bytes 32768 | tf_op jit(solution)/shard_map/all_to_all | solution.py:175
  115.3 7.3 %all-to-all-done.2 = f32[32,1,2]{2,1,0:T(1,128)} async-done(((f32[32,1,2]{2,1,0:T(1,128)}), f32[32,1,2]{2,1,0:T(1,128)}, u32[]{:S(2)}, u32[]{:S(2)}) %all-to-all-start.2) | async-done | bytes 288 | tf_op jit(solution)/shard_map/all_to_all | solution.py:175
  128.5 5.1 %collective-permute-done.10 = bf16[3,3,16,256]{3,2,1,0:T(8,128)(2,1)} collective-permute-done((bf16[3,3,16,256]{3,2,1,0:T(8,128)(2,1)}, bf16[3,3,16,256]{3,2,1,0:T(8,128)(2,1)}, u32[]{:S(2)}, u32[]{:S(2)}) %collective-permute-start.10) | collective-permute-done | bytes 73760 | tf_op jit(solution)/shard_map/ppermute | solution.py:85
  136.4 5.0 %collective-permute-done.11 = bf16[3,3,2,16,256]{4,3,2,1,0:T(8,128)(2,1)} collective-permute-done((bf16[3,3,2,16,256]{4,3,2,1,0:T(8,128)(2,1)}, bf16[3,3,2,16,256]{4,3,2,1,0:T(8,128)(2,1)}, u32[]{:S(2)}, u32[]{:S(2)}) %collective-permute-start.11) | collective-permute-done | bytes 147488 | tf_op jit(solution)/shard_map/ppermute | solution.py:85
  147.0 5.3 %collective-permute-done.12 = bf16[3,3,2,2,16,256]{5,4,3,2,1,0:T(8,128)(2,1)} collective-permute-done((bf16[3,3,2,2,16,256]{5,4,3,2,1,0:T(8,128)(2,1)}, bf16[3,3,2,2,16,256]{5,4,3,2,1,0:T(8,128)(2,1)}, u32[]{:S(2)}, u32[]{:S(2)}) %collective-permute-start.12) | collective-permute-done | bytes 294944 | tf_op jit(solution)/shard_map/ppermute | solution.py:85
  157.5 3.3 %collective-permute-done.16 = bf16[2,8,512]{2,1,0:T(8,128)(2,1)} collective-permute-done((bf16[2,8,512]{2,1,0:T(8,128)(2,1)}, bf16[2,8,512]{2,1,0:T(8,128)(2,1)}, u32[]{:S(2)}, u32[]{:S(2)}) %collective-permute-start.16) | collective-permute-done | bytes 16416 | tf_op jit(solution)/shard_map/ppermute | solution.py:85
  161.5 2.3 collective-permute-start.17
  163.8 3.5 %collective-permute-done.13 = bf16[3,3,2,2,2,16,256]{6,5,4,3,2,1,0:T(8,128)(2,1)} collective-permute-done((bf16[3,3,2,2,2,16,256]{6,5,4,3,2,1,0:T(8,128)(2,1)}, bf16[3,3,2,2,2,16,256]{6,5,4,3,2,1,0:T(8,128)(2,1)}, u32[]{:S(2)}, u32[]{:S(2)}) %collective-permute-start.13) | collective-permute-done | bytes 589856 | tf_op jit(solution)/shard_map/ppermute | solution.py:85
  170.8 3.8 %collective-permute-done.18 = bf16[2,2,2,8,512]{4,3,2,1,0:T(8,128)(2,1)S(1)} collective-permute-done((bf16[2,2,2,8,512]{4,3,2,1,0:T(8,128)(2,1)S(1)}, bf16[2,2,2,8,512]{4,3,2,1,0:T(8,128)(2,1)S(1)}, u32[]{:S(2)}, u32[]{:S(2)}) %collective-permute-start.18) | collective-permute-done | bytes 65568 | tf_op jit(solution)/shard_map/ppermute | solution.py:85
  208.3 3.9 %copy_select_fusion = f32[3,3,2,2,2,2,16,256]{7,6,1,0,2,3,4,5:T(8,128)S(1)} fusion(bf16[3,3,2,2,2,2,16,256]{7,6,1,0,2,3,4,5:T(8,128)(2,1)} %collective-permute-done.20, pred[]{:T(512)S(6)} %eq.26, f32[3,3,2,2,2,2,2,16,256]{8,7,6,5,4,3,2,1,0:T(8,128)} %bitcast.500, s32[]{:T(128)S(6)} %select_n.271), kind=kLoop, calls=%fused_computation.49 | loop fusion | flops 2949120 | bytes 9438720 | tf_op jit(solution)/shard_map/jit(_where)/select_n | solution.py:165
  215.2 7.8 %collective-permute-done.26 = bf16[2,2,2,8,512]{4,3,0,1,2:T(8,128)(2,1)S(1)} collective-permute-done((bf16[2,2,2,8,512]{4,3,0,1,2:T(8,128)(2,1)S(1)}, bf16[2,2,2,8,512]{4,3,0,1,2:T(8,128)(2,1)S(1)}, u32[]{:S(2)}, u32[]{:S(2)}) %collective-permute-start.26) | collective-permute-done | bytes 65568 | tf_op jit(solution)/shard_map/ppermute | solution.py:85
  224.7 2.3 collective-permute-start.22
  229.5 3.7 %collective-permute-done.22 = bf16[3,3,2,2,16,256]{5,4,1,0,2,3:T(8,128)(2,1)S(1)} collective-permute-done((bf16[3,3,2,2,16,256]{5,4,1,0,2,3:T(8,128)(2,1)S(1)}, bf16[3,3,2,2,16,256]{5,4,1,0,2,3:T(8,128)(2,1)S(1)}, u32[]{:S(2)}, u32[]{:S(2)}) %collective-permute-start.22) | collective-permute-done | bytes 294944 | tf_op jit(solution)/shard_map/ppermute | solution.py:85
  233.9 2.2 collective-permute-start.29
  236.1 2.4 collective-permute-done.23
  240.4 4.2 %collective-permute-done.24 = bf16[3,3,16,256]{3,2,1,0:T(8,128)(2,1)S(1)} collective-permute-done((bf16[3,3,16,256]{3,2,1,0:T(8,128)(2,1)S(1)}, bf16[3,3,16,256]{3,2,1,0:T(8,128)(2,1)S(1)}, u32[]{:S(2)}, u32[]{:S(2)}) %collective-permute-start.24) | collective-permute-done | bytes 73760 | tf_op jit(solution)/shard_map/ppermute | solution.py:85
  247.8 4.6 %all-to-all-start.3 = ((f32[32,1,2]{2,1,0:T(1,128)}), f32[32,1,2]{2,1,0:T(1,128)S(1)}, u32[]{:S(2)}, u32[]{:S(2)}) async-start(f32[32,1,2]{2,1,0:T(1,128)} %broadcast_in_dim.20), calls=%async_computation.3 | async-start | bytes 32768 | tf_op jit(solution)/shard_map/all_to_all | solution.py:175
  253.0 6.7 %all-to-all-done.3 = f32[32,1,2]{2,1,0:T(1,128)S(1)} async-done(((f32[32,1,2]{2,1,0:T(1,128)}), f32[32,1,2]{2,1,0:T(1,128)S(1)}, u32[]{:S(2)}, u32[]{:S(2)}) %all-to-all-start.3) | async-done | bytes 288 | tf_op jit(solution)/shard_map/all_to_all | solution.py:175
  (267 shorter events, 113.9 us)
Async XLA Ops:
  4.8 9.7 %all-to-all-start.1 = ((bf16[4,2,192]{2,1,0:T(2,128)(2,1)}), bf16[4,2,192]{2,1,0:T(2,128)(2,1)S(1)}, u32[]{:S(2)}, u32[]{:S(2)}) async-start(bf16[4,2,192]{2,1,0:T(2,128)(2,1)} %reshape.198), calls=%async_computation.1 | async-start | bytes 8192 | tf_op jit(solution)/shard_map/all_to_all | solution.py:138
  14.5 23.9 %all-to-all-start = ((bf16[4,6,8,8,512]{4,3,2,1,0:T(8,128)(2,1)}), bf16[4,6,8,8,512]{4,3,2,1,0:T(8,128)(2,1)S(1)}, u32[]{:S(2)}, u32[]{:S(2)}) async-start(bf16[4,6,8,8,512]{4,3,2,1,0:T(8,128)(2,1)} %scatter_fusion), calls=%async_computation | async-start | bytes 3145728 | tf_op jit(solution)/shard_map/all_to_all | solution.py:137
  64.0 3.2 %collective-permute-start = (bf16[3,3,2,2,2,2,16,256]{7,6,1,0,2,3,4,5:T(8,128)(2,1)}, bf16[3,3,2,2,2,2,16,256]{7,6,1,0,2,3,4,5:T(8,128)(2,1)}, u32[]{:S(2)}, u32[]{:S(2)}) collective-permute-start(bf16[3,3,2,2,2,2,16,256]{7,6,1,0,2,3,4,5:T(8,128)(2,1)} %fusion.30), channel_id=1, source_target_pairs={{0,1},{1,0},{2,3},{3,2},{4,5},{5,4},{6,7},{7,6},{8,9},{9,8},{10,11... | collective-permute-start | bytes 3538952 | tf_op jit(solution)/shard_map/ppermute | solution.py:85
  66.7 6.2 %collective-permute-start.5 = (bf16[2,2,2,2,8,512]{5,4,0,1,2,3:T(8,128)(2,1)S(1)}, bf16[2,2,2,2,8,512]{5,4,0,1,2,3:T(8,128)(2,1)S(1)}, u32[]{:S(2)}, u32[]{:S(2)}) collective-permute-start(bf16[2,2,2,2,8,512]{5,4,0,1,2,3:T(8,128)(2,1)S(1)} %fusion.44), channel_id=1, source_target_pairs={{0,1},{1,0},{2,3},{3,2},{4,5},{5,4},{6,7},{7,6},{8,9},{9,8},{10,11... | collective-permute-start | bytes 393224 | tf_op jit(solution)/shard_map/ppermute | solution.py:85
  71.3 14.0 %collective-permute-start.1 = (bf16[3,3,2,2,2,16,256]{6,5,1,0,2,3,4:T(8,128)(2,1)S(1)}, bf16[3,3,2,2,2,16,256]{6,5,1,0,2,3,4:T(8,128)(2,1)S(1)}, u32[]{:S(2)}, u32[]{:S(2)}) collective-permute-start(bf16[3,3,2,2,2,16,256]{6,5,1,0,2,3,4:T(8,128)(2,1)S(1)} %fusion.32), channel_id=1, source_target_pairs={{0,2},{1,9},{2,0},{3,11},{4,6},{5,13},{6,4},{7,15},{8,10},{9,1},{1... | collective-permute-start | bytes 1769480 | tf_op jit(solution)/shard_map/ppermute | solution.py:85
  73.0 8.9 %collective-permute-start.6 = (bf16[2,2,2,8,512]{4,3,0,1,2:T(8,128)(2,1)S(1)}, bf16[2,2,2,8,512]{4,3,0,1,2:T(8,128)(2,1)S(1)}, u32[]{:S(2)}, u32[]{:S(2)}) collective-permute-start(bf16[2,2,2,8,512]{4,3,0,1,2:T(8,128)(2,1)S(1)} %fusion.62), channel_id=1, source_target_pairs={{0,2},{1,9},{2,0},{3,11},{4,6},{5,13},{6,4},{7,15},{8,10},{9,1},{1... | collective-permute-start | bytes 196616 | tf_op jit(solution)/shard_map/ppermute | solution.py:85
  82.0 5.5 %collective-permute-start.7 = (bf16[2,2,8,512]{3,2,0,1:T(8,128)(2,1)S(1)}, bf16[2,2,8,512]{3,2,0,1:T(8,128)(2,1)S(1)}, u32[]{:S(2)}, u32[]{:S(2)}) collective-permute-start(bf16[2,2,8,512]{3,2,0,1:T(8,128)(2,1)S(1)} %fusion.72), channel_id=1, source_target_pairs={{0,4},{1,17},{2,6},{3,19},{4,0},{5,21},{6,2},{7,23},{8,12},{9,25},... | collective-permute-start | bytes 98312 | tf_op jit(solution)/shard_map/ppermute | solution.py:85
  85.5 8.5 %collective-permute-start.2 = (bf16[3,3,2,2,16,256]{5,4,1,0,2,3:T(8,128)(2,1)S(1)}, bf16[3,3,2,2,16,256]{5,4,1,0,2,3:T(8,128)(2,1)S(1)}, u32[]{:S(2)}, u32[]{:S(2)}) collective-permute-start(bf16[3,3,2,2,16,256]{5,4,1,0,2,3:T(8,128)(2,1)S(1)} %fusion.34), channel_id=1, source_target_pairs={{0,4},{1,17},{2,6},{3,19},{4,0},{5,21},{6,2},{7,23},{8,12},{9,25},... | collective-permute-start | bytes 884744 | tf_op jit(solution)/shard_map/ppermute | solution.py:85
  87.5 8.6 %collective-permute-start.8 = (bf16[2,8,512]{2,1,0:T(8,128)(2,1)S(1)}, bf16[2,8,512]{2,1,0:T(8,128)(2,1)S(1)}, u32[]{:S(2)}, u32[]{:S(2)}) collective-permute-start(bf16[2,8,512]{2,1,0:T(8,128)(2,1)S(1)} %fusion.74), channel_id=1, source_target_pairs={{0,8},{1,3},{2,10},{3,1},{4,12},{5,7},{6,14},{7,5},{8,0},{9,11},{1... | collective-permute-start | bytes 49160 | tf_op jit(solution)/shard_map/ppermute | solution.py:85
  94.1 5.7 %collective-permute-start.3 = (bf16[3,3,2,16,256]{4,3,1,0,2:T(8,128)(2,1)S(1)}, bf16[3,3,2,16,256]{4,3,1,0,2:T(8,128)(2,1)S(1)}, u32[]{:S(2)}, u32[]{:S(2)}) collective-permute-start(bf16[3,3,2,16,256]{4,3,1,0,2:T(8,128)(2,1)S(1)} %fusion.42), channel_id=1, source_target_pairs={{0,8},{1,3},{2,10},{3,1},{4,12},{5,7},{6,14},{7,5},{8,0},{9,11},{1... | collective-permute-start | bytes 442376 | tf_op jit(solution)/shard_map/ppermute | solution.py:85
  96.2 7.2 %collective-permute-start.9 = (bf16[8,512]{1,0:T(8,128)(2,1)S(1)}, bf16[8,512]{1,0:T(8,128)(2,1)S(1)}, u32[]{:S(2)}, u32[]{:S(2)}) collective-permute-start(bf16[8,512]{1,0:T(8,128)(2,1)S(1)} %fusion.76), channel_id=1, source_target_pairs={{0,16},{1,5},{2,18},{3,7},{4,20},{5,1},{6,22},{7,3},{8,24},{9,13},... | collective-permute-start | bytes 24584 | tf_op jit(solution)/shard_map/ppermute | solution.py:85
  99.9 5.9 %collective-permute-start.4 = (bf16[3,3,16,256]{3,2,1,0:T(8,128)(2,1)S(1)}, bf16[3,3,16,256]{3,2,1,0:T(8,128)(2,1)S(1)}, u32[]{:S(2)}, u32[]{:S(2)}) collective-permute-start(bf16[3,3,16,256]{3,2,1,0:T(8,128)(2,1)S(1)} %fusion.60), channel_id=1, source_target_pairs={{0,16},{1,5},{2,18},{3,7},{4,20},{5,1},{6,22},{7,3},{8,24},{9,13},... | collective-permute-start | bytes 221192 | tf_op jit(solution)/shard_map/ppermute | solution.py:85
  109.1 13.4 %all-to-all-start.2 = ((f32[32,1,2]{2,1,0:T(1,128)}), f32[32,1,2]{2,1,0:T(1,128)}, u32[]{:S(2)}, u32[]{:S(2)}) async-start(f32[32,1,2]{2,1,0:T(1,128)} %broadcast_in_dim.19), calls=%async_computation.2 | async-start | bytes 32768 | tf_op jit(solution)/shard_map/all_to_all | solution.py:175
  127.4 6.2 %collective-permute-start.10 = (bf16[3,3,16,256]{3,2,1,0:T(8,128)(2,1)}, bf16[3,3,16,256]{3,2,1,0:T(8,128)(2,1)}, u32[]{:S(2)}, u32[]{:S(2)}) collective-permute-start(bf16[3,3,16,256]{3,2,1,0:T(8,128)(2,1)} %fusion.83), channel_id=1, source_target_pairs={{0,16},{1,17},{2,18},{3,19},{4,20},{5,21},{6,22},{7,23},{8,24},{9,... | collective-permute-start | bytes 221192 | tf_op jit(solution)/shard_map/ppermute | solution.py:85
  135.9 5.5 %collective-permute-start.11 = (bf16[3,3,2,16,256]{4,3,2,1,0:T(8,128)(2,1)}, bf16[3,3,2,16,256]{4,3,2,1,0:T(8,128)(2,1)}, u32[]{:S(2)}, u32[]{:S(2)}) collective-permute-start(bf16[3,3,2,16,256]{4,3,2,1,0:T(8,128)(2,1)} %pad_maximum_fusion.5), channel_id=1, source_target_pairs={{0,8},{1,9},{2,10},{3,11},{4,12},{5,13},{6,14},{7,15},{8,0},{9,1},... | collective-permute-start | bytes 442376 | tf_op jit(solution)/shard_map/ppermute | solution.py:85
  143.8 8.5 %collective-permute-start.12 = (bf16[3,3,2,2,16,256]{5,4,3,2,1,0:T(8,128)(2,1)}, bf16[3,3,2,2,16,256]{5,4,3,2,1,0:T(8,128)(2,1)}, u32[]{:S(2)}, u32[]{:S(2)}) collective-permute-start(bf16[3,3,2,2,16,256]{5,4,3,2,1,0:T(8,128)(2,1)} %pad_maximum_fusion.3), channel_id=1, source_target_pairs={{0,4},{1,5},{2,6},{3,7},{4,0},{5,1},{6,2},{7,3},{8,12},{9,13},{10,... | collective-permute-start | bytes 884744 | tf_op jit(solution)/shard_map/ppermute | solution.py:85
  145.6 9.9 %collective-permute-start.15 = (bf16[8,512]{1,0:T(8,128)(2,1)S(1)}, bf16[8,512]{1,0:T(8,128)(2,1)S(1)}, u32[]{:S(2)}, u32[]{:S(2)}) collective-permute-start(bf16[8,512]{1,0:T(8,128)(2,1)S(1)} %fusion.82), channel_id=1, source_target_pairs={{0,16},{1,17},{2,18},{3,19},{4,20},{5,21},{6,22},{7,23},{8,24},{9,... | collective-permute-start | bytes 24584 | tf_op jit(solution)/shard_map/ppermute | solution.py:85
  155.1 12.2 %collective-permute-start.13 = (bf16[3,3,2,2,2,16,256]{6,5,4,3,2,1,0:T(8,128)(2,1)}, bf16[3,3,2,2,2,16,256]{6,5,4,3,2,1,0:T(8,128)(2,1)}, u32[]{:S(2)}, u32[]{:S(2)}) collective-permute-start(bf16[3,3,2,2,2,16,256]{6,5,4,3,2,1,0:T(8,128)(2,1)} %pad_maximum_fusion.2), channel_id=1, source_target_pairs={{0,2},{1,3},{2,0},{3,1},{4,6},{5,7},{6,4},{7,5},{8,10},{9,11},{10,... | collective-permute-start | bytes 1769480 | tf_op jit(solution)/shard_map/ppermute | solution.py:85
  156.7 4.1 %collective-permute-start.16 = (bf16[2,8,512]{2,1,0:T(8,128)(2,1)}, bf16[2,8,512]{2,1,0:T(8,128)(2,1)}, u32[]{:S(2)}, u32[]{:S(2)}) collective-permute-start(bf16[2,8,512]{2,1,0:T(8,128)(2,1)} %pad_maximum_fusion.9), channel_id=1, source_target_pairs={{0,8},{1,9},{2,10},{3,11},{4,12},{5,13},{6,14},{7,15},{8,0},{9,1},... | collective-permute-start | bytes 49160 | tf_op jit(solution)/shard_map/ppermute | solution.py:85
  161.5 8.2 %collective-permute-start.17 = (bf16[2,2,8,512]{3,2,1,0:T(8,128)(2,1)S(1)}, bf16[2,2,8,512]{3,2,1,0:T(8,128)(2,1)S(1)}, u32[]{:S(2)}, u32[]{:S(2)}) collective-permute-start(bf16[2,2,8,512]{3,2,1,0:T(8,128)(2,1)S(1)} %pad_maximum_fusion.8), channel_id=1, source_target_pairs={{0,4},{1,5},{2,6},{3,7},{4,0},{5,1},{6,2},{7,3},{8,12},{9,13},{10,... | collective-permute-start | bytes 98312 | tf_op jit(solution)/shard_map/ppermute | solution.py:85
  169.8 7.4 %collective-permute-start.14 = (bf16[3,3,2,2,2,2,16,256]{7,6,5,4,3,2,1,0:T(8,128)(2,1)}, bf16[3,3,2,2,2,2,16,256]{7,6,5,4,3,2,1,0:T(8,128)(2,1)}, u32[]{:S(2)}, u32[]{:S(2)}) collective-permute-start(bf16[3,3,2,2,2,2,16,256]{7,6,5,4,3,2,1,0:T(8,128)(2,1)} %pad_maximum_fusion.1), channel_id=1, source_target_pairs={{0,1},{1,0},{2,3},{3,2},{4,5},{5,4},{6,7},{7,6},{8,9},{9,8},{10,11... | collective-permute-start | bytes 3538952 | tf_op jit(solution)/shard_map/ppermute | solution.py:85
  169.8 4.8 %collective-permute-start.18 = (bf16[2,2,2,8,512]{4,3,2,1,0:T(8,128)(2,1)S(1)}, bf16[2,2,2,8,512]{4,3,2,1,0:T(8,128)(2,1)S(1)}, u32[]{:S(2)}, u32[]{:S(2)}) collective-permute-start(bf16[2,2,2,8,512]{4,3,2,1,0:T(8,128)(2,1)S(1)} %pad_maximum_fusion.7), channel_id=1, source_target_pairs={{0,2},{1,3},{2,0},{3,1},{4,6},{5,7},{6,4},{7,5},{8,10},{9,11},{10,... | collective-permute-start | bytes 196616 | tf_op jit(solution)/shard_map/ppermute | solution.py:85
  207.7 5.5 %collective-permute-start.25 = (bf16[2,2,2,2,8,512]{5,4,0,1,2,3:T(8,128)(2,1)S(1)}, bf16[2,2,2,2,8,512]{5,4,0,1,2,3:T(8,128)(2,1)S(1)}, u32[]{:S(2)}, u32[]{:S(2)}) collective-permute-start(bf16[2,2,2,2,8,512]{5,4,0,1,2,3:T(8,128)(2,1)S(1)} %fusion.45), channel_id=1, source_target_pairs={{0,1},{1,0},{2,3},{3,2},{4,5},{5,4},{6,7},{7,6},{8,9},{9,8},{10,11... | collective-permute-start | bytes 393224 | tf_op jit(solution)/shard_map/ppermute | solution.py:85
  212.4 12.1 %collective-permute-start.21 = (bf16[3,3,2,2,2,16,256]{6,5,1,0,2,3,4:T(8,128)(2,1)S(1)}, bf16[3,3,2,2,2,16,256]{6,5,1,0,2,3,4:T(8,128)(2,1)S(1)}, u32[]{:S(2)}, u32[]{:S(2)}) collective-permute-start(bf16[3,3,2,2,2,16,256]{6,5,1,0,2,3,4:T(8,128)(2,1)S(1)} %fusion.33), channel_id=1, source_target_pairs={{0,2},{1,9},{2,0},{3,11},{4,6},{5,13},{6,4},{7,15},{8,10},{9,1},{1... | collective-permute-start | bytes 1769480 | tf_op jit(solution)/shard_map/ppermute | solution.py:85
  213.2 9.8 %collective-permute-start.26 = (bf16[2,2,2,8,512]{4,3,0,1,2:T(8,128)(2,1)S(1)}, bf16[2,2,2,8,512]{4,3,0,1,2:T(8,128)(2,1)S(1)}, u32[]{:S(2)}, u32[]{:S(2)}) collective-permute-start(bf16[2,2,2,8,512]{4,3,0,1,2:T(8,128)(2,1)S(1)} %fusion.63), channel_id=1, source_target_pairs={{0,2},{1,9},{2,0},{3,11},{4,6},{5,13},{6,4},{7,15},{8,10},{9,1},{1... | collective-permute-start | bytes 196616 | tf_op jit(solution)/shard_map/ppermute | solution.py:85
  223.1 5.5 %collective-permute-start.27 = (bf16[2,2,8,512]{3,2,0,1:T(8,128)(2,1)S(1)}, bf16[2,2,8,512]{3,2,0,1:T(8,128)(2,1)S(1)}, u32[]{:S(2)}, u32[]{:S(2)}) collective-permute-start(bf16[2,2,8,512]{3,2,0,1:T(8,128)(2,1)S(1)} %fusion.73), channel_id=1, source_target_pairs={{0,4},{1,17},{2,6},{3,19},{4,0},{5,21},{6,2},{7,23},{8,12},{9,25},... | collective-permute-start | bytes 98312 | tf_op jit(solution)/shard_map/ppermute | solution.py:85
  224.7 8.5 %collective-permute-start.22 = (bf16[3,3,2,2,16,256]{5,4,1,0,2,3:T(8,128)(2,1)S(1)}, bf16[3,3,2,2,16,256]{5,4,1,0,2,3:T(8,128)(2,1)S(1)}, u32[]{:S(2)}, u32[]{:S(2)}) collective-permute-start(bf16[3,3,2,2,16,256]{5,4,1,0,2,3:T(8,128)(2,1)S(1)} %fusion.35), channel_id=1, source_target_pairs={{0,4},{1,17},{2,6},{3,19},{4,0},{5,21},{6,2},{7,23},{8,12},{9,25},... | collective-permute-start | bytes 884744 | tf_op jit(solution)/shard_map/ppermute | solution.py:85
  228.6 5.2 %collective-permute-start.28 = (bf16[2,8,512]{2,1,0:T(8,128)(2,1)S(1)}, bf16[2,8,512]{2,1,0:T(8,128)(2,1)S(1)}, u32[]{:S(2)}, u32[]{:S(2)}) collective-permute-start(bf16[2,8,512]{2,1,0:T(8,128)(2,1)S(1)} %fusion.75), channel_id=1, source_target_pairs={{0,8},{1,3},{2,10},{3,1},{4,12},{5,7},{6,14},{7,5},{8,0},{9,11},{1... | collective-permute-start | bytes 49160 | tf_op jit(solution)/shard_map/ppermute | solution.py:85
  233.3 5.2 %collective-permute-start.23 = (bf16[3,3,2,16,256]{4,3,1,0,2:T(8,128)(2,1)S(1)}, bf16[3,3,2,16,256]{4,3,1,0,2:T(8,128)(2,1)S(1)}, u32[]{:S(2)}, u32[]{:S(2)}) collective-permute-start(bf16[3,3,2,16,256]{4,3,1,0,2:T(8,128)(2,1)S(1)} %fusion.43), channel_id=1, source_target_pairs={{0,8},{1,3},{2,10},{3,1},{4,12},{5,7},{6,14},{7,5},{8,0},{9,11},{1... | collective-permute-start | bytes 442376 | tf_op jit(solution)/shard_map/ppermute | solution.py:85
  233.9 5.9 %collective-permute-start.29 = (bf16[8,512]{1,0:T(8,128)(2,1)S(1)}, bf16[8,512]{1,0:T(8,128)(2,1)S(1)}, u32[]{:S(2)}, u32[]{:S(2)}) collective-permute-start(bf16[8,512]{1,0:T(8,128)(2,1)S(1)} %fusion.77), channel_id=1, source_target_pairs={{0,16},{1,5},{2,18},{3,7},{4,20},{5,1},{6,22},{7,3},{8,24},{9,13},... | collective-permute-start | bytes 24584 | tf_op jit(solution)/shard_map/ppermute | solution.py:85
  238.6 5.9 %collective-permute-start.24 = (bf16[3,3,16,256]{3,2,1,0:T(8,128)(2,1)S(1)}, bf16[3,3,16,256]{3,2,1,0:T(8,128)(2,1)S(1)}, u32[]{:S(2)}, u32[]{:S(2)}) collective-permute-start(bf16[3,3,16,256]{3,2,1,0:T(8,128)(2,1)S(1)} %fusion.61), channel_id=1, source_target_pairs={{0,16},{1,5},{2,18},{3,7},{4,20},{5,1},{6,22},{7,3},{8,24},{9,13},... | collective-permute-start | bytes 221192 | tf_op jit(solution)/shard_map/ppermute | solution.py:85
  247.8 11.9 %all-to-all-start.3 = ((f32[32,1,2]{2,1,0:T(1,128)}), f32[32,1,2]{2,1,0:T(1,128)S(1)}, u32[]{:S(2)}, u32[]{:S(2)}) async-start(f32[32,1,2]{2,1,0:T(1,128)} %broadcast_in_dim.20), calls=%async_computation.3 | async-start | bytes 32768 | tf_op jit(solution)/shard_map/all_to_all | solution.py:175
  (44 other events, 382.2 us)
